TPU v7x, 32 devices: a whole 2x2x4 slice. The times are simulated.
32 devices in a mesh: groups: 2 (over y), ctx: 8 (over z, x), tensor: 2 (over core).
Axes of the slice: x: 2, y: 2, z: 4, core: 2. Of those that a mesh axis runs over, the one named last changes fastest.
Arguments:
- light_query: bfloat16 [2048, 4096], P(('groups', 'ctx'), 'tensor'), parts along dimension 0, may hold values from -6 to 6
- light_key: bfloat16 [2048, 4096], P(('groups', 'ctx'), 'tensor'), parts along dimension 0, may hold values from -6 to 6
- light_value: bfloat16 [2048, 4096], P(('groups', 'ctx'), 'tensor'), parts along dimension 0, may hold values from -500 to 500
- light_gate: bfloat16 [2048, 4096], P(('groups', 'ctx'), 'tensor'), parts along dimension 0, may hold values from -6 to 6
- log_decay: float32 [32, 2048], P('tensor', ('groups', 'ctx')), parts along dimension 1, may hold values from -2.2 to 0
- norm_gain: float32 [4096], P('tensor'), may hold values from 0.1 to 1.9
- soft_query: bfloat16 [2048, 4096], P(('groups', 'ctx'), 'tensor'), parts along dimension 0, may hold values from -9 to 9
- soft_key: bfloat16 [2048, 512], P(('groups', 'ctx'), 'tensor'), parts along dimension 0, may hold values from -9 to 9
- soft_value: bfloat16 [2048, 512], P(('groups', 'ctx'), 'tensor'), parts along dimension 0, may hold values from -6 to 6
- segment_ids: int32 [2048], P(('groups', 'ctx')), parts along dimension 0, may hold values from 0 to 3, never falling along the last dimension, each value on 1 to 512 neighbouring positions
Outputs:
- light_out: bfloat16 [2048, 4096], P(('groups', 'ctx'), 'tensor'), parts along dimension 0
- soft_out: bfloat16 [2048, 4096], P(('groups', 'ctx'), 'tensor'), parts along dimension 0
There are 2 independent parts, one for each index of `groups`. A program takes and returns all parts, laid end to end along the dimension named above; an argument that names none is the same for every part. Nothing has to cross between parts.
Inputs may be any that keep to these rules, and one draw needn't show every extreme that they name: `segment_ids`: segment ids never fall along the slab; every prompt covers 1 to 512 consecutive positions and some prompt covers exactly 512.
All inputs are finite; a program needn't handle non-finite values.
Results may differ from a plain program's by a relative error of at most 0.007.
Values may be sent and summed in bfloat16 or wider, within the bound.
No kernel may reach another device: no remote copies, remote signals or barrier semaphores. Data moves between devices by JAX's collectives and lax.ppermute only.
A program may use at most 256 MiB of HBM per device.

v0:
```python
import jax
import jax.numpy as jnp
from jax import lax
from jax.sharding import PartitionSpec as P

NEG_BIG = -1e30


def prefix(shard, axis, join, neutral):
    place = lax.axis_index(axis)
    gathered = jax.tree.map(
        lambda a, kind: lax.all_gather(a.astype(kind), axis),
        shard,
        (jnp.bfloat16, jnp.bfloat16, jnp.bfloat16, jnp.bfloat16),
    )
    state = jax.tree.map(lambda a, e: jnp.zeros_like(a) + jnp.asarray(e, a.dtype), shard, neutral)

    def one(step, state):
        return join(
            state,
            jax.tree.map(
                lambda a, own: lax.dynamic_index_in_dim(a, step, 0, False).astype(own.dtype),
                gathered,
                shard,
            ),
        )

    return lax.fori_loop(0, place, one, state)


def passed_along(block, axis, distance):
    devices = range(lax.axis_size(axis))
    route = [(i - distance, i) for i in devices if i - distance in devices]
    return lax.ppermute(block, axis, route)


def link_states(former, latter):
    former_first, former_last, former_decay, former_state = former
    latter_first, latter_last, latter_decay, latter_state = latter
    former_live = former_first > 0.5
    latter_live = latter_first > 0.5
    joined = (former_last == latter_first) & (latter_first == latter_last)
    carried = jnp.where(joined, latter_decay, 0.0)
    merged_state = jnp.where(
        latter_live, latter_state + carried[:, None, None] * former_state, former_state
    )
    merged_decay = jnp.where(
        former_live, jnp.where(latter_live, former_decay * latter_decay, former_decay), latter_decay
    )
    merged_first = jnp.where(former_live, former_first, latter_first)
    merged_last = jnp.where(latter_live, latter_last, former_last)
    return (merged_first, merged_last, merged_decay, merged_state)


def light_layer(light_query, light_key, light_value, light_gate, log_decay, norm_gain, seg_code):
    tok_rows = light_query.shape[0]
    heads_here = log_decay.shape[0]
    head_size = light_query.shape[1] // heads_here
    query_heads = light_query.reshape(tok_rows, heads_here, head_size)
    key_heads = light_key.reshape(tok_rows, heads_here, head_size)
    value_heads = light_value.reshape(tok_rows, heads_here, head_size)
    decay_sum = jnp.cumsum(log_decay, axis=1)
    token_position = jnp.arange(tok_rows)
    allowed = (seg_code[:, None] == seg_code[None, :]) & (
        token_position[None, :] <= token_position[:, None]
    )
    decay_gap = jnp.where(allowed[None], decay_sum[:, :, None] - decay_sum[:, None, :], -jnp.inf)
    products = jnp.einsum(
        "thd,shd->hts", query_heads, key_heads, preferred_element_type=jnp.float32
    )
    weights = (products * jnp.exp(decay_gap)).astype(jnp.bfloat16)
    mixed = jnp.einsum("hts,shd->thd", weights, value_heads, preferred_element_type=jnp.float32)
    to_end = jnp.where(
        (seg_code == seg_code[-1])[None, :], jnp.exp(decay_sum[:, -1:] - decay_sum), 0.0
    )
    key_weighted = (key_heads * to_end.T[:, :, None]).astype(jnp.bfloat16)
    local_state = jnp.einsum(
        "shd,she->hde", key_weighted, value_heads, preferred_element_type=jnp.float32
    )
    block_first = seg_code[:1]
    block_last = seg_code[-1:]
    block_decay = jnp.exp(decay_sum[:, -1])
    blank = (
        jnp.zeros((1,), jnp.float32),
        jnp.zeros((1,), jnp.float32),
        jnp.zeros((heads_here,), jnp.float32),
        jnp.zeros_like(local_state),
    )
    incoming = prefix(
        (block_first, block_last, block_decay, local_state), "ctx", link_states, blank
    )
    incoming_last = incoming[1]
    incoming_state = incoming[3]
    uses_state = seg_code == incoming_last
    carried_in = jnp.einsum(
        "thd,hde->the",
        query_heads.astype(jnp.float32),
        incoming_state,
        precision=lax.Precision.HIGHEST,
    )
    scale_in = jnp.where(uses_state[None, :], jnp.exp(decay_sum), 0.0)
    mixed = mixed + carried_in * scale_in.T[:, :, None]
    squares = jnp.sum(mixed * mixed, axis=(1, 2))
    squares = lax.psum(squares, "tensor")
    features = heads_here * head_size * lax.axis_size("tensor")
    inverse = lax.rsqrt(squares / features + 1e-06)
    gate_open = jax.nn.sigmoid(light_gate.astype(jnp.float32)).reshape(
        tok_rows, heads_here, head_size
    )
    normed = mixed * inverse[:, None, None] * norm_gain.reshape(heads_here, head_size) * gate_open
    return normed.reshape(tok_rows, heads_here * head_size).astype(jnp.bfloat16)


def attend(carry_state, queries, key_block, value_block, key_code, query_code, causal, score_scale):
    run_max, run_total, run_sum = carry_state
    scores = (
        jnp.einsum("tkgd,skd->kgts", queries, key_block, preferred_element_type=jnp.float32)
        * score_scale
    )
    allowed = query_code[:, None] == key_code.astype(jnp.float32)[None, :]
    if causal is not None:
        allowed = allowed & causal
    scores = jnp.where(allowed, scores, NEG_BIG)
    new_max = jnp.maximum(run_max, jnp.max(scores, axis=-1))
    shrink = jnp.exp(run_max - new_max)
    prob_block = jnp.exp(scores - new_max[..., None])
    run_total = run_total * shrink + jnp.sum(prob_block, axis=-1)
    run_sum = run_sum * shrink[..., None] + jnp.einsum(
        "kgts,skd->kgtd",
        prob_block.astype(jnp.bfloat16),
        value_block,
        preferred_element_type=jnp.float32,
    )
    return (new_max, run_total, run_sum)


def soft_layer(soft_query, soft_key, soft_value, seg_code, heads_here):
    tok_rows = soft_query.shape[0]
    head_size = soft_query.shape[1] // heads_here
    kv_here = soft_key.shape[1] // head_size
    group = heads_here // kv_here
    queries = soft_query.reshape(tok_rows, kv_here, group, head_size)
    key_heads = soft_key.reshape(tok_rows, kv_here, head_size)
    value_heads = soft_value.reshape(tok_rows, kv_here, head_size)
    score_scale = head_size ** (-0.5)
    code_wire = seg_code.astype(jnp.bfloat16)
    token_position = jnp.arange(tok_rows)
    causal = token_position[None, :] <= token_position[:, None]
    carry_state = (
        jnp.full((kv_here, group, tok_rows), NEG_BIG, jnp.float32),
        jnp.zeros((kv_here, group, tok_rows), jnp.float32),
        jnp.zeros((kv_here, group, tok_rows, head_size), jnp.float32),
    )
    carry_state = attend(
        carry_state, queries, key_heads, value_heads, code_wire, seg_code, causal, score_scale
    )
    reach_span = min(4, lax.axis_size("ctx") // 2)

    def pass_step(step_index, pass_carry):
        moving, inner_state = pass_carry
        moving = passed_along((moving[0], moving[1], moving[2]), "ctx", 1)
        inner_state = attend(
            inner_state, queries, moving[0], moving[1], moving[2], seg_code, None, score_scale
        )
        return (moving, inner_state)

    unused, carry_state = lax.fori_loop(
        0, reach_span, pass_step, ((key_heads, value_heads, code_wire), carry_state)
    )
    run_max, run_total, run_sum = carry_state
    output = (
        (run_sum / run_total[..., None])
        .transpose(2, 0, 1, 3)
        .reshape(tok_rows, heads_here * head_size)
    )
    return output.astype(jnp.bfloat16)


def on_device(
    light_query,
    light_key,
    light_value,
    light_gate,
    log_decay,
    norm_gain,
    soft_query,
    soft_key,
    soft_value,
    segment_ids,
):
    seg_code = segment_ids.astype(jnp.float32) + 1.0
    light_out = light_layer(
        light_query, light_key, light_value, light_gate, log_decay, norm_gain, seg_code
    )
    soft_out = soft_layer(soft_query, soft_key, soft_value, seg_code, log_decay.shape[0])
    return (light_out, soft_out)


def solution(mesh):
    in_specs = (
        P(("groups", "ctx"), "tensor"),
        P(("groups", "ctx"), "tensor"),
        P(("groups", "ctx"), "tensor"),
        P(("groups", "ctx"), "tensor"),
        P("tensor", ("groups", "ctx")),
        P("tensor"),
        P(("groups", "ctx"), "tensor"),
        P(("groups", "ctx"), "tensor"),
        P(("groups", "ctx"), "tensor"),
        P(("groups", "ctx")),
    )
    out_specs = (P(("groups", "ctx"), "tensor"), P(("groups", "ctx"), "tensor"))
    return jax.shard_map(
        on_device, mesh=mesh, in_specs=in_specs, out_specs=out_specs, check_vma=False
    )
```

profile of v0, /device:TPU:27, one launch (start us, length us, event | category | flops | bytes accessed | tf_op | source)
XLA Modules:
  0.0 155.4 jit_solution(16771228735265800746)
XLA Ops:
  7.2 0.7 convert_convert_fusion
  8.0 0.6 slice.13
  8.5 1.3 broadcast_compare_fusion.2
  9.8 1.0 reduce_window_sum.11
  11.0 1.3 copy.77
  12.4 1.1 convolution_convert_fusion
  13.5 0.6 slice.21
  14.1 1.2 dynamic-slice
  16.0 1.4 dynamic-update-slice.1
  17.4 0.8 dynamic-update-slice
  18.6 14.0 %all-reduce.3 = (bf16[8]{0:T(256)(128)(2,1)S(1)}, bf16[8]{0:T(256)(128)(2,1)S(1)}, bf16[128]{0:T(256)(128)(2,1)S(1)}) all-reduce(bf16[8]{0:T(256)(128)(2,1)S(1)} %dynamic-update-slice, bf16[8]{0:T(256)(128)(2,1)S(1)} %dynamic-update-slice.1, bf16[128]{0:T(256)(128)(2,1)S(1)} %dynamic-update-slice.2), channel_id=2, replica_groups=mesh['groups'=2,'ctx'=8,'tensor'=2] {'ctx'}, use_global_device_ids=true, to_apply=%add | all-reduce | flops 144 | bytes 576
  32.9 1.3 copy.55
  35.6 0.5 convolution_add_fusion.1
  36.1 51.0 %while.36 = (s32[]{:T(128)}, bf16[128,2,128]{2,0,1:T(8,128)(2,1)S(1)}, bf16[128,2,128]{2,0,1:T(8,128)(2,1)S(1)}, bf16[128]{0:T(256)(128)(2,1)S(1)}, f32[2,8,128]...) while((s32[]{:T(128)}, ...), condition=%wide.region_10.11_spmd, body=%wide.region_7.10_spmd.sunk | while | flops 137121920 | bytes 6884829 | solution.py:167
  36.1 1.3 collective-permute-start.2
  37.4 1.3 collective-permute-start
  38.7 1.3 collective-permute-start.1
  40.0 0.8 collective-permute-done.2
  40.9 2.1 %collective-permute-done = bf16[128,2,128]{2,0,1:T(8,128)(2,1)S(1)} collective-permute-done((bf16[128,2,128]{2,0,1:T(8,128)(2,1)S(1)}, bf16[128,2,128]{2,0,1:T(8,128)(2,1)S(1)}, u32[]{:S(2)}, u32[]{:S(2)}) %collective-permute-start) | collective-permute-done | bytes 65568 | tf_op jit(solution)/shard_map/while/body/eval_jaxpr/ppermute | solution.py:34
  43.6 1.3 collective-permute-done.1
  45.0 0.7 convolution_add_fusion.3
  45.7 1.3 collective-permute-start.2
  47.0 1.3 collective-permute-start
  48.3 1.3 collective-permute-start.1
  49.6 1.7 %collective-permute-done.2 = bf16[128]{0:T(256)(128)(2,1)S(1)} collective-permute-done((bf16[128]{0:T(256)(128)(2,1)S(1)}, bf16[128]{0:T(256)(128)(2,1)S(1)}, u32[]{:S(2)}, u32[]{:S(2)}) %collective-permute-start.2) | collective-permute-done | bytes 288 | tf_op jit(solution)/shard_map/while/body/eval_jaxpr/ppermute | solution.py:34
  51.4 4.0 %collective-permute-done = bf16[128,2,128]{2,0,1:T(8,128)(2,1)S(1)} collective-permute-done((bf16[128,2,128]{2,0,1:T(8,128)(2,1)S(1)}, bf16[128,2,128]{2,0,1:T(8,128)(2,1)S(1)}, u32[]{:S(2)}, u32[]{:S(2)}) %collective-permute-start) | collective-permute-done | bytes 65568 | tf_op jit(solution)/shard_map/while/body/eval_jaxpr/ppermute | solution.py:34
  56.0 1.5 collective-permute-done.1
  57.6 0.7 convolution_add_fusion.3
  58.3 1.3 collective-permute-start.2
  59.6 1.3 collective-permute-start
  60.9 1.3 collective-permute-start.1
  62.2 4.0 %collective-permute-done.2 = bf16[128]{0:T(256)(128)(2,1)S(1)} collective-permute-done((bf16[128]{0:T(256)(128)(2,1)S(1)}, bf16[128]{0:T(256)(128)(2,1)S(1)}, u32[]{:S(2)}, u32[]{:S(2)}) %collective-permute-start.2) | collective-permute-done | bytes 288 | tf_op jit(solution)/shard_map/while/body/eval_jaxpr/ppermute | solution.py:34
  66.3 4.0 %collective-permute-done = bf16[128,2,128]{2,0,1:T(8,128)(2,1)S(1)} collective-permute-done((bf16[128,2,128]{2,0,1:T(8,128)(2,1)S(1)}, bf16[128,2,128]{2,0,1:T(8,128)(2,1)S(1)}, u32[]{:S(2)}, u32[]{:S(2)}) %collective-permute-start) | collective-permute-done | bytes 65568 | tf_op jit(solution)/shard_map/while/body/eval_jaxpr/ppermute | solution.py:34
  71.0 1.5 collective-permute-done.1
  72.5 0.7 convolution_add_fusion.3
  73.2 1.3 collective-permute-start.2
  74.5 1.3 collective-permute-start
  75.8 1.3 collective-permute-start.1
  77.1 4.8 %collective-permute-done.2 = bf16[128]{0:T(256)(128)(2,1)S(1)} collective-permute-done((bf16[128]{0:T(256)(128)(2,1)S(1)}, bf16[128]{0:T(256)(128)(2,1)S(1)}, u32[]{:S(2)}, u32[]{:S(2)}) %collective-permute-start.2) | collective-permute-done | bytes 288 | tf_op jit(solution)/shard_map/while/body/eval_jaxpr/ppermute | solution.py:34
  82.0 2.5 %collective-permute-done = bf16[128,2,128]{2,0,1:T(8,128)(2,1)S(1)} collective-permute-done((bf16[128,2,128]{2,0,1:T(8,128)(2,1)S(1)}, bf16[128,2,128]{2,0,1:T(8,128)(2,1)S(1)}, u32[]{:S(2)}, u32[]{:S(2)}) %collective-permute-start) | collective-permute-done | bytes 65568 | tf_op jit(solution)/shard_map/while/body/eval_jaxpr/ppermute | solution.py:34
  85.1 1.3 collective-permute-done.1
  86.4 0.7 convolution_add_fusion.3
  87.8 0.9 copy.103
  88.9 1.3 add_divide_fusion
  90.5 1.9 %all-gather.6.cloned.1.call-done = bf16[128,128,128]{2,1,0:T(8,128)(2,1)} async-done(((bf16[16,128,128]{2,1,0:T(8,128)(2,1)}), bf16[128,128,128]{2,1,0:T(8,128)(2,1)}) %all-gather.6.cloned.1.call-update) | async-done | bytes 4194320 | tf_op jit(solution)/shard_map/all_gather | solution.py:12
  92.5 37.9 %while.35 = (s32[]{:T(128)}, f32[1]{0:T(128)}, f32[16,128,128]{2,1,0:T(8,128)S(1)}, s32[]{:T(128)}, bf16[8,1]{0,1:T(2,128)(2,1)S(1)}, /*index=5*/bf16[8,1]{0,1:T...) while((s32[]{:T(128)}, f32[1]{0:T(128)}, ...), condition=%wide.region_2.3_spmd, body=%wide.region_1.2_spmd.sunk | while | flops 1048618 | bytes 2621806 | solution.py:28
  92.5 0.7 constant_dynamic-slice_fusion.4
  96.0 1.3 fusion.67
  97.9 0.7 constant_dynamic-slice_fusion.4
  101.4 1.3 fusion.67
  103.3 0.7 constant_dynamic-slice_fusion.4
  106.8 1.3 fusion.67
  108.8 0.7 constant_dynamic-slice_fusion.4
  112.2 1.3 fusion.67
  114.2 0.7 constant_dynamic-slice_fusion.4
  117.6 1.3 fusion.67
  119.6 0.7 constant_dynamic-slice_fusion.4
  123.0 1.3 fusion.67
  125.0 0.7 constant_dynamic-slice_fusion.4
  128.4 1.3 fusion.67
  130.4 3.0 %fusion.16 = f32[128,16,128]{0,2,1:T(8,128)} fusion(f32[16,128,128]{2,1,0:T(8,128)S(1)} %get-tuple-element.120, f32[128,16]{0,1:T(8,128)S(1)} %select_bitcast_fusion, bf16[128,2048]{1,0:T(8,128)(2,1)} %param.14), kind=kOutput, calls=%fused_computation.32 | convolution fusion | flops 402915328 | bytes 2629632 | tf_op jit(solution)/shard_map/thd,hde->the/dot_general | solution.py:95
  133.5 2.1 %multiply_reduce_fusion = (f32[128]{0:T(128)S(1)}, f32[128,16,128]{0,2,1:T(8,128)S(1)}) fusion(f32[128,16,128]{0,2,1:T(8,128)} %fusion.16, bf16[128,16,128]{0,2,1:T(8,128)(2,1)S(1)} %bitcast.129, f32[16,128]{1,0:T(8,128)S(1)} %reduce_window_sum.11, pred[128,128]{1,0:T(8,128)(4,1)S(1)} %get-tuple-element.194, bf16[128,2048]{1,0:T(8,128)(2,1)S(1)} %copy-done, ...), kind=kOutput, calls=%fused_computation.39 | convolution fusion | flops 136052608 | bytes 3695104 | tf_op jit(solution)/shard_map/hts,shd->thd/dot_general | solution.py:72
  135.6 11.6 %psum.7 = f32[128]{0:T(128)S(1)} all-reduce(f32[128]{0:T(128)S(1)} %get-tuple-element.198), channel_id=1, replica_groups=mesh['groups'=2,'ctx'=8,'tensor'=2] {'tensor'}, use_global_device_ids=true, to_apply=%region_4.5 | all-reduce | flops 128 | bytes 1024 | tf_op jit(solution)/shard_map/psum | solution.py:104
  147.5 1.0 copy.64
  (86 shorter events, 6.4 us)
Async XLA Ops:
  7.2 5.2 %copy-start = (bf16[128,2048]{1,0:T(8,128)(2,1)S(1)}, bf16[128,2048]{1,0:T(8,128)(2,1)}, u32[]{:S(2)}) copy-start(bf16[128,2048]{1,0:T(8,128)(2,1)} %param.16) | copy-start | bytes 1572868
  7.2 27.0 %copy-start.1 = (bf16[128,256]{1,0:T(8,128)(2,1)S(1)}, bf16[128,256]{1,0:T(8,128)(2,1)}, u32[]{:S(2)}) copy-start(bf16[128,256]{1,0:T(8,128)(2,1)} %param.21) | copy-start | bytes 196612
  7.2 27.2 %copy-start.2 = (bf16[128,256]{1,0:T(8,128)(2,1)S(1)}, bf16[128,256]{1,0:T(8,128)(2,1)}, u32[]{:S(2)}) copy-start(bf16[128,256]{1,0:T(8,128)(2,1)} %param.22) | copy-start | bytes 196612
  7.2 85.2 %all-gather.6.cloned.1.call-start = ((), (), s32[]{:S(2)}) async-start(), calls=%async_computation | async-start | bytes 4718592 | tf_op jit(solution)/shard_map/all_gather | solution.py:12
  36.1 4.7 %collective-permute-start.2 = (bf16[128]{0:T(256)(128)(2,1)S(1)}, bf16[128]{0:T(256)(128)(2,1)S(1)}, u32[]{:S(2)}, u32[]{:S(2)}) collective-permute-start(bf16[128]{0:T(256)(128)(2,1)S(1)} %get-tuple-element.368), channel_id=1, source_target_pairs={{0,2},{2,4},{4,6},{6,8},{8,10},{10,12},{12,14},{1,3},{3,5},{5,7},{... | collective-permute-start | bytes 776 | tf_op jit(solution)/shard_map/while/body/eval_jaxpr/ppermute | solution.py:34
  37.4 5.6 %collective-permute-start = (bf16[128,2,128]{2,0,1:T(8,128)(2,1)S(1)}, bf16[128,2,128]{2,0,1:T(8,128)(2,1)S(1)}, u32[]{:S(2)}, u32[]{:S(2)}) collective-permute-start(bf16[128,2,128]{2,0,1:T(8,128)(2,1)S(1)} %get-tuple-element.366), channel_id=1, source_target_pairs={{0,2},{2,4},{4,6},{6,8},{8,10},{10,12},{12,14},{1,3},{3,5},{5,7},{... | collective-permute-start | bytes 196616 | tf_op jit(solution)/shard_map/while/body/eval_jaxpr/ppermute | solution.py:34
  38.7 6.3 %collective-permute-start.1 = (bf16[128,2,128]{2,0,1:T(8,128)(2,1)S(1)}, bf16[128,2,128]{2,0,1:T(8,128)(2,1)S(1)}, u32[]{:S(2)}, u32[]{:S(2)}) collective-permute-start(bf16[128,2,128]{2,0,1:T(8,128)(2,1)S(1)} %get-tuple-element.367), channel_id=1, source_target_pairs={{0,2},{2,4},{4,6},{6,8},{8,10},{10,12},{12,14},{1,3},{3,5},{5,7},{... | collective-permute-start | bytes 196616 | tf_op jit(solution)/shard_map/while/body/eval_jaxpr/ppermute | solution.py:34
  45.7 5.6 %collective-permute-start.2 = (bf16[128]{0:T(256)(128)(2,1)S(1)}, bf16[128]{0:T(256)(128)(2,1)S(1)}, u32[]{:S(2)}, u32[]{:S(2)}) collective-permute-start(bf16[128]{0:T(256)(128)(2,1)S(1)} %get-tuple-element.368), channel_id=1, source_target_pairs={{0,2},{2,4},{4,6},{6,8},{8,10},{10,12},{12,14},{1,3},{3,5},{5,7},{... | collective-permute-start | bytes 776 | tf_op jit(solution)/shard_map/while/body/eval_jaxpr/ppermute | solution.py:34
  47.0 8.5 %collective-permute-start = (bf16[128,2,128]{2,0,1:T(8,128)(2,1)S(1)}, bf16[128,2,128]{2,0,1:T(8,128)(2,1)S(1)}, u32[]{:S(2)}, u32[]{:S(2)}) collective-permute-start(bf16[128,2,128]{2,0,1:T(8,128)(2,1)S(1)} %get-tuple-element.366), channel_id=1, source_target_pairs={{0,2},{2,4},{4,6},{6,8},{8,10},{10,12},{12,14},{1,3},{3,5},{5,7},{... | collective-permute-start | bytes 196616 | tf_op jit(solution)/shard_map/while/body/eval_jaxpr/ppermute | solution.py:34
  48.3 9.3 %collective-permute-start.1 = (bf16[128,2,128]{2,0,1:T(8,128)(2,1)S(1)}, bf16[128,2,128]{2,0,1:T(8,128)(2,1)S(1)}, u32[]{:S(2)}, u32[]{:S(2)}) collective-permute-start(bf16[128,2,128]{2,0,1:T(8,128)(2,1)S(1)} %get-tuple-element.367), channel_id=1, source_target_pairs={{0,2},{2,4},{4,6},{6,8},{8,10},{10,12},{12,14},{1,3},{3,5},{5,7},{... | collective-permute-start | bytes 196616 | tf_op jit(solution)/shard_map/while/body/eval_jaxpr/ppermute | solution.py:34
  58.3 7.9 %collective-permute-start.2 = (bf16[128]{0:T(256)(128)(2,1)S(1)}, bf16[128]{0:T(256)(128)(2,1)S(1)}, u32[]{:S(2)}, u32[]{:S(2)}) collective-permute-start(bf16[128]{0:T(256)(128)(2,1)S(1)} %get-tuple-element.368), channel_id=1, source_target_pairs={{0,2},{2,4},{4,6},{6,8},{8,10},{10,12},{12,14},{1,3},{3,5},{5,7},{... | collective-permute-start | bytes 776 | tf_op jit(solution)/shard_map/while/body/eval_jaxpr/ppermute | solution.py:34
  59.6 10.8 %collective-permute-start = (bf16[128,2,128]{2,0,1:T(8,128)(2,1)S(1)}, bf16[128,2,128]{2,0,1:T(8,128)(2,1)S(1)}, u32[]{:S(2)}, u32[]{:S(2)}) collective-permute-start(bf16[128,2,128]{2,0,1:T(8,128)(2,1)S(1)} %get-tuple-element.366), channel_id=1, source_target_pairs={{0,2},{2,4},{4,6},{6,8},{8,10},{10,12},{12,14},{1,3},{3,5},{5,7},{... | collective-permute-start | bytes 196616 | tf_op jit(solution)/shard_map/while/body/eval_jaxpr/ppermute | solution.py:34
  60.9 11.6 %collective-permute-start.1 = (bf16[128,2,128]{2,0,1:T(8,128)(2,1)S(1)}, bf16[128,2,128]{2,0,1:T(8,128)(2,1)S(1)}, u32[]{:S(2)}, u32[]{:S(2)}) collective-permute-start(bf16[128,2,128]{2,0,1:T(8,128)(2,1)S(1)} %get-tuple-element.367), channel_id=1, source_target_pairs={{0,2},{2,4},{4,6},{6,8},{8,10},{10,12},{12,14},{1,3},{3,5},{5,7},{... | collective-permute-start | bytes 196616 | tf_op jit(solution)/shard_map/while/body/eval_jaxpr/ppermute | solution.py:34
  73.2 8.7 %collective-permute-start.2 = (bf16[128]{0:T(256)(128)(2,1)S(1)}, bf16[128]{0:T(256)(128)(2,1)S(1)}, u32[]{:S(2)}, u32[]{:S(2)}) collective-permute-start(bf16[128]{0:T(256)(128)(2,1)S(1)} %get-tuple-element.368), channel_id=1, source_target_pairs={{0,2},{2,4},{4,6},{6,8},{8,10},{10,12},{12,14},{1,3},{3,5},{5,7},{... | collective-permute-start | bytes 776 | tf_op jit(solution)/shard_map/while/body/eval_jaxpr/ppermute | solution.py:34
  74.5 10.0 %collective-permute-start = (bf16[128,2,128]{2,0,1:T(8,128)(2,1)S(1)}, bf16[128,2,128]{2,0,1:T(8,128)(2,1)S(1)}, u32[]{:S(2)}, u32[]{:S(2)}) collective-permute-start(bf16[128,2,128]{2,0,1:T(8,128)(2,1)S(1)} %get-tuple-element.366), channel_id=1, source_target_pairs={{0,2},{2,4},{4,6},{6,8},{8,10},{10,12},{12,14},{1,3},{3,5},{5,7},{... | collective-permute-start | bytes 196616 | tf_op jit(solution)/shard_map/while/body/eval_jaxpr/ppermute | solution.py:34
  75.8 10.6 %collective-permute-start.1 = (bf16[128,2,128]{2,0,1:T(8,128)(2,1)S(1)}, bf16[128,2,128]{2,0,1:T(8,128)(2,1)S(1)}, u32[]{:S(2)}, u32[]{:S(2)}) collective-permute-start(bf16[128,2,128]{2,0,1:T(8,128)(2,1)S(1)} %get-tuple-element.367), channel_id=1, source_target_pairs={{0,2},{2,4},{4,6},{6,8},{8,10},{10,12},{12,14},{1,3},{3,5},{5,7},{... | collective-permute-start | bytes 196616 | tf_op jit(solution)/shard_map/while/body/eval_jaxpr/ppermute | solution.py:34
  92.5 37.9 %copy-start.4 = (s32[128]{0:T(128)S(1)}, s32[128]{0:T(128)}, u32[]{:S(2)}) copy-start(s32[128]{0:T(128)} %param.23) | copy-start | bytes 1540
  130.4 16.8 %copy-start.3 = (f32[2048]{0:T(1024)S(1)}, f32[2048]{0:T(1024)}, u32[]{:S(2)}) copy-start(f32[2048]{0:T(1024)} %param.19) | copy-start | bytes 24580
Sparse Core Ops, SparseCore 0:
  13.7 78.6 all-gather.5
where the time goes:
time: 157 us; the launch traced here: 155 us
  waiting for transfers between devices  31.7 us (20%)
  blocking collectives  25.6 us (16%)
  loops' own time  24.4 us (16%)
  local copies, waits for them, and re-layouts  16.1 us (10%)
  other arithmetic  15.9 us (10%)
  starting transfers between devices  15.5 us (10%)
  between operations  14.9 us (9%)
  matrix products  11.1 us (7%)
    ppermute x12, waiting for transfers between devices, passed_along(): return lax.ppermute(block, axis, route)  29.8 us
    another operation x1, loops' own time, prefix(): return lax.fori_loop(0, place, one, state)  24 us
    ppermute x12, starting transfers between devices, passed_along(): return lax.ppermute(block, axis, route)  15.5 us
    unnamed x1, blocking collectives  14 us
    psum x1, blocking collectives, light_layer(): squares = lax.psum(squares, 'tensor')  11.6 us
    select_n x7, other arithmetic, link_states(): jnp.where(latter_live, latter_state + carried[:, None, None] * former_sta...  9.09 us
    unnamed x22, local copies, waits for them, and re-layouts  7.18 us
    dynamic_slice x7, local copies, waits for them, and re-layouts, one(): lax.dynamic_index_in_dim(a, step, 0, False).astype(own.dtype)  4.69 us
  transfers between devices with their start and end apart: 13, of which 13 were waited for; matrix products, arithmetic and copies ran while one was open for 11% of the time, Pallas kernels for 0%

commit v1 on v0

v1 whole, which is shorter than its diff:
```python
import jax
import jax.numpy as jnp
from jax import lax
from jax.sharding import PartitionSpec as P

NEG_BIG = -1e30
MAXDOC = 512
F32 = jnp.float32
BF16 = jnp.bfloat16


def shifted(block, axis, distance):
    devices = lax.axis_size(axis)
    route = [(i, i + distance) for i in range(devices - distance)]
    return lax.ppermute(block, axis, route)


def light_local(light_query, light_key, light_value, decay_sum, code):
    tok_rows, heads_here = light_query.shape[0], decay_sum.shape[0]
    head_size = light_query.shape[1] // heads_here
    query_heads = light_query.reshape(tok_rows, heads_here, head_size)
    key_heads = light_key.reshape(tok_rows, heads_here, head_size)
    value_heads = light_value.reshape(tok_rows, heads_here, head_size)
    token_position = jnp.arange(tok_rows)
    allowed = (code[:, None] == code[None, :]) & (token_position[None, :] <= token_position[:, None])
    decay_gap = jnp.where(allowed[None], decay_sum[:, :, None] - decay_sum[:, None, :], -jnp.inf)
    products = jnp.einsum("thd,shd->hts", query_heads, key_heads, preferred_element_type=F32)
    weights = (products * jnp.exp(decay_gap)).astype(BF16)
    mixed = jnp.einsum("hts,shd->thd", weights, value_heads, preferred_element_type=F32)
    to_end = jnp.where((code == code[-1])[None, :], jnp.exp(decay_sum[:, -1:] - decay_sum), 0.0)
    key_weighted = (key_heads * to_end.T[:, :, None]).astype(BF16)
    local_state = jnp.einsum("shd,she->hde", key_weighted, value_heads, preferred_element_type=F32)
    return mixed, local_state


def soft_window(soft_query, keys, values, code, code_window, heads_here):
    tok_rows = soft_query.shape[0]
    span = keys.shape[0]
    head_size = soft_query.shape[1] // heads_here
    kv_here = keys.shape[1] // head_size
    group = heads_here // kv_here
    queries = soft_query.reshape(tok_rows, kv_here, group, head_size)
    key_heads = keys.reshape(span, kv_here, head_size)
    value_heads = values.reshape(span, kv_here, head_size)
    key_position = jnp.arange(span)
    query_position = jnp.arange(tok_rows) + (span - tok_rows)
    allowed = (code[:, None] == code_window[None, :]) & (key_position[None, :] <= query_position[:, None])
    scores = jnp.einsum("tkgd,skd->kgts", queries, key_heads, preferred_element_type=F32) * head_size ** (-0.5)
    scores = jnp.where(allowed, scores, NEG_BIG)
    row_max = jnp.max(scores, axis=-1)
    prob_block = jnp.exp(scores - row_max[..., None])
    row_total = jnp.sum(prob_block, axis=-1)
    weighted = jnp.einsum("kgts,skd->kgtd", prob_block.astype(BF16), value_heads, preferred_element_type=F32)
    output = (weighted / row_total[..., None]).transpose(2, 0, 1, 3).reshape(tok_rows, heads_here * head_size)
    return output.astype(BF16)


def on_device(
    light_query,
    light_key,
    light_value,
    light_gate,
    log_decay,
    norm_gain,
    soft_query,
    soft_key,
    soft_value,
    segment_ids,
):
    tok_rows = light_query.shape[0]
    heads_here = log_decay.shape[0]
    head_size = light_query.shape[1] // heads_here
    kv_cols = soft_key.shape[1]
    assert -(-MAXDOC // tok_rows) == 4
    code = segment_ids.astype(F32) + 1.0
    decay_sum = jnp.cumsum(log_decay, axis=1)

    mixed, local_state = light_local(light_query, light_key, light_value, decay_sum, code)
    block_decay = jnp.exp(decay_sum[:, -1])

    soft_kv = jnp.concatenate([soft_key, soft_value], axis=1)
    meta = jnp.concatenate([code, block_decay])
    own = (local_state.astype(BF16), soft_kv, meta)
    from_1 = shifted(own, "ctx", 1)
    from_2 = shifted(own, "ctx", 2)
    state_1, kv_1, meta_1 = from_1
    state_2, kv_2, meta_2 = from_2
    code_1, decay_1 = meta_1[:tok_rows], meta_1[tok_rows:]
    code_2, decay_2 = meta_2[:tok_rows], meta_2[tok_rows:]

    link_1 = (code_2[-1] == code_1[0]) & (code_1[0] == code_1[-1])
    pair_state = state_1.astype(F32) + jnp.where(link_1, decay_1, 0.0)[:, None, None] * state_2.astype(F32)

    relay = (pair_state.astype(BF16), jnp.stack([kv_2, kv_1]), jnp.concatenate([code_2, code_1]))
    from_far = shifted(relay, "ctx", 2)
    state_far, kv_far, code_far = from_far

    link_2 = (code_far[-1] == code_2[0]) & (code_2[0] == code_1[-1])
    carry_scale = jnp.where(link_2, decay_2 * decay_1, 0.0)
    incoming_state = pair_state + carry_scale[:, None, None] * state_far.astype(F32)

    query_heads = light_query.reshape(tok_rows, heads_here, head_size)
    carried_in = jnp.einsum(
        "thd,hde->the", query_heads.astype(F32), incoming_state, precision=lax.Precision.HIGHEST
    )
    uses_state = code == code_1[-1]
    scale_in = jnp.where(uses_state[None, :], jnp.exp(decay_sum), 0.0)
    mixed = mixed + carried_in * scale_in.T[:, :, None]
    squares = jnp.sum(mixed * mixed, axis=(1, 2))
    squares = lax.psum(squares, "tensor")
    features = heads_here * head_size * lax.axis_size("tensor")
    inverse = lax.rsqrt(squares / features + 1e-06)
    gate_open = jax.nn.sigmoid(light_gate.astype(F32)).reshape(tok_rows, heads_here, head_size)
    normed = mixed * inverse[:, None, None] * norm_gain.reshape(heads_here, head_size) * gate_open
    light_out = normed.reshape(tok_rows, heads_here * head_size).astype(BF16)

    kv_window = jnp.concatenate([kv_far[0], kv_far[1], kv_2, kv_1, soft_kv], axis=0)
    code_window = jnp.concatenate([code_far, code_2, code_1, code])
    soft_out = soft_window(
        soft_query, kv_window[:, :kv_cols], kv_window[:, kv_cols:], code, code_window, heads_here
    )
    return (light_out, soft_out)


def solution(mesh):
    in_specs = (
        P(("groups", "ctx"), "tensor"),
        P(("groups", "ctx"), "tensor"),
        P(("groups", "ctx"), "tensor"),
        P(("groups", "ctx"), "tensor"),
        P("tensor", ("groups", "ctx")),
        P("tensor"),
        P(("groups", "ctx"), "tensor"),
        P(("groups", "ctx"), "tensor"),
        P(("groups", "ctx"), "tensor"),
        P(("groups", "ctx")),
    )
    out_specs = (P(("groups", "ctx"), "tensor"), P(("groups", "ctx"), "tensor"))
    return jax.shard_map(
        on_device, mesh=mesh, in_specs=in_specs, out_specs=out_specs, check_vma=False
    )
```

time: 157 us -> 94 us (0.60)
  the two profiles are of different devices: /device:TPU:27 before, /device:TPU:11 now
where the time goes in v1:
time: 94 us; the launch traced here: 93 us
  starting transfers between devices  22.1 us (24%)
  waiting for transfers between devices  21 us (22%)
  local copies, waits for them, and re-layouts  14 us (15%)
  other arithmetic  13.6 us (14%)
  matrix products  10 us (11%)
  blocking collectives  6.55 us (7%)
  between operations  5.78 us (6%)
    ppermute x9, starting transfers between devices, shifted(): return lax.ppermute(block, axis, route)  22.1 us
    ppermute x9, waiting for transfers between devices, shifted(): return lax.ppermute(block, axis, route)  21 us
    unnamed x35, local copies, waits for them, and re-layouts  7.1 us
    psum x1, blocking collectives, on_device(): squares = lax.psum(squares, 'tensor')  6.55 us
    dot_general x1, matrix products, on_device(): jnp.einsum('thd,hde->the', query_heads.astype(F32), incoming_state, preci...  3.51 us
    slice x2, local copies, waits for them, and re-layouts, on_device(): link_2 = (code_far[-1] == code_2[0]) & (code_2[0] == code_1[-1])  2.59 us
    dot_general x1, matrix products, soft_window(): jnp.einsum('kgts,skd->kgtd', prob_block.astype(BF16), value_heads, prefer...  2.23 us
    dot_general x1, matrix products, light_local(): jnp.einsum('hts,shd->thd', weights, value_heads, preferred_element_type=F32)  2.13 us
  transfers between devices with their start and end apart: 9, of which 3 were waited for; matrix products, arithmetic and copies ran while one was open for 29% of the time, Pallas kernels for 0%

profile of v1, /device:TPU:11, one launch (start us, length us, event | category | flops | bytes accessed | tf_op | source)
XLA Modules:
  0.0 93.0 jit_solution(12532592164801104958)
XLA Ops:
  0.6 0.0 copy-start
  0.6 0.0 copy-start.12
  0.7 0.7 convert_add_fusion
  1.4 1.0 %reduce_window_sum.11 = f32[16,128]{1,0:T(8,128)S(1)} reduce-window(f32[16,128]{1,0:T(8,128)} %param.14, f32[]{:T(128)} %constant.9.clone.1), window={size=1x128 pad=0_0x127_0}, to_apply=%region_0.0 | reduce-window | flops 260096 | bytes 16388 | tf_op jit(solution)/shard_map/jit(cumsum)/reduce_window_sum | solution.py:76
  2.4 0.2 slice_reduce_fusion
  2.6 0.6 pad_maximum_fusion.3
  3.2 3.2 %collective-permute-start.1 = (f32[144]{0:T(256)}, f32[144]{0:T(256)}, u32[]{:S(2)}, u32[]{:S(2)}) collective-permute-start(f32[144]{0:T(256)} %pad_maximum_fusion.3), channel_id=1, source_target_pairs={{0,4},{2,6},{4,8},{6,10},{8,12},{10,14},{1,5},{3,7},{5,9},{7,11},{... | collective-permute-start | bytes 1736 | tf_op jit(solution)/shard_map/ppermute | solution.py:15
  6.4 3.2 %collective-permute-start.2 = (f32[144]{0:T(256)}, f32[144]{0:T(256)S(1)}, u32[]{:S(2)}, u32[]{:S(2)}) collective-permute-start(f32[144]{0:T(256)} %pad_maximum_fusion.3), channel_id=1, source_target_pairs={{0,2},{2,4},{4,6},{6,8},{8,10},{10,12},{12,14},{1,3},{3,5},{5,7},{... | collective-permute-start | bytes 1736 | tf_op jit(solution)/shard_map/ppermute | solution.py:15
  9.5 1.0 %copy.29 = bf16[128,256]{0,1:T(8,128)(2,1)S(1)} copy(bf16[128,256]{1,0:T(8,128)(2,1)} %param.17) | data formatting | bytes 131072 | tf_op args[7]
  10.5 1.0 %copy.30 = bf16[128,256]{0,1:T(8,128)(2,1)S(1)} copy(bf16[128,256]{1,0:T(8,128)(2,1)} %param.18) | data formatting | bytes 131072 | tf_op args[8]
  11.5 0.7 pad_maximum_fusion.1
  12.1 1.9 %collective-permute-start.6 = (bf16[128,512]{0,1:T(8,128)(2,1)}, bf16[128,512]{0,1:T(8,128)(2,1)S(1)}, u32[]{:S(2)}, u32[]{:S(2)}) collective-permute-start(bf16[128,512]{0,1:T(8,128)(2,1)} %pad_maximum_fusion.1), channel_id=1, source_target_pairs={{0,4},{2,6},{4,8},{6,10},{8,12},{10,14},{1,5},{3,7},{5,9},{7,11},{... | collective-permute-start | bytes 393224 | tf_op jit(solution)/shard_map/ppermute | solution.py:15
  14.1 3.1 %collective-permute-start.7 = (bf16[128,512]{0,1:T(8,128)(2,1)}, bf16[128,512]{0,1:T(8,128)(2,1)S(1)}, u32[]{:S(2)}, u32[]{:S(2)}) collective-permute-start(bf16[128,512]{0,1:T(8,128)(2,1)} %pad_maximum_fusion.1), channel_id=1, source_target_pairs={{0,2},{2,4},{4,6},{6,8},{8,10},{10,12},{12,14},{1,3},{3,5},{5,7},{... | collective-permute-start | bytes 393224 | tf_op jit(solution)/shard_map/ppermute | solution.py:15
  17.2 0.7 fusion.43
  17.9 1.3 %add_divide_fusion = f32[128,2048]{1,0:T(8,128)S(1)} fusion(bf16[128,2048]{1,0:T(8,128)(2,1)} %param.13), kind=kLoop, calls=%fused_computation.17 | loop fusion | flops 1048576 | bytes 1572864 | tf_op jit(solution)/shard_map/div | solution.py:113
  19.2 0.6 iota_add_fusion
  19.8 0.6 slice.54
  20.4 1.9 %copy.45 = bf16[16,8,16,128]{3,2,1,0:T(8,128)(2,1)} copy(bf16[16,8,16,128]{3,1,2,0:T(8,128)(2,1)} %bitcast.103) | data formatting | bytes 1048576
  22.3 0.0 copy-done.3
  22.3 0.0 copy-done.9
  22.3 1.3 %copy.40 = bf16[128,2048]{0,1:T(8,128)(2,1)S(1)} copy(bf16[128,2048]{1,0:T(8,128)(2,1)} %param.11) | data formatting | bytes 1048576 | tf_op jit(solution)/shard_map/reshape | solution.py:22
  23.6 0.3 copy.28
  24.0 0.0 copy-start.1
  24.0 0.0 collective-permute-done.2
  24.0 0.0 copy-start.7
  24.0 0.6 fusion.49
  24.5 0.0 copy-done.12
  24.5 1.2 %broadcast_compare_fusion = (pred[128]{0:T(512)(128)(4,1)S(1)}, pred[128]{0:T(512)(128)(4,1)S(1)}) fusion(f32[]{:T(128)} %bitcast.6, s32[128]{0:T(128)S(1)} %copy-done.12, f32[]{:T(128)} %bitcast.2), kind=kLoop, calls=%fused_computation.69 | loop fusion | flops 512 | bytes 776 | tf_op jit(solution)/shard_map/eq | solution.py:106
  25.7 0.0 copy-done.7
  25.8 0.7 select_bitcast_fusion
  26.4 1.1 %convolution_convert_fusion = bf16[16,128,128]{2,1,0:T(8,128)(2,1)} fusion(bf16[128,16,128]{0,2,1:T(8,128)(2,1)S(1)} %bitcast.98, f32[128,16]{0,1:T(8,128)S(1)} %get-tuple-element.9, bf16[128,2048]{1,0:T(8,128)(2,1)S(1)} %copy-done), kind=kOutput, calls=%fused_computation.13 | convolution fusion | flops 68157440 | bytes 1581056 | tf_op jit(solution)/shard_map/shd,she->hde/dot_general | solution.py:32
  27.6 1.9 %collective-permute-start = (bf16[16,128,128]{2,1,0:T(8,128)(2,1)}, bf16[16,128,128]{2,1,0:T(8,128)(2,1)S(1)}, u32[]{:S(2)}, u32[]{:S(2)}) collective-permute-start(bf16[16,128,128]{2,1,0:T(8,128)(2,1)} %convolution_convert_fusion), channel_id=1, source_target_pairs={{0,2},{2,4},{4,6},{6,8},{8,10},{10,12},{12,14},{1,3},{3,5},{5,7},{... | collective-permute-start | bytes 1572872 | tf_op jit(solution)/shard_map/ppermute | solution.py:15
  29.5 1.9 %collective-permute-start.3 = (bf16[16,128,128]{2,1,0:T(8,128)(2,1)}, bf16[16,128,128]{2,1,0:T(8,128)(2,1)}, u32[]{:S(2)}, u32[]{:S(2)}) collective-permute-start(bf16[16,128,128]{2,1,0:T(8,128)(2,1)} %convolution_convert_fusion), channel_id=1, source_target_pairs={{0,4},{2,6},{4,8},{6,10},{8,12},{10,14},{1,5},{3,7},{5,9},{7,11},{... | collective-permute-start | bytes 1572872 | tf_op jit(solution)/shard_map/ppermute | solution.py:15
  31.4 0.7 slice.61
  32.1 0.0 collective-permute-done.1
  32.1 0.6 slice.60
  32.7 0.0 copy-done.10
  32.7 0.6 pad_maximum_fusion.4
  33.3 1.9 %collective-permute-start.4 = (f32[256]{0:T(256)}, f32[256]{0:T(256)}, u32[]{:S(2)}, u32[]{:S(2)}) collective-permute-start(f32[256]{0:T(256)} %pad_maximum_fusion.4), channel_id=1, source_target_pairs={{0,4},{2,6},{4,8},{6,10},{8,12},{10,14},{1,5},{3,7},{5,9},{7,11},{... | collective-permute-start | bytes 3080 | tf_op jit(solution)/shard_map/ppermute | solution.py:15
  35.3 1.3 %fusion.48 = (f32[1]{0:T(128)}, f32[1]{0:T(128)}) fusion(f32[144]{0:T(256)} %collective-permute-done.1), kind=kLoop, calls=%fused_computation.75 | loop fusion | bytes 16 | tf_op jit(solution)/shard_map/slice | solution.py:98
  40.2 12.8 %collective-permute-done.4 = f32[256]{0:T(256)} collective-permute-done((f32[256]{0:T(256)}, f32[256]{0:T(256)}, u32[]{:S(2)}, u32[]{:S(2)}) %collective-permute-start.4) | collective-permute-done | bytes 1056 | tf_op jit(solution)/shard_map/ppermute | solution.py:15
  53.0 1.3 %slice.62 = f32[1]{0:T(128)} slice(f32[256]{0:T(256)} %collective-permute-done.4), slice={[255:256]} | slice | bytes 8 | tf_op jit(solution)/shard_map/slice | solution.py:98
  55.5 1.2 %broadcast_select_fusion = (f32[16]{0:T(128)}, f32[16]{0:T(128)S(1)}) fusion(pred[]{:T(512)S(6)} %and.18, f32[144]{0:T(256)} %collective-permute-done.1, f32[144]{0:T(256)} %copy-done.7, pred[]{:T(512)S(6)} %and.17), kind=kLoop, calls=%fused_computation.64 | loop fusion | flops 48 | bytes 258 | tf_op jit(solution)/shard_map/jit(_where)/select_n | solution.py:99
  56.7 0.0 collective-permute-done.6
  56.7 0.0 collective-permute-done.7
  56.7 2.2 %collective-permute-start.8 = (bf16[2,128,512]{1,2,0:T(8,128)(2,1)S(1)}, bf16[2,128,512]{1,2,0:T(8,128)(2,1)S(1)}, u32[]{:S(2)}, u32[]{:S(2)}) collective-permute-start(bf16[2,128,512]{1,2,0:T(8,128)(2,1)S(1)} %pad_maximum_fusion), channel_id=1, source_target_pairs={{0,4},{2,6},{4,8},{6,10},{8,12},{10,14},{1,5},{3,7},{5,9},{7,11},{... | collective-permute-start | bytes 786440 | tf_op jit(solution)/shard_map/ppermute | solution.py:15
  58.9 0.7 pad_maximum_fusion.2
  59.6 0.8 fusion.40
  60.5 3.3 %collective-permute-done.8 = bf16[2,128,512]{1,2,0:T(8,128)(2,1)S(1)} collective-permute-done((bf16[2,128,512]{1,2,0:T(8,128)(2,1)S(1)}, bf16[2,128,512]{1,2,0:T(8,128)(2,1)S(1)}, u32[]{:S(2)}, u32[]{:S(2)}) %collective-permute-start.8) | collective-permute-done | bytes 262176 | tf_op jit(solution)/shard_map/ppermute | solution.py:15
  64.0 0.1 fusion.47
  64.1 1.0 %fusion.2 = (f32[2,8,128]{2,1,0:T(8,128)S(1)}, f32[2,640,128,8]{2,1,3,0:T(8,128)S(1)}) fusion(pred[128,640]{0,1:T(8,128)(4,1)S(1)} %fusion.40, bf16[640,2,128,1]{0,2,3,1:T(8,128)(2,1)S(1)} %bitcast.102, bf16[128,2,8,128]{3,2,1,0:T(8,128)(2,1)S(1)} %bitcast.100), kind=kOutput, calls=%fused_computation.4 | convolution fusion | flops 339474432 | bytes 6184960 | tf_op jit(solution)/shard_map/tkgd,skd->kgts/dot_general | solution.py:48
  65.1 1.1 %fusion = f32[2,8,128]{2,1,0:T(8,128)S(1)} fusion(f32[2,640,128,8]{2,1,3,0:T(8,128)S(1)} %get-tuple-element.21, f32[2,8,128]{2,1,0:T(8,128)S(1)} %get-tuple-element.20, pred[128,640]{0,1:T(8,128)(4,1)S(1)} %fusion.40), kind=kLoop, calls=%fused_computation.2 | loop fusion | flops 5240832 | bytes 5341184 | tf_op jit(solution)/shard_map/reduce_sum | solution.py:52
  66.2 0.0 collective-permute-done
  66.2 0.0 collective-permute-done.3
  66.3 1.3 %fusion.20 = bf16[16,128,128]{2,1,0:T(8,128)(2,1)S(1)} fusion(bf16[16,128,128]{2,1,0:T(8,128)(2,1)} %collective-permute-done.3, bf16[16,128,128]{2,1,0:T(8,128)(2,1)S(1)} %collective-permute-done, f32[16]{0:T(128)S(1)} %get-tuple-element.11), kind=kLoop, calls=%fused_computation.27 | loop fusion | flops 1310720 | bytes 1572928 | tf_op jit(solution)/shard_map/convert_element_type | solution.py:94
  67.5 2.7 %collective-permute-start.5 = (bf16[16,128,128]{2,1,0:T(8,128)(2,1)S(1)}, bf16[16,128,128]{2,1,0:T(8,128)(2,1)}, u32[]{:S(2)}, u32[]{:S(2)}) collective-permute-start(bf16[16,128,128]{2,1,0:T(8,128)(2,1)S(1)} %fusion.20), channel_id=1, source_target_pairs={{0,4},{2,6},{4,8},{6,10},{8,12},{10,14},{1,5},{3,7},{5,9},{7,11},{... | collective-permute-start | bytes 1572872 | tf_op jit(solution)/shard_map/ppermute | solution.py:15
  70.3 2.2 %divide_convert_fusion = bf16[128,2,8,128]{0,3,2,1:T(8,128)(2,1)} fusion(bf16[640,2,128,1]{0,2,3,1:T(8,128)(2,1)S(1)} %bitcast.107, f32[2,640,128,8]{2,1,3,0:T(8,128)S(1)} %get-tuple-element.21, f32[2,8,128]{2,1,0:T(8,128)S(1)} %get-tuple-element.20, pred[128,640]{0,1:T(8,128)(4,1)S(1)} %fusion.40, f32[128,2,8]{0,2,1:T(8,128)S(1)} %bitcast.109), kind=kOutput, calls=%fused_computation.15 | convolution fusion | flops 341311488 | bytes 6193152 | tf_op jit(solution)/shard_map/kgts,skd->kgtd/dot_general | solution.py:53
  72.5 2.1 %copy.35 = bf16[128,2048]{1,0:T(8,128)(2,1)} copy(bf16[128,2048]{0,1:T(8,128)(2,1)} %bitcast.104) | data formatting | bytes 1048576
  74.6 4.9 %collective-permute-done.5 = bf16[16,128,128]{2,1,0:T(8,128)(2,1)} collective-permute-done((bf16[16,128,128]{2,1,0:T(8,128)(2,1)S(1)}, bf16[16,128,128]{2,1,0:T(8,128)(2,1)}, u32[]{:S(2)}, u32[]{:S(2)}) %collective-permute-start.5) | collective-permute-done | bytes 524320 | tf_op jit(solution)/shard_map/ppermute | solution.py:15
  79.5 3.5 %fusion.10 = f32[128,16,128]{0,2,1:T(8,128)} fusion(bf16[16,128,128]{2,1,0:T(8,128)(2,1)} %collective-permute-done.5, bf16[16,128,128]{2,1,0:T(8,128)(2,1)} %collective-permute-done.3, bf16[16,128,128]{2,1,0:T(8,128)(2,1)S(1)} %collective-permute-done, f32[128,16]{0,1:T(8,128)S(1)} %get-tuple-element.8, f32[16]{0:T(128)S(1)} %copy-done.8, ...), kind=kOutput, calls=%fused_computation.12 | convolution fusion | flops 404750336 | bytes 3154048 | tf_op jit(solution)/shard_map/thd,hde->the/dot_general | solution.py:103
  83.0 2.1 %multiply_reduce_fusion = (f32[128]{0:T(128)S(1)}, f32[128,16,128]{0,2,1:T(8,128)S(1)}) fusion(f32[128,16,128]{0,2,1:T(8,128)} %fusion.10, bf16[128,16,128]{0,2,1:T(8,128)(2,1)S(1)} %bitcast.99, f32[16,128]{1,0:T(8,128)S(1)} %reduce_window_sum.11, pred[128,128]{1,0:T(8,128)(4,1)S(1)} %copy-done.2, bf16[128,2048]{1,0:T(8,128)(2,1)S(1)} %copy-done, ...), kind=kOutput, calls=%fused_computation.18 | convolution fusion | flops 136052608 | bytes 3695104 | tf_op jit(solution)/shard_map/hts,shd->thd/dot_general | solution.py:29
  85.1 6.6 %psum.7 = f32[128]{0:T(128)S(1)} all-reduce(f32[128]{0:T(128)S(1)} %get-tuple-element.18), channel_id=1, replica_groups=mesh['groups'=2,'ctx'=8,'tensor'=2] {'tensor'}, use_global_device_ids=true, to_apply=%region_2.3 | all-reduce | flops 128 | bytes 1024 | tf_op jit(solution)/shard_map/psum | solution.py:110
  91.7 0.3 multiply_convert_fusion
  92.0 1.0 %copy.34 = bf16[128,2048]{1,0:T(8,128)(2,1)} copy(bf16[128,2048]{0,1:T(8,128)(2,1)S(1)} %bitcast.101) | data formatting | bytes 1048576
  (25 shorter events, 0.2 us)
Async XLA Ops:
  0.6 25.8 %copy-start = (bf16[128,2048]{1,0:T(8,128)(2,1)S(1)}, bf16[128,2048]{1,0:T(8,128)(2,1)}, u32[]{:S(2)}) copy-start(bf16[128,2048]{1,0:T(8,128)(2,1)} %param.12) | copy-start | bytes 1572868
  0.6 23.9 %copy-start.12 = (s32[128]{0:T(128)S(1)}, s32[128]{0:T(128)}, u32[]{:S(2)}) copy-start(s32[128]{0:T(128)} %param.19) | copy-start | bytes 1540
  1.4 20.9 %copy-start.3 = (f32[128]{0:T(128)}, f32[128]{0:T(128)S(1)}, u32[]{:S(2)}) copy-start(f32[128]{0:T(128)S(1)} %convert_add_fusion) | copy-start | bytes 1540
  2.5 19.8 %copy-start.9 = (f32[16]{0:T(128)}, f32[16]{0:T(128)S(1)}, u32[]{:S(2)}) copy-start(f32[16]{0:T(128)S(1)} %slice_reduce_fusion) | copy-start | bytes 196
  3.2 28.9 %collective-permute-start.1 = (f32[144]{0:T(256)}, f32[144]{0:T(256)}, u32[]{:S(2)}, u32[]{:S(2)}) collective-permute-start(f32[144]{0:T(256)} %pad_maximum_fusion.3), channel_id=1, source_target_pairs={{0,4},{2,6},{4,8},{6,10},{8,12},{10,14},{1,5},{3,7},{5,9},{7,11},{... | collective-permute-start | bytes 1736 | tf_op jit(solution)/shard_map/ppermute | solution.py:15
  6.4 17.6 %collective-permute-start.2 = (f32[144]{0:T(256)}, f32[144]{0:T(256)S(1)}, u32[]{:S(2)}, u32[]{:S(2)}) collective-permute-start(f32[144]{0:T(256)} %pad_maximum_fusion.3), channel_id=1, source_target_pairs={{0,2},{2,4},{4,6},{6,8},{8,10},{10,12},{12,14},{1,3},{3,5},{5,7},{... | collective-permute-start | bytes 1736 | tf_op jit(solution)/shard_map/ppermute | solution.py:15
  12.1 44.5 %collective-permute-start.6 = (bf16[128,512]{0,1:T(8,128)(2,1)}, bf16[128,512]{0,1:T(8,128)(2,1)S(1)}, u32[]{:S(2)}, u32[]{:S(2)}) collective-permute-start(bf16[128,512]{0,1:T(8,128)(2,1)} %pad_maximum_fusion.1), channel_id=1, source_target_pairs={{0,4},{2,6},{4,8},{6,10},{8,12},{10,14},{1,5},{3,7},{5,9},{7,11},{... | collective-permute-start | bytes 393224 | tf_op jit(solution)/shard_map/ppermute | solution.py:15
  14.1 42.6 %collective-permute-start.7 = (bf16[128,512]{0,1:T(8,128)(2,1)}, bf16[128,512]{0,1:T(8,128)(2,1)S(1)}, u32[]{:S(2)}, u32[]{:S(2)}) collective-permute-start(bf16[128,512]{0,1:T(8,128)(2,1)} %pad_maximum_fusion.1), channel_id=1, source_target_pairs={{0,2},{2,4},{4,6},{6,8},{8,10},{10,12},{12,14},{1,3},{3,5},{5,7},{... | collective-permute-start | bytes 393224 | tf_op jit(solution)/shard_map/ppermute | solution.py:15
  24.0 40.1 %copy-start.1 = (bf16[16,8,16,128]{3,2,1,0:T(8,128)(2,1)S(1)}, bf16[16,8,16,128]{3,2,1,0:T(8,128)(2,1)}, u32[]{:S(2)}) copy-start(bf16[16,8,16,128]{3,2,1,0:T(8,128)(2,1)} %copy.45) | copy-start | bytes 1572868
  24.0 1.8 %copy-start.7 = (f32[144]{0:T(256)}, f32[144]{0:T(256)S(1)}, u32[]{:S(2)}) copy-start(f32[144]{0:T(256)S(1)} %collective-permute-done.2) | copy-start | bytes 1732
  27.6 38.7 %collective-permute-start = (bf16[16,128,128]{2,1,0:T(8,128)(2,1)}, bf16[16,128,128]{2,1,0:T(8,128)(2,1)S(1)}, u32[]{:S(2)}, u32[]{:S(2)}) collective-permute-start(bf16[16,128,128]{2,1,0:T(8,128)(2,1)} %convolution_convert_fusion), channel_id=1, source_target_pairs={{0,2},{2,4},{4,6},{6,8},{8,10},{10,12},{12,14},{1,3},{3,5},{5,7},{... | collective-permute-start | bytes 1572872 | tf_op jit(solution)/shard_map/ppermute | solution.py:15
  29.5 36.8 %collective-permute-start.3 = (bf16[16,128,128]{2,1,0:T(8,128)(2,1)}, bf16[16,128,128]{2,1,0:T(8,128)(2,1)}, u32[]{:S(2)}, u32[]{:S(2)}) collective-permute-start(bf16[16,128,128]{2,1,0:T(8,128)(2,1)} %convolution_convert_fusion), channel_id=1, source_target_pairs={{0,4},{2,6},{4,8},{6,10},{8,12},{10,14},{1,5},{3,7},{5,9},{7,11},{... | collective-permute-start | bytes 1572872 | tf_op jit(solution)/shard_map/ppermute | solution.py:15
  32.1 0.6 copy-start.10
  32.7 0.6 copy-start.11
  33.3 19.6 %collective-permute-start.4 = (f32[256]{0:T(256)}, f32[256]{0:T(256)}, u32[]{:S(2)}, u32[]{:S(2)}) collective-permute-start(f32[256]{0:T(256)} %pad_maximum_fusion.4), channel_id=1, source_target_pairs={{0,4},{2,6},{4,8},{6,10},{8,12},{10,14},{1,5},{3,7},{5,9},{7,11},{... | collective-permute-start | bytes 3080 | tf_op jit(solution)/shard_map/ppermute | solution.py:15
  56.7 9.6 %copy-start.5 = (f32[16]{0:T(128)}, f32[16]{0:T(128)S(1)}, u32[]{:S(2)}) copy-start(f32[16]{0:T(128)S(1)} %get-tuple-element.11) | copy-start | bytes 196
  56.7 7.1 %collective-permute-start.8 = (bf16[2,128,512]{1,2,0:T(8,128)(2,1)S(1)}, bf16[2,128,512]{1,2,0:T(8,128)(2,1)S(1)}, u32[]{:S(2)}, u32[]{:S(2)}) collective-permute-start(bf16[2,128,512]{1,2,0:T(8,128)(2,1)S(1)} %pad_maximum_fusion), channel_id=1, source_target_pairs={{0,4},{2,6},{4,8},{6,10},{8,12},{10,14},{1,5},{3,7},{5,9},{7,11},{... | collective-permute-start | bytes 786440 | tf_op jit(solution)/shard_map/ppermute | solution.py:15
  67.5 11.9 %collective-permute-start.5 = (bf16[16,128,128]{2,1,0:T(8,128)(2,1)S(1)}, bf16[16,128,128]{2,1,0:T(8,128)(2,1)}, u32[]{:S(2)}, u32[]{:S(2)}) collective-permute-start(bf16[16,128,128]{2,1,0:T(8,128)(2,1)S(1)} %fusion.20), channel_id=1, source_target_pairs={{0,4},{2,6},{4,8},{6,10},{8,12},{10,14},{1,5},{3,7},{5,9},{7,11},{... | collective-permute-start | bytes 1572872 | tf_op jit(solution)/shard_map/ppermute | solution.py:15
  70.3 9.2 %copy-start.6 = (f32[16]{0:T(128)S(1)}, f32[16]{0:T(128)}, u32[]{:S(2)}) copy-start(f32[16]{0:T(128)} %copy-done.5) | copy-start | bytes 196
  70.3 9.2 %copy-start.8 = (f32[16]{0:T(128)S(1)}, f32[16]{0:T(128)}, u32[]{:S(2)}) copy-start(f32[16]{0:T(128)} %get-tuple-element.10) | copy-start | bytes 196
  70.3 12.7 %copy-start.2 = (pred[128,128]{1,0:T(8,128)(4,1)S(1)}, pred[128,128]{1,0:T(8,128)(4,1)}, u32[]{:S(2)}) copy-start(pred[128,128]{1,0:T(8,128)(4,1)} %fusion.43) | copy-start | bytes 49156
  72.5 19.1 %copy-start.4 = (f32[2048]{0:T(1024)S(1)}, f32[2048]{0:T(1024)}, u32[]{:S(2)}) copy-start(f32[2048]{0:T(1024)} %param.15) | copy-start | bytes 24580

commit v2 on v1

--- a/solution.py
+++ b/solution.py
@@ -33,26 +33,41 @@
     return mixed, local_state
 
 
-def soft_window(soft_query, keys, values, code, code_window, heads_here):
+def soft_window(soft_query, key_heads, value_heads, code, code_window, heads_here):
     tok_rows = soft_query.shape[0]
-    span = keys.shape[0]
-    head_size = soft_query.shape[1] // heads_here
-    kv_here = keys.shape[1] // head_size
+    kv_here, span, head_size = key_heads.shape
     group = heads_here // kv_here
     queries = soft_query.reshape(tok_rows, kv_here, group, head_size)
-    key_heads = keys.reshape(span, kv_here, head_size)
-    value_heads = values.reshape(span, kv_here, head_size)
     key_position = jnp.arange(span)
     query_position = jnp.arange(tok_rows) + (span - tok_rows)
     allowed = (code[:, None] == code_window[None, :]) & (key_position[None, :] <= query_position[:, None])
-    scores = jnp.einsum("tkgd,skd->kgts", queries, key_heads, preferred_element_type=F32) * head_size ** (-0.5)
+    scores = jnp.einsum("tkgd,ksd->kgts", queries, key_heads, preferred_element_type=F32) * head_size ** (-0.5)
     scores = jnp.where(allowed, scores, NEG_BIG)
     row_max = jnp.max(scores, axis=-1)
     prob_block = jnp.exp(scores - row_max[..., None])
     row_total = jnp.sum(prob_block, axis=-1)
-    weighted = jnp.einsum("kgts,skd->kgtd", prob_block.astype(BF16), value_heads, preferred_element_type=F32)
+    weighted = jnp.einsum("kgts,ksd->kgtd", prob_block.astype(BF16), value_heads, preferred_element_type=F32)
     output = (weighted / row_total[..., None]).transpose(2, 0, 1, 3).reshape(tok_rows, heads_here * head_size)
     return output.astype(BF16)
+
+
+def split_parts(value):
+    high = lax.reduce_precision(value, exponent_bits=8, mantissa_bits=7)
+    rest = value - high
+    middle = lax.reduce_precision(rest, exponent_bits=8, mantissa_bits=7)
+    return jnp.concatenate([high, middle, rest - middle])
+
+
+def join_parts(parts):
+    third = parts.shape[0] // 3
+    parts = parts.astype(F32)
+    return (parts[:third] + parts[third : 2 * third]) + parts[2 * third :]
+
+
+def rows_of(flat, width):
+    tile = 16 * width
+    padded = -(-flat.shape[0] // tile) * tile
+    return jnp.pad(flat, (0, padded - flat.shape[0])).reshape(-1, width).astype(BF16)
 
 
 def on_device(
@@ -70,7 +85,7 @@
     tok_rows = light_query.shape[0]
     heads_here = log_decay.shape[0]
     head_size = light_query.shape[1] // heads_here
-    kv_cols = soft_key.shape[1]
+    kv_here = soft_key.shape[1] // head_size
     assert -(-MAXDOC // tok_rows) == 4
     code = segment_ids.astype(F32) + 1.0
     decay_sum = jnp.cumsum(log_decay, axis=1)
@@ -78,26 +93,57 @@
     mixed, local_state = light_local(light_query, light_key, light_value, decay_sum, code)
     block_decay = jnp.exp(decay_sum[:, -1])
 
-    soft_kv = jnp.concatenate([soft_key, soft_value], axis=1)
-    meta = jnp.concatenate([code, block_decay])
-    own = (local_state.astype(BF16), soft_kv, meta)
+    own_keys = soft_key.reshape(tok_rows, kv_here, head_size).transpose(1, 0, 2)
+    own_values = soft_value.reshape(tok_rows, kv_here, head_size).transpose(1, 0, 2)
+    state_rows = heads_here * head_size
+    kv_rows = kv_here * tok_rows
+    own = jnp.concatenate(
+        [
+            local_state.astype(BF16).reshape(state_rows, head_size),
+            own_keys.reshape(kv_rows, head_size),
+            own_values.reshape(kv_rows, head_size),
+            rows_of(jnp.concatenate([code, split_parts(block_decay)]), head_size),
+        ]
+    )
     from_1 = shifted(own, "ctx", 1)
     from_2 = shifted(own, "ctx", 2)
-    state_1, kv_1, meta_1 = from_1
-    state_2, kv_2, meta_2 = from_2
-    code_1, decay_1 = meta_1[:tok_rows], meta_1[tok_rows:]
-    code_2, decay_2 = meta_2[:tok_rows], meta_2[tok_rows:]
+
+    def unpack(block):
+        state = block[:state_rows].reshape(heads_here, head_size, head_size).astype(F32)
+        keys = block[state_rows : state_rows + kv_rows].reshape(kv_here, tok_rows, head_size)
+        values = block[state_rows + kv_rows : state_rows + 2 * kv_rows].reshape(kv_here, tok_rows, head_size)
+        meta = block[state_rows + 2 * kv_rows :].reshape(-1)
+        codes = meta[:tok_rows].astype(F32)
+        decay = join_parts(meta[tok_rows : tok_rows + 3 * heads_here])
+        return state, keys, values, codes, decay
+
+    state_1, keys_1, values_1, code_1, decay_1 = unpack(from_1)
+    state_2, keys_2, values_2, code_2, decay_2 = unpack(from_2)
 
     link_1 = (code_2[-1] == code_1[0]) & (code_1[0] == code_1[-1])
-    pair_state = state_1.astype(F32) + jnp.where(link_1, decay_1, 0.0)[:, None, None] * state_2.astype(F32)
+    pair_state = state_1 + jnp.where(link_1, decay_1, 0.0)[:, None, None] * state_2
 
-    relay = (pair_state.astype(BF16), jnp.stack([kv_2, kv_1]), jnp.concatenate([code_2, code_1]))
+    relay = jnp.concatenate(
+        [
+            pair_state.astype(BF16).reshape(state_rows, head_size),
+            keys_2.reshape(kv_rows, head_size),
+            keys_1.reshape(kv_rows, head_size),
+            values_2.reshape(kv_rows, head_size),
+            values_1.reshape(kv_rows, head_size),
+            rows_of(jnp.concatenate([code_2, code_1]), head_size),
+        ]
+    )
     from_far = shifted(relay, "ctx", 2)
-    state_far, kv_far, code_far = from_far
+    state_far = from_far[:state_rows].reshape(heads_here, head_size, head_size).astype(F32)
+    keys_far = from_far[state_rows : state_rows + 2 * kv_rows].reshape(2, kv_here, tok_rows, head_size)
+    values_far = from_far[state_rows + 2 * kv_rows : state_rows + 4 * kv_rows].reshape(
+        2, kv_here, tok_rows, head_size
+    )
+    code_far = from_far[state_rows + 4 * kv_rows :].reshape(-1)[: 2 * tok_rows].astype(F32)
 
     link_2 = (code_far[-1] == code_2[0]) & (code_2[0] == code_1[-1])
     carry_scale = jnp.where(link_2, decay_2 * decay_1, 0.0)
-    incoming_state = pair_state + carry_scale[:, None, None] * state_far.astype(F32)
+    incoming_state = pair_state + carry_scale[:, None, None] * state_far
 
     query_heads = light_query.reshape(tok_rows, heads_here, head_size)
     carried_in = jnp.einsum(
@@ -114,11 +160,10 @@
     normed = mixed * inverse[:, None, None] * norm_gain.reshape(heads_here, head_size) * gate_open
     light_out = normed.reshape(tok_rows, heads_here * head_size).astype(BF16)
 
-    kv_window = jnp.concatenate([kv_far[0], kv_far[1], kv_2, kv_1, soft_kv], axis=0)
+    key_window = jnp.concatenate([keys_far[0], keys_far[1], keys_2, keys_1, own_keys], axis=1)
+    value_window = jnp.concatenate([values_far[0], values_far[1], values_2, values_1, own_values], axis=1)
     code_window = jnp.concatenate([code_far, code_2, code_1, code])
-    soft_out = soft_window(
-        soft_query, kv_window[:, :kv_cols], kv_window[:, kv_cols:], code, code_window, heads_here
-    )
+    soft_out = soft_window(soft_query, key_window, value_window, code, code_window, heads_here)
     return (light_out, soft_out)
 
 

time: 94 us -> 111 us (1.18)
  the two profiles are of different devices: /device:TPU:11 before, /device:TPU:0 now
where the time goes in v2:
time: 111 us; the launch traced here: 110 us
  local copies, waits for them, and re-layouts  29.2 us (26%)
  starting transfers between devices  25.5 us (23%)
  waiting for transfers between devices  18.7 us (17%)
  other arithmetic  18.4 us (17%)
  matrix products  9.88 us (9%)
  between operations  5.95 us (5%)
  blocking collectives  2.44 us (2%)
    ppermute x3, starting transfers between devices, shifted(): return lax.ppermute(block, axis, route)  25.5 us
    ppermute x3, waiting for transfers between devices, shifted(): return lax.ppermute(block, axis, route)  18.7 us
    unnamed x57, local copies, waits for them, and re-layouts  11 us
    dot_general x1, matrix products, on_device(): jnp.einsum('thd,hde->the', query_heads.astype(F32), incoming_state, preci...  3.96 us
    dot_general x1, matrix products, light_local(): jnp.einsum('hts,shd->thd', weights, value_heads, preferred_element_type=F32)  3.27 us
    slice x2, local copies, waits for them, and re-layouts, unpack(): block[state_rows + kv_rows:state_rows + 2 * kv_rows]  3.13 us
    convert_element_type x2, local copies, waits for them, and re-layouts, unpack(): block[:state_rows].reshape(heads_here, head_size, head_size).astype(F32)  2.62 us
    psum x1, blocking collectives, on_device(): squares = lax.psum(squares, 'tensor')  2.44 us
  transfers between devices with their start and end apart: 3, of which 3 were waited for; matrix products, arithmetic and copies ran while one was open for 10% of the time, Pallas kernels for 0%

profile of v2, /device:TPU:0, one launch (start us, length us, event | category | flops | bytes accessed | tf_op | source)
XLA Modules:
  0.0 110.0 jit_solution(7279763827046362361)
XLA Ops:
  0.6 0.7 convert_add_fusion
  1.4 0.6 slice.119
  1.9 1.3 %broadcast_compare_fusion.1 = pred[128]{0:T(512)(128)(4,1)S(1)} fusion(f32[]{:T(128)} %bitcast.2, s32[128]{0:T(128)} %param.19), kind=kLoop, calls=%fused_computation.109 | loop fusion | flops 384 | bytes 644 | tf_op jit(solution)/shard_map/eq | solution.py:30
  3.3 1.0 reduce_window_sum.11
  4.2 0.2 slice_reduce_fusion
  4.5 1.0 copy.28
  5.5 0.1 copy.29
  5.6 1.0 copy.30
  6.6 0.1 copy.31
  6.7 1.3 %copy.48 = bf16[128,2048]{0,1:T(8,128)(2,1)S(1)} copy(bf16[128,2048]{1,0:T(8,128)(2,1)} %param.11) | data formatting | bytes 1048576 | tf_op jit(solution)/shard_map/reshape | solution.py:22
  8.0 0.3 convolution_convert_fusion
  8.3 0.1 fusion.54
  8.4 0.9 pad_maximum_fusion
  9.3 5.0 %collective-permute-start.1 = (bf16[2576,128]{1,0:T(8,128)(2,1)}, bf16[2576,128]{1,0:T(8,128)(2,1)S(1)}, u32[]{:S(2)}, u32[]{:S(2)}) collective-permute-start(bf16[2576,128]{1,0:T(8,128)(2,1)} %pad_maximum_fusion), channel_id=1, source_target_pairs={{0,4},{2,6},{4,8},{6,10},{8,12},{10,14},{1,5},{3,7},{5,9},{7,11},{... | collective-permute-start | bytes 1978376 | tf_op jit(solution)/shard_map/ppermute | solution.py:15
  14.3 3.4 %collective-permute-start = (bf16[2576,128]{1,0:T(8,128)(2,1)}, bf16[2576,128]{1,0:T(8,128)(2,1)S(1)}, u32[]{:S(2)}, u32[]{:S(2)}) collective-permute-start(bf16[2576,128]{1,0:T(8,128)(2,1)} %pad_maximum_fusion), channel_id=1, source_target_pairs={{0,2},{2,4},{4,6},{6,8},{8,10},{10,12},{12,14},{1,3},{3,5},{5,7},{... | collective-permute-start | bytes 1978376 | tf_op jit(solution)/shard_map/ppermute | solution.py:15
  17.8 1.1 %copy.51 = bf16[16,8,16,128]{3,2,1,0:T(8,128)(2,1)S(1)} copy(bf16[16,8,16,128]{3,1,2,0:T(8,128)(2,1)} %bitcast.144) | data formatting | bytes 1048576
  19.0 1.3 %add_divide_fusion = f32[128,2048]{1,0:T(8,128)S(1)} fusion(bf16[128,2048]{1,0:T(8,128)(2,1)} %param.13), kind=kLoop, calls=%fused_computation.17 | loop fusion | flops 1048576 | bytes 1572864 | tf_op jit(solution)/shard_map/div | solution.py:159
  20.3 1.3 %copy.36 = f32[128,2048]{0,1:T(8,128)} copy(f32[128,2048]{1,0:T(8,128)S(1)} %add_divide_fusion) | data formatting | bytes 2097152 | tf_op jit(solution)/shard_map/div | solution.py:159
  21.6 0.6 iota_add_fusion
  22.2 1.4 %fusion.44 = pred[128,128]{1,0:T(8,128)(4,1)} fusion(f32[128]{0:T(128)} %copy-done.11), kind=kLoop, calls=%fused_computation.55 | loop fusion | flops 49152 | bytes 16896 | tf_op jit(solution)/shard_map/and | solution.py:25
  23.6 5.1 %collective-permute-done.1 = bf16[2576,128]{1,0:T(8,128)(2,1)S(1)} collective-permute-done((bf16[2576,128]{1,0:T(8,128)(2,1)}, bf16[2576,128]{1,0:T(8,128)(2,1)S(1)}, u32[]{:S(2)}, u32[]{:S(2)}) %collective-permute-start.1) | collective-permute-done | bytes 659488 | tf_op jit(solution)/shard_map/ppermute | solution.py:15
  28.7 0.6 fusion.62
  29.3 0.6 fusion.68
  29.9 1.9 %collective-permute-done = bf16[2576,128]{1,0:T(8,128)(2,1)S(1)} collective-permute-done((bf16[2576,128]{1,0:T(8,128)(2,1)}, bf16[2576,128]{1,0:T(8,128)(2,1)S(1)}, u32[]{:S(2)}, u32[]{:S(2)}) %collective-permute-start) | collective-permute-done | bytes 659488 | tf_op jit(solution)/shard_map/ppermute | solution.py:15
  31.8 0.6 fusion.63
  32.5 0.6 fusion.69
  36.8 0.7 broadcast_select_fusion.1
  37.5 0.5 copy-done.13
  38.1 2.4 %slice_convert_fusion = (f32[2048,128]{1,0:T(8,128)S(1)}, bf16[3088,128]{1,0:T(8,128)(2,1)}, f32[2048,128]{1,0:T(8,128)S(1)}) fusion(bf16[2576,128]{1,0:T(8,128)(2,1)} %copy-done.4, f32[2048]{0:T(1024)S(1)} %broadcast_bitcast_fusion, bf16[2576,128]{1,0:T(8,128)(2,1)} %copy-done.5), kind=kLoop, calls=%fused_computation.34 | loop fusion | flops 1310719 | bytes 3678208 | tf_op jit(solution)/shard_map/convert_element_type | solution.py:112
  40.4 1.3 %copy.32 = f32[16,128,128]{1,2,0:T(8,128)} copy(f32[16,128,128]{2,1,0:T(8,128)S(1)} %bitcast.133) | data formatting | bytes 2097152 | tf_op jit(solution)/shard_map/convert_element_type | solution.py:112
  41.7 1.6 %fusion.67 = (bf16[256,128]{1,0:T(8,128)(2,1)S(1)}, bf16[3088,128]{1,0:T(8,128)(2,1)}, bf16[256,128]{1,0:T(8,128)(2,1)S(1)}) fusion(bf16[2576,128]{1,0:T(8,128)(2,1)} %copy-done.4, bf16[3088,128]{1,0:T(8,128)(2,1)} %get-tuple-element.25), kind=kLoop, calls=%fused_computation.120 | loop fusion | bytes 327680 | tf_op jit(solution)/shard_map/slice | solution.py:114
  43.4 0.1 copy.40
  43.5 1.5 %fusion.66 = (bf16[256,128]{1,0:T(8,128)(2,1)S(1)}, bf16[3088,128]{1,0:T(8,128)(2,1)}, bf16[256,128]{1,0:T(8,128)(2,1)S(1)}) fusion(bf16[2576,128]{1,0:T(8,128)(2,1)} %copy-done.5, bf16[3088,128]{1,0:T(8,128)(2,1)} %get-tuple-element.16), kind=kLoop, calls=%fused_computation.119 | loop fusion | bytes 327680 | tf_op jit(solution)/shard_map/slice | solution.py:114
  45.0 0.7 copy.41
  45.7 1.5 %constant_dynamic-update-slice_fusion.2 = bf16[3088,128]{1,0:T(8,128)(2,1)} fusion(bf16[3088,128]{1,0:T(8,128)(2,1)} %get-tuple-element.13, bf16[2576,128]{1,0:T(8,128)(2,1)} %copy-done.4), kind=kLoop, calls=%fused_computation.58 | loop fusion | bytes 131072
  47.2 1.5 %constant_dynamic-update-slice_fusion.1 = bf16[3088,128]{1,0:T(8,128)(2,1)} fusion(bf16[3088,128]{1,0:T(8,128)(2,1)} %constant_dynamic-update-slice_fusion.2, bf16[2576,128]{1,0:T(8,128)(2,1)} %copy-done.5), kind=kLoop, calls=%fused_computation.57 | loop fusion | bytes 131072
  48.7 0.6 constant_dynamic-update-slice_fusion
  49.3 17.1 %collective-permute-start.2 = (bf16[3088,128]{1,0:T(8,128)(2,1)}, bf16[3088,128]{1,0:T(8,128)(2,1)}, u32[]{:S(2)}, u32[]{:S(2)}) collective-permute-start(bf16[3088,128]{1,0:T(8,128)(2,1)} %constant_dynamic-update-slice_fusion), channel_id=1, source_target_pairs={{0,4},{2,6},{4,8},{6,10},{8,12},{10,14},{1,5},{3,7},{5,9},{7,11},{... | collective-permute-start | bytes 2371592 | tf_op jit(solution)/shard_map/ppermute | solution.py:15
  66.4 1.3 %copy.33 = f32[16,128,128]{1,2,0:T(8,128)} copy(f32[16,128,128]{2,1,0:T(8,128)S(1)} %bitcast.132) | data formatting | bytes 2097152 | tf_op jit(solution)/shard_map/convert_element_type | solution.py:112
  67.7 1.2 %broadcast_compare_fusion = pred[128]{0:T(512)(128)(4,1)S(1)} fusion(f32[]{:T(128)} %bitcast.15, s32[128]{0:T(128)} %param.19), kind=kLoop, calls=%fused_computation.108 | loop fusion | flops 384 | bytes 644 | tf_op jit(solution)/shard_map/eq | solution.py:152
  68.9 0.7 slice_bitcast_fusion
  69.6 0.6 select_bitcast_fusion
  70.2 11.6 %collective-permute-done.2 = bf16[3088,128]{1,0:T(8,128)(2,1)} collective-permute-done((bf16[3088,128]{1,0:T(8,128)(2,1)}, bf16[3088,128]{1,0:T(8,128)(2,1)}, u32[]{:S(2)}, u32[]{:S(2)}) %collective-permute-start.2) | collective-permute-done | bytes 790560 | tf_op jit(solution)/shard_map/ppermute | solution.py:15
  81.8 0.7 fusion.58
  82.5 0.6 slice.138
  84.4 1.0 fusion.65
  85.3 0.1 copy.39
  85.5 0.1 copy.38
  85.7 0.9 constant_dynamic-update-slice_fusion.6
  86.7 0.6 copy-done.8
  87.3 0.7 copy-done.6
  88.0 1.9 %slice.164 = bf16[2048,128]{1,0:T(8,128)(2,1)} slice(bf16[3088,128]{1,0:T(8,128)(2,1)} %collective-permute-done.2), slice={[0:2048], [0:128]} | slice | bytes 1048576 | tf_op jit(solution)/shard_map/slice | solution.py:137
  89.9 2.3 %copy.34 = f32[16,128,128]{1,2,0:T(8,128)} copy(bf16[16,128,128]{2,1,0:T(8,128)(2,1)} %bitcast.139) | data formatting | bytes 1572864 | tf_op jit(solution)/shard_map/convert_element_type | solution.py:137
  92.2 0.8 broadcast_select_fusion
  93.0 4.0 %fusion.10 = f32[128,16,128]{0,2,1:T(8,128)} fusion(f32[16,128,128]{1,2,0:T(8,128)} %copy.34, f32[16,128,128]{1,2,0:T(8,128)} %copy.33, f32[16,128,128]{1,2,0:T(8,128)S(1)} %copy-done.2, f32[128,16]{0,1:T(8,128)} %select_bitcast_fusion, f32[16]{0:T(128)S(1)} %broadcast_select_fusion, f32[16]{0:T(128)} %copy-done.13, bf16[128,2048]{1,0:T(8,128)(2,1)} %param.10), kind=kOutput, calls=%fused_computation.12 | convolution fusion | flops 403963904 | bytes 4726912 | tf_op jit(solution)/shard_map/thd,hde->the/dot_general | solution.py:149
  97.0 3.3 %multiply_reduce_fusion = (f32[128]{0:T(128)S(1)}, f32[128,16,128]{0,2,1:T(8,128)}) fusion(f32[128,16,128]{0,2,1:T(8,128)} %fusion.10, bf16[128,16,128]{0,2,1:T(8,128)(2,1)} %bitcast.137, f32[16,128]{1,0:T(8,128)S(1)} %reduce_window_sum.11, pred[128,128]{1,0:T(8,128)(4,1)} %fusion.44, bf16[128,2048]{1,0:T(8,128)(2,1)S(1)} %copy-done, ...), kind=kOutput, calls=%fused_computation.18 | convolution fusion | flops 136052608 | bytes 3695104 | tf_op jit(solution)/shard_map/hts,shd->thd/dot_general | solution.py:29
  100.3 2.4 %psum.7 = f32[128]{0:T(128)S(1)} all-reduce(f32[128]{0:T(128)S(1)} %get-tuple-element.36), channel_id=1, replica_groups=mesh['groups'=2,'ctx'=8,'tensor'=2] {'tensor'}, use_global_device_ids=true, to_apply=%region_2.3 | all-reduce | flops 128 | bytes 1024 | tf_op jit(solution)/shard_map/psum | solution.py:156
  102.7 1.6 %multiply_convert_fusion = bf16[128,16,128]{0,2,1:T(8,128)(2,1)S(1)} fusion(f32[128,16,128]{0,2,1:T(8,128)S(1)} %bitcast.134, f32[128,16,128]{0,2,1:T(8,128)} %get-tuple-element.37, f32[16,128]{1,0:T(8,128)S(1)} %bitcast.156, f32[128]{0:T(128)S(1)} %add_rsqrt_fusion), kind=kLoop, calls=%fused_computation.16 | loop fusion | flops 1048576 | bytes 2630144 | tf_op jit(solution)/shard_map/convert_element_type | solution.py:161
  104.3 1.0 copy.43
  105.4 0.2 fusion.43
  105.5 0.9 fusion.2
  106.5 1.1 fusion
  107.5 1.4 %divide_convert_fusion = bf16[128,2,8,128]{0,3,2,1:T(8,128)(2,1)S(1)} fusion(f32[2,640,128,8]{2,1,3,0:T(8,128)S(1)} %get-tuple-element.39, f32[2,8,128]{2,1,0:T(8,128)S(1)} %get-tuple-element.38, pred[128,640]{0,1:T(8,128)(4,1)S(1)} %fusion.43, f32[128,2,8]{0,2,1:T(8,128)S(1)} %bitcast.157, bf16[2,640,128]{1,2,0:T(8,128)(2,1)S(1)} %copy-done.9), kind=kOutput, calls=%fused_computation.15 | convolution fusion | flops 341311488 | bytes 6193152 | tf_op jit(solution)/shard_map/kgts,ksd->kgtd/dot_general | solution.py:49
  109.0 1.0 copy.44
  (56 shorter events, 0.4 us)
Async XLA Ops:
  0.6 7.4 %copy-start = (bf16[128,2048]{1,0:T(8,128)(2,1)S(1)}, bf16[128,2048]{1,0:T(8,128)(2,1)}, u32[]{:S(2)}) copy-start(bf16[128,2048]{1,0:T(8,128)(2,1)} %param.12) | copy-start | bytes 1572868
  1.4 0.6 copy-start.11
  8.0 9.8 %copy-start.3 = (bf16[128,2048]{0,1:T(8,128)(2,1)}, bf16[128,2048]{0,1:T(8,128)(2,1)S(1)}, u32[]{:S(2)}) copy-start(bf16[128,2048]{0,1:T(8,128)(2,1)S(1)} %copy.48) | copy-start | bytes 1572868
  9.3 19.3 %collective-permute-start.1 = (bf16[2576,128]{1,0:T(8,128)(2,1)}, bf16[2576,128]{1,0:T(8,128)(2,1)S(1)}, u32[]{:S(2)}, u32[]{:S(2)}) collective-permute-start(bf16[2576,128]{1,0:T(8,128)(2,1)} %pad_maximum_fusion), channel_id=1, source_target_pairs={{0,4},{2,6},{4,8},{6,10},{8,12},{10,14},{1,5},{3,7},{5,9},{7,11},{... | collective-permute-start | bytes 1978376 | tf_op jit(solution)/shard_map/ppermute | solution.py:15
  14.3 17.5 %collective-permute-start = (bf16[2576,128]{1,0:T(8,128)(2,1)}, bf16[2576,128]{1,0:T(8,128)(2,1)S(1)}, u32[]{:S(2)}, u32[]{:S(2)}) collective-permute-start(bf16[2576,128]{1,0:T(8,128)(2,1)} %pad_maximum_fusion), channel_id=1, source_target_pairs={{0,2},{2,4},{4,6},{6,8},{8,10},{10,12},{12,14},{1,3},{3,5},{5,7},{... | collective-permute-start | bytes 1978376 | tf_op jit(solution)/shard_map/ppermute | solution.py:15
  28.7 8.8 %copy-start.4 = (bf16[2576,128]{1,0:T(8,128)(2,1)}, bf16[2576,128]{1,0:T(8,128)(2,1)S(1)}, u32[]{:S(2)}) copy-start(bf16[2576,128]{1,0:T(8,128)(2,1)S(1)} %collective-permute-done.1) | copy-start | bytes 1978372
  31.8 5.6 %copy-start.5 = (bf16[2576,128]{1,0:T(8,128)(2,1)}, bf16[2576,128]{1,0:T(8,128)(2,1)S(1)}, u32[]{:S(2)}) copy-start(bf16[2576,128]{1,0:T(8,128)(2,1)S(1)} %collective-permute-done) | copy-start | bytes 1978372
  37.4 0.5 copy-start.13
  38.1 10.6 %copy-start.14 = (bf16[128]{0:T(256)(128)(2,1)S(1)}, bf16[128]{0:T(256)(128)(2,1)}, u32[]{:S(2)}) copy-start(bf16[128]{0:T(256)(128)(2,1)} %get-tuple-element.19) | copy-start | bytes 772
  38.1 10.6 %copy-start.15 = (bf16[128]{0:T(256)(128)(2,1)S(1)}, bf16[128]{0:T(256)(128)(2,1)}, u32[]{:S(2)}) copy-start(bf16[128]{0:T(256)(128)(2,1)} %get-tuple-element.22) | copy-start | bytes 772
  41.7 51.3 %copy-start.2 = (f32[16,128,128]{1,2,0:T(8,128)S(1)}, f32[16,128,128]{1,2,0:T(8,128)}, u32[]{:S(2)}) copy-start(f32[16,128,128]{1,2,0:T(8,128)} %copy.32) | copy-start | bytes 3145732
  49.3 32.5 %collective-permute-start.2 = (bf16[3088,128]{1,0:T(8,128)(2,1)}, bf16[3088,128]{1,0:T(8,128)(2,1)}, u32[]{:S(2)}, u32[]{:S(2)}) collective-permute-start(bf16[3088,128]{1,0:T(8,128)(2,1)} %constant_dynamic-update-slice_fusion), channel_id=1, source_target_pairs={{0,4},{2,6},{4,8},{6,10},{8,12},{10,14},{1,5},{3,7},{5,9},{7,11},{... | collective-permute-start | bytes 2371592 | tf_op jit(solution)/shard_map/ppermute | solution.py:15
  82.5 9.8 %copy-start.18 = (f32[256]{0:T(256)}, f32[256]{0:T(256)S(1)}, u32[]{:S(2)}) copy-start(f32[256]{0:T(256)S(1)} %fusion.58) | copy-start | bytes 3076
  86.6 0.7 copy-start.8
  87.3 0.7 copy-start.6
  89.9 12.8 %copy-start.1 = (f32[128,2048]{0,1:T(8,128)S(1)}, f32[128,2048]{0,1:T(8,128)}, u32[]{:S(2)}) copy-start(f32[128,2048]{0,1:T(8,128)} %copy.36) | copy-start | bytes 3145732
  89.9 12.8 %copy-start.10 = (f32[2048]{0:T(1024)S(1)}, f32[2048]{0:T(1024)}, u32[]{:S(2)}) copy-start(f32[2048]{0:T(1024)} %param.15) | copy-start | bytes 24580
  93.0 12.3 %copy-start.12 = (f32[128]{0:T(128)S(1)}, f32[128]{0:T(128)}, u32[]{:S(2)}) copy-start(f32[128]{0:T(128)} %copy-done.11) | copy-start | bytes 1540
  93.0 12.3 %copy-start.16 = (f32[128]{0:T(128)S(1)}, f32[128]{0:T(128)}, u32[]{:S(2)}) copy-start(f32[128]{0:T(128)} %get-tuple-element.18) | copy-start | bytes 1540
  93.0 12.3 %copy-start.17 = (f32[128]{0:T(128)S(1)}, f32[128]{0:T(128)}, u32[]{:S(2)}) copy-start(f32[128]{0:T(128)} %get-tuple-element.21) | copy-start | bytes 1540
  93.0 12.3 %copy-start.19 = (f32[256]{0:T(256)S(1)}, f32[256]{0:T(256)}, u32[]{:S(2)}) copy-start(f32[256]{0:T(256)} %copy-done.18) | copy-start | bytes 3076
  93.0 12.3 %copy-start.20 = (s32[128]{0:T(128)S(1)}, s32[128]{0:T(128)}, u32[]{:S(2)}) copy-start(s32[128]{0:T(128)} %iota_add_fusion) | copy-start | bytes 1540
  93.0 12.5 %copy-start.7 = (bf16[2,640,128]{2,1,0:T(8,128)(2,1)S(1)}, bf16[2,640,128]{2,1,0:T(8,128)(2,1)}, u32[]{:S(2)}) copy-start(bf16[2,640,128]{2,1,0:T(8,128)(2,1)} %copy-done.6) | copy-start | bytes 983044
  105.5 2.0 %copy-start.9 = (bf16[2,640,128]{1,2,0:T(8,128)(2,1)S(1)}, bf16[2,640,128]{1,2,0:T(8,128)(2,1)}, u32[]{:S(2)}) copy-start(bf16[2,640,128]{1,2,0:T(8,128)(2,1)} %copy-done.8) | copy-start | bytes 983044

commit v3 on v2

--- a/solution.py
+++ b/solution.py
@@ -107,6 +107,15 @@
     )
     from_1 = shifted(own, "ctx", 1)
     from_2 = shifted(own, "ctx", 2)
+    kv_only = jnp.concatenate(
+        [
+            own_keys.reshape(kv_rows, head_size),
+            own_values.reshape(kv_rows, head_size),
+            rows_of(code, head_size),
+        ]
+    )
+    from_3 = shifted(kv_only, "ctx", 3)
+    from_4 = shifted(kv_only, "ctx", 4)
 
     def unpack(block):
         state = block[:state_rows].reshape(heads_here, head_size, head_size).astype(F32)
@@ -117,31 +126,24 @@
         decay = join_parts(meta[tok_rows : tok_rows + 3 * heads_here])
         return state, keys, values, codes, decay
 
+    def unpack_kv(block):
+        keys = block[:kv_rows].reshape(kv_here, tok_rows, head_size)
+        values = block[kv_rows : 2 * kv_rows].reshape(kv_here, tok_rows, head_size)
+        codes = block[2 * kv_rows :].reshape(-1)[:tok_rows].astype(F32)
+        return keys, values, codes
+
     state_1, keys_1, values_1, code_1, decay_1 = unpack(from_1)
     state_2, keys_2, values_2, code_2, decay_2 = unpack(from_2)
+    keys_3, values_3, code_3 = unpack_kv(from_3)
+    keys_4, values_4, code_4 = unpack_kv(from_4)
 
     link_1 = (code_2[-1] == code_1[0]) & (code_1[0] == code_1[-1])
     pair_state = state_1 + jnp.where(link_1, decay_1, 0.0)[:, None, None] * state_2
 
-    relay = jnp.concatenate(
-        [
-            pair_state.astype(BF16).reshape(state_rows, head_size),
-            keys_2.reshape(kv_rows, head_size),
-            keys_1.reshape(kv_rows, head_size),
-            values_2.reshape(kv_rows, head_size),
-            values_1.reshape(kv_rows, head_size),
-            rows_of(jnp.concatenate([code_2, code_1]), head_size),
-        ]
-    )
-    from_far = shifted(relay, "ctx", 2)
-    state_far = from_far[:state_rows].reshape(heads_here, head_size, head_size).astype(F32)
-    keys_far = from_far[state_rows : state_rows + 2 * kv_rows].reshape(2, kv_here, tok_rows, head_size)
-    values_far = from_far[state_rows + 2 * kv_rows : state_rows + 4 * kv_rows].reshape(
-        2, kv_here, tok_rows, head_size
-    )
-    code_far = from_far[state_rows + 4 * kv_rows :].reshape(-1)[: 2 * tok_rows].astype(F32)
+    from_far = shifted(pair_state.astype(BF16), "ctx", 2)
+    state_far = from_far.astype(F32)
 
-    link_2 = (code_far[-1] == code_2[0]) & (code_2[0] == code_1[-1])
+    link_2 = (code_3[-1] == code_2[0]) & (code_2[0] == code_1[-1])
     carry_scale = jnp.where(link_2, decay_2 * decay_1, 0.0)
     incoming_state = pair_state + carry_scale[:, None, None] * state_far
 
@@ -160,9 +162,9 @@
     normed = mixed * inverse[:, None, None] * norm_gain.reshape(heads_here, head_size) * gate_open
     light_out = normed.reshape(tok_rows, heads_here * head_size).astype(BF16)
 
-    key_window = jnp.concatenate([keys_far[0], keys_far[1], keys_2, keys_1, own_keys], axis=1)
-    value_window = jnp.concatenate([values_far[0], values_far[1], values_2, values_1, own_values], axis=1)
-    code_window = jnp.concatenate([code_far, code_2, code_1, code])
+    key_window = jnp.concatenate([keys_4, keys_3, keys_2, keys_1, own_keys], axis=1)
+    value_window = jnp.concatenate([values_4, values_3, values_2, values_1, own_values], axis=1)
+    code_window = jnp.concatenate([code_4, code_3, code_2, code_1, code])
     soft_out = soft_window(soft_query, key_window, value_window, code, code_window, heads_here)
     return (light_out, soft_out)
 

time: 111 us -> 99.2 us (0.89)
  the two profiles are of different devices: /device:TPU:0 before, /device:TPU:17 now
where the time goes in v3:
time: 99.2 us; the launch traced here: 97.9 us
  local copies, waits for them, and re-layouts  25 us (25%)
  other arithmetic  21.9 us (22%)
  waiting for transfers between devices  19.9 us (20%)
  starting transfers between devices  11.5 us (12%)
  matrix products  10.1 us (10%)
  between operations  5.97 us (6%)
  blocking collectives  3.47 us (3%)
    ppermute x5, waiting for transfers between devices, shifted(): return lax.ppermute(block, axis, route)  19.9 us
    ppermute x5, starting transfers between devices, shifted(): return lax.ppermute(block, axis, route)  11.5 us
    unnamed x37, local copies, waits for them, and re-layouts  8.57 us
    unnamed x5, other arithmetic  5.16 us
    psum x1, blocking collectives, on_device(): squares = lax.psum(squares, 'tensor')  3.47 us
    dot_general x1, matrix products, on_device(): jnp.einsum('thd,hde->the', query_heads.astype(F32), incoming_state, preci...  3.43 us
    slice x2, local copies, waits for them, and re-layouts, unpack(): block[:state_rows].reshape(heads_here, head_size, head_size).astype(F32)  3 us
    dot_general x1, matrix products, soft_window(): jnp.einsum('kgts,ksd->kgtd', prob_block.astype(BF16), value_heads, prefer...  2.24 us
  transfers between devices with their start and end apart: 5, of which 3 were waited for; matrix products, arithmetic and copies ran while one was open for 30% of the time, Pallas kernels for 0%

profile of v3, /device:TPU:17, one launch (start us, length us, event | category | flops | bytes accessed | tf_op | source)
XLA Modules:
  0.0 97.9 jit_solution(2043715211390604770)
XLA Ops:
  0.7 0.7 convert_add_fusion
  1.4 1.0 %reduce_window_sum.11 = f32[16,128]{1,0:T(8,128)S(1)} reduce-window(f32[16,128]{1,0:T(8,128)} %param.14, f32[]{:T(128)} %constant.10.clone.1), window={size=1x128 pad=0_0x127_0}, to_apply=%region_0.0 | reduce-window | flops 260096 | bytes 16388 | tf_op jit(solution)/shard_map/jit(cumsum)/reduce_window_sum | solution.py:91
  2.4 0.2 slice_reduce_fusion
  2.6 1.0 copy.27
  3.7 1.0 copy.29
  4.9 1.3 %collective-permute-start.4 = (bf16[528,128]{1,0:T(8,128)(2,1)S(1)}, bf16[528,128]{1,0:T(8,128)(2,1)}, u32[]{:S(2)}, u32[]{:S(2)}) collective-permute-start(bf16[528,128]{1,0:T(8,128)(2,1)S(1)} %pad_maximum_fusion.1), channel_id=1, source_target_pairs={{0,8},{2,10},{4,12},{6,14},{1,9},{3,11},{5,13},{7,15},{16,24},{18,... | collective-permute-start | bytes 405512 | tf_op jit(solution)/shard_map/ppermute | solution.py:15
  6.2 4.1 %collective-permute-start.2 = (bf16[528,128]{1,0:T(8,128)(2,1)S(1)}, bf16[528,128]{1,0:T(8,128)(2,1)}, u32[]{:S(2)}, u32[]{:S(2)}) collective-permute-start(bf16[528,128]{1,0:T(8,128)(2,1)S(1)} %pad_maximum_fusion.1), channel_id=1, source_target_pairs={{0,6},{2,8},{4,10},{6,12},{8,14},{1,7},{3,9},{5,11},{7,13},{9,15},... | collective-permute-start | bytes 405512 | tf_op jit(solution)/shard_map/ppermute | solution.py:15
  10.3 0.6 slice.113
  10.9 1.3 %broadcast_compare_fusion.1 = pred[128]{0:T(512)(128)(4,1)S(1)} fusion(f32[]{:T(128)} %bitcast.2, s32[128]{0:T(128)} %param.19), kind=kLoop, calls=%fused_computation.101 | loop fusion | flops 384 | bytes 644 | tf_op jit(solution)/shard_map/eq | solution.py:30
  12.3 1.3 %copy.46 = bf16[128,2048]{0,1:T(8,128)(2,1)S(1)} copy(bf16[128,2048]{1,0:T(8,128)(2,1)} %param.11) | data formatting | bytes 1048576 | tf_op jit(solution)/shard_map/reshape | solution.py:22
  13.6 0.3 convolution_convert_fusion
  14.0 1.9 %collective-permute-start.1 = (bf16[2576,128]{1,0:T(8,128)(2,1)S(1)}, bf16[2576,128]{1,0:T(8,128)(2,1)}, u32[]{:S(2)}, u32[]{:S(2)}) collective-permute-start(bf16[2576,128]{1,0:T(8,128)(2,1)S(1)} %pad_maximum_fusion), channel_id=1, source_target_pairs={{0,4},{2,6},{4,8},{6,10},{8,12},{10,14},{1,5},{3,7},{5,9},{7,11},{... | collective-permute-start | bytes 1978376 | tf_op jit(solution)/shard_map/ppermute | solution.py:15
  15.9 1.9 %collective-permute-start = (bf16[2576,128]{1,0:T(8,128)(2,1)S(1)}, bf16[2576,128]{1,0:T(8,128)(2,1)}, u32[]{:S(2)}, u32[]{:S(2)}) collective-permute-start(bf16[2576,128]{1,0:T(8,128)(2,1)S(1)} %pad_maximum_fusion), channel_id=1, source_target_pairs={{0,2},{2,4},{4,6},{6,8},{8,10},{10,12},{12,14},{1,3},{3,5},{5,7},{... | collective-permute-start | bytes 1978376 | tf_op jit(solution)/shard_map/ppermute | solution.py:15
  17.8 1.3 %add_divide_fusion = f32[128,2048]{1,0:T(8,128)S(1)} fusion(bf16[128,2048]{1,0:T(8,128)(2,1)} %param.13), kind=kLoop, calls=%fused_computation.17 | loop fusion | flops 1048576 | bytes 1572864 | tf_op jit(solution)/shard_map/div | solution.py:161
  19.2 1.4 %fusion.42 = pred[128,128]{1,0:T(8,128)(4,1)} fusion(f32[128]{0:T(128)} %copy-done.8), kind=kLoop, calls=%fused_computation.52 | loop fusion | flops 49152 | bytes 16896 | tf_op jit(solution)/shard_map/and | solution.py:25
  20.6 0.9 copy.49
  21.5 1.3 %copy.34 = f32[128,2048]{0,1:T(8,128)} copy(f32[128,2048]{1,0:T(8,128)S(1)} %add_divide_fusion) | data formatting | bytes 2097152 | tf_op jit(solution)/shard_map/div | solution.py:161
  22.8 0.5 iota_add_fusion
  23.3 0.9 fusion.60
  24.4 0.7 slice_convert_fusion.1
  25.0 0.6 slice.128
  25.6 0.9 fusion.59
  26.7 1.3 %constant_dynamic-update-slice_fusion.5 = f32[640]{0:T(1024)} fusion(f32[640]{0:T(1024)} %custom-call.1, bf16[528,128]{1,0:T(8,128)(2,1)} %collective-permute-done.4), kind=kLoop, calls=%fused_computation.58 | loop fusion | flops 128 | bytes 1024
  28.0 1.3 %constant_dynamic-update-slice_fusion.13 = f32[640]{0:T(1024)} fusion(f32[640]{0:T(1024)} %constant_dynamic-update-slice_fusion.5, bf16[528,128]{1,0:T(8,128)(2,1)} %collective-permute-done.2), kind=kLoop, calls=%fused_computation.72 | loop fusion | flops 128 | bytes 1024
  29.3 3.2 %collective-permute-done.1 = bf16[2576,128]{1,0:T(8,128)(2,1)} collective-permute-done((bf16[2576,128]{1,0:T(8,128)(2,1)S(1)}, bf16[2576,128]{1,0:T(8,128)(2,1)}, u32[]{:S(2)}, u32[]{:S(2)}) %collective-permute-start.1) | collective-permute-done | bytes 659488 | tf_op jit(solution)/shard_map/ppermute | solution.py:15
  32.5 0.7 slice_convert_fusion.4
  33.1 0.6 fusion.62
  33.7 0.9 fusion.58
  34.7 1.1 %slice.150 = bf16[2048,128]{1,0:T(8,128)(2,1)S(1)} slice(bf16[2576,128]{1,0:T(8,128)(2,1)} %collective-permute-done.1), slice={[0:2048], [0:128]} | slice | bytes 1048576 | tf_op jit(solution)/shard_map/slice | solution.py:121
  35.8 0.2 copy.31
  36.1 0.7 slice_bitcast_fusion
  36.7 0.6 slice_convert_fusion
  37.3 1.3 %constant_dynamic-update-slice_fusion.12 = f32[640]{0:T(1024)} fusion(f32[640]{0:T(1024)} %constant_dynamic-update-slice_fusion.13, bf16[2576,128]{1,0:T(8,128)(2,1)} %collective-permute-done.1), kind=kLoop, calls=%fused_computation.71 | loop fusion | flops 128 | bytes 1024
  38.6 12.6 %collective-permute-done = bf16[2576,128]{1,0:T(8,128)(2,1)} collective-permute-done((bf16[2576,128]{1,0:T(8,128)(2,1)S(1)}, bf16[2576,128]{1,0:T(8,128)(2,1)}, u32[]{:S(2)}, u32[]{:S(2)}) %collective-permute-start) | collective-permute-done | bytes 659488 | tf_op jit(solution)/shard_map/ppermute | solution.py:15
  51.2 1.3 %constant_dynamic-update-slice_fusion.11 = f32[640]{0:T(1024)} fusion(f32[640]{0:T(1024)} %constant_dynamic-update-slice_fusion.12, bf16[2576,128]{1,0:T(8,128)(2,1)} %collective-permute-done), kind=kLoop, calls=%fused_computation.70 | loop fusion | flops 128 | bytes 1024
  52.5 1.3 %constant_dynamic-update-slice_fusion.10 = f32[640]{0:T(1024)} fusion(f32[640]{0:T(1024)} %constant_dynamic-update-slice_fusion.11, s32[128]{0:T(128)} %param.19), kind=kLoop, calls=%fused_computation.69 | loop fusion | flops 256 | bytes 1024 | tf_op jit(solution)/shard_map/concatenate | solution.py:167
  53.8 0.7 slice_convert_fusion.3
  54.5 0.6 fusion.61
  60.0 0.7 slice_bitcast_fusion.1
  60.7 0.5 slice_convert_fusion.2
  61.2 0.9 fusion.57
  62.2 0.6 constant_dynamic-update-slice_fusion.2
  62.8 0.6 constant_dynamic-update-slice_fusion.1
  63.5 0.6 constant_dynamic-update-slice_fusion
  64.1 0.6 constant_dynamic-update-slice_fusion.7
  64.8 0.6 constant_dynamic-update-slice_fusion.6
  65.4 0.6 bitcast_dynamic-update-slice_fusion
  66.0 1.9 %slice.145 = bf16[2048,128]{1,0:T(8,128)(2,1)} slice(bf16[2576,128]{1,0:T(8,128)(2,1)} %collective-permute-done), slice={[0:2048], [0:128]} | slice | bytes 1048576 | tf_op jit(solution)/shard_map/slice | solution.py:121
  67.9 1.2 %copy.32 = f32[16,128,128]{1,2,0:T(8,128)S(1)} copy(bf16[16,128,128]{2,1,0:T(8,128)(2,1)} %bitcast.135) | data formatting | bytes 1572864 | tf_op jit(solution)/shard_map/convert_element_type | solution.py:121
  69.2 0.9 broadcast_select_fusion
  70.1 1.0 %fusion.41 = bf16[16,128,128]{1,2,0:T(8,128)(2,1)} fusion(f32[16,128,128]{1,2,0:T(8,128)S(1)} %copy.32, f32[16,128,128]{1,2,0:T(8,128)S(1)} %copy.31, f32[16]{0:T(128)S(1)} %broadcast_select_fusion.1), kind=kLoop, calls=%fused_computation.48 | loop fusion | flops 786432 | bytes 2621504 | tf_op jit(solution)/shard_map/convert_element_type | solution.py:143
  71.0 2.2 %collective-permute-start.3 = (bf16[16,128,128]{1,2,0:T(8,128)(2,1)}, bf16[16,128,128]{1,2,0:T(8,128)(2,1)}, u32[]{:S(2)}, u32[]{:S(2)}) collective-permute-start(bf16[16,128,128]{1,2,0:T(8,128)(2,1)} %fusion.41), channel_id=1, source_target_pairs={{0,4},{2,6},{4,8},{6,10},{8,12},{10,14},{1,5},{3,7},{5,9},{7,11},{... | collective-permute-start | bytes 1572872 | tf_op jit(solution)/shard_map/ppermute | solution.py:15
  73.3 0.7 fusion.40
  74.0 2.0 %fusion.2 = (f32[2,8,128]{2,1,0:T(8,128)S(1)}, f32[2,640,128,8]{2,1,3,0:T(8,128)S(1)}) fusion(pred[128,640]{0,1:T(8,128)(4,1)S(1)} %fusion.40, bf16[128,2,8,128]{3,2,1,0:T(8,128)(2,1)} %bitcast.133, bf16[2,640,128]{2,1,0:T(8,128)(2,1)S(1)} %copy-done.3), kind=kOutput, calls=%fused_computation.4 | convolution fusion | flops 339474432 | bytes 6184960 | tf_op jit(solution)/shard_map/tkgd,ksd->kgts/dot_general | solution.py:44
  76.0 1.1 %fusion = f32[2,8,128]{2,1,0:T(8,128)S(1)} fusion(f32[2,640,128,8]{2,1,3,0:T(8,128)S(1)} %get-tuple-element.30, f32[2,8,128]{2,1,0:T(8,128)S(1)} %get-tuple-element.29, pred[128,640]{0,1:T(8,128)(4,1)S(1)} %fusion.40), kind=kLoop, calls=%fused_computation.2 | loop fusion | flops 5240832 | bytes 5341184 | tf_op jit(solution)/shard_map/reduce_sum | solution.py:48
  77.1 2.2 %divide_convert_fusion = bf16[128,2,8,128]{0,3,2,1:T(8,128)(2,1)} fusion(f32[2,640,128,8]{2,1,3,0:T(8,128)S(1)} %get-tuple-element.30, f32[2,8,128]{2,1,0:T(8,128)S(1)} %get-tuple-element.29, pred[128,640]{0,1:T(8,128)(4,1)S(1)} %fusion.40, f32[128,2,8]{0,2,1:T(8,128)S(1)} %bitcast.156, bf16[2,640,128]{1,2,0:T(8,128)(2,1)S(1)} %copy-done.6), kind=kOutput, calls=%fused_computation.15 | convolution fusion | flops 341311488 | bytes 6193152 | tf_op jit(solution)/shard_map/kgts,ksd->kgtd/dot_general | solution.py:49
  79.4 2.1 %copy.42 = bf16[128,2048]{1,0:T(8,128)(2,1)} copy(bf16[128,2048]{0,1:T(8,128)(2,1)} %bitcast.145) | data formatting | bytes 1048576
  81.4 0.6 broadcast_compare_fusion
  82.1 4.2 %collective-permute-done.3 = bf16[16,128,128]{1,2,0:T(8,128)(2,1)} collective-permute-done((bf16[16,128,128]{1,2,0:T(8,128)(2,1)}, bf16[16,128,128]{1,2,0:T(8,128)(2,1)}, u32[]{:S(2)}, u32[]{:S(2)}) %collective-permute-start.3) | collective-permute-done | bytes 524320 | tf_op jit(solution)/shard_map/ppermute | solution.py:15
  86.2 3.4 %fusion.10 = f32[128,16,128]{0,2,1:T(8,128)} fusion(bf16[16,128,128]{1,2,0:T(8,128)(2,1)} %collective-permute-done.3, f32[128,16]{0,1:T(8,128)S(1)} %select_bitcast_fusion, f32[16]{0:T(128)S(1)} %get-tuple-element.6, f32[16,128,128]{1,2,0:T(8,128)S(1)} %copy.32, f32[16,128,128]{1,2,0:T(8,128)S(1)} %copy.31, f32[16]{0:T(128)S(1)} %broadcast_select_fusion.1, ...), kind=kOutput, calls=%fused_computation.12 | convolution fusion | flops 404226048 | bytes 4202624 | tf_op jit(solution)/shard_map/thd,hde->the/dot_general | solution.py:151
  89.7 2.1 %multiply_reduce_fusion = (f32[128]{0:T(128)S(1)}, f32[128,16,128]{0,2,1:T(8,128)S(1)}) fusion(f32[128,16,128]{0,2,1:T(8,128)} %fusion.10, bf16[128,16,128]{0,2,1:T(8,128)(2,1)S(1)} %bitcast.132, f32[16,128]{1,0:T(8,128)S(1)} %reduce_window_sum.11, pred[128,128]{1,0:T(8,128)(4,1)S(1)} %copy-done.4, bf16[128,2048]{1,0:T(8,128)(2,1)S(1)} %copy-done, ...), kind=kOutput, calls=%fused_computation.18 | convolution fusion | flops 136052608 | bytes 3695104 | tf_op jit(solution)/shard_map/hts,shd->thd/dot_general | solution.py:29
  91.8 3.5 %psum.7 = f32[128]{0:T(128)S(1)} all-reduce(f32[128]{0:T(128)S(1)} %get-tuple-element.27), channel_id=1, replica_groups=mesh['groups'=2,'ctx'=8,'tensor'=2] {'tensor'}, use_global_device_ids=true, to_apply=%region_2.3 | all-reduce | flops 128 | bytes 1024 | tf_op jit(solution)/shard_map/psum | solution.py:158
  95.3 1.6 %multiply_convert_fusion = bf16[128,16,128]{0,2,1:T(8,128)(2,1)S(1)} fusion(f32[128,16,128]{0,2,1:T(8,128)} %bitcast.130, f32[128,16,128]{0,2,1:T(8,128)S(1)} %get-tuple-element.28, f32[16,128]{1,0:T(8,128)S(1)} %bitcast.155, f32[128]{0:T(128)S(1)} %add_rsqrt_fusion), kind=kLoop, calls=%fused_computation.16 | loop fusion | flops 1048576 | bytes 2630144 | tf_op jit(solution)/shard_map/convert_element_type | solution.py:163
  96.9 1.0 %copy.41 = bf16[128,2048]{1,0:T(8,128)(2,1)} copy(bf16[128,2048]{0,1:T(8,128)(2,1)S(1)} %bitcast.137) | data formatting | bytes 1048576
  (45 shorter events, 1.1 us)
Async XLA Ops:
  0.6 13.0 %copy-start = (bf16[128,2048]{1,0:T(8,128)(2,1)S(1)}, bf16[128,2048]{1,0:T(8,128)(2,1)}, u32[]{:S(2)}) copy-start(bf16[128,2048]{1,0:T(8,128)(2,1)} %param.12) | copy-start | bytes 1572868
  0.6 19.9 %copy-start.1 = (bf16[128,2048]{1,0:T(8,128)(2,1)S(1)}, bf16[128,2048]{1,0:T(8,128)(2,1)}, u32[]{:S(2)}) copy-start(bf16[128,2048]{1,0:T(8,128)(2,1)} %param.16) | copy-start | bytes 1572868
  1.4 10.8 %copy-start.8 = (f32[128]{0:T(128)}, f32[128]{0:T(128)S(1)}, u32[]{:S(2)}) copy-start(f32[128]{0:T(128)S(1)} %get-tuple-element.22) | copy-start | bytes 1540
  4.9 18.5 %collective-permute-start.4 = (bf16[528,128]{1,0:T(8,128)(2,1)S(1)}, bf16[528,128]{1,0:T(8,128)(2,1)}, u32[]{:S(2)}, u32[]{:S(2)}) collective-permute-start(bf16[528,128]{1,0:T(8,128)(2,1)S(1)} %pad_maximum_fusion.1), channel_id=1, source_target_pairs={{0,8},{2,10},{4,12},{6,14},{1,9},{3,11},{5,13},{7,15},{16,24},{18,... | collective-permute-start | bytes 405512 | tf_op jit(solution)/shard_map/ppermute | solution.py:15
  6.2 18.2 %collective-permute-start.2 = (bf16[528,128]{1,0:T(8,128)(2,1)S(1)}, bf16[528,128]{1,0:T(8,128)(2,1)}, u32[]{:S(2)}, u32[]{:S(2)}) collective-permute-start(bf16[528,128]{1,0:T(8,128)(2,1)S(1)} %pad_maximum_fusion.1), channel_id=1, source_target_pairs={{0,6},{2,8},{4,10},{6,12},{8,14},{1,7},{3,9},{5,11},{7,13},{9,15},... | collective-permute-start | bytes 405512 | tf_op jit(solution)/shard_map/ppermute | solution.py:15
  14.0 18.5 %collective-permute-start.1 = (bf16[2576,128]{1,0:T(8,128)(2,1)S(1)}, bf16[2576,128]{1,0:T(8,128)(2,1)}, u32[]{:S(2)}, u32[]{:S(2)}) collective-permute-start(bf16[2576,128]{1,0:T(8,128)(2,1)S(1)} %pad_maximum_fusion), channel_id=1, source_target_pairs={{0,4},{2,6},{4,8},{6,10},{8,12},{10,14},{1,5},{3,7},{5,9},{7,11},{... | collective-permute-start | bytes 1978376 | tf_op jit(solution)/shard_map/ppermute | solution.py:15
  15.9 35.3 %collective-permute-start = (bf16[2576,128]{1,0:T(8,128)(2,1)S(1)}, bf16[2576,128]{1,0:T(8,128)(2,1)}, u32[]{:S(2)}, u32[]{:S(2)}) collective-permute-start(bf16[2576,128]{1,0:T(8,128)(2,1)S(1)} %pad_maximum_fusion), channel_id=1, source_target_pairs={{0,2},{2,4},{4,6},{6,8},{8,10},{10,12},{12,14},{1,3},{3,5},{5,7},{... | collective-permute-start | bytes 1978376 | tf_op jit(solution)/shard_map/ppermute | solution.py:15
  24.3 48.9 %copy-start.9 = (f32[128]{0:T(128)S(1)}, f32[128]{0:T(128)}, u32[]{:S(2)}) copy-start(f32[128]{0:T(128)} %copy-done.8) | copy-start | bytes 1540
  26.7 9.1 %copy-start.2 = (bf16[2,640,128]{2,1,0:T(8,128)(2,1)}, bf16[2,640,128]{2,1,0:T(8,128)(2,1)S(1)}, u32[]{:S(2)}) copy-start(bf16[2,640,128]{2,1,0:T(8,128)(2,1)S(1)} %constant_dynamic-update-slice_fusion.8) | copy-start | bytes 983044
  26.7 9.1 %copy-start.5 = (bf16[2,640,128]{1,2,0:T(8,128)(2,1)}, bf16[2,640,128]{1,2,0:T(8,128)(2,1)S(1)}, u32[]{:S(2)}) copy-start(bf16[2,640,128]{1,2,0:T(8,128)(2,1)S(1)} %constant_dynamic-update-slice_fusion.3) | copy-start | bytes 983044
  62.8 10.4 %copy-start.10 = (f32[640]{0:T(1024)S(1)}, f32[640]{0:T(1024)}, u32[]{:S(2)}) copy-start(f32[640]{0:T(1024)} %constant_dynamic-update-slice_fusion.10) | copy-start | bytes 7684
  66.0 8.0 %copy-start.3 = (bf16[2,640,128]{2,1,0:T(8,128)(2,1)S(1)}, bf16[2,640,128]{2,1,0:T(8,128)(2,1)}, u32[]{:S(2)}) copy-start(bf16[2,640,128]{2,1,0:T(8,128)(2,1)} %bitcast_dynamic-update-slice_fusion) | copy-start | bytes 983044
  71.0 15.2 %collective-permute-start.3 = (bf16[16,128,128]{1,2,0:T(8,128)(2,1)}, bf16[16,128,128]{1,2,0:T(8,128)(2,1)}, u32[]{:S(2)}, u32[]{:S(2)}) collective-permute-start(bf16[16,128,128]{1,2,0:T(8,128)(2,1)} %fusion.41), channel_id=1, source_target_pairs={{0,4},{2,6},{4,8},{6,10},{8,12},{10,14},{1,5},{3,7},{5,9},{7,11},{... | collective-permute-start | bytes 1572872 | tf_op jit(solution)/shard_map/ppermute | solution.py:15
  74.0 3.1 %copy-start.6 = (bf16[2,640,128]{1,2,0:T(8,128)(2,1)S(1)}, bf16[2,640,128]{1,2,0:T(8,128)(2,1)}, u32[]{:S(2)}) copy-start(bf16[2,640,128]{1,2,0:T(8,128)(2,1)} %constant_dynamic-update-slice_fusion) | copy-start | bytes 983044
  77.1 4.3 %copy-start.11 = (s32[128]{0:T(128)S(1)}, s32[128]{0:T(128)}, u32[]{:S(2)}) copy-start(s32[128]{0:T(128)} %param.19) | copy-start | bytes 1540
  79.4 10.3 %copy-start.4 = (pred[128,128]{1,0:T(8,128)(4,1)S(1)}, pred[128,128]{1,0:T(8,128)(4,1)}, u32[]{:S(2)}) copy-start(pred[128,128]{1,0:T(8,128)(4,1)} %fusion.42) | copy-start | bytes 49156
  79.4 15.9 %copy-start.7 = (f32[2048]{0:T(1024)S(1)}, f32[2048]{0:T(1024)}, u32[]{:S(2)}) copy-start(f32[2048]{0:T(1024)} %param.15) | copy-start | bytes 24580

commit v4 on v3

--- a/solution.py
+++ b/solution.py
@@ -2,6 +2,7 @@
 import jax.numpy as jnp
 from jax import lax
 from jax.sharding import PartitionSpec as P
+
 
 NEG_BIG = -1e30
 MAXDOC = 512
@@ -70,7 +71,7 @@
     return jnp.pad(flat, (0, padded - flat.shape[0])).reshape(-1, width).astype(BF16)
 
 
-def on_device(
+def on_device_body(
     light_query,
     light_key,
     light_value,
@@ -183,6 +184,4 @@
         P(("groups", "ctx")),
     )
     out_specs = (P(("groups", "ctx"), "tensor"), P(("groups", "ctx"), "tensor"))
-    return jax.shard_map(
-        on_device, mesh=mesh, in_specs=in_specs, out_specs=out_specs, check_vma=False
-    )
+    return jax.shard_map(on_device_body, mesh=mesh, in_specs=in_specs, out_specs=out_specs, check_vma=False)

time: 99.2 us -> 99.2 us (level)
  no operation moved by 1% of the time
where the time goes in v4:
time: 99.2 us; the launch traced here: 97.9 us
  local copies, waits for them, and re-layouts  25 us (25%)
  other arithmetic  21.9 us (22%)
  waiting for transfers between devices  19.9 us (20%)
  starting transfers between devices  11.5 us (12%)
  matrix products  10.1 us (10%)
  between operations  5.97 us (6%)
  blocking collectives  3.47 us (3%)
    ppermute x5, waiting for transfers between devices, shifted(): return lax.ppermute(block, axis, route)  19.9 us
    ppermute x5, starting transfers between devices, shifted(): return lax.ppermute(block, axis, route)  11.5 us
    unnamed x37, local copies, waits for them, and re-layouts  8.57 us
    unnamed x5, other arithmetic  5.16 us
    psum x1, blocking collectives, on_device_body(): squares = lax.psum(squares, 'tensor')  3.47 us
    dot_general x1, matrix products, on_device_body(): jnp.einsum('thd,hde->the', query_heads.astype(F32), incoming_state, preci...  3.43 us
    slice x2, local copies, waits for them, and re-layouts, unpack(): block[:state_rows].reshape(heads_here, head_size, head_size).astype(F32)  3 us
    dot_general x1, matrix products, soft_window(): jnp.einsum('kgts,ksd->kgtd', prob_block.astype(BF16), value_heads, prefer...  2.24 us
  transfers between devices with their start and end apart: 5, of which 3 were waited for; matrix products, arithmetic and copies ran while one was open for 30% of the time, Pallas kernels for 0%

profile of v4, /device:TPU:17, one launch (start us, length us, event | category | flops | bytes accessed | tf_op | source)
XLA Modules:
  0.0 97.9 jit_solution(2043715211390604770)
XLA Ops:
  0.7 0.7 convert_add_fusion
  1.4 1.0 %reduce_window_sum.11 = f32[16,128]{1,0:T(8,128)S(1)} reduce-window(f32[16,128]{1,0:T(8,128)} %param.14, f32[]{:T(128)} %constant.10.clone.1), window={size=1x128 pad=0_0x127_0}, to_apply=%region_0.0 | reduce-window | flops 260096 | bytes 16388 | tf_op jit(solution)/shard_map/jit(cumsum)/reduce_window_sum | solution.py:92
  2.4 0.2 slice_reduce_fusion
  2.6 1.0 copy.27
  3.7 1.0 copy.29
  4.9 1.3 %collective-permute-start.4 = (bf16[528,128]{1,0:T(8,128)(2,1)S(1)}, bf16[528,128]{1,0:T(8,128)(2,1)}, u32[]{:S(2)}, u32[]{:S(2)}) collective-permute-start(bf16[528,128]{1,0:T(8,128)(2,1)S(1)} %pad_maximum_fusion.1), channel_id=1, source_target_pairs={{0,8},{2,10},{4,12},{6,14},{1,9},{3,11},{5,13},{7,15},{16,24},{18,... | collective-permute-start | bytes 405512 | tf_op jit(solution)/shard_map/ppermute | solution.py:16
  6.2 4.1 %collective-permute-start.2 = (bf16[528,128]{1,0:T(8,128)(2,1)S(1)}, bf16[528,128]{1,0:T(8,128)(2,1)}, u32[]{:S(2)}, u32[]{:S(2)}) collective-permute-start(bf16[528,128]{1,0:T(8,128)(2,1)S(1)} %pad_maximum_fusion.1), channel_id=1, source_target_pairs={{0,6},{2,8},{4,10},{6,12},{8,14},{1,7},{3,9},{5,11},{7,13},{9,15},... | collective-permute-start | bytes 405512 | tf_op jit(solution)/shard_map/ppermute | solution.py:16
  10.3 0.6 slice.113
  10.9 1.3 %broadcast_compare_fusion.1 = pred[128]{0:T(512)(128)(4,1)S(1)} fusion(f32[]{:T(128)} %bitcast.2, s32[128]{0:T(128)} %param.19), kind=kLoop, calls=%fused_computation.101 | loop fusion | flops 384 | bytes 644 | tf_op jit(solution)/shard_map/eq | solution.py:31
  12.3 1.3 %copy.46 = bf16[128,2048]{0,1:T(8,128)(2,1)S(1)} copy(bf16[128,2048]{1,0:T(8,128)(2,1)} %param.11) | data formatting | bytes 1048576 | tf_op jit(solution)/shard_map/reshape | solution.py:23
  13.6 0.3 convolution_convert_fusion
  14.0 1.9 %collective-permute-start.1 = (bf16[2576,128]{1,0:T(8,128)(2,1)S(1)}, bf16[2576,128]{1,0:T(8,128)(2,1)}, u32[]{:S(2)}, u32[]{:S(2)}) collective-permute-start(bf16[2576,128]{1,0:T(8,128)(2,1)S(1)} %pad_maximum_fusion), channel_id=1, source_target_pairs={{0,4},{2,6},{4,8},{6,10},{8,12},{10,14},{1,5},{3,7},{5,9},{7,11},{... | collective-permute-start | bytes 1978376 | tf_op jit(solution)/shard_map/ppermute | solution.py:16
  15.9 1.9 %collective-permute-start = (bf16[2576,128]{1,0:T(8,128)(2,1)S(1)}, bf16[2576,128]{1,0:T(8,128)(2,1)}, u32[]{:S(2)}, u32[]{:S(2)}) collective-permute-start(bf16[2576,128]{1,0:T(8,128)(2,1)S(1)} %pad_maximum_fusion), channel_id=1, source_target_pairs={{0,2},{2,4},{4,6},{6,8},{8,10},{10,12},{12,14},{1,3},{3,5},{5,7},{... | collective-permute-start | bytes 1978376 | tf_op jit(solution)/shard_map/ppermute | solution.py:16
  17.8 1.3 %add_divide_fusion = f32[128,2048]{1,0:T(8,128)S(1)} fusion(bf16[128,2048]{1,0:T(8,128)(2,1)} %param.13), kind=kLoop, calls=%fused_computation.17 | loop fusion | flops 1048576 | bytes 1572864 | tf_op jit(solution)/shard_map/div | solution.py:162
  19.2 1.4 %fusion.42 = pred[128,128]{1,0:T(8,128)(4,1)} fusion(f32[128]{0:T(128)} %copy-done.8), kind=kLoop, calls=%fused_computation.52 | loop fusion | flops 49152 | bytes 16896 | tf_op jit(solution)/shard_map/and | solution.py:26
  20.6 0.9 copy.49
  21.5 1.3 %copy.34 = f32[128,2048]{0,1:T(8,128)} copy(f32[128,2048]{1,0:T(8,128)S(1)} %add_divide_fusion) | data formatting | bytes 2097152 | tf_op jit(solution)/shard_map/div | solution.py:162
  22.8 0.5 iota_add_fusion
  23.3 0.9 fusion.60
  24.4 0.7 slice_convert_fusion.1
  25.0 0.6 slice.128
  25.6 0.9 fusion.59
  26.7 1.3 %constant_dynamic-update-slice_fusion.5 = f32[640]{0:T(1024)} fusion(f32[640]{0:T(1024)} %custom-call.1, bf16[528,128]{1,0:T(8,128)(2,1)} %collective-permute-done.4), kind=kLoop, calls=%fused_computation.58 | loop fusion | flops 128 | bytes 1024
  28.0 1.3 %constant_dynamic-update-slice_fusion.13 = f32[640]{0:T(1024)} fusion(f32[640]{0:T(1024)} %constant_dynamic-update-slice_fusion.5, bf16[528,128]{1,0:T(8,128)(2,1)} %collective-permute-done.2), kind=kLoop, calls=%fused_computation.72 | loop fusion | flops 128 | bytes 1024
  29.3 3.2 %collective-permute-done.1 = bf16[2576,128]{1,0:T(8,128)(2,1)} collective-permute-done((bf16[2576,128]{1,0:T(8,128)(2,1)S(1)}, bf16[2576,128]{1,0:T(8,128)(2,1)}, u32[]{:S(2)}, u32[]{:S(2)}) %collective-permute-start.1) | collective-permute-done | bytes 659488 | tf_op jit(solution)/shard_map/ppermute | solution.py:16
  32.5 0.7 slice_convert_fusion.4
  33.1 0.6 fusion.62
  33.7 0.9 fusion.58
  34.7 1.1 %slice.150 = bf16[2048,128]{1,0:T(8,128)(2,1)S(1)} slice(bf16[2576,128]{1,0:T(8,128)(2,1)} %collective-permute-done.1), slice={[0:2048], [0:128]} | slice | bytes 1048576 | tf_op jit(solution)/shard_map/slice | solution.py:122
  35.8 0.2 copy.31
  36.1 0.7 slice_bitcast_fusion
  36.7 0.6 slice_convert_fusion
  37.3 1.3 %constant_dynamic-update-slice_fusion.12 = f32[640]{0:T(1024)} fusion(f32[640]{0:T(1024)} %constant_dynamic-update-slice_fusion.13, bf16[2576,128]{1,0:T(8,128)(2,1)} %collective-permute-done.1), kind=kLoop, calls=%fused_computation.71 | loop fusion | flops 128 | bytes 1024
  38.6 12.6 %collective-permute-done = bf16[2576,128]{1,0:T(8,128)(2,1)} collective-permute-done((bf16[2576,128]{1,0:T(8,128)(2,1)S(1)}, bf16[2576,128]{1,0:T(8,128)(2,1)}, u32[]{:S(2)}, u32[]{:S(2)}) %collective-permute-start) | collective-permute-done | bytes 659488 | tf_op jit(solution)/shard_map/ppermute | solution.py:16
  51.2 1.3 %constant_dynamic-update-slice_fusion.11 = f32[640]{0:T(1024)} fusion(f32[640]{0:T(1024)} %constant_dynamic-update-slice_fusion.12, bf16[2576,128]{1,0:T(8,128)(2,1)} %collective-permute-done), kind=kLoop, calls=%fused_computation.70 | loop fusion | flops 128 | bytes 1024
  52.5 1.3 %constant_dynamic-update-slice_fusion.10 = f32[640]{0:T(1024)} fusion(f32[640]{0:T(1024)} %constant_dynamic-update-slice_fusion.11, s32[128]{0:T(128)} %param.19), kind=kLoop, calls=%fused_computation.69 | loop fusion | flops 256 | bytes 1024 | tf_op jit(solution)/shard_map/concatenate | solution.py:168
  53.8 0.7 slice_convert_fusion.3
  54.5 0.6 fusion.61
  60.0 0.7 slice_bitcast_fusion.1
  60.7 0.5 slice_convert_fusion.2
  61.2 0.9 fusion.57
  62.2 0.6 constant_dynamic-update-slice_fusion.2
  62.8 0.6 constant_dynamic-update-slice_fusion.1
  63.5 0.6 constant_dynamic-update-slice_fusion
  64.1 0.6 constant_dynamic-update-slice_fusion.7
  64.8 0.6 constant_dynamic-update-slice_fusion.6
  65.4 0.6 bitcast_dynamic-update-slice_fusion
  66.0 1.9 %slice.145 = bf16[2048,128]{1,0:T(8,128)(2,1)} slice(bf16[2576,128]{1,0:T(8,128)(2,1)} %collective-permute-done), slice={[0:2048], [0:128]} | slice | bytes 1048576 | tf_op jit(solution)/shard_map/slice | solution.py:122
  67.9 1.2 %copy.32 = f32[16,128,128]{1,2,0:T(8,128)S(1)} copy(bf16[16,128,128]{2,1,0:T(8,128)(2,1)} %bitcast.135) | data formatting | bytes 1572864 | tf_op jit(solution)/shard_map/convert_element_type | solution.py:122
  69.2 0.9 broadcast_select_fusion
  70.1 1.0 %fusion.41 = bf16[16,128,128]{1,2,0:T(8,128)(2,1)} fusion(f32[16,128,128]{1,2,0:T(8,128)S(1)} %copy.32, f32[16,128,128]{1,2,0:T(8,128)S(1)} %copy.31, f32[16]{0:T(128)S(1)} %broadcast_select_fusion.1), kind=kLoop, calls=%fused_computation.48 | loop fusion | flops 786432 | bytes 2621504 | tf_op jit(solution)/shard_map/convert_element_type | solution.py:144
  71.0 2.2 %collective-permute-start.3 = (bf16[16,128,128]{1,2,0:T(8,128)(2,1)}, bf16[16,128,128]{1,2,0:T(8,128)(2,1)}, u32[]{:S(2)}, u32[]{:S(2)}) collective-permute-start(bf16[16,128,128]{1,2,0:T(8,128)(2,1)} %fusion.41), channel_id=1, source_target_pairs={{0,4},{2,6},{4,8},{6,10},{8,12},{10,14},{1,5},{3,7},{5,9},{7,11},{... | collective-permute-start | bytes 1572872 | tf_op jit(solution)/shard_map/ppermute | solution.py:16
  73.3 0.7 fusion.40
  74.0 2.0 %fusion.2 = (f32[2,8,128]{2,1,0:T(8,128)S(1)}, f32[2,640,128,8]{2,1,3,0:T(8,128)S(1)}) fusion(pred[128,640]{0,1:T(8,128)(4,1)S(1)} %fusion.40, bf16[128,2,8,128]{3,2,1,0:T(8,128)(2,1)} %bitcast.133, bf16[2,640,128]{2,1,0:T(8,128)(2,1)S(1)} %copy-done.3), kind=kOutput, calls=%fused_computation.4 | convolution fusion | flops 339474432 | bytes 6184960 | tf_op jit(solution)/shard_map/tkgd,ksd->kgts/dot_general | solution.py:45
  76.0 1.1 %fusion = f32[2,8,128]{2,1,0:T(8,128)S(1)} fusion(f32[2,640,128,8]{2,1,3,0:T(8,128)S(1)} %get-tuple-element.30, f32[2,8,128]{2,1,0:T(8,128)S(1)} %get-tuple-element.29, pred[128,640]{0,1:T(8,128)(4,1)S(1)} %fusion.40), kind=kLoop, calls=%fused_computation.2 | loop fusion | flops 5240832 | bytes 5341184 | tf_op jit(solution)/shard_map/reduce_sum | solution.py:49
  77.1 2.2 %divide_convert_fusion = bf16[128,2,8,128]{0,3,2,1:T(8,128)(2,1)} fusion(f32[2,640,128,8]{2,1,3,0:T(8,128)S(1)} %get-tuple-element.30, f32[2,8,128]{2,1,0:T(8,128)S(1)} %get-tuple-element.29, pred[128,640]{0,1:T(8,128)(4,1)S(1)} %fusion.40, f32[128,2,8]{0,2,1:T(8,128)S(1)} %bitcast.156, bf16[2,640,128]{1,2,0:T(8,128)(2,1)S(1)} %copy-done.6), kind=kOutput, calls=%fused_computation.15 | convolution fusion | flops 341311488 | bytes 6193152 | tf_op jit(solution)/shard_map/kgts,ksd->kgtd/dot_general | solution.py:50
  79.4 2.1 %copy.42 = bf16[128,2048]{1,0:T(8,128)(2,1)} copy(bf16[128,2048]{0,1:T(8,128)(2,1)} %bitcast.145) | data formatting | bytes 1048576
  81.4 0.6 broadcast_compare_fusion
  82.1 4.2 %collective-permute-done.3 = bf16[16,128,128]{1,2,0:T(8,128)(2,1)} collective-permute-done((bf16[16,128,128]{1,2,0:T(8,128)(2,1)}, bf16[16,128,128]{1,2,0:T(8,128)(2,1)}, u32[]{:S(2)}, u32[]{:S(2)}) %collective-permute-start.3) | collective-permute-done | bytes 524320 | tf_op jit(solution)/shard_map/ppermute | solution.py:16
  86.2 3.4 %fusion.10 = f32[128,16,128]{0,2,1:T(8,128)} fusion(bf16[16,128,128]{1,2,0:T(8,128)(2,1)} %collective-permute-done.3, f32[128,16]{0,1:T(8,128)S(1)} %select_bitcast_fusion, f32[16]{0:T(128)S(1)} %get-tuple-element.6, f32[16,128,128]{1,2,0:T(8,128)S(1)} %copy.32, f32[16,128,128]{1,2,0:T(8,128)S(1)} %copy.31, f32[16]{0:T(128)S(1)} %broadcast_select_fusion.1, ...), kind=kOutput, calls=%fused_computation.12 | convolution fusion | flops 404226048 | bytes 4202624 | tf_op jit(solution)/shard_map/thd,hde->the/dot_general | solution.py:152
  89.7 2.1 %multiply_reduce_fusion = (f32[128]{0:T(128)S(1)}, f32[128,16,128]{0,2,1:T(8,128)S(1)}) fusion(f32[128,16,128]{0,2,1:T(8,128)} %fusion.10, bf16[128,16,128]{0,2,1:T(8,128)(2,1)S(1)} %bitcast.132, f32[16,128]{1,0:T(8,128)S(1)} %reduce_window_sum.11, pred[128,128]{1,0:T(8,128)(4,1)S(1)} %copy-done.4, bf16[128,2048]{1,0:T(8,128)(2,1)S(1)} %copy-done, ...), kind=kOutput, calls=%fused_computation.18 | convolution fusion | flops 136052608 | bytes 3695104 | tf_op jit(solution)/shard_map/hts,shd->thd/dot_general | solution.py:30
  91.8 3.5 %psum.7 = f32[128]{0:T(128)S(1)} all-reduce(f32[128]{0:T(128)S(1)} %get-tuple-element.27), channel_id=1, replica_groups=mesh['groups'=2,'ctx'=8,'tensor'=2] {'tensor'}, use_global_device_ids=true, to_apply=%region_2.3 | all-reduce | flops 128 | bytes 1024 | tf_op jit(solution)/shard_map/psum | solution.py:159
  95.3 1.6 %multiply_convert_fusion = bf16[128,16,128]{0,2,1:T(8,128)(2,1)S(1)} fusion(f32[128,16,128]{0,2,1:T(8,128)} %bitcast.130, f32[128,16,128]{0,2,1:T(8,128)S(1)} %get-tuple-element.28, f32[16,128]{1,0:T(8,128)S(1)} %bitcast.155, f32[128]{0:T(128)S(1)} %add_rsqrt_fusion), kind=kLoop, calls=%fused_computation.16 | loop fusion | flops 1048576 | bytes 2630144 | tf_op jit(solution)/shard_map/convert_element_type | solution.py:164
  96.9 1.0 %copy.41 = bf16[128,2048]{1,0:T(8,128)(2,1)} copy(bf16[128,2048]{0,1:T(8,128)(2,1)S(1)} %bitcast.137) | data formatting | bytes 1048576
  (45 shorter events, 1.1 us)
Async XLA Ops:
  0.6 13.0 %copy-start = (bf16[128,2048]{1,0:T(8,128)(2,1)S(1)}, bf16[128,2048]{1,0:T(8,128)(2,1)}, u32[]{:S(2)}) copy-start(bf16[128,2048]{1,0:T(8,128)(2,1)} %param.12) | copy-start | bytes 1572868
  0.6 19.9 %copy-start.1 = (bf16[128,2048]{1,0:T(8,128)(2,1)S(1)}, bf16[128,2048]{1,0:T(8,128)(2,1)}, u32[]{:S(2)}) copy-start(bf16[128,2048]{1,0:T(8,128)(2,1)} %param.16) | copy-start | bytes 1572868
  1.4 10.8 %copy-start.8 = (f32[128]{0:T(128)}, f32[128]{0:T(128)S(1)}, u32[]{:S(2)}) copy-start(f32[128]{0:T(128)S(1)} %get-tuple-element.22) | copy-start | bytes 1540
  4.9 18.5 %collective-permute-start.4 = (bf16[528,128]{1,0:T(8,128)(2,1)S(1)}, bf16[528,128]{1,0:T(8,128)(2,1)}, u32[]{:S(2)}, u32[]{:S(2)}) collective-permute-start(bf16[528,128]{1,0:T(8,128)(2,1)S(1)} %pad_maximum_fusion.1), channel_id=1, source_target_pairs={{0,8},{2,10},{4,12},{6,14},{1,9},{3,11},{5,13},{7,15},{16,24},{18,... | collective-permute-start | bytes 405512 | tf_op jit(solution)/shard_map/ppermute | solution.py:16
  6.2 18.2 %collective-permute-start.2 = (bf16[528,128]{1,0:T(8,128)(2,1)S(1)}, bf16[528,128]{1,0:T(8,128)(2,1)}, u32[]{:S(2)}, u32[]{:S(2)}) collective-permute-start(bf16[528,128]{1,0:T(8,128)(2,1)S(1)} %pad_maximum_fusion.1), channel_id=1, source_target_pairs={{0,6},{2,8},{4,10},{6,12},{8,14},{1,7},{3,9},{5,11},{7,13},{9,15},... | collective-permute-start | bytes 405512 | tf_op jit(solution)/shard_map/ppermute | solution.py:16
  14.0 18.5 %collective-permute-start.1 = (bf16[2576,128]{1,0:T(8,128)(2,1)S(1)}, bf16[2576,128]{1,0:T(8,128)(2,1)}, u32[]{:S(2)}, u32[]{:S(2)}) collective-permute-start(bf16[2576,128]{1,0:T(8,128)(2,1)S(1)} %pad_maximum_fusion), channel_id=1, source_target_pairs={{0,4},{2,6},{4,8},{6,10},{8,12},{10,14},{1,5},{3,7},{5,9},{7,11},{... | collective-permute-start | bytes 1978376 | tf_op jit(solution)/shard_map/ppermute | solution.py:16
  15.9 35.3 %collective-permute-start = (bf16[2576,128]{1,0:T(8,128)(2,1)S(1)}, bf16[2576,128]{1,0:T(8,128)(2,1)}, u32[]{:S(2)}, u32[]{:S(2)}) collective-permute-start(bf16[2576,128]{1,0:T(8,128)(2,1)S(1)} %pad_maximum_fusion), channel_id=1, source_target_pairs={{0,2},{2,4},{4,6},{6,8},{8,10},{10,12},{12,14},{1,3},{3,5},{5,7},{... | collective-permute-start | bytes 1978376 | tf_op jit(solution)/shard_map/ppermute | solution.py:16
  24.3 48.9 %copy-start.9 = (f32[128]{0:T(128)S(1)}, f32[128]{0:T(128)}, u32[]{:S(2)}) copy-start(f32[128]{0:T(128)} %copy-done.8) | copy-start | bytes 1540
  26.7 9.1 %copy-start.2 = (bf16[2,640,128]{2,1,0:T(8,128)(2,1)}, bf16[2,640,128]{2,1,0:T(8,128)(2,1)S(1)}, u32[]{:S(2)}) copy-start(bf16[2,640,128]{2,1,0:T(8,128)(2,1)S(1)} %constant_dynamic-update-slice_fusion.8) | copy-start | bytes 983044
  26.7 9.1 %copy-start.5 = (bf16[2,640,128]{1,2,0:T(8,128)(2,1)}, bf16[2,640,128]{1,2,0:T(8,128)(2,1)S(1)}, u32[]{:S(2)}) copy-start(bf16[2,640,128]{1,2,0:T(8,128)(2,1)S(1)} %constant_dynamic-update-slice_fusion.3) | copy-start | bytes 983044
  62.8 10.4 %copy-start.10 = (f32[640]{0:T(1024)S(1)}, f32[640]{0:T(1024)}, u32[]{:S(2)}) copy-start(f32[640]{0:T(1024)} %constant_dynamic-update-slice_fusion.10) | copy-start | bytes 7684
  66.0 8.0 %copy-start.3 = (bf16[2,640,128]{2,1,0:T(8,128)(2,1)S(1)}, bf16[2,640,128]{2,1,0:T(8,128)(2,1)}, u32[]{:S(2)}) copy-start(bf16[2,640,128]{2,1,0:T(8,128)(2,1)} %bitcast_dynamic-update-slice_fusion) | copy-start | bytes 983044
  71.0 15.2 %collective-permute-start.3 = (bf16[16,128,128]{1,2,0:T(8,128)(2,1)}, bf16[16,128,128]{1,2,0:T(8,128)(2,1)}, u32[]{:S(2)}, u32[]{:S(2)}) collective-permute-start(bf16[16,128,128]{1,2,0:T(8,128)(2,1)} %fusion.41), channel_id=1, source_target_pairs={{0,4},{2,6},{4,8},{6,10},{8,12},{10,14},{1,5},{3,7},{5,9},{7,11},{... | collective-permute-start | bytes 1572872 | tf_op jit(solution)/shard_map/ppermute | solution.py:16
  74.0 3.1 %copy-start.6 = (bf16[2,640,128]{1,2,0:T(8,128)(2,1)S(1)}, bf16[2,640,128]{1,2,0:T(8,128)(2,1)}, u32[]{:S(2)}) copy-start(bf16[2,640,128]{1,2,0:T(8,128)(2,1)} %constant_dynamic-update-slice_fusion) | copy-start | bytes 983044
  77.1 4.3 %copy-start.11 = (s32[128]{0:T(128)S(1)}, s32[128]{0:T(128)}, u32[]{:S(2)}) copy-start(s32[128]{0:T(128)} %param.19) | copy-start | bytes 1540
  79.4 10.3 %copy-start.4 = (pred[128,128]{1,0:T(8,128)(4,1)S(1)}, pred[128,128]{1,0:T(8,128)(4,1)}, u32[]{:S(2)}) copy-start(pred[128,128]{1,0:T(8,128)(4,1)} %fusion.42) | copy-start | bytes 49156
  79.4 15.9 %copy-start.7 = (f32[2048]{0:T(1024)S(1)}, f32[2048]{0:T(1024)}, u32[]{:S(2)}) copy-start(f32[2048]{0:T(1024)} %param.15) | copy-start | bytes 24580

commit v5 on v4

--- a/solution.py
+++ b/solution.py
@@ -120,12 +120,15 @@
 
     def unpack(block):
         state = block[:state_rows].reshape(heads_here, head_size, head_size).astype(F32)
-        keys = block[state_rows : state_rows + kv_rows].reshape(kv_here, tok_rows, head_size)
-        values = block[state_rows + kv_rows : state_rows + 2 * kv_rows].reshape(kv_here, tok_rows, head_size)
         meta = block[state_rows + 2 * kv_rows :].reshape(-1)
         codes = meta[:tok_rows].astype(F32)
         decay = join_parts(meta[tok_rows : tok_rows + 3 * heads_here])
-        return state, keys, values, codes, decay
+        return state, codes, decay
+
+    def unpack_near_kv(block):
+        keys = block[state_rows : state_rows + kv_rows].reshape(kv_here, tok_rows, head_size)
+        values = block[state_rows + kv_rows : state_rows + 2 * kv_rows].reshape(kv_here, tok_rows, head_size)
+        return keys, values
 
     def unpack_kv(block):
         keys = block[:kv_rows].reshape(kv_here, tok_rows, head_size)
@@ -133,10 +136,9 @@
         codes = block[2 * kv_rows :].reshape(-1)[:tok_rows].astype(F32)
         return keys, values, codes
 
-    state_1, keys_1, values_1, code_1, decay_1 = unpack(from_1)
-    state_2, keys_2, values_2, code_2, decay_2 = unpack(from_2)
-    keys_3, values_3, code_3 = unpack_kv(from_3)
-    keys_4, values_4, code_4 = unpack_kv(from_4)
+    state_1, code_1, decay_1 = unpack(from_1)
+    state_2, code_2, decay_2 = unpack(from_2)
+    code_3 = from_3[2 * kv_rows :].reshape(-1)[:tok_rows].astype(F32)
 
     link_1 = (code_2[-1] == code_1[0]) & (code_1[0] == code_1[-1])
     pair_state = state_1 + jnp.where(link_1, decay_1, 0.0)[:, None, None] * state_2
@@ -163,6 +165,10 @@
     normed = mixed * inverse[:, None, None] * norm_gain.reshape(heads_here, head_size) * gate_open
     light_out = normed.reshape(tok_rows, heads_here * head_size).astype(BF16)
 
+    keys_1, values_1 = unpack_near_kv(from_1)
+    keys_2, values_2 = unpack_near_kv(from_2)
+    keys_3, values_3, code_3 = unpack_kv(from_3)
+    keys_4, values_4, code_4 = unpack_kv(from_4)
     key_window = jnp.concatenate([keys_4, keys_3, keys_2, keys_1, own_keys], axis=1)
     value_window = jnp.concatenate([values_4, values_3, values_2, values_1, own_values], axis=1)
     code_window = jnp.concatenate([code_4, code_3, code_2, code_1, code])

time: 99.2 us -> 99.2 us (level)
  no operation moved by 1% of the time
where the time goes in v5:
time: 99.2 us; the launch traced here: 97.9 us
  local copies, waits for them, and re-layouts  25 us (25%)
  other arithmetic  21.9 us (22%)
  waiting for transfers between devices  19.9 us (20%)
  starting transfers between devices  11.5 us (12%)
  matrix products  10.1 us (10%)
  between operations  5.97 us (6%)
  blocking collectives  3.47 us (3%)
    ppermute x5, waiting for transfers between devices, shifted(): return lax.ppermute(block, axis, route)  19.9 us
    ppermute x5, starting transfers between devices, shifted(): return lax.ppermute(block, axis, route)  11.5 us
    unnamed x37, local copies, waits for them, and re-layouts  8.57 us
    unnamed x5, other arithmetic  5.16 us
    psum x1, blocking collectives, on_device_body(): squares = lax.psum(squares, 'tensor')  3.47 us
    dot_general x1, matrix products, on_device_body(): jnp.einsum('thd,hde->the', query_heads.astype(F32), incoming_state, preci...  3.43 us
    slice x2, local copies, waits for them, and re-layouts, unpack(): block[:state_rows].reshape(heads_here, head_size, head_size).astype(F32)  3 us
    dot_general x1, matrix products, soft_window(): jnp.einsum('kgts,ksd->kgtd', prob_block.astype(BF16), value_heads, prefer...  2.24 us
  transfers between devices with their start and end apart: 5, of which 3 were waited for; matrix products, arithmetic and copies ran while one was open for 30% of the time, Pallas kernels for 0%

profile of v5, /device:TPU:17, one launch (start us, length us, event | category | flops | bytes accessed | tf_op | source)
XLA Modules:
  0.0 97.9 jit_solution(2043715211390604770)
XLA Ops:
  0.7 0.7 convert_add_fusion
  1.4 1.0 %reduce_window_sum.11 = f32[16,128]{1,0:T(8,128)S(1)} reduce-window(f32[16,128]{1,0:T(8,128)} %param.14, f32[]{:T(128)} %constant.10.clone.1), window={size=1x128 pad=0_0x127_0}, to_apply=%region_0.0 | reduce-window | flops 260096 | bytes 16388 | tf_op jit(solution)/shard_map/jit(cumsum)/reduce_window_sum | solution.py:92
  2.4 0.2 slice_reduce_fusion
  2.6 1.0 copy.27
  3.7 1.0 copy.29
  4.9 1.3 %collective-permute-start.4 = (bf16[528,128]{1,0:T(8,128)(2,1)S(1)}, bf16[528,128]{1,0:T(8,128)(2,1)}, u32[]{:S(2)}, u32[]{:S(2)}) collective-permute-start(bf16[528,128]{1,0:T(8,128)(2,1)S(1)} %pad_maximum_fusion.1), channel_id=1, source_target_pairs={{0,8},{2,10},{4,12},{6,14},{1,9},{3,11},{5,13},{7,15},{16,24},{18,... | collective-permute-start | bytes 405512 | tf_op jit(solution)/shard_map/ppermute | solution.py:16
  6.2 4.1 %collective-permute-start.2 = (bf16[528,128]{1,0:T(8,128)(2,1)S(1)}, bf16[528,128]{1,0:T(8,128)(2,1)}, u32[]{:S(2)}, u32[]{:S(2)}) collective-permute-start(bf16[528,128]{1,0:T(8,128)(2,1)S(1)} %pad_maximum_fusion.1), channel_id=1, source_target_pairs={{0,6},{2,8},{4,10},{6,12},{8,14},{1,7},{3,9},{5,11},{7,13},{9,15},... | collective-permute-start | bytes 405512 | tf_op jit(solution)/shard_map/ppermute | solution.py:16
  10.3 0.6 slice.115
  10.9 1.3 %broadcast_compare_fusion.1 = pred[128]{0:T(512)(128)(4,1)S(1)} fusion(f32[]{:T(128)} %bitcast.2, s32[128]{0:T(128)} %param.19), kind=kLoop, calls=%fused_computation.101 | loop fusion | flops 384 | bytes 644 | tf_op jit(solution)/shard_map/eq | solution.py:31
  12.3 1.3 %copy.46 = bf16[128,2048]{0,1:T(8,128)(2,1)S(1)} copy(bf16[128,2048]{1,0:T(8,128)(2,1)} %param.11) | data formatting | bytes 1048576 | tf_op jit(solution)/shard_map/reshape | solution.py:23
  13.6 0.3 convolution_convert_fusion
  14.0 1.9 %collective-permute-start.1 = (bf16[2576,128]{1,0:T(8,128)(2,1)S(1)}, bf16[2576,128]{1,0:T(8,128)(2,1)}, u32[]{:S(2)}, u32[]{:S(2)}) collective-permute-start(bf16[2576,128]{1,0:T(8,128)(2,1)S(1)} %pad_maximum_fusion), channel_id=1, source_target_pairs={{0,4},{2,6},{4,8},{6,10},{8,12},{10,14},{1,5},{3,7},{5,9},{7,11},{... | collective-permute-start | bytes 1978376 | tf_op jit(solution)/shard_map/ppermute | solution.py:16
  15.9 1.9 %collective-permute-start = (bf16[2576,128]{1,0:T(8,128)(2,1)S(1)}, bf16[2576,128]{1,0:T(8,128)(2,1)}, u32[]{:S(2)}, u32[]{:S(2)}) collective-permute-start(bf16[2576,128]{1,0:T(8,128)(2,1)S(1)} %pad_maximum_fusion), channel_id=1, source_target_pairs={{0,2},{2,4},{4,6},{6,8},{8,10},{10,12},{12,14},{1,3},{3,5},{5,7},{... | collective-permute-start | bytes 1978376 | tf_op jit(solution)/shard_map/ppermute | solution.py:16
  17.8 1.3 %add_divide_fusion = f32[128,2048]{1,0:T(8,128)S(1)} fusion(bf16[128,2048]{1,0:T(8,128)(2,1)} %param.13), kind=kLoop, calls=%fused_computation.17 | loop fusion | flops 1048576 | bytes 1572864 | tf_op jit(solution)/shard_map/div | solution.py:164
  19.2 1.4 %fusion.42 = pred[128,128]{1,0:T(8,128)(4,1)} fusion(f32[128]{0:T(128)} %copy-done.8), kind=kLoop, calls=%fused_computation.52 | loop fusion | flops 49152 | bytes 16896 | tf_op jit(solution)/shard_map/and | solution.py:26
  20.6 0.9 copy.49
  21.5 1.3 %copy.34 = f32[128,2048]{0,1:T(8,128)} copy(f32[128,2048]{1,0:T(8,128)S(1)} %add_divide_fusion) | data formatting | bytes 2097152 | tf_op jit(solution)/shard_map/div | solution.py:164
  22.8 0.5 iota_add_fusion
  23.3 0.9 fusion.60
  24.4 0.7 slice_convert_fusion.1
  25.0 0.6 slice.130
  25.6 0.9 fusion.59
  26.7 1.3 %constant_dynamic-update-slice_fusion.5 = f32[640]{0:T(1024)} fusion(f32[640]{0:T(1024)} %custom-call.1, bf16[528,128]{1,0:T(8,128)(2,1)} %collective-permute-done.4), kind=kLoop, calls=%fused_computation.58 | loop fusion | flops 128 | bytes 1024
  28.0 1.3 %constant_dynamic-update-slice_fusion.13 = f32[640]{0:T(1024)} fusion(f32[640]{0:T(1024)} %constant_dynamic-update-slice_fusion.5, bf16[528,128]{1,0:T(8,128)(2,1)} %collective-permute-done.2), kind=kLoop, calls=%fused_computation.72 | loop fusion | flops 128 | bytes 1024
  29.3 3.2 %collective-permute-done.1 = bf16[2576,128]{1,0:T(8,128)(2,1)} collective-permute-done((bf16[2576,128]{1,0:T(8,128)(2,1)S(1)}, bf16[2576,128]{1,0:T(8,128)(2,1)}, u32[]{:S(2)}, u32[]{:S(2)}) %collective-permute-start.1) | collective-permute-done | bytes 659488 | tf_op jit(solution)/shard_map/ppermute | solution.py:16
  32.5 0.7 slice_convert_fusion.4
  33.1 0.6 fusion.62
  33.7 0.9 fusion.58
  34.7 1.1 %slice.152 = bf16[2048,128]{1,0:T(8,128)(2,1)S(1)} slice(bf16[2576,128]{1,0:T(8,128)(2,1)} %collective-permute-done.1), slice={[0:2048], [0:128]} | slice | bytes 1048576 | tf_op jit(solution)/shard_map/slice | solution.py:122
  35.8 0.2 copy.31
  36.1 0.7 slice_bitcast_fusion
  36.7 0.6 slice_convert_fusion
  37.3 1.3 %constant_dynamic-update-slice_fusion.12 = f32[640]{0:T(1024)} fusion(f32[640]{0:T(1024)} %constant_dynamic-update-slice_fusion.13, bf16[2576,128]{1,0:T(8,128)(2,1)} %collective-permute-done.1), kind=kLoop, calls=%fused_computation.71 | loop fusion | flops 128 | bytes 1024
  38.6 12.6 %collective-permute-done = bf16[2576,128]{1,0:T(8,128)(2,1)} collective-permute-done((bf16[2576,128]{1,0:T(8,128)(2,1)S(1)}, bf16[2576,128]{1,0:T(8,128)(2,1)}, u32[]{:S(2)}, u32[]{:S(2)}) %collective-permute-start) | collective-permute-done | bytes 659488 | tf_op jit(solution)/shard_map/ppermute | solution.py:16
  51.2 1.3 %constant_dynamic-update-slice_fusion.11 = f32[640]{0:T(1024)} fusion(f32[640]{0:T(1024)} %constant_dynamic-update-slice_fusion.12, bf16[2576,128]{1,0:T(8,128)(2,1)} %collective-permute-done), kind=kLoop, calls=%fused_computation.70 | loop fusion | flops 128 | bytes 1024
  52.5 1.3 %constant_dynamic-update-slice_fusion.10 = f32[640]{0:T(1024)} fusion(f32[640]{0:T(1024)} %constant_dynamic-update-slice_fusion.11, s32[128]{0:T(128)} %param.19), kind=kLoop, calls=%fused_computation.69 | loop fusion | flops 256 | bytes 1024 | tf_op jit(solution)/shard_map/concatenate | solution.py:174
  53.8 0.7 slice_convert_fusion.3
  54.5 0.6 fusion.61
  60.0 0.7 slice_bitcast_fusion.1
  60.7 0.5 slice_convert_fusion.2
  61.2 0.9 fusion.57
  62.2 0.6 constant_dynamic-update-slice_fusion.2
  62.8 0.6 constant_dynamic-update-slice_fusion.1
  63.5 0.6 constant_dynamic-update-slice_fusion
  64.1 0.6 constant_dynamic-update-slice_fusion.7
  64.8 0.6 constant_dynamic-update-slice_fusion.6
  65.4 0.6 bitcast_dynamic-update-slice_fusion
  66.0 1.9 %slice.147 = bf16[2048,128]{1,0:T(8,128)(2,1)} slice(bf16[2576,128]{1,0:T(8,128)(2,1)} %collective-permute-done), slice={[0:2048], [0:128]} | slice | bytes 1048576 | tf_op jit(solution)/shard_map/slice | solution.py:122
  67.9 1.2 %copy.32 = f32[16,128,128]{1,2,0:T(8,128)S(1)} copy(bf16[16,128,128]{2,1,0:T(8,128)(2,1)} %bitcast.135) | data formatting | bytes 1572864 | tf_op jit(solution)/shard_map/convert_element_type | solution.py:122
  69.2 0.9 broadcast_select_fusion
  70.1 1.0 %fusion.41 = bf16[16,128,128]{1,2,0:T(8,128)(2,1)} fusion(f32[16,128,128]{1,2,0:T(8,128)S(1)} %copy.32, f32[16,128,128]{1,2,0:T(8,128)S(1)} %copy.31, f32[16]{0:T(128)S(1)} %broadcast_select_fusion.1), kind=kLoop, calls=%fused_computation.48 | loop fusion | flops 786432 | bytes 2621504 | tf_op jit(solution)/shard_map/convert_element_type | solution.py:146
  71.0 2.2 %collective-permute-start.3 = (bf16[16,128,128]{1,2,0:T(8,128)(2,1)}, bf16[16,128,128]{1,2,0:T(8,128)(2,1)}, u32[]{:S(2)}, u32[]{:S(2)}) collective-permute-start(bf16[16,128,128]{1,2,0:T(8,128)(2,1)} %fusion.41), channel_id=1, source_target_pairs={{0,4},{2,6},{4,8},{6,10},{8,12},{10,14},{1,5},{3,7},{5,9},{7,11},{... | collective-permute-start | bytes 1572872 | tf_op jit(solution)/shard_map/ppermute | solution.py:16
  73.3 0.7 fusion.40
  74.0 2.0 %fusion.2 = (f32[2,8,128]{2,1,0:T(8,128)S(1)}, f32[2,640,128,8]{2,1,3,0:T(8,128)S(1)}) fusion(pred[128,640]{0,1:T(8,128)(4,1)S(1)} %fusion.40, bf16[128,2,8,128]{3,2,1,0:T(8,128)(2,1)} %bitcast.133, bf16[2,640,128]{2,1,0:T(8,128)(2,1)S(1)} %copy-done.3), kind=kOutput, calls=%fused_computation.4 | convolution fusion | flops 339474432 | bytes 6184960 | tf_op jit(solution)/shard_map/tkgd,ksd->kgts/dot_general | solution.py:45
  76.0 1.1 %fusion = f32[2,8,128]{2,1,0:T(8,128)S(1)} fusion(f32[2,640,128,8]{2,1,3,0:T(8,128)S(1)} %get-tuple-element.30, f32[2,8,128]{2,1,0:T(8,128)S(1)} %get-tuple-element.29, pred[128,640]{0,1:T(8,128)(4,1)S(1)} %fusion.40), kind=kLoop, calls=%fused_computation.2 | loop fusion | flops 5240832 | bytes 5341184 | tf_op jit(solution)/shard_map/reduce_sum | solution.py:49
  77.1 2.2 %divide_convert_fusion = bf16[128,2,8,128]{0,3,2,1:T(8,128)(2,1)} fusion(f32[2,640,128,8]{2,1,3,0:T(8,128)S(1)} %get-tuple-element.30, f32[2,8,128]{2,1,0:T(8,128)S(1)} %get-tuple-element.29, pred[128,640]{0,1:T(8,128)(4,1)S(1)} %fusion.40, f32[128,2,8]{0,2,1:T(8,128)S(1)} %bitcast.156, bf16[2,640,128]{1,2,0:T(8,128)(2,1)S(1)} %copy-done.6), kind=kOutput, calls=%fused_computation.15 | convolution fusion | flops 341311488 | bytes 6193152 | tf_op jit(solution)/shard_map/kgts,ksd->kgtd/dot_general | solution.py:50
  79.4 2.1 %copy.42 = bf16[128,2048]{1,0:T(8,128)(2,1)} copy(bf16[128,2048]{0,1:T(8,128)(2,1)} %bitcast.145) | data formatting | bytes 1048576
  81.4 0.6 broadcast_compare_fusion
  82.1 4.2 %collective-permute-done.3 = bf16[16,128,128]{1,2,0:T(8,128)(2,1)} collective-permute-done((bf16[16,128,128]{1,2,0:T(8,128)(2,1)}, bf16[16,128,128]{1,2,0:T(8,128)(2,1)}, u32[]{:S(2)}, u32[]{:S(2)}) %collective-permute-start.3) | collective-permute-done | bytes 524320 | tf_op jit(solution)/shard_map/ppermute | solution.py:16
  86.2 3.4 %fusion.10 = f32[128,16,128]{0,2,1:T(8,128)} fusion(bf16[16,128,128]{1,2,0:T(8,128)(2,1)} %collective-permute-done.3, f32[128,16]{0,1:T(8,128)S(1)} %select_bitcast_fusion, f32[16]{0:T(128)S(1)} %get-tuple-element.6, f32[16,128,128]{1,2,0:T(8,128)S(1)} %copy.32, f32[16,128,128]{1,2,0:T(8,128)S(1)} %copy.31, f32[16]{0:T(128)S(1)} %broadcast_select_fusion.1, ...), kind=kOutput, calls=%fused_computation.12 | convolution fusion | flops 404226048 | bytes 4202624 | tf_op jit(solution)/shard_map/thd,hde->the/dot_general | solution.py:154
  89.7 2.1 %multiply_reduce_fusion = (f32[128]{0:T(128)S(1)}, f32[128,16,128]{0,2,1:T(8,128)S(1)}) fusion(f32[128,16,128]{0,2,1:T(8,128)} %fusion.10, bf16[128,16,128]{0,2,1:T(8,128)(2,1)S(1)} %bitcast.132, f32[16,128]{1,0:T(8,128)S(1)} %reduce_window_sum.11, pred[128,128]{1,0:T(8,128)(4,1)S(1)} %copy-done.4, bf16[128,2048]{1,0:T(8,128)(2,1)S(1)} %copy-done, ...), kind=kOutput, calls=%fused_computation.18 | convolution fusion | flops 136052608 | bytes 3695104 | tf_op jit(solution)/shard_map/hts,shd->thd/dot_general | solution.py:30
  91.8 3.5 %psum.7 = f32[128]{0:T(128)S(1)} all-reduce(f32[128]{0:T(128)S(1)} %get-tuple-element.27), channel_id=1, replica_groups=mesh['groups'=2,'ctx'=8,'tensor'=2] {'tensor'}, use_global_device_ids=true, to_apply=%region_2.3 | all-reduce | flops 128 | bytes 1024 | tf_op jit(solution)/shard_map/psum | solution.py:161
  95.3 1.6 %multiply_convert_fusion = bf16[128,16,128]{0,2,1:T(8,128)(2,1)S(1)} fusion(f32[128,16,128]{0,2,1:T(8,128)} %bitcast.130, f32[128,16,128]{0,2,1:T(8,128)S(1)} %get-tuple-element.28, f32[16,128]{1,0:T(8,128)S(1)} %bitcast.155, f32[128]{0:T(128)S(1)} %add_rsqrt_fusion), kind=kLoop, calls=%fused_computation.16 | loop fusion | flops 1048576 | bytes 2630144 | tf_op jit(solution)/shard_map/convert_element_type | solution.py:166
  96.9 1.0 %copy.41 = bf16[128,2048]{1,0:T(8,128)(2,1)} copy(bf16[128,2048]{0,1:T(8,128)(2,1)S(1)} %bitcast.137) | data formatting | bytes 1048576
  (45 shorter events, 1.1 us)
Async XLA Ops:
  0.6 13.0 %copy-start = (bf16[128,2048]{1,0:T(8,128)(2,1)S(1)}, bf16[128,2048]{1,0:T(8,128)(2,1)}, u32[]{:S(2)}) copy-start(bf16[128,2048]{1,0:T(8,128)(2,1)} %param.12) | copy-start | bytes 1572868
  0.6 19.9 %copy-start.1 = (bf16[128,2048]{1,0:T(8,128)(2,1)S(1)}, bf16[128,2048]{1,0:T(8,128)(2,1)}, u32[]{:S(2)}) copy-start(bf16[128,2048]{1,0:T(8,128)(2,1)} %param.16) | copy-start | bytes 1572868
  1.4 10.8 %copy-start.8 = (f32[128]{0:T(128)}, f32[128]{0:T(128)S(1)}, u32[]{:S(2)}) copy-start(f32[128]{0:T(128)S(1)} %get-tuple-element.22) | copy-start | bytes 1540
  4.9 18.5 %collective-permute-start.4 = (bf16[528,128]{1,0:T(8,128)(2,1)S(1)}, bf16[528,128]{1,0:T(8,128)(2,1)}, u32[]{:S(2)}, u32[]{:S(2)}) collective-permute-start(bf16[528,128]{1,0:T(8,128)(2,1)S(1)} %pad_maximum_fusion.1), channel_id=1, source_target_pairs={{0,8},{2,10},{4,12},{6,14},{1,9},{3,11},{5,13},{7,15},{16,24},{18,... | collective-permute-start | bytes 405512 | tf_op jit(solution)/shard_map/ppermute | solution.py:16
  6.2 18.2 %collective-permute-start.2 = (bf16[528,128]{1,0:T(8,128)(2,1)S(1)}, bf16[528,128]{1,0:T(8,128)(2,1)}, u32[]{:S(2)}, u32[]{:S(2)}) collective-permute-start(bf16[528,128]{1,0:T(8,128)(2,1)S(1)} %pad_maximum_fusion.1), channel_id=1, source_target_pairs={{0,6},{2,8},{4,10},{6,12},{8,14},{1,7},{3,9},{5,11},{7,13},{9,15},... | collective-permute-start | bytes 405512 | tf_op jit(solution)/shard_map/ppermute | solution.py:16
  14.0 18.5 %collective-permute-start.1 = (bf16[2576,128]{1,0:T(8,128)(2,1)S(1)}, bf16[2576,128]{1,0:T(8,128)(2,1)}, u32[]{:S(2)}, u32[]{:S(2)}) collective-permute-start(bf16[2576,128]{1,0:T(8,128)(2,1)S(1)} %pad_maximum_fusion), channel_id=1, source_target_pairs={{0,4},{2,6},{4,8},{6,10},{8,12},{10,14},{1,5},{3,7},{5,9},{7,11},{... | collective-permute-start | bytes 1978376 | tf_op jit(solution)/shard_map/ppermute | solution.py:16
  15.9 35.3 %collective-permute-start = (bf16[2576,128]{1,0:T(8,128)(2,1)S(1)}, bf16[2576,128]{1,0:T(8,128)(2,1)}, u32[]{:S(2)}, u32[]{:S(2)}) collective-permute-start(bf16[2576,128]{1,0:T(8,128)(2,1)S(1)} %pad_maximum_fusion), channel_id=1, source_target_pairs={{0,2},{2,4},{4,6},{6,8},{8,10},{10,12},{12,14},{1,3},{3,5},{5,7},{... | collective-permute-start | bytes 1978376 | tf_op jit(solution)/shard_map/ppermute | solution.py:16
  24.3 48.9 %copy-start.9 = (f32[128]{0:T(128)S(1)}, f32[128]{0:T(128)}, u32[]{:S(2)}) copy-start(f32[128]{0:T(128)} %copy-done.8) | copy-start | bytes 1540
  26.7 9.1 %copy-start.2 = (bf16[2,640,128]{2,1,0:T(8,128)(2,1)}, bf16[2,640,128]{2,1,0:T(8,128)(2,1)S(1)}, u32[]{:S(2)}) copy-start(bf16[2,640,128]{2,1,0:T(8,128)(2,1)S(1)} %constant_dynamic-update-slice_fusion.8) | copy-start | bytes 983044
  26.7 9.1 %copy-start.5 = (bf16[2,640,128]{1,2,0:T(8,128)(2,1)}, bf16[2,640,128]{1,2,0:T(8,128)(2,1)S(1)}, u32[]{:S(2)}) copy-start(bf16[2,640,128]{1,2,0:T(8,128)(2,1)S(1)} %constant_dynamic-update-slice_fusion.3) | copy-start | bytes 983044
  62.8 10.4 %copy-start.10 = (f32[640]{0:T(1024)S(1)}, f32[640]{0:T(1024)}, u32[]{:S(2)}) copy-start(f32[640]{0:T(1024)} %constant_dynamic-update-slice_fusion.10) | copy-start | bytes 7684
  66.0 8.0 %copy-start.3 = (bf16[2,640,128]{2,1,0:T(8,128)(2,1)S(1)}, bf16[2,640,128]{2,1,0:T(8,128)(2,1)}, u32[]{:S(2)}) copy-start(bf16[2,640,128]{2,1,0:T(8,128)(2,1)} %bitcast_dynamic-update-slice_fusion) | copy-start | bytes 983044
  71.0 15.2 %collective-permute-start.3 = (bf16[16,128,128]{1,2,0:T(8,128)(2,1)}, bf16[16,128,128]{1,2,0:T(8,128)(2,1)}, u32[]{:S(2)}, u32[]{:S(2)}) collective-permute-start(bf16[16,128,128]{1,2,0:T(8,128)(2,1)} %fusion.41), channel_id=1, source_target_pairs={{0,4},{2,6},{4,8},{6,10},{8,12},{10,14},{1,5},{3,7},{5,9},{7,11},{... | collective-permute-start | bytes 1572872 | tf_op jit(solution)/shard_map/ppermute | solution.py:16
  74.0 3.1 %copy-start.6 = (bf16[2,640,128]{1,2,0:T(8,128)(2,1)S(1)}, bf16[2,640,128]{1,2,0:T(8,128)(2,1)}, u32[]{:S(2)}) copy-start(bf16[2,640,128]{1,2,0:T(8,128)(2,1)} %constant_dynamic-update-slice_fusion) | copy-start | bytes 983044
  77.1 4.3 %copy-start.11 = (s32[128]{0:T(128)S(1)}, s32[128]{0:T(128)}, u32[]{:S(2)}) copy-start(s32[128]{0:T(128)} %param.19) | copy-start | bytes 1540
  79.4 10.3 %copy-start.4 = (pred[128,128]{1,0:T(8,128)(4,1)S(1)}, pred[128,128]{1,0:T(8,128)(4,1)}, u32[]{:S(2)}) copy-start(pred[128,128]{1,0:T(8,128)(4,1)} %fusion.42) | copy-start | bytes 49156
  79.4 15.9 %copy-start.7 = (f32[2048]{0:T(1024)S(1)}, f32[2048]{0:T(1024)}, u32[]{:S(2)}) copy-start(f32[2048]{0:T(1024)} %param.15) | copy-start | bytes 24580

commit v6 on v3

--- a/solution.py
+++ b/solution.py
@@ -97,51 +97,40 @@
     own_values = soft_value.reshape(tok_rows, kv_here, head_size).transpose(1, 0, 2)
     state_rows = heads_here * head_size
     kv_rows = kv_here * tok_rows
-    own = jnp.concatenate(
+    own_state = local_state.astype(BF16)
+    own_kv = jnp.concatenate(
         [
-            local_state.astype(BF16).reshape(state_rows, head_size),
             own_keys.reshape(kv_rows, head_size),
             own_values.reshape(kv_rows, head_size),
             rows_of(jnp.concatenate([code, split_parts(block_decay)]), head_size),
         ]
     )
-    from_1 = shifted(own, "ctx", 1)
-    from_2 = shifted(own, "ctx", 2)
-    kv_only = jnp.concatenate(
-        [
-            own_keys.reshape(kv_rows, head_size),
-            own_values.reshape(kv_rows, head_size),
-            rows_of(code, head_size),
-        ]
-    )
-    from_3 = shifted(kv_only, "ctx", 3)
-    from_4 = shifted(kv_only, "ctx", 4)
+    state_1, kv_1 = shifted((own_state, own_kv), "ctx", 1)
+    state_2, kv_2 = shifted((own_state, own_kv), "ctx", 2)
 
     def unpack(block):
-        state = block[:state_rows].reshape(heads_here, head_size, head_size).astype(F32)
-        keys = block[state_rows : state_rows + kv_rows].reshape(kv_here, tok_rows, head_size)
-        values = block[state_rows + kv_rows : state_rows + 2 * kv_rows].reshape(kv_here, tok_rows, head_size)
-        meta = block[state_rows + 2 * kv_rows :].reshape(-1)
+        keys = block[:kv_rows].reshape(kv_here, tok_rows, head_size)
+        values = block[kv_rows : 2 * kv_rows].reshape(kv_here, tok_rows, head_size)
+        meta = block[2 * kv_rows :].reshape(-1)
         codes = meta[:tok_rows].astype(F32)
         decay = join_parts(meta[tok_rows : tok_rows + 3 * heads_here])
-        return state, keys, values, codes, decay
+        return keys, values, codes, decay
 
-    def unpack_kv(block):
-        keys = block[:kv_rows].reshape(kv_here, tok_rows, head_size)
-        values = block[kv_rows : 2 * kv_rows].reshape(kv_here, tok_rows, head_size)
-        codes = block[2 * kv_rows :].reshape(-1)[:tok_rows].astype(F32)
-        return keys, values, codes
-
-    state_1, keys_1, values_1, code_1, decay_1 = unpack(from_1)
-    state_2, keys_2, values_2, code_2, decay_2 = unpack(from_2)
-    keys_3, values_3, code_3 = unpack_kv(from_3)
-    keys_4, values_4, code_4 = unpack_kv(from_4)
+    keys_1, values_1, code_1, decay_1 = unpack(kv_1)
+    keys_2, values_2, code_2, decay_2 = unpack(kv_2)
 
     link_1 = (code_2[-1] == code_1[0]) & (code_1[0] == code_1[-1])
-    pair_state = state_1 + jnp.where(link_1, decay_1, 0.0)[:, None, None] * state_2
+    pair_state = state_1.astype(F32) + jnp.where(link_1, decay_1, 0.0)[:, None, None] * state_2.astype(F32)
 
-    from_far = shifted(pair_state.astype(BF16), "ctx", 2)
-    state_far = from_far.astype(F32)
+    relay_kv = jnp.concatenate([kv_2[: 2 * kv_rows], kv_1[: 2 * kv_rows], rows_of(jnp.concatenate([code_2, code_1]), head_size)])
+    state_far, kv_far = shifted((pair_state.astype(BF16), relay_kv), "ctx", 2)
+    state_far = state_far.astype(F32)
+    keys_4 = kv_far[:kv_rows].reshape(kv_here, tok_rows, head_size)
+    values_4 = kv_far[kv_rows : 2 * kv_rows].reshape(kv_here, tok_rows, head_size)
+    keys_3 = kv_far[2 * kv_rows : 3 * kv_rows].reshape(kv_here, tok_rows, head_size)
+    values_3 = kv_far[3 * kv_rows : 4 * kv_rows].reshape(kv_here, tok_rows, head_size)
+    code_far = kv_far[4 * kv_rows :].reshape(-1)[: 2 * tok_rows].astype(F32)
+    code_4, code_3 = code_far[:tok_rows], code_far[tok_rows:]
 
     link_2 = (code_3[-1] == code_2[0]) & (code_2[0] == code_1[-1])
     carry_scale = jnp.where(link_2, decay_2 * decay_1, 0.0)

time: 99.2 us -> 97.9 us (0.987)
  the two profiles are of different devices: /device:TPU:17 before, /device:TPU:11 now
where the time goes in v6:
time: 97.9 us; the launch traced here: 96.7 us
  local copies, waits for them, and re-layouts  25 us (26%)
  other arithmetic  17.6 us (18%)
  starting transfers between devices  16.5 us (17%)
  waiting for transfers between devices  15.6 us (16%)
  matrix products  10.8 us (11%)
  between operations  5.95 us (6%)
  blocking collectives  5.07 us (5%)
    ppermute x6, starting transfers between devices, shifted(): return lax.ppermute(block, axis, route)  16.5 us
    ppermute x6, waiting for transfers between devices, shifted(): return lax.ppermute(block, axis, route)  15.6 us
    unnamed x35, local copies, waits for them, and re-layouts  11.6 us
    psum x1, blocking collectives, on_device(): squares = lax.psum(squares, 'tensor')  5.07 us
    dot_general x1, matrix products, on_device(): jnp.einsum('thd,hde->the', query_heads.astype(F32), incoming_state, preci...  3.5 us
    dot_general x1, matrix products, soft_window(): jnp.einsum('kgts,ksd->kgtd', prob_block.astype(BF16), value_heads, prefer...  2.22 us
    slice x2, local copies, waits for them, and re-layouts, unpack(): values = block[kv_rows:2 * kv_rows].reshape(kv_here, tok_rows, head_size)  2.16 us
    dot_general x1, matrix products, light_local(): jnp.einsum('hts,shd->thd', weights, value_heads, preferred_element_type=F32)  2.13 us
  transfers between devices with their start and end apart: 6, of which 2 were waited for; matrix products, arithmetic and copies ran while one was open for 41% of the time, Pallas kernels for 0%

profile of v6, /device:TPU:11, one launch (start us, length us, event | category | flops | bytes accessed | tf_op | source)
XLA Modules:
  0.0 96.7 jit_solution(9995865392515604665)
XLA Ops:
  0.6 1.0 %reduce_window_sum.11 = f32[16,128]{1,0:T(8,128)S(1)} reduce-window(f32[16,128]{1,0:T(8,128)} %param.14, f32[]{:T(128)} %constant.10.clone.1), window={size=1x128 pad=0_0x127_0}, to_apply=%region_0.0 | reduce-window | flops 260096 | bytes 16388 | tf_op jit(solution)/shard_map/jit(cumsum)/reduce_window_sum | solution.py:91
  1.7 0.2 slice_reduce_fusion
  1.9 0.5 copy-done.10
  2.4 0.7 fusion.63
  3.0 0.9 copy.26
  4.0 0.1 copy.27
  4.1 1.0 copy.28
  5.1 0.1 copy.29
  5.3 3.2 %collective-permute-start.1 = (bf16[528,128]{1,0:T(8,128)(2,1)S(1)}, bf16[528,128]{1,0:T(8,128)(2,1)}, u32[]{:S(2)}, u32[]{:S(2)}) collective-permute-start(bf16[528,128]{1,0:T(8,128)(2,1)S(1)} %pad_maximum_fusion.1), channel_id=1, source_target_pairs={{0,4},{2,6},{4,8},{6,10},{8,12},{10,14},{1,5},{3,7},{5,9},{7,11},{... | collective-permute-start | bytes 405512 | tf_op jit(solution)/shard_map/ppermute | solution.py:15
  8.5 3.2 %collective-permute-start.2 = (bf16[528,128]{1,0:T(8,128)(2,1)S(1)}, bf16[528,128]{1,0:T(8,128)(2,1)S(1)}, u32[]{:S(2)}, u32[]{:S(2)}) collective-permute-start(bf16[528,128]{1,0:T(8,128)(2,1)S(1)} %pad_maximum_fusion.1), channel_id=1, source_target_pairs={{0,2},{2,4},{4,6},{6,8},{8,10},{10,12},{12,14},{1,3},{3,5},{5,7},{... | collective-permute-start | bytes 405512 | tf_op jit(solution)/shard_map/ppermute | solution.py:15
  11.7 1.3 %add_divide_fusion = f32[128,2048]{1,0:T(8,128)S(1)} fusion(bf16[128,2048]{1,0:T(8,128)(2,1)} %param.13), kind=kLoop, calls=%fused_computation.17 | loop fusion | flops 1048576 | bytes 1572864 | tf_op jit(solution)/shard_map/div | solution.py:150
  13.0 0.7 fusion.43
  13.7 0.6 slice.110
  14.3 1.9 %copy.48 = bf16[16,8,16,128]{3,2,1,0:T(8,128)(2,1)} copy(bf16[16,8,16,128]{3,1,2,0:T(8,128)(2,1)} %bitcast.131) | data formatting | bytes 1048576
  16.3 1.3 %copy.45 = bf16[128,2048]{0,1:T(8,128)(2,1)S(1)} copy(bf16[128,2048]{1,0:T(8,128)(2,1)} %param.11) | data formatting | bytes 1048576 | tf_op jit(solution)/shard_map/reshape | solution.py:22
  17.6 0.3 copy.32
  17.9 0.6 iota_add_fusion
  18.5 0.5 fusion.62
  19.0 0.6 fusion.67
  19.6 1.9 %broadcast_compare_fusion = (pred[128]{0:T(512)(128)(4,1)S(1)}, pred[128]{0:T(512)(128)(4,1)S(1)}) fusion(f32[]{:T(128)} %bitcast.13, s32[128]{0:T(128)} %param.19, f32[]{:T(128)} %bitcast.2), kind=kLoop, calls=%fused_computation.100 | loop fusion | flops 512 | bytes 776 | tf_op jit(solution)/shard_map/eq | solution.py:143
  21.6 1.2 %select_bitcast_fusion = (f32[128,16]{0,1:T(8,128)}, f32[128,16]{0,1:T(8,128)S(1)}) fusion(f32[16,128]{1,0:T(8,128)S(1)} %reduce_window_sum.11, pred[128]{0:T(512)(128)(4,1)S(1)} %get-tuple-element.24, f32[16]{0:T(128)} %copy-done.10, pred[128]{0:T(512)(128)(4,1)S(1)} %get-tuple-element.25), kind=kLoop, calls=%fused_computation.72 | loop fusion | flops 6144 | bytes 24896 | tf_op jit(solution)/shard_map/jit(_where)/select_n | solution.py:144
  22.8 1.1 %convolution_convert_fusion = bf16[16,128,128]{2,1,0:T(8,128)(2,1)} fusion(bf16[128,16,128]{0,2,1:T(8,128)(2,1)S(1)} %bitcast.124, f32[128,16]{0,1:T(8,128)S(1)} %get-tuple-element.23, bf16[128,2048]{1,0:T(8,128)(2,1)S(1)} %copy-done), kind=kOutput, calls=%fused_computation.13 | convolution fusion | flops 68157440 | bytes 1581056 | tf_op jit(solution)/shard_map/shd,she->hde/dot_general | solution.py:32
  23.9 3.1 %collective-permute-start = (bf16[16,128,128]{2,1,0:T(8,128)(2,1)}, bf16[16,128,128]{2,1,0:T(8,128)(2,1)S(1)}, u32[]{:S(2)}, u32[]{:S(2)}) collective-permute-start(bf16[16,128,128]{2,1,0:T(8,128)(2,1)} %convolution_convert_fusion), channel_id=1, source_target_pairs={{0,2},{2,4},{4,6},{6,8},{8,10},{10,12},{12,14},{1,3},{3,5},{5,7},{... | collective-permute-start | bytes 1572872 | tf_op jit(solution)/shard_map/ppermute | solution.py:15
  27.0 1.9 %collective-permute-start.3 = (bf16[16,128,128]{2,1,0:T(8,128)(2,1)}, bf16[16,128,128]{2,1,0:T(8,128)(2,1)}, u32[]{:S(2)}, u32[]{:S(2)}) collective-permute-start(bf16[16,128,128]{2,1,0:T(8,128)(2,1)} %convolution_convert_fusion), channel_id=1, source_target_pairs={{0,4},{2,6},{4,8},{6,10},{8,12},{10,14},{1,5},{3,7},{5,9},{7,11},{... | collective-permute-start | bytes 1572872 | tf_op jit(solution)/shard_map/ppermute | solution.py:15
  28.9 1.3 %fusion.61 = (f32[128]{0:T(128)}, bf16[128]{0:T(256)(128)(2,1)S(1)}, f32[1,128]{1,0:T(1,128)S(1)}) fusion(bf16[528,128]{1,0:T(8,128)(2,1)} %collective-permute-done.1), kind=kLoop, calls=%fused_computation.107 | loop fusion | flops 256 | bytes 1536 | tf_op jit(solution)/shard_map/convert_element_type | solution.py:115
  30.2 0.9 slice.145
  31.1 0.7 pad_maximum_fusion
  31.9 1.9 %collective-permute-start.4 = (bf16[1040,128]{1,0:T(8,128)(2,1)}, bf16[1040,128]{1,0:T(8,128)(2,1)}, u32[]{:S(2)}, u32[]{:S(2)}) collective-permute-start(bf16[1040,128]{1,0:T(8,128)(2,1)} %pad_maximum_fusion), channel_id=1, source_target_pairs={{0,4},{2,6},{4,8},{6,10},{8,12},{10,14},{1,5},{3,7},{5,9},{7,11},{... | collective-permute-start | bytes 798728 | tf_op jit(solution)/shard_map/ppermute | solution.py:15
  33.8 0.7 slice_bitcast_fusion
  34.5 0.5 slice_convert_fusion
  35.0 1.5 %fusion.66 = (bf16[256,128]{1,0:T(8,128)(2,1)}, bf16[256,128]{1,0:T(8,128)(2,1)S(1)}) fusion(bf16[528,128]{1,0:T(8,128)(2,1)} %collective-permute-done.1), kind=kLoop, calls=%fused_computation.112 | loop fusion | bytes 262144 | tf_op jit(solution)/shard_map/slice | solution.py:113
  36.5 0.7 fusion.65
  37.1 0.6 slice_bitcast_fusion.1
  37.7 0.7 fusion.68
  38.4 0.9 copy.36
  39.3 1.0 copy.37
  44.1 1.3 %slice_convert_fusion.1 = f32[48]{0:T(128)} fusion(bf16[2048]{0:T(1024)(128)(2,1)} %slice_bitcast_fusion.1), kind=kLoop, calls=%fused_computation.93 | loop fusion | flops 48 | bytes 288 | tf_op jit(solution)/shard_map/convert_element_type | solution.py:63
  45.4 9.8 %collective-permute-done.4 = bf16[1040,128]{1,0:T(8,128)(2,1)} collective-permute-done((bf16[1040,128]{1,0:T(8,128)(2,1)}, bf16[1040,128]{1,0:T(8,128)(2,1)}, u32[]{:S(2)}, u32[]{:S(2)}) %collective-permute-start.4) | collective-permute-done | bytes 266272 | tf_op jit(solution)/shard_map/ppermute | solution.py:15
  55.2 1.6 %fusion.64 = (bf16[256,128]{1,0:T(8,128)(2,1)S(1)}, bf16[256,128]{1,0:T(8,128)(2,1)}, bf16[256,128]{1,0:T(8,128)(2,1)S(1)}, bf16[256,128]{1,0:T(8,128)(2,1)S(1)}) fusion(bf16[1040,128]{1,0:T(8,128)(2,1)} %collective-permute-done.4), kind=kLoop, calls=%fused_computation.110 | loop fusion | bytes 524288 | tf_op jit(solution)/shard_map/slice | solution.py:131
  56.8 0.9 constant_dynamic-update-slice_fusion.5
  57.7 0.7 copy-done.2
  58.4 0.9 copy.34
  59.3 0.7 constant_dynamic-update-slice_fusion.4
  60.0 0.1 copy.35
  60.1 0.7 fusion.57
  60.8 0.6 slice.125
  62.5 0.7 pad_maximum_fusion.2
  63.2 0.8 fusion.42
  64.1 0.7 constant_dynamic-update-slice_fusion.3
  64.7 0.7 constant_dynamic-update-slice_fusion.2
  65.4 0.6 constant_dynamic-update-slice_fusion.1
  66.0 0.9 broadcast_select_fusion
  66.9 1.9 %fusion.2 = (f32[2,8,128]{2,1,0:T(8,128)S(1)}, f32[2,640,128,8]{2,1,3,0:T(8,128)S(1)}) fusion(pred[128,640]{0,1:T(8,128)(4,1)S(1)} %fusion.42, bf16[128,2,8,128]{3,2,1,0:T(8,128)(2,1)S(1)} %bitcast.126, bf16[2,640,128]{2,1,0:T(8,128)(2,1)} %copy-done.2), kind=kOutput, calls=%fused_computation.4 | convolution fusion | flops 339474432 | bytes 6184960 | tf_op jit(solution)/shard_map/tkgd,ksd->kgts/dot_general | solution.py:44
  68.8 1.1 %fusion = f32[2,8,128]{2,1,0:T(8,128)S(1)} fusion(f32[2,640,128,8]{2,1,3,0:T(8,128)S(1)} %get-tuple-element.38, f32[2,8,128]{2,1,0:T(8,128)S(1)} %get-tuple-element.37, pred[128,640]{0,1:T(8,128)(4,1)S(1)} %fusion.42), kind=kLoop, calls=%fused_computation.2 | loop fusion | flops 5240832 | bytes 5341184 | tf_op jit(solution)/shard_map/reduce_sum | solution.py:48
  69.9 1.3 %fusion.20 = bf16[16,128,128]{2,1,0:T(8,128)(2,1)S(1)} fusion(bf16[16,128,128]{2,1,0:T(8,128)(2,1)} %collective-permute-done.3, bf16[16,128,128]{2,1,0:T(8,128)(2,1)S(1)} %collective-permute-done, f32[16]{0:T(128)S(1)} %broadcast_select_fusion.1), kind=kLoop, calls=%fused_computation.27 | loop fusion | flops 1310720 | bytes 1572928 | tf_op jit(solution)/shard_map/convert_element_type | solution.py:126
  71.2 3.2 %collective-permute-start.5 = (bf16[16,128,128]{2,1,0:T(8,128)(2,1)S(1)}, bf16[16,128,128]{2,1,0:T(8,128)(2,1)}, u32[]{:S(2)}, u32[]{:S(2)}) collective-permute-start(bf16[16,128,128]{2,1,0:T(8,128)(2,1)S(1)} %fusion.20), channel_id=1, source_target_pairs={{0,4},{2,6},{4,8},{6,10},{8,12},{10,14},{1,5},{3,7},{5,9},{7,11},{... | collective-permute-start | bytes 1572872 | tf_op jit(solution)/shard_map/ppermute | solution.py:15
  74.5 2.2 %divide_convert_fusion = bf16[128,2,8,128]{0,3,2,1:T(8,128)(2,1)} fusion(f32[2,640,128,8]{2,1,3,0:T(8,128)S(1)} %get-tuple-element.38, f32[2,8,128]{2,1,0:T(8,128)S(1)} %get-tuple-element.37, pred[128,640]{0,1:T(8,128)(4,1)S(1)} %fusion.42, f32[128,2,8]{0,2,1:T(8,128)S(1)} %bitcast.144, bf16[2,640,128]{1,2,0:T(8,128)(2,1)S(1)} %constant_dynamic-update-slice_fusion), kind=kOutput, calls=%fused_computation.15 | convolution fusion | flops 341311488 | bytes 6193152 | tf_op jit(solution)/shard_map/kgts,ksd->kgtd/dot_general | solution.py:49
  76.7 2.1 %copy.40 = bf16[128,2048]{1,0:T(8,128)(2,1)} copy(bf16[128,2048]{0,1:T(8,128)(2,1)} %bitcast.132) | data formatting | bytes 1048576
  78.7 5.9 %collective-permute-done.5 = bf16[16,128,128]{2,1,0:T(8,128)(2,1)} collective-permute-done((bf16[16,128,128]{2,1,0:T(8,128)(2,1)S(1)}, bf16[16,128,128]{2,1,0:T(8,128)(2,1)}, u32[]{:S(2)}, u32[]{:S(2)}) %collective-permute-start.5) | collective-permute-done | bytes 524320 | tf_op jit(solution)/shard_map/ppermute | solution.py:15
  84.6 3.5 %fusion.10 = f32[128,16,128]{0,2,1:T(8,128)} fusion(bf16[16,128,128]{2,1,0:T(8,128)(2,1)} %collective-permute-done.5, bf16[16,128,128]{2,1,0:T(8,128)(2,1)} %collective-permute-done.3, bf16[16,128,128]{2,1,0:T(8,128)(2,1)S(1)} %collective-permute-done, f32[128,16]{0,1:T(8,128)S(1)} %copy-done.5, f32[16]{0:T(128)S(1)} %get-tuple-element.6, ...), kind=kOutput, calls=%fused_computation.12 | convolution fusion | flops 404750336 | bytes 3154048 | tf_op jit(solution)/shard_map/thd,hde->the/dot_general | solution.py:140
  88.1 2.1 %multiply_reduce_fusion = (f32[128]{0:T(128)S(1)}, f32[128,16,128]{0,2,1:T(8,128)S(1)}) fusion(f32[128,16,128]{0,2,1:T(8,128)} %fusion.10, bf16[128,16,128]{0,2,1:T(8,128)(2,1)S(1)} %bitcast.125, f32[16,128]{1,0:T(8,128)S(1)} %copy-done.4, pred[128,128]{1,0:T(8,128)(4,1)S(1)} %copy-done.6, bf16[128,2048]{1,0:T(8,128)(2,1)S(1)} %copy-done, ...), kind=kOutput, calls=%fused_computation.18 | convolution fusion | flops 136052608 | bytes 3695104 | tf_op jit(solution)/shard_map/hts,shd->thd/dot_general | solution.py:29
  90.2 5.1 %psum.7 = f32[128]{0:T(128)S(1)} all-reduce(f32[128]{0:T(128)S(1)} %get-tuple-element.35), channel_id=1, replica_groups=mesh['groups'=2,'ctx'=8,'tensor'=2] {'tensor'}, use_global_device_ids=true, to_apply=%region_2.3 | all-reduce | flops 128 | bytes 1024 | tf_op jit(solution)/shard_map/psum | solution.py:147
  95.3 0.3 multiply_convert_fusion
  95.7 1.0 %copy.39 = bf16[128,2048]{1,0:T(8,128)(2,1)} copy(bf16[128,2048]{0,1:T(8,128)(2,1)S(1)} %bitcast.127) | data formatting | bytes 1048576
  (36 shorter events, 0.3 us)
Async XLA Ops:
  0.6 22.1 %copy-start = (bf16[128,2048]{1,0:T(8,128)(2,1)S(1)}, bf16[128,2048]{1,0:T(8,128)(2,1)}, u32[]{:S(2)}) copy-start(bf16[128,2048]{1,0:T(8,128)(2,1)} %param.12) | copy-start | bytes 1572868
  1.7 32.8 %copy-start.3 = (f32[16,128]{1,0:T(8,128)}, f32[16,128]{1,0:T(8,128)S(1)}, u32[]{:S(2)}) copy-start(f32[16,128]{1,0:T(8,128)S(1)} %reduce_window_sum.11) | copy-start | bytes 24580
  1.9 0.5 copy-start.10
  3.0 11.3 %copy-start.9 = (f32[128]{0:T(128)}, f32[128]{0:T(128)S(1)}, u32[]{:S(2)}) copy-start(f32[128]{0:T(128)S(1)} %get-tuple-element.31) | copy-start | bytes 1540
  5.3 23.6 %collective-permute-start.1 = (bf16[528,128]{1,0:T(8,128)(2,1)S(1)}, bf16[528,128]{1,0:T(8,128)(2,1)}, u32[]{:S(2)}, u32[]{:S(2)}) collective-permute-start(bf16[528,128]{1,0:T(8,128)(2,1)S(1)} %pad_maximum_fusion.1), channel_id=1, source_target_pairs={{0,4},{2,6},{4,8},{6,10},{8,12},{10,14},{1,5},{3,7},{5,9},{7,11},{... | collective-permute-start | bytes 405512 | tf_op jit(solution)/shard_map/ppermute | solution.py:15
  8.5 10.0 %collective-permute-start.2 = (bf16[528,128]{1,0:T(8,128)(2,1)S(1)}, bf16[528,128]{1,0:T(8,128)(2,1)S(1)}, u32[]{:S(2)}, u32[]{:S(2)}) collective-permute-start(bf16[528,128]{1,0:T(8,128)(2,1)S(1)} %pad_maximum_fusion.1), channel_id=1, source_target_pairs={{0,2},{2,4},{4,6},{6,8},{8,10},{10,12},{12,14},{1,3},{3,5},{5,7},{... | collective-permute-start | bytes 405512 | tf_op jit(solution)/shard_map/ppermute | solution.py:15
  17.9 49.0 %copy-start.1 = (bf16[16,8,16,128]{3,2,1,0:T(8,128)(2,1)S(1)}, bf16[16,8,16,128]{3,2,1,0:T(8,128)(2,1)}, u32[]{:S(2)}) copy-start(bf16[16,8,16,128]{3,2,1,0:T(8,128)(2,1)} %copy.48) | copy-start | bytes 1572868
  23.9 46.0 %collective-permute-start = (bf16[16,128,128]{2,1,0:T(8,128)(2,1)}, bf16[16,128,128]{2,1,0:T(8,128)(2,1)S(1)}, u32[]{:S(2)}, u32[]{:S(2)}) collective-permute-start(bf16[16,128,128]{2,1,0:T(8,128)(2,1)} %convolution_convert_fusion), channel_id=1, source_target_pairs={{0,2},{2,4},{4,6},{6,8},{8,10},{10,12},{12,14},{1,3},{3,5},{5,7},{... | collective-permute-start | bytes 1572872 | tf_op jit(solution)/shard_map/ppermute | solution.py:15
  27.0 42.9 %collective-permute-start.3 = (bf16[16,128,128]{2,1,0:T(8,128)(2,1)}, bf16[16,128,128]{2,1,0:T(8,128)(2,1)}, u32[]{:S(2)}, u32[]{:S(2)}) collective-permute-start(bf16[16,128,128]{2,1,0:T(8,128)(2,1)} %convolution_convert_fusion), channel_id=1, source_target_pairs={{0,4},{2,6},{4,8},{6,10},{8,12},{10,14},{1,5},{3,7},{5,9},{7,11},{... | collective-permute-start | bytes 1572872 | tf_op jit(solution)/shard_map/ppermute | solution.py:15
  31.9 23.3 %collective-permute-start.4 = (bf16[1040,128]{1,0:T(8,128)(2,1)}, bf16[1040,128]{1,0:T(8,128)(2,1)}, u32[]{:S(2)}, u32[]{:S(2)}) collective-permute-start(bf16[1040,128]{1,0:T(8,128)(2,1)} %pad_maximum_fusion), channel_id=1, source_target_pairs={{0,4},{2,6},{4,8},{6,10},{8,12},{10,14},{1,5},{3,7},{5,9},{7,11},{... | collective-permute-start | bytes 798728 | tf_op jit(solution)/shard_map/ppermute | solution.py:15
  57.6 0.7 copy-start.2
  66.0 2.8 %copy-start.7 = (bf16[2,640,128]{1,2,0:T(8,128)(2,1)S(1)}, bf16[2,640,128]{1,2,0:T(8,128)(2,1)}, u32[]{:S(2)}) copy-start(bf16[2,640,128]{1,2,0:T(8,128)(2,1)} %constant_dynamic-update-slice_fusion.1) | copy-start | bytes 983044
  71.2 13.4 %collective-permute-start.5 = (bf16[16,128,128]{2,1,0:T(8,128)(2,1)S(1)}, bf16[16,128,128]{2,1,0:T(8,128)(2,1)}, u32[]{:S(2)}, u32[]{:S(2)}) collective-permute-start(bf16[16,128,128]{2,1,0:T(8,128)(2,1)S(1)} %fusion.20), channel_id=1, source_target_pairs={{0,4},{2,6},{4,8},{6,10},{8,12},{10,14},{1,5},{3,7},{5,9},{7,11},{... | collective-permute-start | bytes 1572872 | tf_op jit(solution)/shard_map/ppermute | solution.py:15
  74.4 10.2 %copy-start.5 = (f32[128,16]{0,1:T(8,128)S(1)}, f32[128,16]{0,1:T(8,128)}, u32[]{:S(2)}) copy-start(f32[128,16]{0,1:T(8,128)} %get-tuple-element.22) | copy-start | bytes 24580
  74.4 13.7 %copy-start.4 = (f32[16,128]{1,0:T(8,128)S(1)}, f32[16,128]{1,0:T(8,128)}, u32[]{:S(2)}) copy-start(f32[16,128]{1,0:T(8,128)} %copy-done.3) | copy-start | bytes 24580
  74.4 13.7 %copy-start.6 = (pred[128,128]{1,0:T(8,128)(4,1)S(1)}, pred[128,128]{1,0:T(8,128)(4,1)}, u32[]{:S(2)}) copy-start(pred[128,128]{1,0:T(8,128)(4,1)} %fusion.43) | copy-start | bytes 49156
  76.7 18.6 %copy-start.8 = (f32[2048]{0:T(1024)S(1)}, f32[2048]{0:T(1024)}, u32[]{:S(2)}) copy-start(f32[2048]{0:T(1024)} %param.15) | copy-start | bytes 24580

commit v7 on v6

--- a/solution.py
+++ b/solution.py
@@ -1,6 +1,8 @@
 import jax
 import jax.numpy as jnp
 from jax import lax
+from jax.experimental import pallas as pl
+from jax.experimental.pallas import tpu as pltpu
 from jax.sharding import PartitionSpec as P
 
 NEG_BIG = -1e30
@@ -27,10 +29,34 @@
     products = jnp.einsum("thd,shd->hts", query_heads, key_heads, preferred_element_type=F32)
     weights = (products * jnp.exp(decay_gap)).astype(BF16)
     mixed = jnp.einsum("hts,shd->thd", weights, value_heads, preferred_element_type=F32)
-    to_end = jnp.where((code == code[-1])[None, :], jnp.exp(decay_sum[:, -1:] - decay_sum), 0.0)
-    key_weighted = (key_heads * to_end.T[:, :, None]).astype(BF16)
-    local_state = jnp.einsum("shd,she->hde", key_weighted, value_heads, preferred_element_type=F32)
-    return mixed, local_state
+    return mixed
+
+
+def state_kernel(decay_ref, code_ref, key_ref, value_ref, out_ref):
+    heads_here, head_size = out_ref.shape[0], out_ref.shape[1]
+    tok_rows = code_ref.shape[0]
+    code = code_ref[...]
+    same_end = code == code[tok_rows - 1 :, :]
+    for head in range(heads_here):
+        decay = decay_ref[:, head : head + 1]
+        to_end = jnp.where(same_end, jnp.exp(decay[tok_rows - 1 :, :] - decay), 0.0)
+        columns = slice(head * head_size, (head + 1) * head_size)
+        weighted = (key_ref[:, columns].astype(F32) * to_end).T.astype(BF16)
+        out_ref[head] = jnp.dot(weighted, value_ref[:, columns], preferred_element_type=F32).astype(BF16)
+
+
+def local_state_of(decay_sum, code, light_key, light_value):
+    heads_here = decay_sum.shape[0]
+    head_size = light_key.shape[1] // heads_here
+    tok_rows = light_key.shape[0]
+    flops = 2 * heads_here * tok_rows * head_size * head_size
+    return pl.pallas_call(
+        state_kernel,
+        out_shape=jax.ShapeDtypeStruct((heads_here, head_size, head_size), BF16),
+        in_specs=[pl.BlockSpec(memory_space=pltpu.VMEM)] * 4,
+        out_specs=pl.BlockSpec(memory_space=pltpu.VMEM),
+        cost_estimate=pl.CostEstimate(flops=flops, bytes_accessed=3 * light_key.size, transcendentals=heads_here * tok_rows),
+    )(decay_sum.T, code[:, None], light_key, light_value)
 
 
 def soft_window(soft_query, key_heads, value_heads, code, code_window, heads_here):
@@ -90,14 +116,14 @@
     code = segment_ids.astype(F32) + 1.0
     decay_sum = jnp.cumsum(log_decay, axis=1)
 
-    mixed, local_state = light_local(light_query, light_key, light_value, decay_sum, code)
+    own_state = local_state_of(decay_sum, code, light_key, light_value)
+    mixed = light_local(light_query, light_key, light_value, decay_sum, code)
     block_decay = jnp.exp(decay_sum[:, -1])
 
     own_keys = soft_key.reshape(tok_rows, kv_here, head_size).transpose(1, 0, 2)
     own_values = soft_value.reshape(tok_rows, kv_here, head_size).transpose(1, 0, 2)
     state_rows = heads_here * head_size
     kv_rows = kv_here * tok_rows
-    own_state = local_state.astype(BF16)
     own_kv = jnp.concatenate(
         [
             own_keys.reshape(kv_rows, head_size),

time: 97.9 us -> 84.7 us (0.87)
  other arithmetic: 17.6 us -> 9.69 us
  local copies, waits for them, and re-layouts: 25 us -> 17.6 us
  Pallas kernels: 0 us -> 3.7 us
  matrix products: 10.8 us -> 7.62 us
  waiting for transfers between devices: 15.6 us -> 17.3 us
    unnamed x35 -> x29, local copies, waits for them, and re-layouts: 11.6 us -> 6.72 us
    pallas_call x0 -> x1, Pallas kernels: none -> 3.7 us  [local_state_of(): pl.pallas_call(state_kernel, out_shape=jax.ShapeDtypeStruct((heads_here,...]
    convert_element_type x2, other arithmetic: 1.79 us -> 0.01 us  [join_parts(): parts = parts.astype(F32)]
    ppermute x6, waiting for transfers between devices: 15.6 us -> 17.3 us  [shifted(): return lax.ppermute(block, axis, route)]
    reshape x2, local copies, waits for them, and re-layouts: 1.9 us -> 0.25 us  [unpack(): values = block[kv_rows:2 * kv_rows].reshape(kv_here, tok_rows, head_size)]
    slice x1, local copies, waits for them, and re-layouts: 1.57 us -> 0.02 us  [on_device(): kv_far[3 * kv_rows:4 * kv_rows].reshape(kv_here, tok_rows, head_size)]
    eq x1, other arithmetic: 1.93 us -> 0.63 us  [on_device(): uses_state = code == code_1[-1]]
    slice x2, local copies, waits for them, and re-layouts: 2.16 us -> 0.89 us  [unpack(): values = block[kv_rows:2 * kv_rows].reshape(kv_here, tok_rows, head_size)]
  transfers between devices with their start and end apart: 6 -> 6, of which waited for: 2 -> 2; matrix products, arithmetic and copies ran while one was open for 41% -> 25% of each run, Pallas kernels for 0% -> 4%
where the time goes in v7:
time: 84.7 us; the launch traced here: 83.9 us
  local copies, waits for them, and re-layouts  17.6 us (21%)
  waiting for transfers between devices  17.3 us (20%)
  starting transfers between devices  16.5 us (19%)
  other arithmetic  9.69 us (11%)
  matrix products  7.62 us (9%)
  between operations  6.35 us (7%)
  blocking collectives  5.05 us (6%)
  Pallas kernels  3.7 us (4%)
    ppermute x6, waiting for transfers between devices, shifted(): return lax.ppermute(block, axis, route)  17.3 us
    ppermute x6, starting transfers between devices, shifted(): return lax.ppermute(block, axis, route)  16.5 us
    unnamed x29, local copies, waits for them, and re-layouts  6.72 us
    psum x1, blocking collectives, on_device(): squares = lax.psum(squares, 'tensor')  5.05 us
    pallas_call x1, Pallas kernels, local_state_of(): pl.pallas_call(state_kernel, out_shape=jax.ShapeDtypeStruct((heads_here,...  3.7 us
    dot_general x1, matrix products, light_local(): jnp.einsum('hts,shd->thd', weights, value_heads, preferred_element_type=F32)  2.69 us
    dot_general x1, matrix products, on_device(): jnp.einsum('thd,hde->the', query_heads.astype(F32), incoming_state, preci...  2.53 us
    reshape x1, local copies, waits for them, and re-layouts, light_local(): key_heads = light_key.reshape(tok_rows, heads_here, head_size)  2.05 us
  transfers between devices with their start and end apart: 6, of which 2 were waited for; matrix products, arithmetic and copies ran while one was open for 25% of the time, Pallas kernels for 4%

profile of v7, /device:TPU:11, one launch (start us, length us, event | category | flops | bytes accessed | tf_op | source)
XLA Modules:
  0.0 83.9 jit_solution(12518159894682282)
XLA Ops:
  0.6 0.0 copy-start
  0.6 0.0 copy-start.1
  0.7 1.1 %reduce_window_sum.11 = f32[16,128]{1,0:T(8,128)S(1)} reduce-window(f32[16,128]{1,0:T(8,128)} %param.14, f32[]{:T(128)} %constant.10.clone.1), window={size=1x128 pad=0_0x127_0}, to_apply=%region_0.0 | reduce-window | flops 260096 | bytes 16388 | tf_op jit(solution)/shard_map/jit(cumsum)/reduce_window_sum | solution.py:117
  1.8 0.2 fusion.45
  2.0 0.7 convert_add_fusion
  2.6 0.9 %copy.29 = bf16[128,256]{0,1:T(8,128)(2,1)S(1)} copy(bf16[128,256]{1,0:T(8,128)(2,1)} %param.18) | data formatting | bytes 131072 | tf_op args[8]
  3.6 0.0 copy-start.7
  3.6 0.1 copy.30
  3.7 1.0 %copy.27 = bf16[128,256]{0,1:T(8,128)(2,1)S(1)} copy(bf16[128,256]{1,0:T(8,128)(2,1)} %param.17) | data formatting | bytes 131072 | tf_op args[7]
  4.7 0.1 copy.28
  4.8 0.1 fusion.49
  4.9 0.7 pad_maximum_fusion.1
  5.6 3.2 %collective-permute-start.1 = (bf16[528,128]{1,0:T(8,128)(2,1)}, bf16[528,128]{1,0:T(8,128)(2,1)}, u32[]{:S(2)}, u32[]{:S(2)}) collective-permute-start(bf16[528,128]{1,0:T(8,128)(2,1)} %pad_maximum_fusion.1), channel_id=1, source_target_pairs={{0,4},{2,6},{4,8},{6,10},{8,12},{10,14},{1,5},{3,7},{5,9},{7,11},{... | collective-permute-start | bytes 405512 | tf_op jit(solution)/shard_map/ppermute | solution.py:17
  8.8 3.2 %collective-permute-start.2 = (bf16[528,128]{1,0:T(8,128)(2,1)}, bf16[528,128]{1,0:T(8,128)(2,1)S(1)}, u32[]{:S(2)}, u32[]{:S(2)}) collective-permute-start(bf16[528,128]{1,0:T(8,128)(2,1)} %pad_maximum_fusion.1), channel_id=1, source_target_pairs={{0,2},{2,4},{4,6},{6,8},{8,10},{10,12},{12,14},{1,3},{3,5},{5,7},{... | collective-permute-start | bytes 405512 | tf_op jit(solution)/shard_map/ppermute | solution.py:17
  11.9 0.7 copy.25
  12.7 0.7 copy.26.code_ref
  13.4 3.7 %shard_map.113 = bf16[16,128,128]{2,1,0:T(8,128)(2,1)} custom-call(f32[128,16]{1,0:T(8,128)} %bitcast.116, f32[128,1]{1,0:T(8,128)} %copy.26.code_ref, bf16[128,2048]{1,0:T(8,128)(2,1)} %key_ref.1, bf16[128,2048]{1,0:T(8,128)(2,1)} %value_ref.1), custom_call_target="tpu_custom_call" | custom-call | flops 67108864 | bytes 786432 | tf_op jit(solution)/shard_map/pallas_call | solution.py:53
  17.1 3.1 %collective-permute-start = (bf16[16,128,128]{2,1,0:T(8,128)(2,1)}, bf16[16,128,128]{2,1,0:T(8,128)(2,1)}, u32[]{:S(2)}, u32[]{:S(2)}) collective-permute-start(bf16[16,128,128]{2,1,0:T(8,128)(2,1)} %shard_map.113), channel_id=1, source_target_pairs={{0,2},{2,4},{4,6},{6,8},{8,10},{10,12},{12,14},{1,3},{3,5},{5,7},{... | collective-permute-start | bytes 1572872 | tf_op jit(solution)/shard_map/ppermute | solution.py:17
  20.2 1.9 %collective-permute-start.3 = (bf16[16,128,128]{2,1,0:T(8,128)(2,1)}, bf16[16,128,128]{2,1,0:T(8,128)(2,1)}, u32[]{:S(2)}, u32[]{:S(2)}) collective-permute-start(bf16[16,128,128]{2,1,0:T(8,128)(2,1)} %shard_map.113), channel_id=1, source_target_pairs={{0,4},{2,6},{4,8},{6,10},{8,12},{10,14},{1,5},{3,7},{5,9},{7,11},{... | collective-permute-start | bytes 1572872 | tf_op jit(solution)/shard_map/ppermute | solution.py:17
  22.2 1.3 %add_divide_fusion = f32[128,2048]{1,0:T(8,128)S(1)} fusion(bf16[128,2048]{1,0:T(8,128)(2,1)} %param.13), kind=kLoop, calls=%fused_computation.16 | loop fusion | flops 1048576 | bytes 1572864 | tf_op jit(solution)/shard_map/div | solution.py:176
  23.5 0.1 fusion.38
  23.6 2.1 %copy.48 = bf16[128,2048]{0,1:T(8,128)(2,1)} copy(bf16[128,2048]{1,0:T(8,128)(2,1)} %key_ref.1) | data formatting | bytes 1048576 | tf_op jit(solution)/shard_map/reshape | solution.py:24
  25.6 1.0 %copy.49 = bf16[128,2048]{0,1:T(8,128)(2,1)} copy(bf16[128,2048]{1,0:T(8,128)(2,1)S(1)} %copy-done.1) | data formatting | bytes 1048576 | tf_op jit(solution)/shard_map/reshape | solution.py:25
  26.6 0.1 copy.51
  26.8 0.3 copy.34
  27.1 0.0 collective-permute-done.1
  27.1 0.7 fusion.57
  27.8 0.9 %slice.140 = bf16[512,128]{1,0:T(8,128)(2,1)S(1)} slice(bf16[528,128]{1,0:T(8,128)(2,1)} %collective-permute-done.1), slice={[0:512], [0:128]} | slice | bytes 262144 | tf_op jit(solution)/shard_map/slice | solution.py:151
  28.8 1.9 %collective-permute-start.4 = (bf16[1040,128]{1,0:T(8,128)(2,1)S(1)}, bf16[1040,128]{1,0:T(8,128)(2,1)S(1)}, u32[]{:S(2)}, u32[]{:S(2)}) collective-permute-start(bf16[1040,128]{1,0:T(8,128)(2,1)S(1)} %pad_maximum_fusion), channel_id=1, source_target_pairs={{0,4},{2,6},{4,8},{6,10},{8,12},{10,14},{1,5},{3,7},{5,9},{7,11},{... | collective-permute-start | bytes 798728 | tf_op jit(solution)/shard_map/ppermute | solution.py:17
  30.7 0.6 fusion.64
  31.3 0.7 slice_bitcast_fusion
  32.0 0.6 broadcast_compare_fusion
  32.7 0.1 exponential_select_fusion
  32.8 0.9 %fusion.63 = (bf16[256,128]{1,0:T(8,128)(2,1)S(1)}, bf16[256,128]{1,0:T(8,128)(2,1)S(1)}) fusion(bf16[528,128]{1,0:T(8,128)(2,1)} %collective-permute-done.1), kind=kLoop, calls=%fused_computation.105 | loop fusion | bytes 262144 | tf_op jit(solution)/shard_map/slice | solution.py:139
  33.7 0.6 fusion.65
  34.3 0.1 copy.38
  34.4 0.1 copy.39
  38.6 0.1 copy.33
  38.6 9.7 %collective-permute-done.4 = bf16[1040,128]{1,0:T(8,128)(2,1)S(1)} collective-permute-done((bf16[1040,128]{1,0:T(8,128)(2,1)S(1)}, bf16[1040,128]{1,0:T(8,128)(2,1)S(1)}, u32[]{:S(2)}, u32[]{:S(2)}) %collective-permute-start.4) | collective-permute-done | bytes 266272 | tf_op jit(solution)/shard_map/ppermute | solution.py:17
  48.4 0.1 copy.36
  48.5 0.7 constant_dynamic-update-slice_fusion.4
  49.2 0.1 copy.37
  49.3 0.6 slice.120
  51.4 0.2 fusion.37
  51.5 0.6 constant_dynamic-update-slice_fusion.3
  52.2 0.6 constant_dynamic-update-slice_fusion.2
  52.8 0.6 constant_dynamic-update-slice_fusion.1
  53.4 0.1 broadcast_select_fusion
  53.5 0.9 %fusion.2 = (f32[2,8,128]{2,1,0:T(8,128)S(1)}, f32[2,640,128,8]{2,1,3,0:T(8,128)S(1)}) fusion(pred[128,640]{0,1:T(8,128)(4,1)S(1)} %fusion.37, bf16[128,2,8,128]{3,2,1,0:T(8,128)(2,1)S(1)} %bitcast.111, bf16[2,640,128]{2,1,0:T(8,128)(2,1)S(1)} %bitcast_dynamic-update-slice_fusion), kind=kOutput, calls=%fused_computation.4 | convolution fusion | flops 339474432 | bytes 6184960 | tf_op jit(solution)/shard_map/tkgd,ksd->kgts/dot_general | solution.py:70
  54.5 0.6 constant_dynamic-update-slice_fusion
  55.1 1.1 %fusion = f32[2,8,128]{2,1,0:T(8,128)S(1)} fusion(f32[2,640,128,8]{2,1,3,0:T(8,128)S(1)} %get-tuple-element.35, f32[2,8,128]{2,1,0:T(8,128)S(1)} %get-tuple-element.34, pred[128,640]{0,1:T(8,128)(4,1)S(1)} %fusion.37), kind=kLoop, calls=%fused_computation.2 | loop fusion | flops 5240832 | bytes 5341184 | tf_op jit(solution)/shard_map/reduce_sum | solution.py:74
  56.2 0.0 collective-permute-done
  56.2 0.0 collective-permute-done.3
  56.2 1.4 %fusion.20 = bf16[16,128,128]{2,1,0:T(8,128)(2,1)S(1)} fusion(bf16[16,128,128]{2,1,0:T(8,128)(2,1)} %collective-permute-done.3, bf16[16,128,128]{2,1,0:T(8,128)(2,1)} %collective-permute-done, f32[16]{0:T(128)S(1)} %broadcast_select_fusion.1), kind=kLoop, calls=%fused_computation.25 | loop fusion | flops 1310720 | bytes 1572928 | tf_op jit(solution)/shard_map/convert_element_type | solution.py:152
  57.6 3.2 %collective-permute-start.5 = (bf16[16,128,128]{2,1,0:T(8,128)(2,1)S(1)}, bf16[16,128,128]{2,1,0:T(8,128)(2,1)}, u32[]{:S(2)}, u32[]{:S(2)}) collective-permute-start(bf16[16,128,128]{2,1,0:T(8,128)(2,1)S(1)} %fusion.20), channel_id=1, source_target_pairs={{0,4},{2,6},{4,8},{6,10},{8,12},{10,14},{1,5},{3,7},{5,9},{7,11},{... | collective-permute-start | bytes 1572872 | tf_op jit(solution)/shard_map/ppermute | solution.py:17
  60.9 1.5 %divide_convert_fusion = bf16[128,2,8,128]{0,3,2,1:T(8,128)(2,1)S(1)} fusion(f32[2,640,128,8]{2,1,3,0:T(8,128)S(1)} %get-tuple-element.35, f32[2,8,128]{2,1,0:T(8,128)S(1)} %get-tuple-element.34, pred[128,640]{0,1:T(8,128)(4,1)S(1)} %fusion.37, f32[128,2,8]{0,2,1:T(8,128)S(1)} %bitcast.132, bf16[2,640,128]{1,2,0:T(8,128)(2,1)S(1)} %copy-done.5), kind=kOutput, calls=%fused_computation.14 | convolution fusion | flops 341311488 | bytes 6193152 | tf_op jit(solution)/shard_map/kgts,ksd->kgtd/dot_general | solution.py:75
  62.3 0.0 copy-start.6
  62.4 1.0 %copy.42 = bf16[128,2048]{1,0:T(8,128)(2,1)} copy(bf16[128,2048]{0,1:T(8,128)(2,1)S(1)} %bitcast.120) | data formatting | bytes 1048576
  63.4 7.6 %collective-permute-done.5 = bf16[16,128,128]{2,1,0:T(8,128)(2,1)} collective-permute-done((bf16[16,128,128]{2,1,0:T(8,128)(2,1)S(1)}, bf16[16,128,128]{2,1,0:T(8,128)(2,1)}, u32[]{:S(2)}, u32[]{:S(2)}) %collective-permute-start.5) | collective-permute-done | bytes 524320 | tf_op jit(solution)/shard_map/ppermute | solution.py:17
  71.0 2.5 %fusion.10 = f32[128,16,128]{0,2,1:T(8,128)S(1)} fusion(bf16[16,128,128]{2,1,0:T(8,128)(2,1)} %collective-permute-done.5, bf16[16,128,128]{2,1,0:T(8,128)(2,1)} %collective-permute-done.3, bf16[16,128,128]{2,1,0:T(8,128)(2,1)} %collective-permute-done, f32[128,16]{0,1:T(8,128)S(1)} %copy.33, f32[16]{0:T(128)S(1)} %get-tuple-element.6, ...), kind=kOutput, calls=%fused_computation.12 | convolution fusion | flops 404750336 | bytes 3154048 | tf_op jit(solution)/shard_map/thd,hde->the/dot_general | solution.py:166
  73.6 2.7 %multiply_reduce_fusion = (f32[128]{0:T(128)S(1)}, f32[128,16,128]{0,2,1:T(8,128)}) fusion(f32[128,16,128]{0,2,1:T(8,128)S(1)} %fusion.10, bf16[128,16,128]{0,2,1:T(8,128)(2,1)} %bitcast.119, bf16[128,16,128]{0,2,1:T(8,128)(2,1)S(1)} %bitcast.118, f32[16,128]{1,0:T(8,128)S(1)} %reduce_window_sum.11, pred[128,128]{1,0:T(8,128)(4,1)S(1)} %fusion.38, ...), kind=kOutput, calls=%fused_computation.17 | convolution fusion | flops 136052608 | bytes 3695104 | tf_op jit(solution)/shard_map/hts,shd->thd/dot_general | solution.py:31
  76.2 5.1 %psum.7 = f32[128]{0:T(128)S(1)} all-reduce(f32[128]{0:T(128)S(1)} %get-tuple-element.32), channel_id=1, replica_groups=mesh['groups'=2,'ctx'=8,'tensor'=2] {'tensor'}, use_global_device_ids=true, to_apply=%region_2.3 | all-reduce | flops 128 | bytes 1024 | tf_op jit(solution)/shard_map/psum | solution.py:173
  81.3 1.6 %multiply_convert_fusion = bf16[128,16,128]{0,2,1:T(8,128)(2,1)S(1)} fusion(f32[128,16,128]{0,2,1:T(8,128)S(1)} %bitcast.110, f32[128,16,128]{0,2,1:T(8,128)} %get-tuple-element.33, f32[16,128]{1,0:T(8,128)S(1)} %bitcast.131, f32[128]{0:T(128)S(1)} %add_rsqrt_fusion), kind=kLoop, calls=%fused_computation.15 | loop fusion | flops 1048576 | bytes 2630144 | tf_op jit(solution)/shard_map/convert_element_type | solution.py:178
  82.9 1.0 %copy.41 = bf16[128,2048]{1,0:T(8,128)(2,1)} copy(bf16[128,2048]{0,1:T(8,128)(2,1)S(1)} %bitcast.112) | data formatting | bytes 1048576
  (33 shorter events, 0.2 us)
Async XLA Ops:
  0.6 70.4 %copy-start = (bf16[128,2048]{1,0:T(8,128)(2,1)S(1)}, bf16[128,2048]{1,0:T(8,128)(2,1)}, u32[]{:S(2)}) copy-start(bf16[128,2048]{1,0:T(8,128)(2,1)} %param.10) | copy-start | bytes 1572868
  0.6 25.0 %copy-start.1 = (bf16[128,2048]{1,0:T(8,128)(2,1)S(1)}, bf16[128,2048]{1,0:T(8,128)(2,1)}, u32[]{:S(2)}) copy-start(bf16[128,2048]{1,0:T(8,128)(2,1)} %value_ref.1) | copy-start | bytes 1572868
  0.7 26.0 %copy-start.3 = (bf16[128,2048]{1,0:T(8,128)(2,1)S(1)}, bf16[128,2048]{1,0:T(8,128)(2,1)}, u32[]{:S(2)}) copy-start(bf16[128,2048]{1,0:T(8,128)(2,1)} %param.16) | copy-start | bytes 1572868
  3.6 28.4 %copy-start.7 = (s32[128]{0:T(128)S(1)}, s32[128]{0:T(128)}, u32[]{:S(2)}) copy-start(s32[128]{0:T(128)} %param.19) | copy-start | bytes 1540
  5.6 21.5 %collective-permute-start.1 = (bf16[528,128]{1,0:T(8,128)(2,1)}, bf16[528,128]{1,0:T(8,128)(2,1)}, u32[]{:S(2)}, u32[]{:S(2)}) collective-permute-start(bf16[528,128]{1,0:T(8,128)(2,1)} %pad_maximum_fusion.1), channel_id=1, source_target_pairs={{0,4},{2,6},{4,8},{6,10},{8,12},{10,14},{1,5},{3,7},{5,9},{7,11},{... | collective-permute-start | bytes 405512 | tf_op jit(solution)/shard_map/ppermute | solution.py:17
  8.8 19.0 %collective-permute-start.2 = (bf16[528,128]{1,0:T(8,128)(2,1)}, bf16[528,128]{1,0:T(8,128)(2,1)S(1)}, u32[]{:S(2)}, u32[]{:S(2)}) collective-permute-start(bf16[528,128]{1,0:T(8,128)(2,1)} %pad_maximum_fusion.1), channel_id=1, source_target_pairs={{0,2},{2,4},{4,6},{6,8},{8,10},{10,12},{12,14},{1,3},{3,5},{5,7},{... | collective-permute-start | bytes 405512 | tf_op jit(solution)/shard_map/ppermute | solution.py:17
  12.7 20.0 %copy-start.2 = (f32[16,128]{0,1:T(8,128)S(1)}, f32[16,128]{0,1:T(8,128)}, u32[]{:S(2)}) copy-start(f32[16,128]{0,1:T(8,128)} %copy.25) | copy-start | bytes 24580
  17.1 39.0 %collective-permute-start = (bf16[16,128,128]{2,1,0:T(8,128)(2,1)}, bf16[16,128,128]{2,1,0:T(8,128)(2,1)}, u32[]{:S(2)}, u32[]{:S(2)}) collective-permute-start(bf16[16,128,128]{2,1,0:T(8,128)(2,1)} %shard_map.113), channel_id=1, source_target_pairs={{0,2},{2,4},{4,6},{6,8},{8,10},{10,12},{12,14},{1,3},{3,5},{5,7},{... | collective-permute-start | bytes 1572872 | tf_op jit(solution)/shard_map/ppermute | solution.py:17
  20.2 35.9 %collective-permute-start.3 = (bf16[16,128,128]{2,1,0:T(8,128)(2,1)}, bf16[16,128,128]{2,1,0:T(8,128)(2,1)}, u32[]{:S(2)}, u32[]{:S(2)}) collective-permute-start(bf16[16,128,128]{2,1,0:T(8,128)(2,1)} %shard_map.113), channel_id=1, source_target_pairs={{0,4},{2,6},{4,8},{6,10},{8,12},{10,14},{1,5},{3,7},{5,9},{7,11},{... | collective-permute-start | bytes 1572872 | tf_op jit(solution)/shard_map/ppermute | solution.py:17
  28.8 19.5 %collective-permute-start.4 = (bf16[1040,128]{1,0:T(8,128)(2,1)S(1)}, bf16[1040,128]{1,0:T(8,128)(2,1)S(1)}, u32[]{:S(2)}, u32[]{:S(2)}) collective-permute-start(bf16[1040,128]{1,0:T(8,128)(2,1)S(1)} %pad_maximum_fusion), channel_id=1, source_target_pairs={{0,4},{2,6},{4,8},{6,10},{8,12},{10,14},{1,5},{3,7},{5,9},{7,11},{... | collective-permute-start | bytes 798728 | tf_op jit(solution)/shard_map/ppermute | solution.py:17
  55.1 5.8 %copy-start.5 = (bf16[2,640,128]{1,2,0:T(8,128)(2,1)S(1)}, bf16[2,640,128]{1,2,0:T(8,128)(2,1)}, u32[]{:S(2)}) copy-start(bf16[2,640,128]{1,2,0:T(8,128)(2,1)} %constant_dynamic-update-slice_fusion) | copy-start | bytes 983044
  57.6 13.4 %collective-permute-start.5 = (bf16[16,128,128]{2,1,0:T(8,128)(2,1)S(1)}, bf16[16,128,128]{2,1,0:T(8,128)(2,1)}, u32[]{:S(2)}, u32[]{:S(2)}) collective-permute-start(bf16[16,128,128]{2,1,0:T(8,128)(2,1)S(1)} %fusion.20), channel_id=1, source_target_pairs={{0,4},{2,6},{4,8},{6,10},{8,12},{10,14},{1,5},{3,7},{5,9},{7,11},{... | collective-permute-start | bytes 1572872 | tf_op jit(solution)/shard_map/ppermute | solution.py:17
  60.8 12.7 %copy-start.4 = (bf16[128,2048]{0,1:T(8,128)(2,1)S(1)}, bf16[128,2048]{0,1:T(8,128)(2,1)}, u32[]{:S(2)}) copy-start(bf16[128,2048]{0,1:T(8,128)(2,1)} %copy.48) | copy-start | bytes 1572868
  62.3 19.0 %copy-start.6 = (f32[2048]{0:T(1024)S(1)}, f32[2048]{0:T(1024)}, u32[]{:S(2)}) copy-start(f32[2048]{0:T(1024)} %param.15) | copy-start | bytes 24580

commit v8 on v7

--- a/solution.py
+++ b/solution.py
@@ -4,6 +4,7 @@
 from jax.experimental import pallas as pl
 from jax.experimental.pallas import tpu as pltpu
 from jax.sharding import PartitionSpec as P
+
 
 NEG_BIG = -1e30
 MAXDOC = 512
@@ -96,7 +97,7 @@
     return jnp.pad(flat, (0, padded - flat.shape[0])).reshape(-1, width).astype(BF16)
 
 
-def on_device(
+def on_device_body(
     light_query,
     light_key,
     light_value,
@@ -122,7 +123,6 @@
 
     own_keys = soft_key.reshape(tok_rows, kv_here, head_size).transpose(1, 0, 2)
     own_values = soft_value.reshape(tok_rows, kv_here, head_size).transpose(1, 0, 2)
-    state_rows = heads_here * head_size
     kv_rows = kv_here * tok_rows
     own_kv = jnp.concatenate(
         [
@@ -131,8 +131,10 @@
             rows_of(jnp.concatenate([code, split_parts(block_decay)]), head_size),
         ]
     )
-    state_1, kv_1 = shifted((own_state, own_kv), "ctx", 1)
-    state_2, kv_2 = shifted((own_state, own_kv), "ctx", 2)
+    state_1 = shifted(own_state, "ctx", 1)
+    state_2 = shifted(own_state, "ctx", 2)
+    kv_1 = shifted(own_kv, "ctx", 1)
+    kv_2 = shifted(own_kv, "ctx", 2)
 
     def unpack(block):
         keys = block[:kv_rows].reshape(kv_here, tok_rows, head_size)
@@ -149,7 +151,8 @@
     pair_state = state_1.astype(F32) + jnp.where(link_1, decay_1, 0.0)[:, None, None] * state_2.astype(F32)
 
     relay_kv = jnp.concatenate([kv_2[: 2 * kv_rows], kv_1[: 2 * kv_rows], rows_of(jnp.concatenate([code_2, code_1]), head_size)])
-    state_far, kv_far = shifted((pair_state.astype(BF16), relay_kv), "ctx", 2)
+    state_far = shifted(pair_state.astype(BF16), "ctx", 2)
+    kv_far = shifted(relay_kv, "ctx", 2)
     state_far = state_far.astype(F32)
     keys_4 = kv_far[:kv_rows].reshape(kv_here, tok_rows, head_size)
     values_4 = kv_far[kv_rows : 2 * kv_rows].reshape(kv_here, tok_rows, head_size)
@@ -198,6 +201,4 @@
         P(("groups", "ctx")),
     )
     out_specs = (P(("groups", "ctx"), "tensor"), P(("groups", "ctx"), "tensor"))
-    return jax.shard_map(
-        on_device, mesh=mesh, in_specs=in_specs, out_specs=out_specs, check_vma=False
-    )
+    return jax.shard_map(on_device_body, mesh=mesh, in_specs=in_specs, out_specs=out_specs, check_vma=False)

time: 84.7 us -> 84.7 us (level)
  no operation moved by 1% of the time
where the time goes in v8:
time: 84.7 us; the launch traced here: 83.9 us
  local copies, waits for them, and re-layouts  17.6 us (21%)
  waiting for transfers between devices  17.3 us (20%)
  starting transfers between devices  16.5 us (19%)
  other arithmetic  9.69 us (11%)
  matrix products  7.62 us (9%)
  between operations  6.35 us (7%)
  blocking collectives  5.05 us (6%)
  Pallas kernels  3.7 us (4%)
    ppermute x6, waiting for transfers between devices, shifted(): return lax.ppermute(block, axis, route)  17.3 us
    ppermute x6, starting transfers between devices, shifted(): return lax.ppermute(block, axis, route)  16.5 us
    unnamed x29, local copies, waits for them, and re-layouts  6.72 us
    psum x1, blocking collectives, on_device_body(): squares = lax.psum(squares, 'tensor')  5.05 us
    pallas_call x1, Pallas kernels, local_state_of(): pl.pallas_call(state_kernel, out_shape=jax.ShapeDtypeStruct((heads_here,...  3.7 us
    dot_general x1, matrix products, light_local(): jnp.einsum('hts,shd->thd', weights, value_heads, preferred_element_type=F32)  2.69 us
    dot_general x1, matrix products, on_device_body(): jnp.einsum('thd,hde->the', query_heads.astype(F32), incoming_state, preci...  2.53 us
    reshape x1, local copies, waits for them, and re-layouts, light_local(): key_heads = light_key.reshape(tok_rows, heads_here, head_size)  2.05 us
  transfers between devices with their start and end apart: 6, of which 2 were waited for; matrix products, arithmetic and copies ran while one was open for 25% of the time, Pallas kernels for 4%

profile of v8, /device:TPU:11, one launch (start us, length us, event | category | flops | bytes accessed | tf_op | source)
XLA Modules:
  0.0 83.9 jit_solution(12518159894682282)
XLA Ops:
  0.6 0.0 copy-start
  0.6 0.0 copy-start.1
  0.7 1.1 %reduce_window_sum.11 = f32[16,128]{1,0:T(8,128)S(1)} reduce-window(f32[16,128]{1,0:T(8,128)} %param.14, f32[]{:T(128)} %constant.10.clone.1), window={size=1x128 pad=0_0x127_0}, to_apply=%region_0.0 | reduce-window | flops 260096 | bytes 16388 | tf_op jit(solution)/shard_map/jit(cumsum)/reduce_window_sum | solution.py:118
  1.8 0.2 fusion.45
  2.0 0.7 convert_add_fusion
  2.6 0.9 %copy.29 = bf16[128,256]{0,1:T(8,128)(2,1)S(1)} copy(bf16[128,256]{1,0:T(8,128)(2,1)} %param.18) | data formatting | bytes 131072 | tf_op args[8]
  3.6 0.0 copy-start.7
  3.6 0.1 copy.30
  3.7 1.0 %copy.27 = bf16[128,256]{0,1:T(8,128)(2,1)S(1)} copy(bf16[128,256]{1,0:T(8,128)(2,1)} %param.17) | data formatting | bytes 131072 | tf_op args[7]
  4.7 0.1 copy.28
  4.8 0.1 fusion.49
  4.9 0.7 pad_maximum_fusion.1
  5.6 3.2 %collective-permute-start.1 = (bf16[528,128]{1,0:T(8,128)(2,1)}, bf16[528,128]{1,0:T(8,128)(2,1)}, u32[]{:S(2)}, u32[]{:S(2)}) collective-permute-start(bf16[528,128]{1,0:T(8,128)(2,1)} %pad_maximum_fusion.1), channel_id=1, source_target_pairs={{0,4},{2,6},{4,8},{6,10},{8,12},{10,14},{1,5},{3,7},{5,9},{7,11},{... | collective-permute-start | bytes 405512 | tf_op jit(solution)/shard_map/ppermute | solution.py:18
  8.8 3.2 %collective-permute-start.2 = (bf16[528,128]{1,0:T(8,128)(2,1)}, bf16[528,128]{1,0:T(8,128)(2,1)S(1)}, u32[]{:S(2)}, u32[]{:S(2)}) collective-permute-start(bf16[528,128]{1,0:T(8,128)(2,1)} %pad_maximum_fusion.1), channel_id=1, source_target_pairs={{0,2},{2,4},{4,6},{6,8},{8,10},{10,12},{12,14},{1,3},{3,5},{5,7},{... | collective-permute-start | bytes 405512 | tf_op jit(solution)/shard_map/ppermute | solution.py:18
  11.9 0.7 copy.25
  12.7 0.7 copy.26.code_ref
  13.4 3.7 %shard_map.113 = bf16[16,128,128]{2,1,0:T(8,128)(2,1)} custom-call(f32[128,16]{1,0:T(8,128)} %bitcast.116, f32[128,1]{1,0:T(8,128)} %copy.26.code_ref, bf16[128,2048]{1,0:T(8,128)(2,1)} %key_ref.1, bf16[128,2048]{1,0:T(8,128)(2,1)} %value_ref.1), custom_call_target="tpu_custom_call" | custom-call | flops 67108864 | bytes 786432 | tf_op jit(solution)/shard_map/pallas_call | solution.py:54
  17.1 3.1 %collective-permute-start = (bf16[16,128,128]{2,1,0:T(8,128)(2,1)}, bf16[16,128,128]{2,1,0:T(8,128)(2,1)}, u32[]{:S(2)}, u32[]{:S(2)}) collective-permute-start(bf16[16,128,128]{2,1,0:T(8,128)(2,1)} %shard_map.113), channel_id=1, source_target_pairs={{0,2},{2,4},{4,6},{6,8},{8,10},{10,12},{12,14},{1,3},{3,5},{5,7},{... | collective-permute-start | bytes 1572872 | tf_op jit(solution)/shard_map/ppermute | solution.py:18
  20.2 1.9 %collective-permute-start.3 = (bf16[16,128,128]{2,1,0:T(8,128)(2,1)}, bf16[16,128,128]{2,1,0:T(8,128)(2,1)}, u32[]{:S(2)}, u32[]{:S(2)}) collective-permute-start(bf16[16,128,128]{2,1,0:T(8,128)(2,1)} %shard_map.113), channel_id=1, source_target_pairs={{0,4},{2,6},{4,8},{6,10},{8,12},{10,14},{1,5},{3,7},{5,9},{7,11},{... | collective-permute-start | bytes 1572872 | tf_op jit(solution)/shard_map/ppermute | solution.py:18
  22.2 1.3 %add_divide_fusion = f32[128,2048]{1,0:T(8,128)S(1)} fusion(bf16[128,2048]{1,0:T(8,128)(2,1)} %param.13), kind=kLoop, calls=%fused_computation.16 | loop fusion | flops 1048576 | bytes 1572864 | tf_op jit(solution)/shard_map/div | solution.py:179
  23.5 0.1 fusion.38
  23.6 2.1 %copy.48 = bf16[128,2048]{0,1:T(8,128)(2,1)} copy(bf16[128,2048]{1,0:T(8,128)(2,1)} %key_ref.1) | data formatting | bytes 1048576 | tf_op jit(solution)/shard_map/reshape | solution.py:25
  25.6 1.0 %copy.49 = bf16[128,2048]{0,1:T(8,128)(2,1)} copy(bf16[128,2048]{1,0:T(8,128)(2,1)S(1)} %copy-done.1) | data formatting | bytes 1048576 | tf_op jit(solution)/shard_map/reshape | solution.py:26
  26.6 0.1 copy.51
  26.8 0.3 copy.34
  27.1 0.0 collective-permute-done.1
  27.1 0.7 fusion.57
  27.8 0.0 collective-permute-done.2
  27.8 0.9 %slice.140 = bf16[512,128]{1,0:T(8,128)(2,1)S(1)} slice(bf16[528,128]{1,0:T(8,128)(2,1)} %collective-permute-done.1), slice={[0:512], [0:128]} | slice | bytes 262144 | tf_op jit(solution)/shard_map/slice | solution.py:153
  28.8 1.9 %collective-permute-start.4 = (bf16[1040,128]{1,0:T(8,128)(2,1)S(1)}, bf16[1040,128]{1,0:T(8,128)(2,1)S(1)}, u32[]{:S(2)}, u32[]{:S(2)}) collective-permute-start(bf16[1040,128]{1,0:T(8,128)(2,1)S(1)} %pad_maximum_fusion), channel_id=1, source_target_pairs={{0,4},{2,6},{4,8},{6,10},{8,12},{10,14},{1,5},{3,7},{5,9},{7,11},{... | collective-permute-start | bytes 798728 | tf_op jit(solution)/shard_map/ppermute | solution.py:18
  30.7 0.6 fusion.64
  31.3 0.7 slice_bitcast_fusion
  32.0 0.6 broadcast_compare_fusion
  32.7 0.1 exponential_select_fusion
  32.8 0.9 %fusion.63 = (bf16[256,128]{1,0:T(8,128)(2,1)S(1)}, bf16[256,128]{1,0:T(8,128)(2,1)S(1)}) fusion(bf16[528,128]{1,0:T(8,128)(2,1)} %collective-permute-done.1), kind=kLoop, calls=%fused_computation.105 | loop fusion | bytes 262144 | tf_op jit(solution)/shard_map/slice | solution.py:141
  33.7 0.6 fusion.65
  34.3 0.1 copy.38
  34.4 0.1 copy.39
  38.6 0.1 copy.33
  38.6 9.7 %collective-permute-done.4 = bf16[1040,128]{1,0:T(8,128)(2,1)S(1)} collective-permute-done((bf16[1040,128]{1,0:T(8,128)(2,1)S(1)}, bf16[1040,128]{1,0:T(8,128)(2,1)S(1)}, u32[]{:S(2)}, u32[]{:S(2)}) %collective-permute-start.4) | collective-permute-done | bytes 266272 | tf_op jit(solution)/shard_map/ppermute | solution.py:18
  48.4 0.1 copy.36
  48.5 0.7 constant_dynamic-update-slice_fusion.4
  49.2 0.1 copy.37
  49.3 0.6 slice.120
  51.4 0.2 fusion.37
  51.5 0.6 constant_dynamic-update-slice_fusion.3
  52.2 0.6 constant_dynamic-update-slice_fusion.2
  52.8 0.6 constant_dynamic-update-slice_fusion.1
  53.4 0.1 broadcast_select_fusion
  53.5 0.9 %fusion.2 = (f32[2,8,128]{2,1,0:T(8,128)S(1)}, f32[2,640,128,8]{2,1,3,0:T(8,128)S(1)}) fusion(pred[128,640]{0,1:T(8,128)(4,1)S(1)} %fusion.37, bf16[128,2,8,128]{3,2,1,0:T(8,128)(2,1)S(1)} %bitcast.111, bf16[2,640,128]{2,1,0:T(8,128)(2,1)S(1)} %bitcast_dynamic-update-slice_fusion), kind=kOutput, calls=%fused_computation.4 | convolution fusion | flops 339474432 | bytes 6184960 | tf_op jit(solution)/shard_map/tkgd,ksd->kgts/dot_general | solution.py:71
  54.5 0.6 constant_dynamic-update-slice_fusion
  55.1 1.1 %fusion = f32[2,8,128]{2,1,0:T(8,128)S(1)} fusion(f32[2,640,128,8]{2,1,3,0:T(8,128)S(1)} %get-tuple-element.35, f32[2,8,128]{2,1,0:T(8,128)S(1)} %get-tuple-element.34, pred[128,640]{0,1:T(8,128)(4,1)S(1)} %fusion.37), kind=kLoop, calls=%fused_computation.2 | loop fusion | flops 5240832 | bytes 5341184 | tf_op jit(solution)/shard_map/reduce_sum | solution.py:75
  56.2 0.0 collective-permute-done.3
  56.2 1.4 %fusion.20 = bf16[16,128,128]{2,1,0:T(8,128)(2,1)S(1)} fusion(bf16[16,128,128]{2,1,0:T(8,128)(2,1)} %collective-permute-done.3, bf16[16,128,128]{2,1,0:T(8,128)(2,1)} %collective-permute-done, f32[16]{0:T(128)S(1)} %broadcast_select_fusion.1), kind=kLoop, calls=%fused_computation.25 | loop fusion | flops 1310720 | bytes 1572928 | tf_op jit(solution)/shard_map/convert_element_type | solution.py:154
  57.6 3.2 %collective-permute-start.5 = (bf16[16,128,128]{2,1,0:T(8,128)(2,1)S(1)}, bf16[16,128,128]{2,1,0:T(8,128)(2,1)}, u32[]{:S(2)}, u32[]{:S(2)}) collective-permute-start(bf16[16,128,128]{2,1,0:T(8,128)(2,1)S(1)} %fusion.20), channel_id=1, source_target_pairs={{0,4},{2,6},{4,8},{6,10},{8,12},{10,14},{1,5},{3,7},{5,9},{7,11},{... | collective-permute-start | bytes 1572872 | tf_op jit(solution)/shard_map/ppermute | solution.py:18
  60.9 1.5 %divide_convert_fusion = bf16[128,2,8,128]{0,3,2,1:T(8,128)(2,1)S(1)} fusion(f32[2,640,128,8]{2,1,3,0:T(8,128)S(1)} %get-tuple-element.35, f32[2,8,128]{2,1,0:T(8,128)S(1)} %get-tuple-element.34, pred[128,640]{0,1:T(8,128)(4,1)S(1)} %fusion.37, f32[128,2,8]{0,2,1:T(8,128)S(1)} %bitcast.132, bf16[2,640,128]{1,2,0:T(8,128)(2,1)S(1)} %copy-done.5), kind=kOutput, calls=%fused_computation.14 | convolution fusion | flops 341311488 | bytes 6193152 | tf_op jit(solution)/shard_map/kgts,ksd->kgtd/dot_general | solution.py:76
  62.3 0.0 copy-start.6
  62.4 1.0 %copy.42 = bf16[128,2048]{1,0:T(8,128)(2,1)} copy(bf16[128,2048]{0,1:T(8,128)(2,1)S(1)} %bitcast.120) | data formatting | bytes 1048576
  63.4 7.6 %collective-permute-done.5 = bf16[16,128,128]{2,1,0:T(8,128)(2,1)} collective-permute-done((bf16[16,128,128]{2,1,0:T(8,128)(2,1)S(1)}, bf16[16,128,128]{2,1,0:T(8,128)(2,1)}, u32[]{:S(2)}, u32[]{:S(2)}) %collective-permute-start.5) | collective-permute-done | bytes 524320 | tf_op jit(solution)/shard_map/ppermute | solution.py:18
  71.0 2.5 %fusion.10 = f32[128,16,128]{0,2,1:T(8,128)S(1)} fusion(bf16[16,128,128]{2,1,0:T(8,128)(2,1)} %collective-permute-done.5, bf16[16,128,128]{2,1,0:T(8,128)(2,1)} %collective-permute-done.3, bf16[16,128,128]{2,1,0:T(8,128)(2,1)} %collective-permute-done, f32[128,16]{0,1:T(8,128)S(1)} %copy.33, f32[16]{0:T(128)S(1)} %get-tuple-element.6, ...), kind=kOutput, calls=%fused_computation.12 | convolution fusion | flops 404750336 | bytes 3154048 | tf_op jit(solution)/shard_map/thd,hde->the/dot_general | solution.py:169
  73.6 2.7 %multiply_reduce_fusion = (f32[128]{0:T(128)S(1)}, f32[128,16,128]{0,2,1:T(8,128)}) fusion(f32[128,16,128]{0,2,1:T(8,128)S(1)} %fusion.10, bf16[128,16,128]{0,2,1:T(8,128)(2,1)} %bitcast.119, bf16[128,16,128]{0,2,1:T(8,128)(2,1)S(1)} %bitcast.118, f32[16,128]{1,0:T(8,128)S(1)} %reduce_window_sum.11, pred[128,128]{1,0:T(8,128)(4,1)S(1)} %fusion.38, ...), kind=kOutput, calls=%fused_computation.17 | convolution fusion | flops 136052608 | bytes 3695104 | tf_op jit(solution)/shard_map/hts,shd->thd/dot_general | solution.py:32
  76.2 5.1 %psum.7 = f32[128]{0:T(128)S(1)} all-reduce(f32[128]{0:T(128)S(1)} %get-tuple-element.32), channel_id=1, replica_groups=mesh['groups'=2,'ctx'=8,'tensor'=2] {'tensor'}, use_global_device_ids=true, to_apply=%region_2.3 | all-reduce | flops 128 | bytes 1024 | tf_op jit(solution)/shard_map/psum | solution.py:176
  81.3 1.6 %multiply_convert_fusion = bf16[128,16,128]{0,2,1:T(8,128)(2,1)S(1)} fusion(f32[128,16,128]{0,2,1:T(8,128)S(1)} %bitcast.110, f32[128,16,128]{0,2,1:T(8,128)} %get-tuple-element.33, f32[16,128]{1,0:T(8,128)S(1)} %bitcast.131, f32[128]{0:T(128)S(1)} %add_rsqrt_fusion), kind=kLoop, calls=%fused_computation.15 | loop fusion | flops 1048576 | bytes 2630144 | tf_op jit(solution)/shard_map/convert_element_type | solution.py:181
  82.9 1.0 %copy.41 = bf16[128,2048]{1,0:T(8,128)(2,1)} copy(bf16[128,2048]{0,1:T(8,128)(2,1)S(1)} %bitcast.112) | data formatting | bytes 1048576
  (33 shorter events, 0.2 us)
Async XLA Ops:
  0.6 70.4 %copy-start = (bf16[128,2048]{1,0:T(8,128)(2,1)S(1)}, bf16[128,2048]{1,0:T(8,128)(2,1)}, u32[]{:S(2)}) copy-start(bf16[128,2048]{1,0:T(8,128)(2,1)} %param.10) | copy-start | bytes 1572868
  0.6 25.0 %copy-start.1 = (bf16[128,2048]{1,0:T(8,128)(2,1)S(1)}, bf16[128,2048]{1,0:T(8,128)(2,1)}, u32[]{:S(2)}) copy-start(bf16[128,2048]{1,0:T(8,128)(2,1)} %value_ref.1) | copy-start | bytes 1572868
  0.7 26.0 %copy-start.3 = (bf16[128,2048]{1,0:T(8,128)(2,1)S(1)}, bf16[128,2048]{1,0:T(8,128)(2,1)}, u32[]{:S(2)}) copy-start(bf16[128,2048]{1,0:T(8,128)(2,1)} %param.16) | copy-start | bytes 1572868
  3.6 28.4 %copy-start.7 = (s32[128]{0:T(128)S(1)}, s32[128]{0:T(128)}, u32[]{:S(2)}) copy-start(s32[128]{0:T(128)} %param.19) | copy-start | bytes 1540
  5.6 21.5 %collective-permute-start.1 = (bf16[528,128]{1,0:T(8,128)(2,1)}, bf16[528,128]{1,0:T(8,128)(2,1)}, u32[]{:S(2)}, u32[]{:S(2)}) collective-permute-start(bf16[528,128]{1,0:T(8,128)(2,1)} %pad_maximum_fusion.1), channel_id=1, source_target_pairs={{0,4},{2,6},{4,8},{6,10},{8,12},{10,14},{1,5},{3,7},{5,9},{7,11},{... | collective-permute-start | bytes 405512 | tf_op jit(solution)/shard_map/ppermute | solution.py:18
  8.8 19.0 %collective-permute-start.2 = (bf16[528,128]{1,0:T(8,128)(2,1)}, bf16[528,128]{1,0:T(8,128)(2,1)S(1)}, u32[]{:S(2)}, u32[]{:S(2)}) collective-permute-start(bf16[528,128]{1,0:T(8,128)(2,1)} %pad_maximum_fusion.1), channel_id=1, source_target_pairs={{0,2},{2,4},{4,6},{6,8},{8,10},{10,12},{12,14},{1,3},{3,5},{5,7},{... | collective-permute-start | bytes 405512 | tf_op jit(solution)/shard_map/ppermute | solution.py:18
  12.7 20.0 %copy-start.2 = (f32[16,128]{0,1:T(8,128)S(1)}, f32[16,128]{0,1:T(8,128)}, u32[]{:S(2)}) copy-start(f32[16,128]{0,1:T(8,128)} %copy.25) | copy-start | bytes 24580
  17.1 39.0 %collective-permute-start = (bf16[16,128,128]{2,1,0:T(8,128)(2,1)}, bf16[16,128,128]{2,1,0:T(8,128)(2,1)}, u32[]{:S(2)}, u32[]{:S(2)}) collective-permute-start(bf16[16,128,128]{2,1,0:T(8,128)(2,1)} %shard_map.113), channel_id=1, source_target_pairs={{0,2},{2,4},{4,6},{6,8},{8,10},{10,12},{12,14},{1,3},{3,5},{5,7},{... | collective-permute-start | bytes 1572872 | tf_op jit(solution)/shard_map/ppermute | solution.py:18
  20.2 35.9 %collective-permute-start.3 = (bf16[16,128,128]{2,1,0:T(8,128)(2,1)}, bf16[16,128,128]{2,1,0:T(8,128)(2,1)}, u32[]{:S(2)}, u32[]{:S(2)}) collective-permute-start(bf16[16,128,128]{2,1,0:T(8,128)(2,1)} %shard_map.113), channel_id=1, source_target_pairs={{0,4},{2,6},{4,8},{6,10},{8,12},{10,14},{1,5},{3,7},{5,9},{7,11},{... | collective-permute-start | bytes 1572872 | tf_op jit(solution)/shard_map/ppermute | solution.py:18
  28.8 19.5 %collective-permute-start.4 = (bf16[1040,128]{1,0:T(8,128)(2,1)S(1)}, bf16[1040,128]{1,0:T(8,128)(2,1)S(1)}, u32[]{:S(2)}, u32[]{:S(2)}) collective-permute-start(bf16[1040,128]{1,0:T(8,128)(2,1)S(1)} %pad_maximum_fusion), channel_id=1, source_target_pairs={{0,4},{2,6},{4,8},{6,10},{8,12},{10,14},{1,5},{3,7},{5,9},{7,11},{... | collective-permute-start | bytes 798728 | tf_op jit(solution)/shard_map/ppermute | solution.py:18
  55.1 5.8 %copy-start.5 = (bf16[2,640,128]{1,2,0:T(8,128)(2,1)S(1)}, bf16[2,640,128]{1,2,0:T(8,128)(2,1)}, u32[]{:S(2)}) copy-start(bf16[2,640,128]{1,2,0:T(8,128)(2,1)} %constant_dynamic-update-slice_fusion) | copy-start | bytes 983044
  57.6 13.4 %collective-permute-start.5 = (bf16[16,128,128]{2,1,0:T(8,128)(2,1)S(1)}, bf16[16,128,128]{2,1,0:T(8,128)(2,1)}, u32[]{:S(2)}, u32[]{:S(2)}) collective-permute-start(bf16[16,128,128]{2,1,0:T(8,128)(2,1)S(1)} %fusion.20), channel_id=1, source_target_pairs={{0,4},{2,6},{4,8},{6,10},{8,12},{10,14},{1,5},{3,7},{5,9},{7,11},{... | collective-permute-start | bytes 1572872 | tf_op jit(solution)/shard_map/ppermute | solution.py:18
  60.8 12.7 %copy-start.4 = (bf16[128,2048]{0,1:T(8,128)(2,1)S(1)}, bf16[128,2048]{0,1:T(8,128)(2,1)}, u32[]{:S(2)}) copy-start(bf16[128,2048]{0,1:T(8,128)(2,1)} %copy.48) | copy-start | bytes 1572868
  62.3 19.0 %copy-start.6 = (f32[2048]{0:T(1024)S(1)}, f32[2048]{0:T(1024)}, u32[]{:S(2)}) copy-start(f32[2048]{0:T(1024)} %param.15) | copy-start | bytes 24580

commit v9 on v7

--- a/solution.py
+++ b/solution.py
@@ -57,6 +57,64 @@
         out_specs=pl.BlockSpec(memory_space=pltpu.VMEM),
         cost_estimate=pl.CostEstimate(flops=flops, bytes_accessed=3 * light_key.size, transcendentals=heads_here * tok_rows),
     )(decay_sum.T, code[:, None], light_key, light_value)
+
+
+def intra_kernel(decay_ref, decay_t_ref, code_row_ref, code_col_ref, query_ref, key_ref, value_ref, out_ref):
+    heads_here = decay_ref.shape[0]
+    tok_rows = code_col_ref.shape[0]
+    head_size = query_ref.shape[1] // heads_here
+    rows = lax.broadcasted_iota(jnp.int32, (tok_rows, tok_rows), 0)
+    cols = lax.broadcasted_iota(jnp.int32, (tok_rows, tok_rows), 1)
+    allowed = (code_col_ref[...] == code_row_ref[...]) & (cols <= rows)
+    for head in range(heads_here):
+        columns = slice(head * head_size, (head + 1) * head_size)
+        gap = jnp.where(allowed, decay_t_ref[:, head : head + 1] - decay_ref[head : head + 1, :], -jnp.inf)
+        products = lax.dot_general(
+            query_ref[:, columns], key_ref[:, columns], (((1,), (1,)), ((), ())), preferred_element_type=F32
+        )
+        weights = (products * jnp.exp(gap)).astype(BF16)
+        out_ref[:, columns] = jnp.dot(weights, value_ref[:, columns], preferred_element_type=F32)
+
+
+def intra_mixed(decay_sum, code, light_query, light_key, light_value):
+    heads_here = decay_sum.shape[0]
+    tok_rows, width = light_query.shape
+    flops = 4 * tok_rows * tok_rows * width
+    return pl.pallas_call(
+        intra_kernel,
+        out_shape=jax.ShapeDtypeStruct((tok_rows, width), F32),
+        in_specs=[pl.BlockSpec(memory_space=pltpu.VMEM)] * 7,
+        out_specs=pl.BlockSpec(memory_space=pltpu.VMEM),
+        cost_estimate=pl.CostEstimate(flops=flops, bytes_accessed=10 * light_query.size, transcendentals=heads_here * tok_rows * tok_rows),
+    )(decay_sum, decay_sum.T, code[None, :], code[:, None], light_query, light_key, light_value)
+
+
+def final_kernel(carry_ref, scale_t_ref, query_ref, mixed_ref, pair_ref, far_ref, out_ref, squares_ref):
+    heads_here, head_size = pair_ref.shape[0], pair_ref.shape[1]
+    squares = jnp.zeros((query_ref.shape[0], 1), F32)
+    for head in range(heads_here):
+        columns = slice(head * head_size, (head + 1) * head_size)
+        state = pair_ref[head] + carry_ref[head] * far_ref[head].astype(F32)
+        carried = jnp.dot(
+            query_ref[:, columns].astype(F32), state, precision=lax.Precision.HIGHEST, preferred_element_type=F32
+        )
+        total = mixed_ref[:, columns] + carried * scale_t_ref[:, head : head + 1]
+        out_ref[:, columns] = total
+        squares = squares + jnp.sum(total * total, axis=1, keepdims=True)
+    squares_ref[...] = squares
+
+
+def final_mixed(carry_scale, scale_in, light_query, mixed, pair_state, state_far):
+    tok_rows, width = light_query.shape
+    heads_here = pair_state.shape[0]
+    flops = 12 * tok_rows * width * pair_state.shape[1]
+    return pl.pallas_call(
+        final_kernel,
+        out_shape=(jax.ShapeDtypeStruct((tok_rows, width), F32), jax.ShapeDtypeStruct((tok_rows, 1), F32)),
+        in_specs=[pl.BlockSpec(memory_space=pltpu.SMEM)] + [pl.BlockSpec(memory_space=pltpu.VMEM)] * 5,
+        out_specs=(pl.BlockSpec(memory_space=pltpu.VMEM), pl.BlockSpec(memory_space=pltpu.VMEM)),
+        cost_estimate=pl.CostEstimate(flops=flops, bytes_accessed=4 * mixed.size * 3, transcendentals=0),
+    )(carry_scale, scale_in.T, light_query, mixed, pair_state, state_far)
 
 
 def soft_window(soft_query, key_heads, value_heads, code, code_window, heads_here):
@@ -117,7 +175,7 @@
     decay_sum = jnp.cumsum(log_decay, axis=1)
 
     own_state = local_state_of(decay_sum, code, light_key, light_value)
-    mixed = light_local(light_query, light_key, light_value, decay_sum, code)
+    mixed = intra_mixed(decay_sum, code, light_query, light_key, light_value)
     block_decay = jnp.exp(decay_sum[:, -1])
 
     own_keys = soft_key.reshape(tok_rows, kv_here, head_size).transpose(1, 0, 2)
@@ -150,7 +208,6 @@
 
     relay_kv = jnp.concatenate([kv_2[: 2 * kv_rows], kv_1[: 2 * kv_rows], rows_of(jnp.concatenate([code_2, code_1]), head_size)])
     state_far, kv_far = shifted((pair_state.astype(BF16), relay_kv), "ctx", 2)
-    state_far = state_far.astype(F32)
     keys_4 = kv_far[:kv_rows].reshape(kv_here, tok_rows, head_size)
     values_4 = kv_far[kv_rows : 2 * kv_rows].reshape(kv_here, tok_rows, head_size)
     keys_3 = kv_far[2 * kv_rows : 3 * kv_rows].reshape(kv_here, tok_rows, head_size)
@@ -160,17 +217,11 @@
 
     link_2 = (code_3[-1] == code_2[0]) & (code_2[0] == code_1[-1])
     carry_scale = jnp.where(link_2, decay_2 * decay_1, 0.0)
-    incoming_state = pair_state + carry_scale[:, None, None] * state_far
-
-    query_heads = light_query.reshape(tok_rows, heads_here, head_size)
-    carried_in = jnp.einsum(
-        "thd,hde->the", query_heads.astype(F32), incoming_state, precision=lax.Precision.HIGHEST
-    )
     uses_state = code == code_1[-1]
     scale_in = jnp.where(uses_state[None, :], jnp.exp(decay_sum), 0.0)
-    mixed = mixed + carried_in * scale_in.T[:, :, None]
-    squares = jnp.sum(mixed * mixed, axis=(1, 2))
-    squares = lax.psum(squares, "tensor")
+    mixed, squares = final_mixed(carry_scale, scale_in, light_query, mixed, pair_state, state_far)
+    mixed = mixed.reshape(tok_rows, heads_here, head_size)
+    squares = lax.psum(squares[:, 0], "tensor")
     features = heads_here * head_size * lax.axis_size("tensor")
     inverse = lax.rsqrt(squares / features + 1e-06)
     gate_open = jax.nn.sigmoid(light_gate.astype(F32)).reshape(tok_rows, heads_here, head_size)

time: 84.7 us -> 80 us (0.945)
  Pallas kernels: 3.7 us -> 12.9 us
  local copies, waits for them, and re-layouts: 17.6 us -> 9.31 us
  matrix products: 7.62 us -> 2.35 us
    pallas_call x0 -> x2, Pallas kernels: none -> 9.25 us  [the longest x1 5.03 us: intra_mixed(): pl.pallas_call(intra_kernel, out_shape=jax.ShapeDtypeStruct((tok_rows, wi...]
    dot_general x2 -> x0, matrix products: 5.22 us -> none  [the longest x1 2.69 us: light_local(): jnp.einsum('hts,shd->thd', weights, value_heads, preferred_element_type=F32)]
    reshape x2 -> x0, local copies, waits for them, and re-layouts: 3.05 us -> none  [the longest x1 2.05 us: light_local(): key_heads = light_key.reshape(tok_rows, heads_here, head_size)]
    unnamed x29 -> x24, local copies, waits for them, and re-layouts: 6.72 us -> 5 us
    div x1 -> x0, other arithmetic: 1.32 us -> none  [on_device(): jax.nn.sigmoid(light_gate.astype(F32))]
    pallas_call x0 -> x1, other arithmetic: none -> 0.94 us  [final_mixed(): pl.pallas_call(final_kernel, out_shape=(jax.ShapeDtypeStruct((tok_rows, w...]
    slice x1, local copies, waits for them, and re-layouts: 0.91 us -> 0.01 us  [on_device(): kv_2[:2 * kv_rows]]
    slice x2, local copies, waits for them, and re-layouts: 0.89 us -> 0.02 us  [unpack(): values = block[kv_rows:2 * kv_rows].reshape(kv_here, tok_rows, head_size)]
  transfers between devices with their start and end apart: 6 -> 6, of which waited for: 2 -> 2; matrix products, arithmetic and copies ran while one was open for 25% -> 15% of each run, Pallas kernels for 4% -> 11%
where the time goes in v9:
time: 80 us; the launch traced here: 79.4 us
  waiting for transfers between devices  16.8 us (21%)
  starting transfers between devices  16.5 us (21%)
  Pallas kernels  12.9 us (16%)
  other arithmetic  10.2 us (13%)
  local copies, waits for them, and re-layouts  9.31 us (12%)
  between operations  6.13 us (8%)
  blocking collectives  5.08 us (6%)
  matrix products  2.35 us (3%)
    ppermute x6, waiting for transfers between devices, shifted(): return lax.ppermute(block, axis, route)  16.8 us
    ppermute x6, starting transfers between devices, shifted(): return lax.ppermute(block, axis, route)  16.5 us
    psum x1, blocking collectives, on_device(): squares = lax.psum(squares[:, 0], 'tensor')  5.08 us
    pallas_call x1, Pallas kernels, intra_mixed(): pl.pallas_call(intra_kernel, out_shape=jax.ShapeDtypeStruct((tok_rows, wi...  5.03 us
    unnamed x24, local copies, waits for them, and re-layouts  5 us
    pallas_call x1, Pallas kernels, final_mixed(): pl.pallas_call(final_kernel, out_shape=(jax.ShapeDtypeStruct((tok_rows, w...  4.22 us
    pallas_call x1, Pallas kernels, local_state_of(): pl.pallas_call(state_kernel, out_shape=jax.ShapeDtypeStruct((heads_here,...  3.7 us
    convert_element_type x1, other arithmetic, on_device(): light_out = normed.reshape(tok_rows, heads_here * head_size).astype(BF16)  2.34 us
  transfers between devices with their start and end apart: 6, of which 2 were waited for; matrix products, arithmetic and copies ran while one was open for 15% of the time, Pallas kernels for 11%

profile of v9, /device:TPU:11, one launch (start us, length us, event | category | flops | bytes accessed | tf_op | source)
XLA Modules:
  0.0 79.4 jit_solution(6056914500878738069)
XLA Ops:
  0.6 0.0 copy-start.5
  0.6 1.0 %reduce_window_sum.13.decay_ref = f32[16,128]{1,0:T(8,128)S(1)} reduce-window(f32[16,128]{1,0:T(8,128)} %param.14, f32[]{:T(128)} %constant.10.clone.1), window={size=1x128 pad=0_0x127_0}, to_apply=%region_0.0 | reduce-window | flops 260096 | bytes 16388 | tf_op jit(solution)/shard_map/jit(cumsum)/reduce_window_sum | solution.py:175
  1.6 0.0 copy-start.3
  1.6 0.2 fusion.22
  1.8 1.2 %convert_add_fusion = (f32[128]{0:T(128)S(1)}, bf16[128]{0:T(256)(128)(2,1)S(1)}, f32[1,128]{1,0:T(1,128)}, f32[128,1]{0,1:T(1,128)S(1)}) fusion(s32[128]{0:T(128)} %param.19), kind=kLoop, calls=%fused_computation.65 | loop fusion | flops 384 | bytes 2304 | tf_op jit(solution)/shard_map/add | solution.py:174
  3.1 0.9 %copy.19 = bf16[128,256]{0,1:T(8,128)(2,1)S(1)} copy(bf16[128,256]{1,0:T(8,128)(2,1)} %param.17) | data formatting | bytes 131072 | tf_op args[7]
  4.0 0.1 copy.20
  4.2 1.0 %copy.21 = bf16[128,256]{0,1:T(8,128)(2,1)S(1)} copy(bf16[128,256]{1,0:T(8,128)(2,1)} %param.18) | data formatting | bytes 131072 | tf_op args[8]
  5.1 0.1 copy.22
  5.3 0.1 fusion.26
  5.4 3.2 %collective-permute-start = (bf16[528,128]{1,0:T(8,128)(2,1)S(1)}, bf16[528,128]{1,0:T(8,128)(2,1)S(1)}, u32[]{:S(2)}, u32[]{:S(2)}) collective-permute-start(bf16[528,128]{1,0:T(8,128)(2,1)S(1)} %pad_maximum_fusion.1), channel_id=1, source_target_pairs={{0,4},{2,6},{4,8},{6,10},{8,12},{10,14},{1,5},{3,7},{5,9},{7,11},{... | collective-permute-start | bytes 405512 | tf_op jit(solution)/shard_map/ppermute | solution.py:17
  8.6 3.2 %collective-permute-start.1 = (bf16[528,128]{1,0:T(8,128)(2,1)S(1)}, bf16[528,128]{1,0:T(8,128)(2,1)S(1)}, u32[]{:S(2)}, u32[]{:S(2)}) collective-permute-start(bf16[528,128]{1,0:T(8,128)(2,1)S(1)} %pad_maximum_fusion.1), channel_id=1, source_target_pairs={{0,2},{2,4},{4,6},{6,8},{8,10},{10,12},{12,14},{1,3},{3,5},{5,7},{... | collective-permute-start | bytes 405512 | tf_op jit(solution)/shard_map/ppermute | solution.py:17
  11.7 0.7 copy.23
  12.5 0.0 copy-start
  12.5 0.7 copy.24.code_col_ref.code_ref
  13.2 3.7 %shard_map.114 = bf16[16,128,128]{2,1,0:T(8,128)(2,1)} custom-call(f32[128,16]{1,0:T(8,128)} %bitcast.82, f32[128,1]{1,0:T(8,128)} %copy.24.code_col_ref.code_ref, bf16[128,2048]{1,0:T(8,128)(2,1)} %key_ref.3, bf16[128,2048]{1,0:T(8,128)(2,1)} %value_ref.3), custom_call_target="tpu_custom_call" | custom-call | flops 67108864 | bytes 786432 | tf_op jit(solution)/shard_map/pallas_call | solution.py:53
  16.9 3.1 %collective-permute-start.3 = (bf16[16,128,128]{2,1,0:T(8,128)(2,1)}, bf16[16,128,128]{2,1,0:T(8,128)(2,1)S(1)}, u32[]{:S(2)}, u32[]{:S(2)}) collective-permute-start(bf16[16,128,128]{2,1,0:T(8,128)(2,1)} %shard_map.114), channel_id=1, source_target_pairs={{0,2},{2,4},{4,6},{6,8},{8,10},{10,12},{12,14},{1,3},{3,5},{5,7},{... | collective-permute-start | bytes 1572872 | tf_op jit(solution)/shard_map/ppermute | solution.py:17
  20.0 1.9 %collective-permute-start.4 = (bf16[16,128,128]{2,1,0:T(8,128)(2,1)}, bf16[16,128,128]{2,1,0:T(8,128)(2,1)S(1)}, u32[]{:S(2)}, u32[]{:S(2)}) collective-permute-start(bf16[16,128,128]{2,1,0:T(8,128)(2,1)} %shard_map.114), channel_id=1, source_target_pairs={{0,4},{2,6},{4,8},{6,10},{8,12},{10,14},{1,5},{3,7},{5,9},{7,11},{... | collective-permute-start | bytes 1572872 | tf_op jit(solution)/shard_map/ppermute | solution.py:17
  21.9 1.1 %copy.36 = bf16[16,8,16,128]{3,2,1,0:T(8,128)(2,1)S(1)} copy(bf16[16,8,16,128]{3,1,2,0:T(8,128)(2,1)} %bitcast.87) | data formatting | bytes 1048576
  23.1 0.0 copy-done.3
  23.1 5.0 %shard_map.113.mixed_ref = f32[128,2048]{1,0:T(8,128)} custom-call(f32[16,128]{1,0:T(8,128)} %copy-done.3, f32[128,16]{1,0:T(8,128)} %bitcast.83, f32[1,128]{1,0:T(1,128)} %get-tuple-element.30.code_row_ref, f32[128,1]{1,0:T(8,128)} %copy.24.code_col_ref.code_ref, bf16[128,2048]{1,0:T(8,128)(2,1)} %query_ref.3, bf16[128,2048]{1,0:T(8,128)(2,1)} %key_ref.3, ...), custom_call_target="tpu_custom_call" | custom-call | flops 134217728 | bytes 2621440 | tf_op jit(solution)/shard_map/pallas_call | solution.py:83
  28.1 0.0 collective-permute-done
  28.2 0.0 collective-permute-done.1
  28.3 1.9 %collective-permute-start.2 = (bf16[1040,128]{1,0:T(8,128)(2,1)S(1)}, bf16[1040,128]{1,0:T(8,128)(2,1)S(1)}, u32[]{:S(2)}, u32[]{:S(2)}) collective-permute-start(bf16[1040,128]{1,0:T(8,128)(2,1)S(1)} %pad_maximum_fusion), channel_id=1, source_target_pairs={{0,4},{2,6},{4,8},{6,10},{8,12},{10,14},{1,5},{3,7},{5,9},{7,11},{... | collective-permute-start | bytes 798728 | tf_op jit(solution)/shard_map/ppermute | solution.py:17
  30.2 0.6 fusion.43
  30.8 0.6 fusion.42
  34.0 0.1 broadcast_select_fusion
  34.1 0.0 copy-done.5
  34.1 0.6 broadcast_compare_fusion
  34.7 0.1 copy.29
  34.8 0.1 copy.30
  36.2 0.0 copy-done
  36.3 0.7 exponential_select_fusion.scale_t_ref
  37.0 11.1 %collective-permute-done.2 = bf16[1040,128]{1,0:T(8,128)(2,1)S(1)} collective-permute-done((bf16[1040,128]{1,0:T(8,128)(2,1)S(1)}, bf16[1040,128]{1,0:T(8,128)(2,1)S(1)}, u32[]{:S(2)}, u32[]{:S(2)}) %collective-permute-start.2) | collective-permute-done | bytes 266272 | tf_op jit(solution)/shard_map/ppermute | solution.py:17
  48.2 0.1 copy.27
  48.4 0.1 copy.28
  48.5 0.6 slice.112
  49.1 0.2 fusion.15
  49.3 0.9 %fusion.2 = (f32[2,8,128]{2,1,0:T(8,128)S(1)}, f32[2,640,128,8]{2,1,3,0:T(8,128)S(1)}) fusion(pred[128,640]{0,1:T(8,128)(4,1)S(1)} %fusion.15, bf16[128,2,8,128]{3,2,1,0:T(8,128)(2,1)S(1)} %bitcast.81, bf16[2,640,128]{2,1,0:T(8,128)(2,1)S(1)} %bitcast_dynamic-update-slice_fusion), kind=kOutput, calls=%fused_computation.4 | convolution fusion | flops 339474432 | bytes 6184960 | tf_op jit(solution)/shard_map/tkgd,ksd->kgts/dot_general | solution.py:128
  50.3 1.1 %fusion = f32[2,8,128]{2,1,0:T(8,128)S(1)} fusion(f32[2,640,128,8]{2,1,3,0:T(8,128)S(1)} %get-tuple-element.40, f32[2,8,128]{2,1,0:T(8,128)S(1)} %get-tuple-element.39, pred[128,640]{0,1:T(8,128)(4,1)S(1)} %fusion.15), kind=kLoop, calls=%fused_computation.2 | loop fusion | flops 5240832 | bytes 5341184 | tf_op jit(solution)/shard_map/reduce_sum | solution.py:132
  51.4 0.0 collective-permute-done.3
  51.4 0.0 collective-permute-done.4
  51.4 1.3 %fusion.38 = (bf16[16,128,128]{2,1,0:T(8,128)(2,1)S(1)}, f32[16,128,128]{2,1,0:T(8,128)}) fusion(bf16[16,128,128]{2,1,0:T(8,128)(2,1)S(1)} %collective-permute-done.4, f32[16]{0:T(128)S(1)} %get-tuple-element.12, bf16[16,128,128]{2,1,0:T(8,128)(2,1)S(1)} %collective-permute-done.3), kind=kLoop, calls=%fused_computation.76 | loop fusion | flops 1310720 | bytes 2621504 | tf_op jit(solution)/shard_map/convert_element_type | solution.py:210
  52.7 3.2 %collective-permute-start.5 = (bf16[16,128,128]{2,1,0:T(8,128)(2,1)S(1)}, bf16[16,128,128]{2,1,0:T(8,128)(2,1)S(1)}, u32[]{:S(2)}, u32[]{:S(2)}) collective-permute-start(bf16[16,128,128]{2,1,0:T(8,128)(2,1)S(1)} %get-tuple-element.10), channel_id=1, source_target_pairs={{0,4},{2,6},{4,8},{6,10},{8,12},{10,14},{1,5},{3,7},{5,9},{7,11},{... | collective-permute-start | bytes 1572872 | tf_op jit(solution)/shard_map/ppermute | solution.py:17
  55.9 0.0 copy-start.1
  55.9 0.0 copy-start.4
  55.9 1.4 %divide_convert_fusion = bf16[128,2,8,128]{0,3,2,1:T(8,128)(2,1)S(1)} fusion(f32[2,640,128,8]{2,1,3,0:T(8,128)S(1)} %get-tuple-element.40, f32[2,8,128]{2,1,0:T(8,128)S(1)} %get-tuple-element.39, pred[128,640]{0,1:T(8,128)(4,1)S(1)} %fusion.15, f32[128,2,8]{0,2,1:T(8,128)S(1)} %bitcast.99, bf16[2,640,128]{1,2,0:T(8,128)(2,1)S(1)} %constant_dynamic-update-slice_fusion), kind=kOutput, calls=%fused_computation.8 | convolution fusion | flops 341311488 | bytes 6193152 | tf_op jit(solution)/shard_map/kgts,ksd->kgtd/dot_general | solution.py:133
  57.4 1.0 %copy.32 = bf16[128,2048]{1,0:T(8,128)(2,1)} copy(bf16[128,2048]{0,1:T(8,128)(2,1)S(1)} %bitcast.88) | data formatting | bytes 1048576
  59.7 0.6 broadcast_select_fusion.1.carry_ref
  60.3 5.7 %collective-permute-done.5.far_ref = bf16[16,128,128]{2,1,0:T(8,128)(2,1)S(1)} collective-permute-done((bf16[16,128,128]{2,1,0:T(8,128)(2,1)S(1)}, bf16[16,128,128]{2,1,0:T(8,128)(2,1)S(1)}, u32[]{:S(2)}, u32[]{:S(2)}) %collective-permute-start.5) | collective-permute-done | bytes 524320 | tf_op jit(solution)/shard_map/ppermute | solution.py:17
  66.0 0.0 copy-start.2
  66.0 0.8 copy-done.2
  66.8 4.2 %shard_map.115 = (f32[128,2048]{1,0:T(8,128)}, f32[128,1]{1,0:T(8,128)}) custom-call(f32[16]{0:T(128)} %broadcast_select_fusion.1.carry_ref, f32[128,16]{1,0:T(8,128)} %exponential_select_fusion.scale_t_ref, bf16[128,2048]{1,0:T(8,128)(2,1)} %query_ref.3, f32[128,2048]{1,0:T(8,128)} %shard_map.113.mixed_ref, f32[16,128,128]{2,1,0:T(8,128)} %get-tuple-element.11.pair_ref, ...), custom_call_target="tpu_custom_call" | custom-call | flops 402653184 | bytes 3145728 | tf_op jit(solution)/shard_map/pallas_call | solution.py:111
  71.0 0.9 %reduce.1 = f32[128]{0:T(128)S(1)} reduce(f32[128,1]{1,0:T(8,128)} %get-tuple-element.5, f32[]{:T(128)} %constant.29), dimensions={1}, to_apply=%get-tuple-element.5.reduce_sub_computation | reduce | bytes 1028 | tf_op jit(solution)/shard_map/pallas_call | solution.py:111
  71.9 5.1 %psum.7 = f32[128]{0:T(128)S(1)} all-reduce(f32[128]{0:T(128)S(1)} %reduce.1), channel_id=1, replica_groups=mesh['groups'=2,'ctx'=8,'tensor'=2] {'tensor'}, use_global_device_ids=true, to_apply=%region_1.2 | all-reduce | flops 128 | bytes 1024 | tf_op jit(solution)/shard_map/psum | solution.py:224
  77.0 0.0 copy-done.1
  77.0 0.0 copy-done.4
  77.0 2.3 %multiply_convert_fusion = bf16[128,2048]{1,0:T(8,128)(2,1)} fusion(bf16[128,2048]{1,0:T(8,128)(2,1)S(1)} %copy-done.1, f32[128,2048]{1,0:T(8,128)} %get-tuple-element.4, f32[2048]{0:T(1024)S(1)} %copy-done.4, f32[128]{0:T(128)S(1)} %add_rsqrt_fusion), kind=kLoop, calls=%fused_computation.9 | loop fusion | flops 2097152 | bytes 2105856 | tf_op jit(solution)/shard_map/convert_element_type | solution.py:229
  (29 shorter events, 0.3 us)
Async XLA Ops:
  0.6 33.4 %copy-start.5 = (s32[128]{0:T(128)S(1)}, s32[128]{0:T(128)}, u32[]{:S(2)}) copy-start(s32[128]{0:T(128)} %param.19) | copy-start | bytes 1540
  1.6 21.5 %copy-start.3 = (f32[16,128]{1,0:T(8,128)}, f32[16,128]{1,0:T(8,128)S(1)}, u32[]{:S(2)}) copy-start(f32[16,128]{1,0:T(8,128)S(1)} %reduce_window_sum.13.decay_ref) | copy-start | bytes 24580
  5.4 22.8 %collective-permute-start = (bf16[528,128]{1,0:T(8,128)(2,1)S(1)}, bf16[528,128]{1,0:T(8,128)(2,1)S(1)}, u32[]{:S(2)}, u32[]{:S(2)}) collective-permute-start(bf16[528,128]{1,0:T(8,128)(2,1)S(1)} %pad_maximum_fusion.1), channel_id=1, source_target_pairs={{0,4},{2,6},{4,8},{6,10},{8,12},{10,14},{1,5},{3,7},{5,9},{7,11},{... | collective-permute-start | bytes 405512 | tf_op jit(solution)/shard_map/ppermute | solution.py:17
  8.6 19.6 %collective-permute-start.1 = (bf16[528,128]{1,0:T(8,128)(2,1)S(1)}, bf16[528,128]{1,0:T(8,128)(2,1)S(1)}, u32[]{:S(2)}, u32[]{:S(2)}) collective-permute-start(bf16[528,128]{1,0:T(8,128)(2,1)S(1)} %pad_maximum_fusion.1), channel_id=1, source_target_pairs={{0,2},{2,4},{4,6},{6,8},{8,10},{10,12},{12,14},{1,3},{3,5},{5,7},{... | collective-permute-start | bytes 405512 | tf_op jit(solution)/shard_map/ppermute | solution.py:17
  12.5 23.8 %copy-start = (f32[16,128]{0,1:T(8,128)S(1)}, f32[16,128]{0,1:T(8,128)}, u32[]{:S(2)}) copy-start(f32[16,128]{0,1:T(8,128)} %copy.23) | copy-start | bytes 24580
  16.9 34.5 %collective-permute-start.3 = (bf16[16,128,128]{2,1,0:T(8,128)(2,1)}, bf16[16,128,128]{2,1,0:T(8,128)(2,1)S(1)}, u32[]{:S(2)}, u32[]{:S(2)}) collective-permute-start(bf16[16,128,128]{2,1,0:T(8,128)(2,1)} %shard_map.114), channel_id=1, source_target_pairs={{0,2},{2,4},{4,6},{6,8},{8,10},{10,12},{12,14},{1,3},{3,5},{5,7},{... | collective-permute-start | bytes 1572872 | tf_op jit(solution)/shard_map/ppermute | solution.py:17
  20.0 31.3 %collective-permute-start.4 = (bf16[16,128,128]{2,1,0:T(8,128)(2,1)}, bf16[16,128,128]{2,1,0:T(8,128)(2,1)S(1)}, u32[]{:S(2)}, u32[]{:S(2)}) collective-permute-start(bf16[16,128,128]{2,1,0:T(8,128)(2,1)} %shard_map.114), channel_id=1, source_target_pairs={{0,4},{2,6},{4,8},{6,10},{8,12},{10,14},{1,5},{3,7},{5,9},{7,11},{... | collective-permute-start | bytes 1572872 | tf_op jit(solution)/shard_map/ppermute | solution.py:17
  28.3 19.8 %collective-permute-start.2 = (bf16[1040,128]{1,0:T(8,128)(2,1)S(1)}, bf16[1040,128]{1,0:T(8,128)(2,1)S(1)}, u32[]{:S(2)}, u32[]{:S(2)}) collective-permute-start(bf16[1040,128]{1,0:T(8,128)(2,1)S(1)} %pad_maximum_fusion), channel_id=1, source_target_pairs={{0,4},{2,6},{4,8},{6,10},{8,12},{10,14},{1,5},{3,7},{5,9},{7,11},{... | collective-permute-start | bytes 798728 | tf_op jit(solution)/shard_map/ppermute | solution.py:17
  52.7 13.3 %collective-permute-start.5 = (bf16[16,128,128]{2,1,0:T(8,128)(2,1)S(1)}, bf16[16,128,128]{2,1,0:T(8,128)(2,1)S(1)}, u32[]{:S(2)}, u32[]{:S(2)}) collective-permute-start(bf16[16,128,128]{2,1,0:T(8,128)(2,1)S(1)} %get-tuple-element.10), channel_id=1, source_target_pairs={{0,4},{2,6},{4,8},{6,10},{8,12},{10,14},{1,5},{3,7},{5,9},{7,11},{... | collective-permute-start | bytes 1572872 | tf_op jit(solution)/shard_map/ppermute | solution.py:17
  55.9 21.1 %copy-start.1 = (bf16[128,2048]{1,0:T(8,128)(2,1)S(1)}, bf16[128,2048]{1,0:T(8,128)(2,1)}, u32[]{:S(2)}) copy-start(bf16[128,2048]{1,0:T(8,128)(2,1)} %param.13) | copy-start | bytes 1572868
  55.9 21.1 %copy-start.4 = (f32[2048]{0:T(1024)S(1)}, f32[2048]{0:T(1024)}, u32[]{:S(2)}) copy-start(f32[2048]{0:T(1024)} %param.15) | copy-start | bytes 24580
  66.0 0.8 copy-start.2

commit v10 on v9

--- a/solution.py
+++ b/solution.py
@@ -5,6 +5,7 @@
 from jax.experimental.pallas import tpu as pltpu
 from jax.sharding import PartitionSpec as P
 
+
 NEG_BIG = -1e30
 MAXDOC = 512
 F32 = jnp.float32
@@ -15,21 +16,6 @@
     devices = lax.axis_size(axis)
     route = [(i, i + distance) for i in range(devices - distance)]
     return lax.ppermute(block, axis, route)
-
-
-def light_local(light_query, light_key, light_value, decay_sum, code):
-    tok_rows, heads_here = light_query.shape[0], decay_sum.shape[0]
-    head_size = light_query.shape[1] // heads_here
-    query_heads = light_query.reshape(tok_rows, heads_here, head_size)
-    key_heads = light_key.reshape(tok_rows, heads_here, head_size)
-    value_heads = light_value.reshape(tok_rows, heads_here, head_size)
-    token_position = jnp.arange(tok_rows)
-    allowed = (code[:, None] == code[None, :]) & (token_position[None, :] <= token_position[:, None])
-    decay_gap = jnp.where(allowed[None], decay_sum[:, :, None] - decay_sum[:, None, :], -jnp.inf)
-    products = jnp.einsum("thd,shd->hts", query_heads, key_heads, preferred_element_type=F32)
-    weights = (products * jnp.exp(decay_gap)).astype(BF16)
-    mixed = jnp.einsum("hts,shd->thd", weights, value_heads, preferred_element_type=F32)
-    return mixed
 
 
 def state_kernel(decay_ref, code_ref, key_ref, value_ref, out_ref):
@@ -106,7 +92,6 @@
 
 def final_mixed(carry_scale, scale_in, light_query, mixed, pair_state, state_far):
     tok_rows, width = light_query.shape
-    heads_here = pair_state.shape[0]
     flops = 12 * tok_rows * width * pair_state.shape[1]
     return pl.pallas_call(
         final_kernel,
@@ -154,7 +139,7 @@
     return jnp.pad(flat, (0, padded - flat.shape[0])).reshape(-1, width).astype(BF16)
 
 
-def on_device(
+def on_device_body(
     light_query,
     light_key,
     light_value,
@@ -180,7 +165,6 @@
 
     own_keys = soft_key.reshape(tok_rows, kv_here, head_size).transpose(1, 0, 2)
     own_values = soft_value.reshape(tok_rows, kv_here, head_size).transpose(1, 0, 2)
-    state_rows = heads_here * head_size
     kv_rows = kv_here * tok_rows
     own_kv = jnp.concatenate(
         [
@@ -207,7 +191,8 @@
     pair_state = state_1.astype(F32) + jnp.where(link_1, decay_1, 0.0)[:, None, None] * state_2.astype(F32)
 
     relay_kv = jnp.concatenate([kv_2[: 2 * kv_rows], kv_1[: 2 * kv_rows], rows_of(jnp.concatenate([code_2, code_1]), head_size)])
-    state_far, kv_far = shifted((pair_state.astype(BF16), relay_kv), "ctx", 2)
+    state_far = shifted(pair_state.astype(BF16), "ctx", 2)
+    kv_far = shifted(relay_kv, "ctx", 2)
     keys_4 = kv_far[:kv_rows].reshape(kv_here, tok_rows, head_size)
     values_4 = kv_far[kv_rows : 2 * kv_rows].reshape(kv_here, tok_rows, head_size)
     keys_3 = kv_far[2 * kv_rows : 3 * kv_rows].reshape(kv_here, tok_rows, head_size)
@@ -249,6 +234,4 @@
         P(("groups", "ctx")),
     )
     out_specs = (P(("groups", "ctx"), "tensor"), P(("groups", "ctx"), "tensor"))
-    return jax.shard_map(
-        on_device, mesh=mesh, in_specs=in_specs, out_specs=out_specs, check_vma=False
-    )
+    return jax.shard_map(on_device_body, mesh=mesh, in_specs=in_specs, out_specs=out_specs, check_vma=False)

time: 80 us -> 80 us (level)
  no operation moved by 1% of the time
where the time goes in v10:
time: 80 us; the launch traced here: 79.4 us
  waiting for transfers between devices  16.8 us (21%)
  starting transfers between devices  16.5 us (21%)
  Pallas kernels  12.9 us (16%)
  other arithmetic  10.2 us (13%)
  local copies, waits for them, and re-layouts  9.31 us (12%)
  between operations  6.13 us (8%)
  blocking collectives  5.08 us (6%)
  matrix products  2.35 us (3%)
    ppermute x6, waiting for transfers between devices, shifted(): return lax.ppermute(block, axis, route)  16.8 us
    ppermute x6, starting transfers between devices, shifted(): return lax.ppermute(block, axis, route)  16.5 us
    psum x1, blocking collectives, on_device_body(): squares = lax.psum(squares[:, 0], 'tensor')  5.08 us
    pallas_call x1, Pallas kernels, intra_mixed(): pl.pallas_call(intra_kernel, out_shape=jax.ShapeDtypeStruct((tok_rows, wi...  5.03 us
    unnamed x24, local copies, waits for them, and re-layouts  5 us
    pallas_call x1, Pallas kernels, final_mixed(): pl.pallas_call(final_kernel, out_shape=(jax.ShapeDtypeStruct((tok_rows, w...  4.22 us
    pallas_call x1, Pallas kernels, local_state_of(): pl.pallas_call(state_kernel, out_shape=jax.ShapeDtypeStruct((heads_here,...  3.7 us
    convert_element_type x1, other arithmetic, on_device_body(): light_out = normed.reshape(tok_rows, heads_here * head_size).astype(BF16)  2.34 us
  transfers between devices with their start and end apart: 6, of which 2 were waited for; matrix products, arithmetic and copies ran while one was open for 15% of the time, Pallas kernels for 11%

profile of v10, /device:TPU:11, one launch (start us, length us, event | category | flops | bytes accessed | tf_op | source)
XLA Modules:
  0.0 79.4 jit_solution(6056914500878738069)
XLA Ops:
  0.6 0.0 copy-start.5
  0.6 1.0 %reduce_window_sum.13.decay_ref = f32[16,128]{1,0:T(8,128)S(1)} reduce-window(f32[16,128]{1,0:T(8,128)} %param.14, f32[]{:T(128)} %constant.10.clone.1), window={size=1x128 pad=0_0x127_0}, to_apply=%region_0.0 | reduce-window | flops 260096 | bytes 16388 | tf_op jit(solution)/shard_map/jit(cumsum)/reduce_window_sum | solution.py:160
  1.6 0.0 copy-start.3
  1.6 0.2 fusion.22
  1.8 1.2 %convert_add_fusion = (f32[128]{0:T(128)S(1)}, bf16[128]{0:T(256)(128)(2,1)S(1)}, f32[1,128]{1,0:T(1,128)}, f32[128,1]{0,1:T(1,128)S(1)}) fusion(s32[128]{0:T(128)} %param.19), kind=kLoop, calls=%fused_computation.65 | loop fusion | flops 384 | bytes 2304 | tf_op jit(solution)/shard_map/add | solution.py:159
  3.1 0.9 %copy.19 = bf16[128,256]{0,1:T(8,128)(2,1)S(1)} copy(bf16[128,256]{1,0:T(8,128)(2,1)} %param.17) | data formatting | bytes 131072 | tf_op args[7]
  4.0 0.1 copy.20
  4.2 1.0 %copy.21 = bf16[128,256]{0,1:T(8,128)(2,1)S(1)} copy(bf16[128,256]{1,0:T(8,128)(2,1)} %param.18) | data formatting | bytes 131072 | tf_op args[8]
  5.1 0.1 copy.22
  5.3 0.1 fusion.26
  5.4 3.2 %collective-permute-start = (bf16[528,128]{1,0:T(8,128)(2,1)S(1)}, bf16[528,128]{1,0:T(8,128)(2,1)S(1)}, u32[]{:S(2)}, u32[]{:S(2)}) collective-permute-start(bf16[528,128]{1,0:T(8,128)(2,1)S(1)} %pad_maximum_fusion.1), channel_id=1, source_target_pairs={{0,4},{2,6},{4,8},{6,10},{8,12},{10,14},{1,5},{3,7},{5,9},{7,11},{... | collective-permute-start | bytes 405512 | tf_op jit(solution)/shard_map/ppermute | solution.py:18
  8.6 3.2 %collective-permute-start.1 = (bf16[528,128]{1,0:T(8,128)(2,1)S(1)}, bf16[528,128]{1,0:T(8,128)(2,1)S(1)}, u32[]{:S(2)}, u32[]{:S(2)}) collective-permute-start(bf16[528,128]{1,0:T(8,128)(2,1)S(1)} %pad_maximum_fusion.1), channel_id=1, source_target_pairs={{0,2},{2,4},{4,6},{6,8},{8,10},{10,12},{12,14},{1,3},{3,5},{5,7},{... | collective-permute-start | bytes 405512 | tf_op jit(solution)/shard_map/ppermute | solution.py:18
  11.7 0.7 copy.23
  12.5 0.0 copy-start
  12.5 0.7 copy.24.code_col_ref.code_ref
  13.2 3.7 %shard_map.114 = bf16[16,128,128]{2,1,0:T(8,128)(2,1)} custom-call(f32[128,16]{1,0:T(8,128)} %bitcast.82, f32[128,1]{1,0:T(8,128)} %copy.24.code_col_ref.code_ref, bf16[128,2048]{1,0:T(8,128)(2,1)} %key_ref.3, bf16[128,2048]{1,0:T(8,128)(2,1)} %value_ref.3), custom_call_target="tpu_custom_call" | custom-call | flops 67108864 | bytes 786432 | tf_op jit(solution)/shard_map/pallas_call | solution.py:39
  16.9 3.1 %collective-permute-start.3 = (bf16[16,128,128]{2,1,0:T(8,128)(2,1)}, bf16[16,128,128]{2,1,0:T(8,128)(2,1)S(1)}, u32[]{:S(2)}, u32[]{:S(2)}) collective-permute-start(bf16[16,128,128]{2,1,0:T(8,128)(2,1)} %shard_map.114), channel_id=1, source_target_pairs={{0,2},{2,4},{4,6},{6,8},{8,10},{10,12},{12,14},{1,3},{3,5},{5,7},{... | collective-permute-start | bytes 1572872 | tf_op jit(solution)/shard_map/ppermute | solution.py:18
  20.0 1.9 %collective-permute-start.4 = (bf16[16,128,128]{2,1,0:T(8,128)(2,1)}, bf16[16,128,128]{2,1,0:T(8,128)(2,1)S(1)}, u32[]{:S(2)}, u32[]{:S(2)}) collective-permute-start(bf16[16,128,128]{2,1,0:T(8,128)(2,1)} %shard_map.114), channel_id=1, source_target_pairs={{0,4},{2,6},{4,8},{6,10},{8,12},{10,14},{1,5},{3,7},{5,9},{7,11},{... | collective-permute-start | bytes 1572872 | tf_op jit(solution)/shard_map/ppermute | solution.py:18
  21.9 1.1 %copy.36 = bf16[16,8,16,128]{3,2,1,0:T(8,128)(2,1)S(1)} copy(bf16[16,8,16,128]{3,1,2,0:T(8,128)(2,1)} %bitcast.87) | data formatting | bytes 1048576
  23.1 0.0 copy-done.3
  23.1 5.0 %shard_map.113.mixed_ref = f32[128,2048]{1,0:T(8,128)} custom-call(f32[16,128]{1,0:T(8,128)} %copy-done.3, f32[128,16]{1,0:T(8,128)} %bitcast.83, f32[1,128]{1,0:T(1,128)} %get-tuple-element.30.code_row_ref, f32[128,1]{1,0:T(8,128)} %copy.24.code_col_ref.code_ref, bf16[128,2048]{1,0:T(8,128)(2,1)} %query_ref.3, bf16[128,2048]{1,0:T(8,128)(2,1)} %key_ref.3, ...), custom_call_target="tpu_custom_call" | custom-call | flops 134217728 | bytes 2621440 | tf_op jit(solution)/shard_map/pallas_call | solution.py:69
  28.1 0.0 collective-permute-done
  28.2 0.0 collective-permute-done.1
  28.3 1.9 %collective-permute-start.2 = (bf16[1040,128]{1,0:T(8,128)(2,1)S(1)}, bf16[1040,128]{1,0:T(8,128)(2,1)S(1)}, u32[]{:S(2)}, u32[]{:S(2)}) collective-permute-start(bf16[1040,128]{1,0:T(8,128)(2,1)S(1)} %pad_maximum_fusion), channel_id=1, source_target_pairs={{0,4},{2,6},{4,8},{6,10},{8,12},{10,14},{1,5},{3,7},{5,9},{7,11},{... | collective-permute-start | bytes 798728 | tf_op jit(solution)/shard_map/ppermute | solution.py:18
  30.2 0.6 fusion.43
  30.8 0.6 fusion.42
  34.0 0.1 broadcast_select_fusion
  34.1 0.0 copy-done.5
  34.1 0.6 broadcast_compare_fusion
  34.7 0.1 copy.29
  34.8 0.1 copy.30
  36.2 0.0 copy-done
  36.3 0.7 exponential_select_fusion.scale_t_ref
  37.0 11.1 %collective-permute-done.2 = bf16[1040,128]{1,0:T(8,128)(2,1)S(1)} collective-permute-done((bf16[1040,128]{1,0:T(8,128)(2,1)S(1)}, bf16[1040,128]{1,0:T(8,128)(2,1)S(1)}, u32[]{:S(2)}, u32[]{:S(2)}) %collective-permute-start.2) | collective-permute-done | bytes 266272 | tf_op jit(solution)/shard_map/ppermute | solution.py:18
  48.2 0.1 copy.27
  48.4 0.1 copy.28
  48.5 0.6 slice.112
  49.1 0.2 fusion.15
  49.3 0.9 %fusion.2 = (f32[2,8,128]{2,1,0:T(8,128)S(1)}, f32[2,640,128,8]{2,1,3,0:T(8,128)S(1)}) fusion(pred[128,640]{0,1:T(8,128)(4,1)S(1)} %fusion.15, bf16[128,2,8,128]{3,2,1,0:T(8,128)(2,1)S(1)} %bitcast.81, bf16[2,640,128]{2,1,0:T(8,128)(2,1)S(1)} %bitcast_dynamic-update-slice_fusion), kind=kOutput, calls=%fused_computation.4 | convolution fusion | flops 339474432 | bytes 6184960 | tf_op jit(solution)/shard_map/tkgd,ksd->kgts/dot_general | solution.py:113
  50.3 1.1 %fusion = f32[2,8,128]{2,1,0:T(8,128)S(1)} fusion(f32[2,640,128,8]{2,1,3,0:T(8,128)S(1)} %get-tuple-element.40, f32[2,8,128]{2,1,0:T(8,128)S(1)} %get-tuple-element.39, pred[128,640]{0,1:T(8,128)(4,1)S(1)} %fusion.15), kind=kLoop, calls=%fused_computation.2 | loop fusion | flops 5240832 | bytes 5341184 | tf_op jit(solution)/shard_map/reduce_sum | solution.py:117
  51.4 0.0 collective-permute-done.3
  51.4 0.0 collective-permute-done.4
  51.4 1.3 %fusion.38 = (bf16[16,128,128]{2,1,0:T(8,128)(2,1)S(1)}, f32[16,128,128]{2,1,0:T(8,128)}) fusion(bf16[16,128,128]{2,1,0:T(8,128)(2,1)S(1)} %collective-permute-done.4, f32[16]{0:T(128)S(1)} %get-tuple-element.12, bf16[16,128,128]{2,1,0:T(8,128)(2,1)S(1)} %collective-permute-done.3), kind=kLoop, calls=%fused_computation.76 | loop fusion | flops 1310720 | bytes 2621504 | tf_op jit(solution)/shard_map/convert_element_type | solution.py:194
  52.7 3.2 %collective-permute-start.5 = (bf16[16,128,128]{2,1,0:T(8,128)(2,1)S(1)}, bf16[16,128,128]{2,1,0:T(8,128)(2,1)S(1)}, u32[]{:S(2)}, u32[]{:S(2)}) collective-permute-start(bf16[16,128,128]{2,1,0:T(8,128)(2,1)S(1)} %get-tuple-element.10), channel_id=1, source_target_pairs={{0,4},{2,6},{4,8},{6,10},{8,12},{10,14},{1,5},{3,7},{5,9},{7,11},{... | collective-permute-start | bytes 1572872 | tf_op jit(solution)/shard_map/ppermute | solution.py:18
  55.9 0.0 copy-start.1
  55.9 0.0 copy-start.4
  55.9 1.4 %divide_convert_fusion = bf16[128,2,8,128]{0,3,2,1:T(8,128)(2,1)S(1)} fusion(f32[2,640,128,8]{2,1,3,0:T(8,128)S(1)} %get-tuple-element.40, f32[2,8,128]{2,1,0:T(8,128)S(1)} %get-tuple-element.39, pred[128,640]{0,1:T(8,128)(4,1)S(1)} %fusion.15, f32[128,2,8]{0,2,1:T(8,128)S(1)} %bitcast.99, bf16[2,640,128]{1,2,0:T(8,128)(2,1)S(1)} %constant_dynamic-update-slice_fusion), kind=kOutput, calls=%fused_computation.8 | convolution fusion | flops 341311488 | bytes 6193152 | tf_op jit(solution)/shard_map/kgts,ksd->kgtd/dot_general | solution.py:118
  57.4 1.0 %copy.32 = bf16[128,2048]{1,0:T(8,128)(2,1)} copy(bf16[128,2048]{0,1:T(8,128)(2,1)S(1)} %bitcast.88) | data formatting | bytes 1048576
  59.7 0.6 broadcast_select_fusion.1.carry_ref
  60.3 5.7 %collective-permute-done.5.far_ref = bf16[16,128,128]{2,1,0:T(8,128)(2,1)S(1)} collective-permute-done((bf16[16,128,128]{2,1,0:T(8,128)(2,1)S(1)}, bf16[16,128,128]{2,1,0:T(8,128)(2,1)S(1)}, u32[]{:S(2)}, u32[]{:S(2)}) %collective-permute-start.5) | collective-permute-done | bytes 524320 | tf_op jit(solution)/shard_map/ppermute | solution.py:18
  66.0 0.0 copy-start.2
  66.0 0.8 copy-done.2
  66.8 4.2 %shard_map.115 = (f32[128,2048]{1,0:T(8,128)}, f32[128,1]{1,0:T(8,128)}) custom-call(f32[16]{0:T(128)} %broadcast_select_fusion.1.carry_ref, f32[128,16]{1,0:T(8,128)} %exponential_select_fusion.scale_t_ref, bf16[128,2048]{1,0:T(8,128)(2,1)} %query_ref.3, f32[128,2048]{1,0:T(8,128)} %shard_map.113.mixed_ref, f32[16,128,128]{2,1,0:T(8,128)} %get-tuple-element.11.pair_ref, ...), custom_call_target="tpu_custom_call" | custom-call | flops 402653184 | bytes 3145728 | tf_op jit(solution)/shard_map/pallas_call | solution.py:96
  71.0 0.9 %reduce.1 = f32[128]{0:T(128)S(1)} reduce(f32[128,1]{1,0:T(8,128)} %get-tuple-element.5, f32[]{:T(128)} %constant.29), dimensions={1}, to_apply=%get-tuple-element.5.reduce_sub_computation | reduce | bytes 1028 | tf_op jit(solution)/shard_map/pallas_call | solution.py:96
  71.9 5.1 %psum.7 = f32[128]{0:T(128)S(1)} all-reduce(f32[128]{0:T(128)S(1)} %reduce.1), channel_id=1, replica_groups=mesh['groups'=2,'ctx'=8,'tensor'=2] {'tensor'}, use_global_device_ids=true, to_apply=%region_1.2 | all-reduce | flops 128 | bytes 1024 | tf_op jit(solution)/shard_map/psum | solution.py:209
  77.0 0.0 copy-done.1
  77.0 0.0 copy-done.4
  77.0 2.3 %multiply_convert_fusion = bf16[128,2048]{1,0:T(8,128)(2,1)} fusion(bf16[128,2048]{1,0:T(8,128)(2,1)S(1)} %copy-done.1, f32[128,2048]{1,0:T(8,128)} %get-tuple-element.4, f32[2048]{0:T(1024)S(1)} %copy-done.4, f32[128]{0:T(128)S(1)} %add_rsqrt_fusion), kind=kLoop, calls=%fused_computation.9 | loop fusion | flops 2097152 | bytes 2105856 | tf_op jit(solution)/shard_map/convert_element_type | solution.py:214
  (29 shorter events, 0.3 us)
Async XLA Ops:
  0.6 33.4 %copy-start.5 = (s32[128]{0:T(128)S(1)}, s32[128]{0:T(128)}, u32[]{:S(2)}) copy-start(s32[128]{0:T(128)} %param.19) | copy-start | bytes 1540
  1.6 21.5 %copy-start.3 = (f32[16,128]{1,0:T(8,128)}, f32[16,128]{1,0:T(8,128)S(1)}, u32[]{:S(2)}) copy-start(f32[16,128]{1,0:T(8,128)S(1)} %reduce_window_sum.13.decay_ref) | copy-start | bytes 24580
  5.4 22.8 %collective-permute-start = (bf16[528,128]{1,0:T(8,128)(2,1)S(1)}, bf16[528,128]{1,0:T(8,128)(2,1)S(1)}, u32[]{:S(2)}, u32[]{:S(2)}) collective-permute-start(bf16[528,128]{1,0:T(8,128)(2,1)S(1)} %pad_maximum_fusion.1), channel_id=1, source_target_pairs={{0,4},{2,6},{4,8},{6,10},{8,12},{10,14},{1,5},{3,7},{5,9},{7,11},{... | collective-permute-start | bytes 405512 | tf_op jit(solution)/shard_map/ppermute | solution.py:18
  8.6 19.6 %collective-permute-start.1 = (bf16[528,128]{1,0:T(8,128)(2,1)S(1)}, bf16[528,128]{1,0:T(8,128)(2,1)S(1)}, u32[]{:S(2)}, u32[]{:S(2)}) collective-permute-start(bf16[528,128]{1,0:T(8,128)(2,1)S(1)} %pad_maximum_fusion.1), channel_id=1, source_target_pairs={{0,2},{2,4},{4,6},{6,8},{8,10},{10,12},{12,14},{1,3},{3,5},{5,7},{... | collective-permute-start | bytes 405512 | tf_op jit(solution)/shard_map/ppermute | solution.py:18
  12.5 23.8 %copy-start = (f32[16,128]{0,1:T(8,128)S(1)}, f32[16,128]{0,1:T(8,128)}, u32[]{:S(2)}) copy-start(f32[16,128]{0,1:T(8,128)} %copy.23) | copy-start | bytes 24580
  16.9 34.5 %collective-permute-start.3 = (bf16[16,128,128]{2,1,0:T(8,128)(2,1)}, bf16[16,128,128]{2,1,0:T(8,128)(2,1)S(1)}, u32[]{:S(2)}, u32[]{:S(2)}) collective-permute-start(bf16[16,128,128]{2,1,0:T(8,128)(2,1)} %shard_map.114), channel_id=1, source_target_pairs={{0,2},{2,4},{4,6},{6,8},{8,10},{10,12},{12,14},{1,3},{3,5},{5,7},{... | collective-permute-start | bytes 1572872 | tf_op jit(solution)/shard_map/ppermute | solution.py:18
  20.0 31.3 %collective-permute-start.4 = (bf16[16,128,128]{2,1,0:T(8,128)(2,1)}, bf16[16,128,128]{2,1,0:T(8,128)(2,1)S(1)}, u32[]{:S(2)}, u32[]{:S(2)}) collective-permute-start(bf16[16,128,128]{2,1,0:T(8,128)(2,1)} %shard_map.114), channel_id=1, source_target_pairs={{0,4},{2,6},{4,8},{6,10},{8,12},{10,14},{1,5},{3,7},{5,9},{7,11},{... | collective-permute-start | bytes 1572872 | tf_op jit(solution)/shard_map/ppermute | solution.py:18
  28.3 19.8 %collective-permute-start.2 = (bf16[1040,128]{1,0:T(8,128)(2,1)S(1)}, bf16[1040,128]{1,0:T(8,128)(2,1)S(1)}, u32[]{:S(2)}, u32[]{:S(2)}) collective-permute-start(bf16[1040,128]{1,0:T(8,128)(2,1)S(1)} %pad_maximum_fusion), channel_id=1, source_target_pairs={{0,4},{2,6},{4,8},{6,10},{8,12},{10,14},{1,5},{3,7},{5,9},{7,11},{... | collective-permute-start | bytes 798728 | tf_op jit(solution)/shard_map/ppermute | solution.py:18
  52.7 13.3 %collective-permute-start.5 = (bf16[16,128,128]{2,1,0:T(8,128)(2,1)S(1)}, bf16[16,128,128]{2,1,0:T(8,128)(2,1)S(1)}, u32[]{:S(2)}, u32[]{:S(2)}) collective-permute-start(bf16[16,128,128]{2,1,0:T(8,128)(2,1)S(1)} %get-tuple-element.10), channel_id=1, source_target_pairs={{0,4},{2,6},{4,8},{6,10},{8,12},{10,14},{1,5},{3,7},{5,9},{7,11},{... | collective-permute-start | bytes 1572872 | tf_op jit(solution)/shard_map/ppermute | solution.py:18
  55.9 21.1 %copy-start.1 = (bf16[128,2048]{1,0:T(8,128)(2,1)S(1)}, bf16[128,2048]{1,0:T(8,128)(2,1)}, u32[]{:S(2)}) copy-start(bf16[128,2048]{1,0:T(8,128)(2,1)} %param.13) | copy-start | bytes 1572868
  55.9 21.1 %copy-start.4 = (f32[2048]{0:T(1024)S(1)}, f32[2048]{0:T(1024)}, u32[]{:S(2)}) copy-start(f32[2048]{0:T(1024)} %param.15) | copy-start | bytes 24580
  66.0 0.8 copy-start.2

commit v11 on v10

--- a/solution.py
+++ b/solution.py
@@ -173,8 +173,12 @@
             rows_of(jnp.concatenate([code, split_parts(block_decay)]), head_size),
         ]
     )
-    state_1, kv_1 = shifted((own_state, own_kv), "ctx", 1)
-    state_2, kv_2 = shifted((own_state, own_kv), "ctx", 2)
+    state_1 = shifted(own_state, "ctx", 1)
+    state_2 = shifted(own_state, "ctx", 2)
+    kv_1 = shifted(own_kv, "ctx", 1)
+    kv_2 = shifted(own_kv, "ctx", 2)
+    kv_3 = shifted(own_kv, "ctx", 3)
+    kv_4 = shifted(own_kv, "ctx", 4)
 
     def unpack(block):
         keys = block[:kv_rows].reshape(kv_here, tok_rows, head_size)
@@ -190,15 +194,9 @@
     link_1 = (code_2[-1] == code_1[0]) & (code_1[0] == code_1[-1])
     pair_state = state_1.astype(F32) + jnp.where(link_1, decay_1, 0.0)[:, None, None] * state_2.astype(F32)
 
-    relay_kv = jnp.concatenate([kv_2[: 2 * kv_rows], kv_1[: 2 * kv_rows], rows_of(jnp.concatenate([code_2, code_1]), head_size)])
     state_far = shifted(pair_state.astype(BF16), "ctx", 2)
-    kv_far = shifted(relay_kv, "ctx", 2)
-    keys_4 = kv_far[:kv_rows].reshape(kv_here, tok_rows, head_size)
-    values_4 = kv_far[kv_rows : 2 * kv_rows].reshape(kv_here, tok_rows, head_size)
-    keys_3 = kv_far[2 * kv_rows : 3 * kv_rows].reshape(kv_here, tok_rows, head_size)
-    values_3 = kv_far[3 * kv_rows : 4 * kv_rows].reshape(kv_here, tok_rows, head_size)
-    code_far = kv_far[4 * kv_rows :].reshape(-1)[: 2 * tok_rows].astype(F32)
-    code_4, code_3 = code_far[:tok_rows], code_far[tok_rows:]
+    keys_3, values_3, code_3, _ = unpack(kv_3)
+    keys_4, values_4, code_4, _ = unpack(kv_4)
 
     link_2 = (code_3[-1] == code_2[0]) & (code_2[0] == code_1[-1])
     carry_scale = jnp.where(link_2, decay_2 * decay_1, 0.0)

time: 80 us -> 89.1 us (1.11)
  starting transfers between devices: 16.5 us -> 21.4 us
  matrix products: 2.35 us -> 4.86 us
  local copies, waits for them, and re-layouts: 9.31 us -> 11.6 us
  blocking collectives: 5.08 us -> 3.76 us
    ppermute x6 -> x7, starting transfers between devices: 16.5 us -> 21.4 us  [shifted(): return lax.ppermute(block, axis, route)]
    dot_general x1, matrix products: 1.44 us -> 3.95 us  [soft_window(): jnp.einsum('kgts,ksd->kgtd', prob_block.astype(BF16), value_heads, prefer...]
    unnamed x24 -> x26, local copies, waits for them, and re-layouts: 5 us -> 7.29 us
    psum x1, blocking collectives: 5.08 us -> 3.76 us  [on_device_body(): squares = lax.psum(squares[:, 0], 'tensor')]
    add x1 -> x0, other arithmetic: 1.25 us -> none  [on_device_body(): code = segment_ids.astype(F32) + 1.0]
    concatenate x1, other arithmetic: 0.01 us -> 1.19 us  [on_device_body(): code_window = jnp.concatenate([code_4, code_3, code_2, code_1, code])]
    ppermute x6 -> x7, waiting for transfers between devices: 16.8 us -> 16.7 us  [shifted(): return lax.ppermute(block, axis, route)]
  transfers between devices with their start and end apart: 6 -> 7, of which waited for: 2 -> 5; matrix products, arithmetic and copies ran while one was open for 15% -> 15% of each run, Pallas kernels for 11% -> 6%
where the time goes in v11:
time: 89.1 us; the launch traced here: 88 us
  starting transfers between devices  21.4 us (24%)
  waiting for transfers between devices  16.7 us (19%)
  Pallas kernels  13 us (15%)
  local copies, waits for them, and re-layouts  11.6 us (13%)
  other arithmetic  10.7 us (12%)
  between operations  6 us (7%)
  matrix products  4.86 us (5%)
  blocking collectives  3.76 us (4%)
    ppermute x7, starting transfers between devices, shifted(): return lax.ppermute(block, axis, route)  21.4 us
    ppermute x7, waiting for transfers between devices, shifted(): return lax.ppermute(block, axis, route)  16.7 us
    unnamed x26, local copies, waits for them, and re-layouts  7.29 us
    pallas_call x1, Pallas kernels, intra_mixed(): pl.pallas_call(intra_kernel, out_shape=jax.ShapeDtypeStruct((tok_rows, wi...  5.09 us
    pallas_call x1, Pallas kernels, final_mixed(): pl.pallas_call(final_kernel, out_shape=(jax.ShapeDtypeStruct((tok_rows, w...  4.22 us
    dot_general x1, matrix products, soft_window(): jnp.einsum('kgts,ksd->kgtd', prob_block.astype(BF16), value_heads, prefer...  3.95 us
    psum x1, blocking collectives, on_device_body(): squares = lax.psum(squares[:, 0], 'tensor')  3.76 us
    pallas_call x1, Pallas kernels, local_state_of(): pl.pallas_call(state_kernel, out_shape=jax.ShapeDtypeStruct((heads_here,...  3.7 us
  transfers between devices with their start and end apart: 7, of which 5 were waited for; matrix products, arithmetic and copies ran while one was open for 15% of the time, Pallas kernels for 6%

profile of v11, /device:TPU:11, one launch (start us, length us, event | category | flops | bytes accessed | tf_op | source)
XLA Modules:
  0.0 88.0 jit_solution(16349405971669613032)
XLA Ops:
  0.6 1.0 %reduce_window_sum.13.decay_ref = f32[16,128]{1,0:T(8,128)S(1)} reduce-window(f32[16,128]{1,0:T(8,128)} %param.14, f32[]{:T(128)} %constant.10.clone.1), window={size=1x128 pad=0_0x127_0}, to_apply=%region_0.0 | reduce-window | flops 260096 | bytes 16388 | tf_op jit(solution)/shard_map/jit(cumsum)/reduce_window_sum | solution.py:160
  1.6 0.0 copy-start.4
  1.6 0.2 fusion.20
  1.8 0.7 fusion.31
  2.5 0.9 %copy.19 = bf16[128,256]{0,1:T(8,128)(2,1)S(1)} copy(bf16[128,256]{1,0:T(8,128)(2,1)} %param.17) | data formatting | bytes 131072 | tf_op args[7]
  3.4 0.1 copy.20
  3.6 1.0 %copy.21 = bf16[128,256]{0,1:T(8,128)(2,1)S(1)} copy(bf16[128,256]{1,0:T(8,128)(2,1)} %param.18) | data formatting | bytes 131072 | tf_op args[8]
  4.5 0.1 copy.22
  4.7 0.1 fusion.24
  4.8 4.2 %collective-permute-start.6 = (bf16[528,128]{1,0:T(8,128)(2,1)S(1)}, bf16[528,128]{1,0:T(8,128)(2,1)S(1)}, u32[]{:S(2)}, u32[]{:S(2)}) collective-permute-start(bf16[528,128]{1,0:T(8,128)(2,1)S(1)} %pad_maximum_fusion), channel_id=1, source_target_pairs={{0,8},{2,10},{4,12},{6,14},{1,9},{3,11},{5,13},{7,15},{16,24},{18,... | collective-permute-start | bytes 405512 | tf_op jit(solution)/shard_map/ppermute | solution.py:18
  9.0 1.9 %collective-permute-start = (bf16[528,128]{1,0:T(8,128)(2,1)S(1)}, bf16[528,128]{1,0:T(8,128)(2,1)S(1)}, u32[]{:S(2)}, u32[]{:S(2)}) collective-permute-start(bf16[528,128]{1,0:T(8,128)(2,1)S(1)} %pad_maximum_fusion), channel_id=1, source_target_pairs={{0,6},{2,8},{4,10},{6,12},{8,14},{1,7},{3,9},{5,11},{7,13},{9,15},... | collective-permute-start | bytes 405512 | tf_op jit(solution)/shard_map/ppermute | solution.py:18
  10.9 1.9 %collective-permute-start.1 = (bf16[528,128]{1,0:T(8,128)(2,1)S(1)}, bf16[528,128]{1,0:T(8,128)(2,1)S(1)}, u32[]{:S(2)}, u32[]{:S(2)}) collective-permute-start(bf16[528,128]{1,0:T(8,128)(2,1)S(1)} %pad_maximum_fusion), channel_id=1, source_target_pairs={{0,4},{2,6},{4,8},{6,10},{8,12},{10,14},{1,5},{3,7},{5,9},{7,11},{... | collective-permute-start | bytes 405512 | tf_op jit(solution)/shard_map/ppermute | solution.py:18
  12.8 2.5 %collective-permute-start.2 = (bf16[528,128]{1,0:T(8,128)(2,1)S(1)}, bf16[528,128]{1,0:T(8,128)(2,1)S(1)}, u32[]{:S(2)}, u32[]{:S(2)}) collective-permute-start(bf16[528,128]{1,0:T(8,128)(2,1)S(1)} %pad_maximum_fusion), channel_id=1, source_target_pairs={{0,2},{2,4},{4,6},{6,8},{8,10},{10,12},{12,14},{1,3},{3,5},{5,7},{... | collective-permute-start | bytes 405512 | tf_op jit(solution)/shard_map/ppermute | solution.py:18
  15.3 0.7 copy.23
  16.0 1.1 %copy.36 = bf16[16,8,16,128]{3,2,1,0:T(8,128)(2,1)S(1)} copy(bf16[16,8,16,128]{3,1,2,0:T(8,128)(2,1)} %bitcast.87) | data formatting | bytes 1048576
  17.2 0.8 collective-permute-done.6
  18.0 2.9 %collective-permute-done = bf16[528,128]{1,0:T(8,128)(2,1)S(1)} collective-permute-done((bf16[528,128]{1,0:T(8,128)(2,1)S(1)}, bf16[528,128]{1,0:T(8,128)(2,1)S(1)}, u32[]{:S(2)}, u32[]{:S(2)}) %collective-permute-start) | collective-permute-done | bytes 135200 | tf_op jit(solution)/shard_map/ppermute | solution.py:18
  20.9 2.9 %collective-permute-done.1 = bf16[528,128]{1,0:T(8,128)(2,1)S(1)} collective-permute-done((bf16[528,128]{1,0:T(8,128)(2,1)S(1)}, bf16[528,128]{1,0:T(8,128)(2,1)S(1)}, u32[]{:S(2)}, u32[]{:S(2)}) %collective-permute-start.1) | collective-permute-done | bytes 135200 | tf_op jit(solution)/shard_map/ppermute | solution.py:18
  23.8 2.9 %collective-permute-done.2 = bf16[528,128]{1,0:T(8,128)(2,1)S(1)} collective-permute-done((bf16[528,128]{1,0:T(8,128)(2,1)S(1)}, bf16[528,128]{1,0:T(8,128)(2,1)S(1)}, u32[]{:S(2)}, u32[]{:S(2)}) %collective-permute-start.2) | collective-permute-done | bytes 135200 | tf_op jit(solution)/shard_map/ppermute | solution.py:18
  26.7 1.2 %constant_dynamic-update-slice_fusion.10 = (f32[640]{0:T(1024)S(1)}, f32[1,128]{1,0:T(1,128)}, f32[128,1]{0,1:T(1,128)S(1)}, f32[128]{0:T(128)S(1)}) fusion(f32[640]{0:T(1024)S(1)} %constant_dynamic-update-slice_fusion.11, s32[128]{0:T(128)} %param.19), kind=kLoop, calls=%fused_computation.37 | loop fusion | flops 256 | bytes 2560 | tf_op jit(solution)/shard_map/concatenate | solution.py:216
  27.9 0.7 copy.24.code_col_ref.code_ref
  28.6 3.7 %shard_map.114 = bf16[16,128,128]{2,1,0:T(8,128)(2,1)} custom-call(f32[128,16]{1,0:T(8,128)} %bitcast.82, f32[128,1]{1,0:T(8,128)} %copy.24.code_col_ref.code_ref, bf16[128,2048]{1,0:T(8,128)(2,1)} %key_ref.3, bf16[128,2048]{1,0:T(8,128)(2,1)} %value_ref.3), custom_call_target="tpu_custom_call" | custom-call | flops 67108864 | bytes 786432 | tf_op jit(solution)/shard_map/pallas_call | solution.py:39
  32.3 5.0 %collective-permute-start.3 = (bf16[16,128,128]{2,1,0:T(8,128)(2,1)}, bf16[16,128,128]{2,1,0:T(8,128)(2,1)S(1)}, u32[]{:S(2)}, u32[]{:S(2)}) collective-permute-start(bf16[16,128,128]{2,1,0:T(8,128)(2,1)} %shard_map.114), channel_id=1, source_target_pairs={{0,2},{2,4},{4,6},{6,8},{8,10},{10,12},{12,14},{1,3},{3,5},{5,7},{... | collective-permute-start | bytes 1572872 | tf_op jit(solution)/shard_map/ppermute | solution.py:18
  37.3 1.9 %collective-permute-start.4 = (bf16[16,128,128]{2,1,0:T(8,128)(2,1)}, bf16[16,128,128]{2,1,0:T(8,128)(2,1)S(1)}, u32[]{:S(2)}, u32[]{:S(2)}) collective-permute-start(bf16[16,128,128]{2,1,0:T(8,128)(2,1)} %shard_map.114), channel_id=1, source_target_pairs={{0,4},{2,6},{4,8},{6,10},{8,12},{10,14},{1,5},{3,7},{5,9},{7,11},{... | collective-permute-start | bytes 1572872 | tf_op jit(solution)/shard_map/ppermute | solution.py:18
  39.4 0.1 copy.28
  39.5 0.1 copy.27
  39.7 0.1 copy.29
  39.8 0.1 copy.30
  40.1 0.6 fusion.37
  40.6 0.6 fusion.38
  43.9 0.2 fusion.15
  44.0 0.9 %fusion.2 = (f32[2,8,128]{2,1,0:T(8,128)S(1)}, f32[2,640,128,8]{2,1,3,0:T(8,128)S(1)}) fusion(pred[128,640]{0,1:T(8,128)(4,1)S(1)} %fusion.15, bf16[128,2,8,128]{3,2,1,0:T(8,128)(2,1)S(1)} %bitcast.81, bf16[2,640,128]{2,1,0:T(8,128)(2,1)S(1)} %bitcast_dynamic-update-slice_fusion), kind=kOutput, calls=%fused_computation.4 | convolution fusion | flops 339474432 | bytes 6184960 | tf_op jit(solution)/shard_map/tkgd,ksd->kgts/dot_general | solution.py:113
  44.9 0.0 copy-done.4
  45.0 0.0 copy-start
  45.0 2.3 %copy-done = f32[2,640,128,8]{2,1,3,0:T(8,128)} copy-done((f32[2,640,128,8]{2,1,3,0:T(8,128)}, f32[2,640,128,8]{2,1,3,0:T(8,128)S(1)}, u32[]{:S(2)}) %copy-start) | copy-done | bytes 5242904
  47.3 1.1 %fusion = f32[2,8,128]{2,1,0:T(8,128)S(1)} fusion(f32[2,640,128,8]{2,1,3,0:T(8,128)S(1)} %get-tuple-element.34, f32[2,8,128]{2,1,0:T(8,128)S(1)} %get-tuple-element.33, pred[128,640]{0,1:T(8,128)(4,1)S(1)} %fusion.15), kind=kLoop, calls=%fused_computation.2 | loop fusion | flops 5240832 | bytes 5341184 | tf_op jit(solution)/shard_map/reduce_sum | solution.py:117
  48.3 0.1 broadcast_select_fusion
  48.4 0.0 copy-start.6
  48.4 3.9 %divide_convert_fusion = bf16[128,2,8,128]{0,3,2,1:T(8,128)(2,1)S(1)} fusion(f32[2,640,128,8]{2,1,3,0:T(8,128)} %copy-done, f32[2,8,128]{2,1,0:T(8,128)S(1)} %get-tuple-element.33, pred[128,640]{0,1:T(8,128)(4,1)S(1)} %fusion.15, f32[128,2,8]{0,2,1:T(8,128)S(1)} %bitcast.99, bf16[2,640,128]{1,2,0:T(8,128)(2,1)S(1)} %constant_dynamic-update-slice_fusion), kind=kOutput, calls=%fused_computation.8 | convolution fusion | flops 341311488 | bytes 6193152 | tf_op jit(solution)/shard_map/kgts,ksd->kgtd/dot_general | solution.py:118
  52.4 0.0 copy-start.1
  52.4 0.0 copy-start.2
  52.4 0.0 copy-start.5
  52.4 0.0 collective-permute-done.3
  52.4 7.2 %collective-permute-done.4 = bf16[16,128,128]{2,1,0:T(8,128)(2,1)S(1)} collective-permute-done((bf16[16,128,128]{2,1,0:T(8,128)(2,1)}, bf16[16,128,128]{2,1,0:T(8,128)(2,1)S(1)}, u32[]{:S(2)}, u32[]{:S(2)}) %collective-permute-start.4) | collective-permute-done | bytes 524320 | tf_op jit(solution)/shard_map/ppermute | solution.py:18
  59.6 1.2 %fusion.32 = (bf16[16,128,128]{2,1,0:T(8,128)(2,1)S(1)}, f32[16,128,128]{2,1,0:T(8,128)}) fusion(bf16[16,128,128]{2,1,0:T(8,128)(2,1)S(1)} %collective-permute-done.4, f32[16]{0:T(128)S(1)} %get-tuple-element.12, bf16[16,128,128]{2,1,0:T(8,128)(2,1)S(1)} %collective-permute-done.3), kind=kLoop, calls=%fused_computation.71 | loop fusion | flops 1310720 | bytes 2621504 | tf_op jit(solution)/shard_map/convert_element_type | solution.py:197
  60.9 4.0 %collective-permute-start.5 = (bf16[16,128,128]{2,1,0:T(8,128)(2,1)S(1)}, bf16[16,128,128]{2,1,0:T(8,128)(2,1)S(1)}, u32[]{:S(2)}, u32[]{:S(2)}) collective-permute-start(bf16[16,128,128]{2,1,0:T(8,128)(2,1)S(1)} %get-tuple-element.10), channel_id=1, source_target_pairs={{0,4},{2,6},{4,8},{6,10},{8,12},{10,14},{1,5},{3,7},{5,9},{7,11},{... | collective-permute-start | bytes 1572872 | tf_op jit(solution)/shard_map/ppermute | solution.py:18
  64.9 0.0 copy-done.6
  64.9 0.6 broadcast_compare_fusion
  65.4 1.0 %copy.32 = bf16[128,2048]{1,0:T(8,128)(2,1)} copy(bf16[128,2048]{0,1:T(8,128)(2,1)S(1)} %bitcast.88) | data formatting | bytes 1048576
  67.6 0.6 slice.105
  69.5 5.1 %shard_map.113.mixed_ref = f32[128,2048]{1,0:T(8,128)} custom-call(f32[16,128]{1,0:T(8,128)} %copy-done.4, f32[128,16]{1,0:T(8,128)} %bitcast.83, f32[1,128]{1,0:T(1,128)} %get-tuple-element.23.code_row_ref, f32[128,1]{1,0:T(8,128)} %copy.24.code_col_ref.code_ref, bf16[128,2048]{1,0:T(8,128)(2,1)} %query_ref.3, bf16[128,2048]{1,0:T(8,128)(2,1)} %key_ref.3, ...), custom_call_target="tpu_custom_call" | custom-call | flops 134217728 | bytes 2621440 | tf_op jit(solution)/shard_map/pallas_call | solution.py:69
  74.6 0.7 broadcast_select_fusion.1.carry_ref
  75.2 0.0 copy-done.1
  75.2 0.7 exponential_select_fusion.scale_t_ref
  76.0 0.0 collective-permute-done.5.far_ref
  76.0 0.0 copy-start.3
  76.0 0.8 copy-done.3
  76.8 4.2 %shard_map.115 = (f32[128,2048]{1,0:T(8,128)}, f32[128,1]{1,0:T(8,128)}) custom-call(f32[16]{0:T(128)} %broadcast_select_fusion.1.carry_ref, f32[128,16]{1,0:T(8,128)} %exponential_select_fusion.scale_t_ref, bf16[128,2048]{1,0:T(8,128)(2,1)} %query_ref.3, f32[128,2048]{1,0:T(8,128)} %shard_map.113.mixed_ref, f32[16,128,128]{2,1,0:T(8,128)} %get-tuple-element.11.pair_ref, ...), custom_call_target="tpu_custom_call" | custom-call | flops 402653184 | bytes 3145728 | tf_op jit(solution)/shard_map/pallas_call | solution.py:96
  81.0 0.9 %reduce.1 = f32[128]{0:T(128)S(1)} reduce(f32[128,1]{1,0:T(8,128)} %get-tuple-element.5, f32[]{:T(128)} %constant.27), dimensions={1}, to_apply=%get-tuple-element.5.reduce_sub_computation | reduce | bytes 1028 | tf_op jit(solution)/shard_map/pallas_call | solution.py:96
  81.9 3.8 %psum.7 = f32[128]{0:T(128)S(1)} all-reduce(f32[128]{0:T(128)S(1)} %reduce.1), channel_id=1, replica_groups=mesh['groups'=2,'ctx'=8,'tensor'=2] {'tensor'}, use_global_device_ids=true, to_apply=%region_1.2 | all-reduce | flops 128 | bytes 1024 | tf_op jit(solution)/shard_map/psum | solution.py:207
  85.7 0.0 copy-done.2
  85.7 0.0 copy-done.5
  85.7 2.3 %multiply_convert_fusion = bf16[128,2048]{1,0:T(8,128)(2,1)} fusion(bf16[128,2048]{1,0:T(8,128)(2,1)S(1)} %copy-done.2, f32[128,2048]{1,0:T(8,128)} %get-tuple-element.4, f32[2048]{0:T(1024)S(1)} %copy-done.5, f32[128]{0:T(128)S(1)} %add_rsqrt_fusion), kind=kLoop, calls=%fused_computation.9 | loop fusion | flops 2097152 | bytes 2105856 | tf_op jit(solution)/shard_map/convert_element_type | solution.py:212
  (30 shorter events, 0.3 us)
Async XLA Ops:
  1.6 43.3 %copy-start.4 = (f32[16,128]{1,0:T(8,128)}, f32[16,128]{1,0:T(8,128)S(1)}, u32[]{:S(2)}) copy-start(f32[16,128]{1,0:T(8,128)S(1)} %reduce_window_sum.13.decay_ref) | copy-start | bytes 24580
  4.8 13.2 %collective-permute-start.6 = (bf16[528,128]{1,0:T(8,128)(2,1)S(1)}, bf16[528,128]{1,0:T(8,128)(2,1)S(1)}, u32[]{:S(2)}, u32[]{:S(2)}) collective-permute-start(bf16[528,128]{1,0:T(8,128)(2,1)S(1)} %pad_maximum_fusion), channel_id=1, source_target_pairs={{0,8},{2,10},{4,12},{6,14},{1,9},{3,11},{5,13},{7,15},{16,24},{18,... | collective-permute-start | bytes 405512 | tf_op jit(solution)/shard_map/ppermute | solution.py:18
  9.0 11.9 %collective-permute-start = (bf16[528,128]{1,0:T(8,128)(2,1)S(1)}, bf16[528,128]{1,0:T(8,128)(2,1)S(1)}, u32[]{:S(2)}, u32[]{:S(2)}) collective-permute-start(bf16[528,128]{1,0:T(8,128)(2,1)S(1)} %pad_maximum_fusion), channel_id=1, source_target_pairs={{0,6},{2,8},{4,10},{6,12},{8,14},{1,7},{3,9},{5,11},{7,13},{9,15},... | collective-permute-start | bytes 405512 | tf_op jit(solution)/shard_map/ppermute | solution.py:18
  10.9 12.9 %collective-permute-start.1 = (bf16[528,128]{1,0:T(8,128)(2,1)S(1)}, bf16[528,128]{1,0:T(8,128)(2,1)S(1)}, u32[]{:S(2)}, u32[]{:S(2)}) collective-permute-start(bf16[528,128]{1,0:T(8,128)(2,1)S(1)} %pad_maximum_fusion), channel_id=1, source_target_pairs={{0,4},{2,6},{4,8},{6,10},{8,12},{10,14},{1,5},{3,7},{5,9},{7,11},{... | collective-permute-start | bytes 405512 | tf_op jit(solution)/shard_map/ppermute | solution.py:18
  12.8 13.8 %collective-permute-start.2 = (bf16[528,128]{1,0:T(8,128)(2,1)S(1)}, bf16[528,128]{1,0:T(8,128)(2,1)S(1)}, u32[]{:S(2)}, u32[]{:S(2)}) collective-permute-start(bf16[528,128]{1,0:T(8,128)(2,1)S(1)} %pad_maximum_fusion), channel_id=1, source_target_pairs={{0,2},{2,4},{4,6},{6,8},{8,10},{10,12},{12,14},{1,3},{3,5},{5,7},{... | collective-permute-start | bytes 405512 | tf_op jit(solution)/shard_map/ppermute | solution.py:18
  32.3 20.1 %collective-permute-start.3 = (bf16[16,128,128]{2,1,0:T(8,128)(2,1)}, bf16[16,128,128]{2,1,0:T(8,128)(2,1)S(1)}, u32[]{:S(2)}, u32[]{:S(2)}) collective-permute-start(bf16[16,128,128]{2,1,0:T(8,128)(2,1)} %shard_map.114), channel_id=1, source_target_pairs={{0,2},{2,4},{4,6},{6,8},{8,10},{10,12},{12,14},{1,3},{3,5},{5,7},{... | collective-permute-start | bytes 1572872 | tf_op jit(solution)/shard_map/ppermute | solution.py:18
  37.3 22.3 %collective-permute-start.4 = (bf16[16,128,128]{2,1,0:T(8,128)(2,1)}, bf16[16,128,128]{2,1,0:T(8,128)(2,1)S(1)}, u32[]{:S(2)}, u32[]{:S(2)}) collective-permute-start(bf16[16,128,128]{2,1,0:T(8,128)(2,1)} %shard_map.114), channel_id=1, source_target_pairs={{0,4},{2,6},{4,8},{6,10},{8,12},{10,14},{1,5},{3,7},{5,9},{7,11},{... | collective-permute-start | bytes 1572872 | tf_op jit(solution)/shard_map/ppermute | solution.py:18
  45.0 2.3 %copy-start = (f32[2,640,128,8]{2,1,3,0:T(8,128)}, f32[2,640,128,8]{2,1,3,0:T(8,128)S(1)}, u32[]{:S(2)}) copy-start(f32[2,640,128,8]{2,1,3,0:T(8,128)S(1)} %get-tuple-element.34) | copy-start | bytes 15728644
  48.4 16.5 %copy-start.6 = (s32[128]{0:T(128)S(1)}, s32[128]{0:T(128)}, u32[]{:S(2)}) copy-start(s32[128]{0:T(128)} %param.19) | copy-start | bytes 1540
  52.4 22.9 %copy-start.1 = (f32[16,128]{0,1:T(8,128)S(1)}, f32[16,128]{0,1:T(8,128)}, u32[]{:S(2)}) copy-start(f32[16,128]{0,1:T(8,128)} %copy.23) | copy-start | bytes 24580
  52.4 33.3 %copy-start.2 = (bf16[128,2048]{1,0:T(8,128)(2,1)S(1)}, bf16[128,2048]{1,0:T(8,128)(2,1)}, u32[]{:S(2)}) copy-start(bf16[128,2048]{1,0:T(8,128)(2,1)} %param.13) | copy-start | bytes 1572868
  52.4 33.3 %copy-start.5 = (f32[2048]{0:T(1024)S(1)}, f32[2048]{0:T(1024)}, u32[]{:S(2)}) copy-start(f32[2048]{0:T(1024)} %param.15) | copy-start | bytes 24580
  60.9 15.1 %collective-permute-start.5 = (bf16[16,128,128]{2,1,0:T(8,128)(2,1)S(1)}, bf16[16,128,128]{2,1,0:T(8,128)(2,1)S(1)}, u32[]{:S(2)}, u32[]{:S(2)}) collective-permute-start(bf16[16,128,128]{2,1,0:T(8,128)(2,1)S(1)} %get-tuple-element.10), channel_id=1, source_target_pairs={{0,4},{2,6},{4,8},{6,10},{8,12},{10,14},{1,5},{3,7},{5,9},{7,11},{... | collective-permute-start | bytes 1572872 | tf_op jit(solution)/shard_map/ppermute | solution.py:18
  76.0 0.8 copy-start.3

commit v12 on v10

--- a/solution.py
+++ b/solution.py
@@ -189,9 +189,10 @@
 
     link_1 = (code_2[-1] == code_1[0]) & (code_1[0] == code_1[-1])
     pair_state = state_1.astype(F32) + jnp.where(link_1, decay_1, 0.0)[:, None, None] * state_2.astype(F32)
+    pair_wire = pair_state.astype(BF16)
 
     relay_kv = jnp.concatenate([kv_2[: 2 * kv_rows], kv_1[: 2 * kv_rows], rows_of(jnp.concatenate([code_2, code_1]), head_size)])
-    state_far = shifted(pair_state.astype(BF16), "ctx", 2)
+    state_far = shifted(pair_wire, "ctx", 2)
     kv_far = shifted(relay_kv, "ctx", 2)
     keys_4 = kv_far[:kv_rows].reshape(kv_here, tok_rows, head_size)
     values_4 = kv_far[kv_rows : 2 * kv_rows].reshape(kv_here, tok_rows, head_size)
@@ -206,7 +207,11 @@
     scale_in = jnp.where(uses_state[None, :], jnp.exp(decay_sum), 0.0)
     mixed, squares = final_mixed(carry_scale, scale_in, light_query, mixed, pair_state, state_far)
     mixed = mixed.reshape(tok_rows, heads_here, head_size)
-    squares = lax.psum(squares[:, 0], "tensor")
+    squares = squares[:, 0]
+    if lax.axis_size("tensor") == 2:
+        squares = squares + lax.ppermute(squares, "tensor", [(0, 1), (1, 0)])
+    else:
+        squares = lax.psum(squares, "tensor")
     features = heads_here * head_size * lax.axis_size("tensor")
     inverse = lax.rsqrt(squares / features + 1e-06)
     gate_open = jax.nn.sigmoid(light_gate.astype(F32)).reshape(tok_rows, heads_here, head_size)

time: 80 us -> 82.7 us (1.034)
  blocking collectives: 5.08 us -> 0 us
  waiting for transfers between devices: 16.8 us -> 20.1 us
  starting transfers between devices: 16.5 us -> 19.5 us
  matrix products: 2.35 us -> 4.96 us
  other arithmetic: 10.2 us -> 9.21 us
    psum x1 -> x0, blocking collectives: 5.08 us -> none  [on_device_body(): squares = lax.psum(squares[:, 0], 'tensor')]
    ppermute x6, waiting for transfers between devices: 16.8 us -> 20.1 us  [shifted(): return lax.ppermute(block, axis, route)]
    ppermute x0 -> x1, starting transfers between devices: none -> 3.02 us  [on_device_body(): squares = squares + lax.ppermute(squares, 'tensor', [(0, 1), (1, 0)])]
    dot_general x1, matrix products: 1.44 us -> 4.05 us  [soft_window(): jnp.einsum('kgts,ksd->kgtd', prob_block.astype(BF16), value_heads, prefer...]
    convert_element_type x1, other arithmetic: 2.34 us -> 1.11 us  [on_device_body(): light_out = normed.reshape(tok_rows, heads_here * head_size).astype(BF16)]
    unnamed x24 -> x28, local copies, waits for them, and re-layouts: 5 us -> 5 us
  transfers between devices with their start and end apart: 6 -> 7, of which waited for: 2 -> 2; matrix products, arithmetic and copies ran while one was open for 15% -> 18% of each run, Pallas kernels for 11% -> 11%
where the time goes in v12:
time: 82.7 us; the launch traced here: 82.1 us
  waiting for transfers between devices  20.1 us (24%)
  starting transfers between devices  19.5 us (24%)
  Pallas kernels  13 us (16%)
  local copies, waits for them, and re-layouts  9.32 us (11%)
  other arithmetic  9.21 us (11%)
  between operations  5.98 us (7%)
  matrix products  4.96 us (6%)
    ppermute x6, waiting for transfers between devices, shifted(): return lax.ppermute(block, axis, route)  20.1 us
    ppermute x6, starting transfers between devices, shifted(): return lax.ppermute(block, axis, route)  16.5 us
    pallas_call x1, Pallas kernels, intra_mixed(): pl.pallas_call(intra_kernel, out_shape=jax.ShapeDtypeStruct((tok_rows, wi...  5.07 us
    unnamed x28, local copies, waits for them, and re-layouts  5 us
    pallas_call x1, Pallas kernels, final_mixed(): pl.pallas_call(final_kernel, out_shape=(jax.ShapeDtypeStruct((tok_rows, w...  4.24 us
    dot_general x1, matrix products, soft_window(): jnp.einsum('kgts,ksd->kgtd', prob_block.astype(BF16), value_heads, prefer...  4.05 us
    pallas_call x1, Pallas kernels, local_state_of(): pl.pallas_call(state_kernel, out_shape=jax.ShapeDtypeStruct((heads_here,...  3.7 us
    ppermute x1, starting transfers between devices, on_device_body(): squares = squares + lax.ppermute(squares, 'tensor', [(0, 1), (1, 0)])  3.02 us
  transfers between devices with their start and end apart: 7, of which 2 were waited for; matrix products, arithmetic and copies ran while one was open for 18% of the time, Pallas kernels for 11%

profile of v12, /device:TPU:11, one launch (start us, length us, event | category | flops | bytes accessed | tf_op | source)
XLA Modules:
  0.0 82.1 jit_solution(9608275651938758056)
XLA Ops:
  0.6 0.0 copy-start.7
  0.6 1.0 %reduce_window_sum.13.decay_ref = f32[16,128]{1,0:T(8,128)S(1)} reduce-window(f32[16,128]{1,0:T(8,128)} %param.14, f32[]{:T(128)} %constant.10.clone.1), window={size=1x128 pad=0_0x127_0}, to_apply=%region_0.0 | reduce-window | flops 260096 | bytes 16388 | tf_op jit(solution)/shard_map/jit(cumsum)/reduce_window_sum | solution.py:160
  1.6 0.0 copy-start.5
  1.6 0.2 fusion.22
  1.8 1.3 %convert_add_fusion = (f32[128]{0:T(128)S(1)}, bf16[128]{0:T(256)(128)(2,1)S(1)}, f32[1,128]{1,0:T(1,128)}, f32[128,1]{0,1:T(1,128)S(1)}) fusion(s32[128]{0:T(128)} %param.19), kind=kLoop, calls=%fused_computation.65 | loop fusion | flops 384 | bytes 2304 | tf_op jit(solution)/shard_map/add | solution.py:159
  3.1 0.9 %copy.19 = bf16[128,256]{0,1:T(8,128)(2,1)S(1)} copy(bf16[128,256]{1,0:T(8,128)(2,1)} %param.17) | data formatting | bytes 131072 | tf_op args[7]
  4.0 0.1 copy.20
  4.2 1.0 %copy.21 = bf16[128,256]{0,1:T(8,128)(2,1)S(1)} copy(bf16[128,256]{1,0:T(8,128)(2,1)} %param.18) | data formatting | bytes 131072 | tf_op args[8]
  5.1 0.1 copy.22
  5.3 0.1 fusion.26
  5.4 3.2 %collective-permute-start = (bf16[528,128]{1,0:T(8,128)(2,1)S(1)}, bf16[528,128]{1,0:T(8,128)(2,1)S(1)}, u32[]{:S(2)}, u32[]{:S(2)}) collective-permute-start(bf16[528,128]{1,0:T(8,128)(2,1)S(1)} %pad_maximum_fusion.1), channel_id=1, source_target_pairs={{0,4},{2,6},{4,8},{6,10},{8,12},{10,14},{1,5},{3,7},{5,9},{7,11},{... | collective-permute-start | bytes 405512 | tf_op jit(solution)/shard_map/ppermute | solution.py:18
  8.6 3.2 %collective-permute-start.1 = (bf16[528,128]{1,0:T(8,128)(2,1)S(1)}, bf16[528,128]{1,0:T(8,128)(2,1)S(1)}, u32[]{:S(2)}, u32[]{:S(2)}) collective-permute-start(bf16[528,128]{1,0:T(8,128)(2,1)S(1)} %pad_maximum_fusion.1), channel_id=1, source_target_pairs={{0,2},{2,4},{4,6},{6,8},{8,10},{10,12},{12,14},{1,3},{3,5},{5,7},{... | collective-permute-start | bytes 405512 | tf_op jit(solution)/shard_map/ppermute | solution.py:18
  11.7 0.7 copy.23
  12.5 0.0 copy-start.2
  12.5 0.7 copy.24.code_col_ref.code_ref
  13.2 3.7 %shard_map.114 = bf16[16,128,128]{2,1,0:T(8,128)(2,1)} custom-call(f32[128,16]{1,0:T(8,128)} %bitcast.82, f32[128,1]{1,0:T(8,128)} %copy.24.code_col_ref.code_ref, bf16[128,2048]{1,0:T(8,128)(2,1)} %key_ref.3, bf16[128,2048]{1,0:T(8,128)(2,1)} %value_ref.3), custom_call_target="tpu_custom_call" | custom-call | flops 67108864 | bytes 786432 | tf_op jit(solution)/shard_map/pallas_call | solution.py:39
  16.9 3.1 %collective-permute-start.3 = (bf16[16,128,128]{2,1,0:T(8,128)(2,1)}, bf16[16,128,128]{2,1,0:T(8,128)(2,1)S(1)}, u32[]{:S(2)}, u32[]{:S(2)}) collective-permute-start(bf16[16,128,128]{2,1,0:T(8,128)(2,1)} %shard_map.114), channel_id=1, source_target_pairs={{0,2},{2,4},{4,6},{6,8},{8,10},{10,12},{12,14},{1,3},{3,5},{5,7},{... | collective-permute-start | bytes 1572872 | tf_op jit(solution)/shard_map/ppermute | solution.py:18
  20.0 1.9 %collective-permute-start.4 = (bf16[16,128,128]{2,1,0:T(8,128)(2,1)}, bf16[16,128,128]{2,1,0:T(8,128)(2,1)S(1)}, u32[]{:S(2)}, u32[]{:S(2)}) collective-permute-start(bf16[16,128,128]{2,1,0:T(8,128)(2,1)} %shard_map.114), channel_id=1, source_target_pairs={{0,4},{2,6},{4,8},{6,10},{8,12},{10,14},{1,5},{3,7},{5,9},{7,11},{... | collective-permute-start | bytes 1572872 | tf_op jit(solution)/shard_map/ppermute | solution.py:18
  22.0 1.1 %copy.36 = bf16[16,8,16,128]{3,2,1,0:T(8,128)(2,1)S(1)} copy(bf16[16,8,16,128]{3,1,2,0:T(8,128)(2,1)} %bitcast.87) | data formatting | bytes 1048576
  23.1 0.0 copy-done.5
  23.1 5.1 %shard_map.113.mixed_ref = f32[128,2048]{1,0:T(8,128)} custom-call(f32[16,128]{1,0:T(8,128)} %copy-done.5, f32[128,16]{1,0:T(8,128)} %bitcast.83, f32[1,128]{1,0:T(1,128)} %get-tuple-element.30.code_row_ref, f32[128,1]{1,0:T(8,128)} %copy.24.code_col_ref.code_ref, bf16[128,2048]{1,0:T(8,128)(2,1)} %query_ref.3, bf16[128,2048]{1,0:T(8,128)(2,1)} %key_ref.3, ...), custom_call_target="tpu_custom_call" | custom-call | flops 134217728 | bytes 2621440 | tf_op jit(solution)/shard_map/pallas_call | solution.py:69
  28.2 0.0 collective-permute-done
  28.2 0.0 collective-permute-done.1
  28.3 1.9 %collective-permute-start.2 = (bf16[1040,128]{1,0:T(8,128)(2,1)S(1)}, bf16[1040,128]{1,0:T(8,128)(2,1)S(1)}, u32[]{:S(2)}, u32[]{:S(2)}) collective-permute-start(bf16[1040,128]{1,0:T(8,128)(2,1)S(1)} %pad_maximum_fusion), channel_id=1, source_target_pairs={{0,4},{2,6},{4,8},{6,10},{8,12},{10,14},{1,5},{3,7},{5,9},{7,11},{... | collective-permute-start | bytes 798728 | tf_op jit(solution)/shard_map/ppermute | solution.py:18
  30.2 0.6 fusion.43
  30.8 0.6 fusion.42
  34.0 0.1 broadcast_select_fusion
  34.1 0.0 copy-done.7
  34.1 0.6 broadcast_compare_fusion
  34.8 0.1 copy.29
  34.9 0.1 copy.30
  36.2 0.0 copy-done.2
  36.3 0.7 exponential_select_fusion.scale_t_ref
  37.0 11.1 %collective-permute-done.2 = bf16[1040,128]{1,0:T(8,128)(2,1)S(1)} collective-permute-done((bf16[1040,128]{1,0:T(8,128)(2,1)S(1)}, bf16[1040,128]{1,0:T(8,128)(2,1)S(1)}, u32[]{:S(2)}, u32[]{:S(2)}) %collective-permute-start.2) | collective-permute-done | bytes 266272 | tf_op jit(solution)/shard_map/ppermute | solution.py:18
  48.2 0.1 copy.27
  48.4 0.1 copy.28
  48.5 0.6 slice.112
  50.3 0.2 fusion.15
  50.5 0.6 broadcast_select_fusion.1.carry_ref
  51.2 0.9 %fusion.2 = (f32[2,8,128]{2,1,0:T(8,128)S(1)}, f32[2,640,128,8]{2,1,3,0:T(8,128)S(1)}) fusion(pred[128,640]{0,1:T(8,128)(4,1)S(1)} %fusion.15, bf16[128,2,8,128]{3,2,1,0:T(8,128)(2,1)S(1)} %bitcast.81, bf16[2,640,128]{2,1,0:T(8,128)(2,1)S(1)} %bitcast_dynamic-update-slice_fusion), kind=kOutput, calls=%fused_computation.4 | convolution fusion | flops 339474432 | bytes 6184960 | tf_op jit(solution)/shard_map/tkgd,ksd->kgts/dot_general | solution.py:113
  52.1 0.0 copy-start
  52.1 0.0 collective-permute-done.3
  52.1 0.0 collective-permute-done.4
  52.1 1.5 %fusion.38 = (bf16[16,128,128]{2,1,0:T(8,128)(2,1)S(1)}, f32[16,128,128]{2,1,0:T(8,128)}) fusion(bf16[16,128,128]{2,1,0:T(8,128)(2,1)S(1)} %collective-permute-done.4, f32[16]{0:T(128)S(1)} %get-tuple-element.12, bf16[16,128,128]{2,1,0:T(8,128)(2,1)S(1)} %collective-permute-done.3), kind=kLoop, calls=%fused_computation.76 | loop fusion | flops 1310720 | bytes 2621504 | tf_op jit(solution)/shard_map/convert_element_type | solution.py:192
  53.6 3.2 %collective-permute-start.5 = (bf16[16,128,128]{2,1,0:T(8,128)(2,1)S(1)}, bf16[16,128,128]{2,1,0:T(8,128)(2,1)S(1)}, u32[]{:S(2)}, u32[]{:S(2)}) collective-permute-start(bf16[16,128,128]{2,1,0:T(8,128)(2,1)S(1)} %get-tuple-element.10), channel_id=1, source_target_pairs={{0,4},{2,6},{4,8},{6,10},{8,12},{10,14},{1,5},{3,7},{5,9},{7,11},{... | collective-permute-start | bytes 1572872 | tf_op jit(solution)/shard_map/ppermute | solution.py:18
  56.8 0.0 copy-done
  56.8 1.1 %fusion = f32[2,8,128]{2,1,0:T(8,128)S(1)} fusion(f32[2,640,128,8]{2,1,3,0:T(8,128)S(1)} %get-tuple-element.40, f32[2,8,128]{2,1,0:T(8,128)S(1)} %get-tuple-element.39, pred[128,640]{0,1:T(8,128)(4,1)S(1)} %fusion.15), kind=kLoop, calls=%fused_computation.2 | loop fusion | flops 5240832 | bytes 5341184 | tf_op jit(solution)/shard_map/reduce_sum | solution.py:117
  57.9 9.0 %collective-permute-done.5.far_ref = bf16[16,128,128]{2,1,0:T(8,128)(2,1)S(1)} collective-permute-done((bf16[16,128,128]{2,1,0:T(8,128)(2,1)S(1)}, bf16[16,128,128]{2,1,0:T(8,128)(2,1)S(1)}, u32[]{:S(2)}, u32[]{:S(2)}) %collective-permute-start.5) | collective-permute-done | bytes 524320 | tf_op jit(solution)/shard_map/ppermute | solution.py:18
  66.9 0.0 copy-start.4
  66.9 0.8 copy-done.4
  67.7 4.2 %shard_map.115 = (f32[128,2048]{1,0:T(8,128)}, f32[128,1]{1,0:T(8,128)}) custom-call(f32[16]{0:T(128)} %broadcast_select_fusion.1.carry_ref, f32[128,16]{1,0:T(8,128)} %exponential_select_fusion.scale_t_ref, bf16[128,2048]{1,0:T(8,128)(2,1)} %query_ref.3, f32[128,2048]{1,0:T(8,128)} %shard_map.113.mixed_ref, f32[16,128,128]{2,1,0:T(8,128)} %get-tuple-element.11.pair_ref, ...), custom_call_target="tpu_custom_call" | custom-call | flops 402653184 | bytes 3145728 | tf_op jit(solution)/shard_map/pallas_call | solution.py:96
  71.9 0.9 %reduce.1 = f32[128]{0:T(128)S(1)} reduce(f32[128,1]{1,0:T(8,128)} %get-tuple-element.5, f32[]{:T(128)} %constant.29), dimensions={1}, to_apply=%get-tuple-element.5.reduce_sub_computation | reduce | bytes 1028 | tf_op jit(solution)/shard_map/pallas_call | solution.py:96
  72.9 3.0 %collective-permute-start.6 = (f32[128]{0:T(128)S(1)}, f32[128]{0:T(128)S(1)}, u32[]{:S(2)}, u32[]{:S(2)}) collective-permute-start(f32[128]{0:T(128)S(1)} %reduce.1), channel_id=1, source_target_pairs={{0,1},{1,0},{2,3},{3,2},{4,5},{5,4},{6,7},{7,6},{8,9},{9,8},{10,11... | collective-permute-start | bytes 1544 | tf_op jit(solution)/shard_map/ppermute | solution.py:212
  75.9 0.0 copy-start.1
  75.9 0.0 copy-start.3
  75.9 0.0 copy-start.6
  75.9 4.0 %divide_convert_fusion = bf16[128,2,8,128]{0,3,2,1:T(8,128)(2,1)S(1)} fusion(f32[2,640,128,8]{2,1,3,0:T(8,128)} %copy-done, f32[2,8,128]{2,1,0:T(8,128)S(1)} %get-tuple-element.39, pred[128,640]{0,1:T(8,128)(4,1)S(1)} %fusion.15, f32[128,2,8]{0,2,1:T(8,128)S(1)} %bitcast.99, bf16[2,640,128]{1,2,0:T(8,128)(2,1)S(1)} %constant_dynamic-update-slice_fusion), kind=kOutput, calls=%fused_computation.8 | convolution fusion | flops 341311488 | bytes 6193152 | tf_op jit(solution)/shard_map/kgts,ksd->kgtd/dot_general | solution.py:118
  79.9 1.0 %copy.32 = bf16[128,2048]{1,0:T(8,128)(2,1)} copy(bf16[128,2048]{0,1:T(8,128)(2,1)S(1)} %bitcast.88) | data formatting | bytes 1048576
  81.0 0.0 collective-permute-done.6
  81.0 0.0 copy-done.1
  81.0 0.0 copy-done.3
  81.0 0.0 copy-done.6
  81.0 1.1 %multiply_convert_fusion = bf16[128,2048]{1,0:T(8,128)(2,1)} fusion(bf16[128,2048]{1,0:T(8,128)(2,1)S(1)} %copy-done.3, f32[128,2048]{1,0:T(8,128)S(1)} %copy-done.1, f32[2048]{0:T(1024)S(1)} %copy-done.6, f32[128]{0:T(128)S(1)} %add_rsqrt_fusion), kind=kLoop, calls=%fused_computation.9 | loop fusion | flops 2097152 | bytes 2105856 | tf_op jit(solution)/shard_map/convert_element_type | solution.py:219
  (29 shorter events, 0.3 us)
Async XLA Ops:
  0.6 33.5 %copy-start.7 = (s32[128]{0:T(128)S(1)}, s32[128]{0:T(128)}, u32[]{:S(2)}) copy-start(s32[128]{0:T(128)} %param.19) | copy-start | bytes 1540
  1.6 21.5 %copy-start.5 = (f32[16,128]{1,0:T(8,128)}, f32[16,128]{1,0:T(8,128)S(1)}, u32[]{:S(2)}) copy-start(f32[16,128]{1,0:T(8,128)S(1)} %reduce_window_sum.13.decay_ref) | copy-start | bytes 24580
  5.4 22.8 %collective-permute-start = (bf16[528,128]{1,0:T(8,128)(2,1)S(1)}, bf16[528,128]{1,0:T(8,128)(2,1)S(1)}, u32[]{:S(2)}, u32[]{:S(2)}) collective-permute-start(bf16[528,128]{1,0:T(8,128)(2,1)S(1)} %pad_maximum_fusion.1), channel_id=1, source_target_pairs={{0,4},{2,6},{4,8},{6,10},{8,12},{10,14},{1,5},{3,7},{5,9},{7,11},{... | collective-permute-start | bytes 405512 | tf_op jit(solution)/shard_map/ppermute | solution.py:18
  8.6 19.6 %collective-permute-start.1 = (bf16[528,128]{1,0:T(8,128)(2,1)S(1)}, bf16[528,128]{1,0:T(8,128)(2,1)S(1)}, u32[]{:S(2)}, u32[]{:S(2)}) collective-permute-start(bf16[528,128]{1,0:T(8,128)(2,1)S(1)} %pad_maximum_fusion.1), channel_id=1, source_target_pairs={{0,2},{2,4},{4,6},{6,8},{8,10},{10,12},{12,14},{1,3},{3,5},{5,7},{... | collective-permute-start | bytes 405512 | tf_op jit(solution)/shard_map/ppermute | solution.py:18
  12.5 23.8 %copy-start.2 = (f32[16,128]{0,1:T(8,128)S(1)}, f32[16,128]{0,1:T(8,128)}, u32[]{:S(2)}) copy-start(f32[16,128]{0,1:T(8,128)} %copy.23) | copy-start | bytes 24580
  16.9 35.2 %collective-permute-start.3 = (bf16[16,128,128]{2,1,0:T(8,128)(2,1)}, bf16[16,128,128]{2,1,0:T(8,128)(2,1)S(1)}, u32[]{:S(2)}, u32[]{:S(2)}) collective-permute-start(bf16[16,128,128]{2,1,0:T(8,128)(2,1)} %shard_map.114), channel_id=1, source_target_pairs={{0,2},{2,4},{4,6},{6,8},{8,10},{10,12},{12,14},{1,3},{3,5},{5,7},{... | collective-permute-start | bytes 1572872 | tf_op jit(solution)/shard_map/ppermute | solution.py:18
  20.0 32.1 %collective-permute-start.4 = (bf16[16,128,128]{2,1,0:T(8,128)(2,1)}, bf16[16,128,128]{2,1,0:T(8,128)(2,1)S(1)}, u32[]{:S(2)}, u32[]{:S(2)}) collective-permute-start(bf16[16,128,128]{2,1,0:T(8,128)(2,1)} %shard_map.114), channel_id=1, source_target_pairs={{0,4},{2,6},{4,8},{6,10},{8,12},{10,14},{1,5},{3,7},{5,9},{7,11},{... | collective-permute-start | bytes 1572872 | tf_op jit(solution)/shard_map/ppermute | solution.py:18
  28.3 19.8 %collective-permute-start.2 = (bf16[1040,128]{1,0:T(8,128)(2,1)S(1)}, bf16[1040,128]{1,0:T(8,128)(2,1)S(1)}, u32[]{:S(2)}, u32[]{:S(2)}) collective-permute-start(bf16[1040,128]{1,0:T(8,128)(2,1)S(1)} %pad_maximum_fusion), channel_id=1, source_target_pairs={{0,4},{2,6},{4,8},{6,10},{8,12},{10,14},{1,5},{3,7},{5,9},{7,11},{... | collective-permute-start | bytes 798728 | tf_op jit(solution)/shard_map/ppermute | solution.py:18
  52.1 4.8 %copy-start = (f32[2,640,128,8]{2,1,3,0:T(8,128)}, f32[2,640,128,8]{2,1,3,0:T(8,128)S(1)}, u32[]{:S(2)}) copy-start(f32[2,640,128,8]{2,1,3,0:T(8,128)S(1)} %get-tuple-element.40) | copy-start | bytes 15728644
  53.6 13.3 %collective-permute-start.5 = (bf16[16,128,128]{2,1,0:T(8,128)(2,1)S(1)}, bf16[16,128,128]{2,1,0:T(8,128)(2,1)S(1)}, u32[]{:S(2)}, u32[]{:S(2)}) collective-permute-start(bf16[16,128,128]{2,1,0:T(8,128)(2,1)S(1)} %get-tuple-element.10), channel_id=1, source_target_pairs={{0,4},{2,6},{4,8},{6,10},{8,12},{10,14},{1,5},{3,7},{5,9},{7,11},{... | collective-permute-start | bytes 1572872 | tf_op jit(solution)/shard_map/ppermute | solution.py:18
  66.9 0.8 copy-start.4
  72.9 8.1 %collective-permute-start.6 = (f32[128]{0:T(128)S(1)}, f32[128]{0:T(128)S(1)}, u32[]{:S(2)}, u32[]{:S(2)}) collective-permute-start(f32[128]{0:T(128)S(1)} %reduce.1), channel_id=1, source_target_pairs={{0,1},{1,0},{2,3},{3,2},{4,5},{5,4},{6,7},{7,6},{8,9},{9,8},{10,11... | collective-permute-start | bytes 1544 | tf_op jit(solution)/shard_map/ppermute | solution.py:212
  75.9 5.1 %copy-start.1 = (f32[128,2048]{1,0:T(8,128)S(1)}, f32[128,2048]{1,0:T(8,128)}, u32[]{:S(2)}) copy-start(f32[128,2048]{1,0:T(8,128)} %get-tuple-element.4) | copy-start | bytes 3145732
  75.9 5.1 %copy-start.3 = (bf16[128,2048]{1,0:T(8,128)(2,1)S(1)}, bf16[128,2048]{1,0:T(8,128)(2,1)}, u32[]{:S(2)}) copy-start(bf16[128,2048]{1,0:T(8,128)(2,1)} %param.13) | copy-start | bytes 1572868
  75.9 5.1 %copy-start.6 = (f32[2048]{0:T(1024)S(1)}, f32[2048]{0:T(1024)}, u32[]{:S(2)}) copy-start(f32[2048]{0:T(1024)} %param.15) | copy-start | bytes 24580

commit v13 on v10

--- a/solution.py
+++ b/solution.py
@@ -173,8 +173,10 @@
             rows_of(jnp.concatenate([code, split_parts(block_decay)]), head_size),
         ]
     )
-    state_1, kv_1 = shifted((own_state, own_kv), "ctx", 1)
-    state_2, kv_2 = shifted((own_state, own_kv), "ctx", 2)
+    state_1 = shifted(own_state, "ctx", 1)
+    state_2 = shifted(own_state, "ctx", 2)
+    kv_1 = shifted(own_kv, "ctx", 1)
+    kv_2 = shifted(own_kv, "ctx", 2)
 
     def unpack(block):
         keys = block[:kv_rows].reshape(kv_here, tok_rows, head_size)
@@ -189,9 +191,10 @@
 
     link_1 = (code_2[-1] == code_1[0]) & (code_1[0] == code_1[-1])
     pair_state = state_1.astype(F32) + jnp.where(link_1, decay_1, 0.0)[:, None, None] * state_2.astype(F32)
+    pair_wire = pair_state.astype(BF16)
 
     relay_kv = jnp.concatenate([kv_2[: 2 * kv_rows], kv_1[: 2 * kv_rows], rows_of(jnp.concatenate([code_2, code_1]), head_size)])
-    state_far = shifted(pair_state.astype(BF16), "ctx", 2)
+    state_far = shifted(pair_wire, "ctx", 2)
     kv_far = shifted(relay_kv, "ctx", 2)
     keys_4 = kv_far[:kv_rows].reshape(kv_here, tok_rows, head_size)
     values_4 = kv_far[kv_rows : 2 * kv_rows].reshape(kv_here, tok_rows, head_size)

time: 80 us -> 80 us (level)
  no operation moved by 1% of the time
where the time goes in v13:
time: 80 us; the launch traced here: 79.4 us
  waiting for transfers between devices  16.8 us (21%)
  starting transfers between devices  16.5 us (21%)
  Pallas kernels  12.9 us (16%)
  other arithmetic  10.2 us (13%)
  local copies, waits for them, and re-layouts  9.31 us (12%)
  between operations  6.13 us (8%)
  blocking collectives  5.08 us (6%)
  matrix products  2.35 us (3%)
    ppermute x6, waiting for transfers between devices, shifted(): return lax.ppermute(block, axis, route)  16.8 us
    ppermute x6, starting transfers between devices, shifted(): return lax.ppermute(block, axis, route)  16.5 us
    psum x1, blocking collectives, on_device_body(): squares = lax.psum(squares[:, 0], 'tensor')  5.08 us
    pallas_call x1, Pallas kernels, intra_mixed(): pl.pallas_call(intra_kernel, out_shape=jax.ShapeDtypeStruct((tok_rows, wi...  5.03 us
    unnamed x24, local copies, waits for them, and re-layouts  5 us
    pallas_call x1, Pallas kernels, final_mixed(): pl.pallas_call(final_kernel, out_shape=(jax.ShapeDtypeStruct((tok_rows, w...  4.22 us
    pallas_call x1, Pallas kernels, local_state_of(): pl.pallas_call(state_kernel, out_shape=jax.ShapeDtypeStruct((heads_here,...  3.7 us
    convert_element_type x1, other arithmetic, on_device_body(): light_out = normed.reshape(tok_rows, heads_here * head_size).astype(BF16)  2.34 us
  transfers between devices with their start and end apart: 6, of which 2 were waited for; matrix products, arithmetic and copies ran while one was open for 15% of the time, Pallas kernels for 11%

profile of v13, /device:TPU:11, one launch (start us, length us, event | category | flops | bytes accessed | tf_op | source)
XLA Modules:
  0.0 79.4 jit_solution(6056914500878738069)
XLA Ops:
  0.6 0.0 copy-start.5
  0.6 1.0 %reduce_window_sum.13.decay_ref = f32[16,128]{1,0:T(8,128)S(1)} reduce-window(f32[16,128]{1,0:T(8,128)} %param.14, f32[]{:T(128)} %constant.10.clone.1), window={size=1x128 pad=0_0x127_0}, to_apply=%region_0.0 | reduce-window | flops 260096 | bytes 16388 | tf_op jit(solution)/shard_map/jit(cumsum)/reduce_window_sum | solution.py:160
  1.6 0.0 copy-start.3
  1.6 0.2 fusion.22
  1.8 1.2 %convert_add_fusion = (f32[128]{0:T(128)S(1)}, bf16[128]{0:T(256)(128)(2,1)S(1)}, f32[1,128]{1,0:T(1,128)}, f32[128,1]{0,1:T(1,128)S(1)}) fusion(s32[128]{0:T(128)} %param.19), kind=kLoop, calls=%fused_computation.65 | loop fusion | flops 384 | bytes 2304 | tf_op jit(solution)/shard_map/add | solution.py:159
  3.1 0.9 %copy.19 = bf16[128,256]{0,1:T(8,128)(2,1)S(1)} copy(bf16[128,256]{1,0:T(8,128)(2,1)} %param.17) | data formatting | bytes 131072 | tf_op args[7]
  4.0 0.1 copy.20
  4.2 1.0 %copy.21 = bf16[128,256]{0,1:T(8,128)(2,1)S(1)} copy(bf16[128,256]{1,0:T(8,128)(2,1)} %param.18) | data formatting | bytes 131072 | tf_op args[8]
  5.1 0.1 copy.22
  5.3 0.1 fusion.26
  5.4 3.2 %collective-permute-start = (bf16[528,128]{1,0:T(8,128)(2,1)S(1)}, bf16[528,128]{1,0:T(8,128)(2,1)S(1)}, u32[]{:S(2)}, u32[]{:S(2)}) collective-permute-start(bf16[528,128]{1,0:T(8,128)(2,1)S(1)} %pad_maximum_fusion.1), channel_id=1, source_target_pairs={{0,4},{2,6},{4,8},{6,10},{8,12},{10,14},{1,5},{3,7},{5,9},{7,11},{... | collective-permute-start | bytes 405512 | tf_op jit(solution)/shard_map/ppermute | solution.py:18
  8.6 3.2 %collective-permute-start.1 = (bf16[528,128]{1,0:T(8,128)(2,1)S(1)}, bf16[528,128]{1,0:T(8,128)(2,1)S(1)}, u32[]{:S(2)}, u32[]{:S(2)}) collective-permute-start(bf16[528,128]{1,0:T(8,128)(2,1)S(1)} %pad_maximum_fusion.1), channel_id=1, source_target_pairs={{0,2},{2,4},{4,6},{6,8},{8,10},{10,12},{12,14},{1,3},{3,5},{5,7},{... | collective-permute-start | bytes 405512 | tf_op jit(solution)/shard_map/ppermute | solution.py:18
  11.7 0.7 copy.23
  12.5 0.0 copy-start
  12.5 0.7 copy.24.code_col_ref.code_ref
  13.2 3.7 %shard_map.114 = bf16[16,128,128]{2,1,0:T(8,128)(2,1)} custom-call(f32[128,16]{1,0:T(8,128)} %bitcast.82, f32[128,1]{1,0:T(8,128)} %copy.24.code_col_ref.code_ref, bf16[128,2048]{1,0:T(8,128)(2,1)} %key_ref.3, bf16[128,2048]{1,0:T(8,128)(2,1)} %value_ref.3), custom_call_target="tpu_custom_call" | custom-call | flops 67108864 | bytes 786432 | tf_op jit(solution)/shard_map/pallas_call | solution.py:39
  16.9 3.1 %collective-permute-start.3 = (bf16[16,128,128]{2,1,0:T(8,128)(2,1)}, bf16[16,128,128]{2,1,0:T(8,128)(2,1)S(1)}, u32[]{:S(2)}, u32[]{:S(2)}) collective-permute-start(bf16[16,128,128]{2,1,0:T(8,128)(2,1)} %shard_map.114), channel_id=1, source_target_pairs={{0,2},{2,4},{4,6},{6,8},{8,10},{10,12},{12,14},{1,3},{3,5},{5,7},{... | collective-permute-start | bytes 1572872 | tf_op jit(solution)/shard_map/ppermute | solution.py:18
  20.0 1.9 %collective-permute-start.4 = (bf16[16,128,128]{2,1,0:T(8,128)(2,1)}, bf16[16,128,128]{2,1,0:T(8,128)(2,1)S(1)}, u32[]{:S(2)}, u32[]{:S(2)}) collective-permute-start(bf16[16,128,128]{2,1,0:T(8,128)(2,1)} %shard_map.114), channel_id=1, source_target_pairs={{0,4},{2,6},{4,8},{6,10},{8,12},{10,14},{1,5},{3,7},{5,9},{7,11},{... | collective-permute-start | bytes 1572872 | tf_op jit(solution)/shard_map/ppermute | solution.py:18
  21.9 1.1 %copy.36 = bf16[16,8,16,128]{3,2,1,0:T(8,128)(2,1)S(1)} copy(bf16[16,8,16,128]{3,1,2,0:T(8,128)(2,1)} %bitcast.87) | data formatting | bytes 1048576
  23.1 0.0 copy-done.3
  23.1 5.0 %shard_map.113.mixed_ref = f32[128,2048]{1,0:T(8,128)} custom-call(f32[16,128]{1,0:T(8,128)} %copy-done.3, f32[128,16]{1,0:T(8,128)} %bitcast.83, f32[1,128]{1,0:T(1,128)} %get-tuple-element.30.code_row_ref, f32[128,1]{1,0:T(8,128)} %copy.24.code_col_ref.code_ref, bf16[128,2048]{1,0:T(8,128)(2,1)} %query_ref.3, bf16[128,2048]{1,0:T(8,128)(2,1)} %key_ref.3, ...), custom_call_target="tpu_custom_call" | custom-call | flops 134217728 | bytes 2621440 | tf_op jit(solution)/shard_map/pallas_call | solution.py:69
  28.1 0.0 collective-permute-done
  28.2 0.0 collective-permute-done.1
  28.3 1.9 %collective-permute-start.2 = (bf16[1040,128]{1,0:T(8,128)(2,1)S(1)}, bf16[1040,128]{1,0:T(8,128)(2,1)S(1)}, u32[]{:S(2)}, u32[]{:S(2)}) collective-permute-start(bf16[1040,128]{1,0:T(8,128)(2,1)S(1)} %pad_maximum_fusion), channel_id=1, source_target_pairs={{0,4},{2,6},{4,8},{6,10},{8,12},{10,14},{1,5},{3,7},{5,9},{7,11},{... | collective-permute-start | bytes 798728 | tf_op jit(solution)/shard_map/ppermute | solution.py:18
  30.2 0.6 fusion.43
  30.8 0.6 fusion.42
  34.0 0.1 broadcast_select_fusion
  34.1 0.0 copy-done.5
  34.1 0.6 broadcast_compare_fusion
  34.7 0.1 copy.29
  34.8 0.1 copy.30
  36.2 0.0 copy-done
  36.3 0.7 exponential_select_fusion.scale_t_ref
  37.0 11.1 %collective-permute-done.2 = bf16[1040,128]{1,0:T(8,128)(2,1)S(1)} collective-permute-done((bf16[1040,128]{1,0:T(8,128)(2,1)S(1)}, bf16[1040,128]{1,0:T(8,128)(2,1)S(1)}, u32[]{:S(2)}, u32[]{:S(2)}) %collective-permute-start.2) | collective-permute-done | bytes 266272 | tf_op jit(solution)/shard_map/ppermute | solution.py:18
  48.2 0.1 copy.27
  48.4 0.1 copy.28
  48.5 0.6 slice.112
  49.1 0.2 fusion.15
  49.3 0.9 %fusion.2 = (f32[2,8,128]{2,1,0:T(8,128)S(1)}, f32[2,640,128,8]{2,1,3,0:T(8,128)S(1)}) fusion(pred[128,640]{0,1:T(8,128)(4,1)S(1)} %fusion.15, bf16[128,2,8,128]{3,2,1,0:T(8,128)(2,1)S(1)} %bitcast.81, bf16[2,640,128]{2,1,0:T(8,128)(2,1)S(1)} %bitcast_dynamic-update-slice_fusion), kind=kOutput, calls=%fused_computation.4 | convolution fusion | flops 339474432 | bytes 6184960 | tf_op jit(solution)/shard_map/tkgd,ksd->kgts/dot_general | solution.py:113
  50.3 1.1 %fusion = f32[2,8,128]{2,1,0:T(8,128)S(1)} fusion(f32[2,640,128,8]{2,1,3,0:T(8,128)S(1)} %get-tuple-element.40, f32[2,8,128]{2,1,0:T(8,128)S(1)} %get-tuple-element.39, pred[128,640]{0,1:T(8,128)(4,1)S(1)} %fusion.15), kind=kLoop, calls=%fused_computation.2 | loop fusion | flops 5240832 | bytes 5341184 | tf_op jit(solution)/shard_map/reduce_sum | solution.py:117
  51.4 0.0 collective-permute-done.3
  51.4 0.0 collective-permute-done.4
  51.4 1.3 %fusion.38 = (bf16[16,128,128]{2,1,0:T(8,128)(2,1)S(1)}, f32[16,128,128]{2,1,0:T(8,128)}) fusion(bf16[16,128,128]{2,1,0:T(8,128)(2,1)S(1)} %collective-permute-done.4, f32[16]{0:T(128)S(1)} %get-tuple-element.12, bf16[16,128,128]{2,1,0:T(8,128)(2,1)S(1)} %collective-permute-done.3), kind=kLoop, calls=%fused_computation.76 | loop fusion | flops 1310720 | bytes 2621504 | tf_op jit(solution)/shard_map/convert_element_type | solution.py:194
  52.7 3.2 %collective-permute-start.5 = (bf16[16,128,128]{2,1,0:T(8,128)(2,1)S(1)}, bf16[16,128,128]{2,1,0:T(8,128)(2,1)S(1)}, u32[]{:S(2)}, u32[]{:S(2)}) collective-permute-start(bf16[16,128,128]{2,1,0:T(8,128)(2,1)S(1)} %get-tuple-element.10), channel_id=1, source_target_pairs={{0,4},{2,6},{4,8},{6,10},{8,12},{10,14},{1,5},{3,7},{5,9},{7,11},{... | collective-permute-start | bytes 1572872 | tf_op jit(solution)/shard_map/ppermute | solution.py:18
  55.9 0.0 copy-start.1
  55.9 0.0 copy-start.4
  55.9 1.4 %divide_convert_fusion = bf16[128,2,8,128]{0,3,2,1:T(8,128)(2,1)S(1)} fusion(f32[2,640,128,8]{2,1,3,0:T(8,128)S(1)} %get-tuple-element.40, f32[2,8,128]{2,1,0:T(8,128)S(1)} %get-tuple-element.39, pred[128,640]{0,1:T(8,128)(4,1)S(1)} %fusion.15, f32[128,2,8]{0,2,1:T(8,128)S(1)} %bitcast.99, bf16[2,640,128]{1,2,0:T(8,128)(2,1)S(1)} %constant_dynamic-update-slice_fusion), kind=kOutput, calls=%fused_computation.8 | convolution fusion | flops 341311488 | bytes 6193152 | tf_op jit(solution)/shard_map/kgts,ksd->kgtd/dot_general | solution.py:118
  57.4 1.0 %copy.32 = bf16[128,2048]{1,0:T(8,128)(2,1)} copy(bf16[128,2048]{0,1:T(8,128)(2,1)S(1)} %bitcast.88) | data formatting | bytes 1048576
  59.7 0.6 broadcast_select_fusion.1.carry_ref
  60.3 5.7 %collective-permute-done.5.far_ref = bf16[16,128,128]{2,1,0:T(8,128)(2,1)S(1)} collective-permute-done((bf16[16,128,128]{2,1,0:T(8,128)(2,1)S(1)}, bf16[16,128,128]{2,1,0:T(8,128)(2,1)S(1)}, u32[]{:S(2)}, u32[]{:S(2)}) %collective-permute-start.5) | collective-permute-done | bytes 524320 | tf_op jit(solution)/shard_map/ppermute | solution.py:18
  66.0 0.0 copy-start.2
  66.0 0.8 copy-done.2
  66.8 4.2 %shard_map.115 = (f32[128,2048]{1,0:T(8,128)}, f32[128,1]{1,0:T(8,128)}) custom-call(f32[16]{0:T(128)} %broadcast_select_fusion.1.carry_ref, f32[128,16]{1,0:T(8,128)} %exponential_select_fusion.scale_t_ref, bf16[128,2048]{1,0:T(8,128)(2,1)} %query_ref.3, f32[128,2048]{1,0:T(8,128)} %shard_map.113.mixed_ref, f32[16,128,128]{2,1,0:T(8,128)} %get-tuple-element.11.pair_ref, ...), custom_call_target="tpu_custom_call" | custom-call | flops 402653184 | bytes 3145728 | tf_op jit(solution)/shard_map/pallas_call | solution.py:96
  71.0 0.9 %reduce.1 = f32[128]{0:T(128)S(1)} reduce(f32[128,1]{1,0:T(8,128)} %get-tuple-element.5, f32[]{:T(128)} %constant.29), dimensions={1}, to_apply=%get-tuple-element.5.reduce_sub_computation | reduce | bytes 1028 | tf_op jit(solution)/shard_map/pallas_call | solution.py:96
  71.9 5.1 %psum.7 = f32[128]{0:T(128)S(1)} all-reduce(f32[128]{0:T(128)S(1)} %reduce.1), channel_id=1, replica_groups=mesh['groups'=2,'ctx'=8,'tensor'=2] {'tensor'}, use_global_device_ids=true, to_apply=%region_1.2 | all-reduce | flops 128 | bytes 1024 | tf_op jit(solution)/shard_map/psum | solution.py:212
  77.0 0.0 copy-done.1
  77.0 0.0 copy-done.4
  77.0 2.3 %multiply_convert_fusion = bf16[128,2048]{1,0:T(8,128)(2,1)} fusion(bf16[128,2048]{1,0:T(8,128)(2,1)S(1)} %copy-done.1, f32[128,2048]{1,0:T(8,128)} %get-tuple-element.4, f32[2048]{0:T(1024)S(1)} %copy-done.4, f32[128]{0:T(128)S(1)} %add_rsqrt_fusion), kind=kLoop, calls=%fused_computation.9 | loop fusion | flops 2097152 | bytes 2105856 | tf_op jit(solution)/shard_map/convert_element_type | solution.py:217
  (29 shorter events, 0.3 us)
Async XLA Ops:
  0.6 33.4 %copy-start.5 = (s32[128]{0:T(128)S(1)}, s32[128]{0:T(128)}, u32[]{:S(2)}) copy-start(s32[128]{0:T(128)} %param.19) | copy-start | bytes 1540
  1.6 21.5 %copy-start.3 = (f32[16,128]{1,0:T(8,128)}, f32[16,128]{1,0:T(8,128)S(1)}, u32[]{:S(2)}) copy-start(f32[16,128]{1,0:T(8,128)S(1)} %reduce_window_sum.13.decay_ref) | copy-start | bytes 24580
  5.4 22.8 %collective-permute-start = (bf16[528,128]{1,0:T(8,128)(2,1)S(1)}, bf16[528,128]{1,0:T(8,128)(2,1)S(1)}, u32[]{:S(2)}, u32[]{:S(2)}) collective-permute-start(bf16[528,128]{1,0:T(8,128)(2,1)S(1)} %pad_maximum_fusion.1), channel_id=1, source_target_pairs={{0,4},{2,6},{4,8},{6,10},{8,12},{10,14},{1,5},{3,7},{5,9},{7,11},{... | collective-permute-start | bytes 405512 | tf_op jit(solution)/shard_map/ppermute | solution.py:18
  8.6 19.6 %collective-permute-start.1 = (bf16[528,128]{1,0:T(8,128)(2,1)S(1)}, bf16[528,128]{1,0:T(8,128)(2,1)S(1)}, u32[]{:S(2)}, u32[]{:S(2)}) collective-permute-start(bf16[528,128]{1,0:T(8,128)(2,1)S(1)} %pad_maximum_fusion.1), channel_id=1, source_target_pairs={{0,2},{2,4},{4,6},{6,8},{8,10},{10,12},{12,14},{1,3},{3,5},{5,7},{... | collective-permute-start | bytes 405512 | tf_op jit(solution)/shard_map/ppermute | solution.py:18
  12.5 23.8 %copy-start = (f32[16,128]{0,1:T(8,128)S(1)}, f32[16,128]{0,1:T(8,128)}, u32[]{:S(2)}) copy-start(f32[16,128]{0,1:T(8,128)} %copy.23) | copy-start | bytes 24580
  16.9 34.5 %collective-permute-start.3 = (bf16[16,128,128]{2,1,0:T(8,128)(2,1)}, bf16[16,128,128]{2,1,0:T(8,128)(2,1)S(1)}, u32[]{:S(2)}, u32[]{:S(2)}) collective-permute-start(bf16[16,128,128]{2,1,0:T(8,128)(2,1)} %shard_map.114), channel_id=1, source_target_pairs={{0,2},{2,4},{4,6},{6,8},{8,10},{10,12},{12,14},{1,3},{3,5},{5,7},{... | collective-permute-start | bytes 1572872 | tf_op jit(solution)/shard_map/ppermute | solution.py:18
  20.0 31.3 %collective-permute-start.4 = (bf16[16,128,128]{2,1,0:T(8,128)(2,1)}, bf16[16,128,128]{2,1,0:T(8,128)(2,1)S(1)}, u32[]{:S(2)}, u32[]{:S(2)}) collective-permute-start(bf16[16,128,128]{2,1,0:T(8,128)(2,1)} %shard_map.114), channel_id=1, source_target_pairs={{0,4},{2,6},{4,8},{6,10},{8,12},{10,14},{1,5},{3,7},{5,9},{7,11},{... | collective-permute-start | bytes 1572872 | tf_op jit(solution)/shard_map/ppermute | solution.py:18
  28.3 19.8 %collective-permute-start.2 = (bf16[1040,128]{1,0:T(8,128)(2,1)S(1)}, bf16[1040,128]{1,0:T(8,128)(2,1)S(1)}, u32[]{:S(2)}, u32[]{:S(2)}) collective-permute-start(bf16[1040,128]{1,0:T(8,128)(2,1)S(1)} %pad_maximum_fusion), channel_id=1, source_target_pairs={{0,4},{2,6},{4,8},{6,10},{8,12},{10,14},{1,5},{3,7},{5,9},{7,11},{... | collective-permute-start | bytes 798728 | tf_op jit(solution)/shard_map/ppermute | solution.py:18
  52.7 13.3 %collective-permute-start.5 = (bf16[16,128,128]{2,1,0:T(8,128)(2,1)S(1)}, bf16[16,128,128]{2,1,0:T(8,128)(2,1)S(1)}, u32[]{:S(2)}, u32[]{:S(2)}) collective-permute-start(bf16[16,128,128]{2,1,0:T(8,128)(2,1)S(1)} %get-tuple-element.10), channel_id=1, source_target_pairs={{0,4},{2,6},{4,8},{6,10},{8,12},{10,14},{1,5},{3,7},{5,9},{7,11},{... | collective-permute-start | bytes 1572872 | tf_op jit(solution)/shard_map/ppermute | solution.py:18
  55.9 21.1 %copy-start.1 = (bf16[128,2048]{1,0:T(8,128)(2,1)S(1)}, bf16[128,2048]{1,0:T(8,128)(2,1)}, u32[]{:S(2)}) copy-start(bf16[128,2048]{1,0:T(8,128)(2,1)} %param.13) | copy-start | bytes 1572868
  55.9 21.1 %copy-start.4 = (f32[2048]{0:T(1024)S(1)}, f32[2048]{0:T(1024)}, u32[]{:S(2)}) copy-start(f32[2048]{0:T(1024)} %param.15) | copy-start | bytes 24580
  66.0 0.8 copy-start.2

commit v14 on v10

--- a/solution.py
+++ b/solution.py
@@ -81,9 +81,14 @@
     for head in range(heads_here):
         columns = slice(head * head_size, (head + 1) * head_size)
         state = pair_ref[head] + carry_ref[head] * far_ref[head].astype(F32)
-        carried = jnp.dot(
-            query_ref[:, columns].astype(F32), state, precision=lax.Precision.HIGHEST, preferred_element_type=F32
-        )
+        query = query_ref[:, columns]
+        high = state.astype(BF16)
+        rest = state - high.astype(F32)
+        middle = rest.astype(BF16)
+        low = (rest - middle.astype(F32)).astype(BF16)
+        carried = jnp.dot(query, high, preferred_element_type=F32)
+        carried = carried + jnp.dot(query, middle, preferred_element_type=F32)
+        carried = carried + jnp.dot(query, low, preferred_element_type=F32)
         total = mixed_ref[:, columns] + carried * scale_t_ref[:, head : head + 1]
         out_ref[:, columns] = total
         squares = squares + jnp.sum(total * total, axis=1, keepdims=True)
@@ -189,9 +194,10 @@
 
     link_1 = (code_2[-1] == code_1[0]) & (code_1[0] == code_1[-1])
     pair_state = state_1.astype(F32) + jnp.where(link_1, decay_1, 0.0)[:, None, None] * state_2.astype(F32)
+    pair_wire = pair_state.astype(BF16)
 
     relay_kv = jnp.concatenate([kv_2[: 2 * kv_rows], kv_1[: 2 * kv_rows], rows_of(jnp.concatenate([code_2, code_1]), head_size)])
-    state_far = shifted(pair_state.astype(BF16), "ctx", 2)
+    state_far = shifted(pair_wire, "ctx", 2)
     kv_far = shifted(relay_kv, "ctx", 2)
     keys_4 = kv_far[:kv_rows].reshape(kv_here, tok_rows, head_size)
     values_4 = kv_far[kv_rows : 2 * kv_rows].reshape(kv_here, tok_rows, head_size)

time: 80 us -> 80.2 us (level)
  no operation moved by 1% of the time
where the time goes in v14:
time: 80.2 us; the launch traced here: 79.5 us
  waiting for transfers between devices  16.8 us (21%)
  starting transfers between devices  16.5 us (21%)
  Pallas kernels  13.1 us (16%)
  other arithmetic  10.2 us (13%)
  local copies, waits for them, and re-layouts  9.31 us (12%)
  between operations  6.13 us (8%)
  blocking collectives  5.07 us (6%)
  matrix products  2.35 us (3%)
    ppermute x6, waiting for transfers between devices, shifted(): return lax.ppermute(block, axis, route)  16.8 us
    ppermute x6, starting transfers between devices, shifted(): return lax.ppermute(block, axis, route)  16.5 us
    psum x1, blocking collectives, on_device_body(): squares = lax.psum(squares[:, 0], 'tensor')  5.07 us
    pallas_call x1, Pallas kernels, intra_mixed(): pl.pallas_call(intra_kernel, out_shape=jax.ShapeDtypeStruct((tok_rows, wi...  5.03 us
    unnamed x24, local copies, waits for them, and re-layouts  5 us
    pallas_call x1, Pallas kernels, final_mixed(): pl.pallas_call(final_kernel, out_shape=(jax.ShapeDtypeStruct((tok_rows, w...  4.42 us
    pallas_call x1, Pallas kernels, local_state_of(): pl.pallas_call(state_kernel, out_shape=jax.ShapeDtypeStruct((heads_here,...  3.7 us
    convert_element_type x1, other arithmetic, on_device_body(): light_out = normed.reshape(tok_rows, heads_here * head_size).astype(BF16)  2.34 us
  transfers between devices with their start and end apart: 6, of which 2 were waited for; matrix products, arithmetic and copies ran while one was open for 15% of the time, Pallas kernels for 11%

profile of v14, /device:TPU:11, one launch (start us, length us, event | category | flops | bytes accessed | tf_op | source)
XLA Modules:
  0.0 79.5 jit_solution(5145696148631823394)
XLA Ops:
  0.6 0.0 copy-start.5
  0.6 1.0 %reduce_window_sum.13.decay_ref = f32[16,128]{1,0:T(8,128)S(1)} reduce-window(f32[16,128]{1,0:T(8,128)} %param.14, f32[]{:T(128)} %constant.10.clone.1), window={size=1x128 pad=0_0x127_0}, to_apply=%region_0.0 | reduce-window | flops 260096 | bytes 16388 | tf_op jit(solution)/shard_map/jit(cumsum)/reduce_window_sum | solution.py:165
  1.6 0.0 copy-start.3
  1.6 0.2 fusion.22
  1.8 1.2 %convert_add_fusion = (f32[128]{0:T(128)S(1)}, bf16[128]{0:T(256)(128)(2,1)S(1)}, f32[1,128]{1,0:T(1,128)}, f32[128,1]{0,1:T(1,128)S(1)}) fusion(s32[128]{0:T(128)} %param.19), kind=kLoop, calls=%fused_computation.65 | loop fusion | flops 384 | bytes 2304 | tf_op jit(solution)/shard_map/add | solution.py:164
  3.1 0.9 %copy.19 = bf16[128,256]{0,1:T(8,128)(2,1)S(1)} copy(bf16[128,256]{1,0:T(8,128)(2,1)} %param.17) | data formatting | bytes 131072 | tf_op args[7]
  4.0 0.1 copy.20
  4.2 1.0 %copy.21 = bf16[128,256]{0,1:T(8,128)(2,1)S(1)} copy(bf16[128,256]{1,0:T(8,128)(2,1)} %param.18) | data formatting | bytes 131072 | tf_op args[8]
  5.1 0.1 copy.22
  5.3 0.1 fusion.26
  5.4 3.2 %collective-permute-start = (bf16[528,128]{1,0:T(8,128)(2,1)S(1)}, bf16[528,128]{1,0:T(8,128)(2,1)S(1)}, u32[]{:S(2)}, u32[]{:S(2)}) collective-permute-start(bf16[528,128]{1,0:T(8,128)(2,1)S(1)} %pad_maximum_fusion.1), channel_id=1, source_target_pairs={{0,4},{2,6},{4,8},{6,10},{8,12},{10,14},{1,5},{3,7},{5,9},{7,11},{... | collective-permute-start | bytes 405512 | tf_op jit(solution)/shard_map/ppermute | solution.py:18
  8.6 3.2 %collective-permute-start.1 = (bf16[528,128]{1,0:T(8,128)(2,1)S(1)}, bf16[528,128]{1,0:T(8,128)(2,1)S(1)}, u32[]{:S(2)}, u32[]{:S(2)}) collective-permute-start(bf16[528,128]{1,0:T(8,128)(2,1)S(1)} %pad_maximum_fusion.1), channel_id=1, source_target_pairs={{0,2},{2,4},{4,6},{6,8},{8,10},{10,12},{12,14},{1,3},{3,5},{5,7},{... | collective-permute-start | bytes 405512 | tf_op jit(solution)/shard_map/ppermute | solution.py:18
  11.7 0.7 copy.23
  12.5 0.0 copy-start
  12.5 0.7 copy.24.code_col_ref.code_ref
  13.2 3.7 %shard_map.114 = bf16[16,128,128]{2,1,0:T(8,128)(2,1)} custom-call(f32[128,16]{1,0:T(8,128)} %bitcast.82, f32[128,1]{1,0:T(8,128)} %copy.24.code_col_ref.code_ref, bf16[128,2048]{1,0:T(8,128)(2,1)} %key_ref.3, bf16[128,2048]{1,0:T(8,128)(2,1)} %value_ref.3), custom_call_target="tpu_custom_call" | custom-call | flops 67108864 | bytes 786432 | tf_op jit(solution)/shard_map/pallas_call | solution.py:39
  16.9 3.1 %collective-permute-start.3 = (bf16[16,128,128]{2,1,0:T(8,128)(2,1)}, bf16[16,128,128]{2,1,0:T(8,128)(2,1)S(1)}, u32[]{:S(2)}, u32[]{:S(2)}) collective-permute-start(bf16[16,128,128]{2,1,0:T(8,128)(2,1)} %shard_map.114), channel_id=1, source_target_pairs={{0,2},{2,4},{4,6},{6,8},{8,10},{10,12},{12,14},{1,3},{3,5},{5,7},{... | collective-permute-start | bytes 1572872 | tf_op jit(solution)/shard_map/ppermute | solution.py:18
  20.0 1.9 %collective-permute-start.4 = (bf16[16,128,128]{2,1,0:T(8,128)(2,1)}, bf16[16,128,128]{2,1,0:T(8,128)(2,1)S(1)}, u32[]{:S(2)}, u32[]{:S(2)}) collective-permute-start(bf16[16,128,128]{2,1,0:T(8,128)(2,1)} %shard_map.114), channel_id=1, source_target_pairs={{0,4},{2,6},{4,8},{6,10},{8,12},{10,14},{1,5},{3,7},{5,9},{7,11},{... | collective-permute-start | bytes 1572872 | tf_op jit(solution)/shard_map/ppermute | solution.py:18
  21.9 1.1 %copy.36 = bf16[16,8,16,128]{3,2,1,0:T(8,128)(2,1)S(1)} copy(bf16[16,8,16,128]{3,1,2,0:T(8,128)(2,1)} %bitcast.87) | data formatting | bytes 1048576
  23.1 0.0 copy-done.3
  23.1 5.0 %shard_map.113.mixed_ref = f32[128,2048]{1,0:T(8,128)} custom-call(f32[16,128]{1,0:T(8,128)} %copy-done.3, f32[128,16]{1,0:T(8,128)} %bitcast.83, f32[1,128]{1,0:T(1,128)} %get-tuple-element.30.code_row_ref, f32[128,1]{1,0:T(8,128)} %copy.24.code_col_ref.code_ref, bf16[128,2048]{1,0:T(8,128)(2,1)} %query_ref.3, bf16[128,2048]{1,0:T(8,128)(2,1)} %key_ref.3, ...), custom_call_target="tpu_custom_call" | custom-call | flops 134217728 | bytes 2621440 | tf_op jit(solution)/shard_map/pallas_call | solution.py:69
  28.1 0.0 collective-permute-done
  28.2 0.0 collective-permute-done.1
  28.3 1.9 %collective-permute-start.2 = (bf16[1040,128]{1,0:T(8,128)(2,1)S(1)}, bf16[1040,128]{1,0:T(8,128)(2,1)S(1)}, u32[]{:S(2)}, u32[]{:S(2)}) collective-permute-start(bf16[1040,128]{1,0:T(8,128)(2,1)S(1)} %pad_maximum_fusion), channel_id=1, source_target_pairs={{0,4},{2,6},{4,8},{6,10},{8,12},{10,14},{1,5},{3,7},{5,9},{7,11},{... | collective-permute-start | bytes 798728 | tf_op jit(solution)/shard_map/ppermute | solution.py:18
  30.2 0.6 fusion.43
  30.8 0.6 fusion.42
  34.0 0.1 broadcast_select_fusion
  34.1 0.0 copy-done.5
  34.1 0.6 broadcast_compare_fusion
  34.7 0.1 copy.29
  34.8 0.1 copy.30
  36.2 0.0 copy-done
  36.3 0.7 exponential_select_fusion.scale_t_ref
  37.0 11.1 %collective-permute-done.2 = bf16[1040,128]{1,0:T(8,128)(2,1)S(1)} collective-permute-done((bf16[1040,128]{1,0:T(8,128)(2,1)S(1)}, bf16[1040,128]{1,0:T(8,128)(2,1)S(1)}, u32[]{:S(2)}, u32[]{:S(2)}) %collective-permute-start.2) | collective-permute-done | bytes 266272 | tf_op jit(solution)/shard_map/ppermute | solution.py:18
  48.2 0.1 copy.27
  48.4 0.1 copy.28
  48.5 0.6 slice.112
  49.1 0.2 fusion.15
  49.3 0.9 %fusion.2 = (f32[2,8,128]{2,1,0:T(8,128)S(1)}, f32[2,640,128,8]{2,1,3,0:T(8,128)S(1)}) fusion(pred[128,640]{0,1:T(8,128)(4,1)S(1)} %fusion.15, bf16[128,2,8,128]{3,2,1,0:T(8,128)(2,1)S(1)} %bitcast.81, bf16[2,640,128]{2,1,0:T(8,128)(2,1)S(1)} %bitcast_dynamic-update-slice_fusion), kind=kOutput, calls=%fused_computation.4 | convolution fusion | flops 339474432 | bytes 6184960 | tf_op jit(solution)/shard_map/tkgd,ksd->kgts/dot_general | solution.py:118
  50.3 1.1 %fusion = f32[2,8,128]{2,1,0:T(8,128)S(1)} fusion(f32[2,640,128,8]{2,1,3,0:T(8,128)S(1)} %get-tuple-element.40, f32[2,8,128]{2,1,0:T(8,128)S(1)} %get-tuple-element.39, pred[128,640]{0,1:T(8,128)(4,1)S(1)} %fusion.15), kind=kLoop, calls=%fused_computation.2 | loop fusion | flops 5240832 | bytes 5341184 | tf_op jit(solution)/shard_map/reduce_sum | solution.py:122
  51.4 0.0 collective-permute-done.3
  51.4 0.0 collective-permute-done.4
  51.4 1.3 %fusion.38 = (bf16[16,128,128]{2,1,0:T(8,128)(2,1)S(1)}, f32[16,128,128]{2,1,0:T(8,128)}) fusion(bf16[16,128,128]{2,1,0:T(8,128)(2,1)S(1)} %collective-permute-done.4, f32[16]{0:T(128)S(1)} %get-tuple-element.12, bf16[16,128,128]{2,1,0:T(8,128)(2,1)S(1)} %collective-permute-done.3), kind=kLoop, calls=%fused_computation.76 | loop fusion | flops 1310720 | bytes 2621504 | tf_op jit(solution)/shard_map/convert_element_type | solution.py:197
  52.7 3.2 %collective-permute-start.5 = (bf16[16,128,128]{2,1,0:T(8,128)(2,1)S(1)}, bf16[16,128,128]{2,1,0:T(8,128)(2,1)S(1)}, u32[]{:S(2)}, u32[]{:S(2)}) collective-permute-start(bf16[16,128,128]{2,1,0:T(8,128)(2,1)S(1)} %get-tuple-element.10), channel_id=1, source_target_pairs={{0,4},{2,6},{4,8},{6,10},{8,12},{10,14},{1,5},{3,7},{5,9},{7,11},{... | collective-permute-start | bytes 1572872 | tf_op jit(solution)/shard_map/ppermute | solution.py:18
  55.9 0.0 copy-start.1
  55.9 0.0 copy-start.4
  55.9 1.4 %divide_convert_fusion = bf16[128,2,8,128]{0,3,2,1:T(8,128)(2,1)S(1)} fusion(f32[2,640,128,8]{2,1,3,0:T(8,128)S(1)} %get-tuple-element.40, f32[2,8,128]{2,1,0:T(8,128)S(1)} %get-tuple-element.39, pred[128,640]{0,1:T(8,128)(4,1)S(1)} %fusion.15, f32[128,2,8]{0,2,1:T(8,128)S(1)} %bitcast.99, bf16[2,640,128]{1,2,0:T(8,128)(2,1)S(1)} %constant_dynamic-update-slice_fusion), kind=kOutput, calls=%fused_computation.8 | convolution fusion | flops 341311488 | bytes 6193152 | tf_op jit(solution)/shard_map/kgts,ksd->kgtd/dot_general | solution.py:123
  57.4 1.0 %copy.32 = bf16[128,2048]{1,0:T(8,128)(2,1)} copy(bf16[128,2048]{0,1:T(8,128)(2,1)S(1)} %bitcast.88) | data formatting | bytes 1048576
  59.7 0.6 broadcast_select_fusion.1.carry_ref
  60.3 5.7 %collective-permute-done.5.far_ref = bf16[16,128,128]{2,1,0:T(8,128)(2,1)S(1)} collective-permute-done((bf16[16,128,128]{2,1,0:T(8,128)(2,1)S(1)}, bf16[16,128,128]{2,1,0:T(8,128)(2,1)S(1)}, u32[]{:S(2)}, u32[]{:S(2)}) %collective-permute-start.5) | collective-permute-done | bytes 524320 | tf_op jit(solution)/shard_map/ppermute | solution.py:18
  66.0 0.0 copy-start.2
  66.0 0.8 copy-done.2
  66.8 4.4 %shard_map.115 = (f32[128,2048]{1,0:T(8,128)}, f32[128,1]{1,0:T(8,128)}) custom-call(f32[16]{0:T(128)} %broadcast_select_fusion.1.carry_ref, f32[128,16]{1,0:T(8,128)} %exponential_select_fusion.scale_t_ref, bf16[128,2048]{1,0:T(8,128)(2,1)} %query_ref.3, f32[128,2048]{1,0:T(8,128)} %shard_map.113.mixed_ref, f32[16,128,128]{2,1,0:T(8,128)} %get-tuple-element.11.pair_ref, ...), custom_call_target="tpu_custom_call" | custom-call | flops 402653184 | bytes 3145728 | tf_op jit(solution)/shard_map/pallas_call | solution.py:101
  71.2 0.9 %reduce.1 = f32[128]{0:T(128)S(1)} reduce(f32[128,1]{1,0:T(8,128)} %get-tuple-element.5, f32[]{:T(128)} %constant.29), dimensions={1}, to_apply=%get-tuple-element.5.reduce_sub_computation | reduce | bytes 1028 | tf_op jit(solution)/shard_map/pallas_call | solution.py:101
  72.1 5.1 %psum.7 = f32[128]{0:T(128)S(1)} all-reduce(f32[128]{0:T(128)S(1)} %reduce.1), channel_id=1, replica_groups=mesh['groups'=2,'ctx'=8,'tensor'=2] {'tensor'}, use_global_device_ids=true, to_apply=%region_1.2 | all-reduce | flops 128 | bytes 1024 | tf_op jit(solution)/shard_map/psum | solution.py:215
  77.2 0.0 copy-done.1
  77.2 0.0 copy-done.4
  77.2 2.3 %multiply_convert_fusion = bf16[128,2048]{1,0:T(8,128)(2,1)} fusion(bf16[128,2048]{1,0:T(8,128)(2,1)S(1)} %copy-done.1, f32[128,2048]{1,0:T(8,128)} %get-tuple-element.4, f32[2048]{0:T(1024)S(1)} %copy-done.4, f32[128]{0:T(128)S(1)} %add_rsqrt_fusion), kind=kLoop, calls=%fused_computation.9 | loop fusion | flops 2097152 | bytes 2105856 | tf_op jit(solution)/shard_map/convert_element_type | solution.py:220
  (29 shorter events, 0.3 us)
Async XLA Ops:
  0.6 33.4 %copy-start.5 = (s32[128]{0:T(128)S(1)}, s32[128]{0:T(128)}, u32[]{:S(2)}) copy-start(s32[128]{0:T(128)} %param.19) | copy-start | bytes 1540
  1.6 21.5 %copy-start.3 = (f32[16,128]{1,0:T(8,128)}, f32[16,128]{1,0:T(8,128)S(1)}, u32[]{:S(2)}) copy-start(f32[16,128]{1,0:T(8,128)S(1)} %reduce_window_sum.13.decay_ref) | copy-start | bytes 24580
  5.4 22.8 %collective-permute-start = (bf16[528,128]{1,0:T(8,128)(2,1)S(1)}, bf16[528,128]{1,0:T(8,128)(2,1)S(1)}, u32[]{:S(2)}, u32[]{:S(2)}) collective-permute-start(bf16[528,128]{1,0:T(8,128)(2,1)S(1)} %pad_maximum_fusion.1), channel_id=1, source_target_pairs={{0,4},{2,6},{4,8},{6,10},{8,12},{10,14},{1,5},{3,7},{5,9},{7,11},{... | collective-permute-start | bytes 405512 | tf_op jit(solution)/shard_map/ppermute | solution.py:18
  8.6 19.6 %collective-permute-start.1 = (bf16[528,128]{1,0:T(8,128)(2,1)S(1)}, bf16[528,128]{1,0:T(8,128)(2,1)S(1)}, u32[]{:S(2)}, u32[]{:S(2)}) collective-permute-start(bf16[528,128]{1,0:T(8,128)(2,1)S(1)} %pad_maximum_fusion.1), channel_id=1, source_target_pairs={{0,2},{2,4},{4,6},{6,8},{8,10},{10,12},{12,14},{1,3},{3,5},{5,7},{... | collective-permute-start | bytes 405512 | tf_op jit(solution)/shard_map/ppermute | solution.py:18
  12.5 23.8 %copy-start = (f32[16,128]{0,1:T(8,128)S(1)}, f32[16,128]{0,1:T(8,128)}, u32[]{:S(2)}) copy-start(f32[16,128]{0,1:T(8,128)} %copy.23) | copy-start | bytes 24580
  16.9 34.5 %collective-permute-start.3 = (bf16[16,128,128]{2,1,0:T(8,128)(2,1)}, bf16[16,128,128]{2,1,0:T(8,128)(2,1)S(1)}, u32[]{:S(2)}, u32[]{:S(2)}) collective-permute-start(bf16[16,128,128]{2,1,0:T(8,128)(2,1)} %shard_map.114), channel_id=1, source_target_pairs={{0,2},{2,4},{4,6},{6,8},{8,10},{10,12},{12,14},{1,3},{3,5},{5,7},{... | collective-permute-start | bytes 1572872 | tf_op jit(solution)/shard_map/ppermute | solution.py:18
  20.0 31.3 %collective-permute-start.4 = (bf16[16,128,128]{2,1,0:T(8,128)(2,1)}, bf16[16,128,128]{2,1,0:T(8,128)(2,1)S(1)}, u32[]{:S(2)}, u32[]{:S(2)}) collective-permute-start(bf16[16,128,128]{2,1,0:T(8,128)(2,1)} %shard_map.114), channel_id=1, source_target_pairs={{0,4},{2,6},{4,8},{6,10},{8,12},{10,14},{1,5},{3,7},{5,9},{7,11},{... | collective-permute-start | bytes 1572872 | tf_op jit(solution)/shard_map/ppermute | solution.py:18
  28.3 19.8 %collective-permute-start.2 = (bf16[1040,128]{1,0:T(8,128)(2,1)S(1)}, bf16[1040,128]{1,0:T(8,128)(2,1)S(1)}, u32[]{:S(2)}, u32[]{:S(2)}) collective-permute-start(bf16[1040,128]{1,0:T(8,128)(2,1)S(1)} %pad_maximum_fusion), channel_id=1, source_target_pairs={{0,4},{2,6},{4,8},{6,10},{8,12},{10,14},{1,5},{3,7},{5,9},{7,11},{... | collective-permute-start | bytes 798728 | tf_op jit(solution)/shard_map/ppermute | solution.py:18
  52.7 13.3 %collective-permute-start.5 = (bf16[16,128,128]{2,1,0:T(8,128)(2,1)S(1)}, bf16[16,128,128]{2,1,0:T(8,128)(2,1)S(1)}, u32[]{:S(2)}, u32[]{:S(2)}) collective-permute-start(bf16[16,128,128]{2,1,0:T(8,128)(2,1)S(1)} %get-tuple-element.10), channel_id=1, source_target_pairs={{0,4},{2,6},{4,8},{6,10},{8,12},{10,14},{1,5},{3,7},{5,9},{7,11},{... | collective-permute-start | bytes 1572872 | tf_op jit(solution)/shard_map/ppermute | solution.py:18
  55.9 21.3 %copy-start.1 = (bf16[128,2048]{1,0:T(8,128)(2,1)S(1)}, bf16[128,2048]{1,0:T(8,128)(2,1)}, u32[]{:S(2)}) copy-start(bf16[128,2048]{1,0:T(8,128)(2,1)} %param.13) | copy-start | bytes 1572868
  55.9 21.3 %copy-start.4 = (f32[2048]{0:T(1024)S(1)}, f32[2048]{0:T(1024)}, u32[]{:S(2)}) copy-start(f32[2048]{0:T(1024)} %param.15) | copy-start | bytes 24580
  66.0 0.8 copy-start.2

commit v15 on v10

--- a/solution.py
+++ b/solution.py
@@ -189,9 +189,10 @@
 
     link_1 = (code_2[-1] == code_1[0]) & (code_1[0] == code_1[-1])
     pair_state = state_1.astype(F32) + jnp.where(link_1, decay_1, 0.0)[:, None, None] * state_2.astype(F32)
+    pair_wire = pair_state.astype(BF16)
 
     relay_kv = jnp.concatenate([kv_2[: 2 * kv_rows], kv_1[: 2 * kv_rows], rows_of(jnp.concatenate([code_2, code_1]), head_size)])
-    state_far = shifted(pair_state.astype(BF16), "ctx", 2)
+    state_far = shifted(pair_wire, "ctx", 2)
     kv_far = shifted(relay_kv, "ctx", 2)
     keys_4 = kv_far[:kv_rows].reshape(kv_here, tok_rows, head_size)
     values_4 = kv_far[kv_rows : 2 * kv_rows].reshape(kv_here, tok_rows, head_size)
@@ -206,11 +207,11 @@
     scale_in = jnp.where(uses_state[None, :], jnp.exp(decay_sum), 0.0)
     mixed, squares = final_mixed(carry_scale, scale_in, light_query, mixed, pair_state, state_far)
     mixed = mixed.reshape(tok_rows, heads_here, head_size)
-    squares = lax.psum(squares[:, 0], "tensor")
+    squares = lax.psum(squares, "tensor")
     features = heads_here * head_size * lax.axis_size("tensor")
     inverse = lax.rsqrt(squares / features + 1e-06)
     gate_open = jax.nn.sigmoid(light_gate.astype(F32)).reshape(tok_rows, heads_here, head_size)
-    normed = mixed * inverse[:, None, None] * norm_gain.reshape(heads_here, head_size) * gate_open
+    normed = mixed * inverse[:, :, None] * norm_gain.reshape(heads_here, head_size) * gate_open
     light_out = normed.reshape(tok_rows, heads_here * head_size).astype(BF16)
 
     key_window = jnp.concatenate([keys_4, keys_3, keys_2, keys_1, own_keys], axis=1)

time: 80 us -> 81.1 us (1.014)
  blocking collectives: 5.08 us -> 6.97 us
  other arithmetic: 10.2 us -> 9.36 us
    psum x1, blocking collectives: 5.08 us -> 6.97 us  [on_device_body(): squares = lax.psum(squares, 'tensor')]
    pallas_call x1 -> x0, other arithmetic: 0.94 us -> none  [final_mixed(): pl.pallas_call(final_kernel, out_shape=(jax.ShapeDtypeStruct((tok_rows, w...]
where the time goes in v15:
time: 81.1 us; the launch traced here: 80.4 us
  waiting for transfers between devices  16.8 us (21%)
  starting transfers between devices  16.5 us (20%)
  Pallas kernels  12.9 us (16%)
  other arithmetic  9.36 us (12%)
  local copies, waits for them, and re-layouts  9.31 us (11%)
  blocking collectives  6.97 us (9%)
  between operations  6.15 us (8%)
  matrix products  2.35 us (3%)
    ppermute x6, waiting for transfers between devices, shifted(): return lax.ppermute(block, axis, route)  16.8 us
    ppermute x6, starting transfers between devices, shifted(): return lax.ppermute(block, axis, route)  16.5 us
    psum x1, blocking collectives, on_device_body(): squares = lax.psum(squares, 'tensor')  6.97 us
    pallas_call x1, Pallas kernels, intra_mixed(): pl.pallas_call(intra_kernel, out_shape=jax.ShapeDtypeStruct((tok_rows, wi...  5.03 us
    unnamed x24, local copies, waits for them, and re-layouts  5 us
    pallas_call x1, Pallas kernels, final_mixed(): pl.pallas_call(final_kernel, out_shape=(jax.ShapeDtypeStruct((tok_rows, w...  4.22 us
    pallas_call x1, Pallas kernels, local_state_of(): pl.pallas_call(state_kernel, out_shape=jax.ShapeDtypeStruct((heads_here,...  3.7 us
    convert_element_type x1, other arithmetic, on_device_body(): light_out = normed.reshape(tok_rows, heads_here * head_size).astype(BF16)  2.34 us
  transfers between devices with their start and end apart: 6, of which 2 were waited for; matrix products, arithmetic and copies ran while one was open for 15% of the time, Pallas kernels for 11%

profile of v15, /device:TPU:11, one launch (start us, length us, event | category | flops | bytes accessed | tf_op | source)
XLA Modules:
  0.0 80.4 jit_solution(16270081114391254669)
XLA Ops:
  0.6 0.0 copy-start.5
  0.6 1.0 %reduce_window_sum.13.decay_ref = f32[16,128]{1,0:T(8,128)S(1)} reduce-window(f32[16,128]{1,0:T(8,128)} %param.14, f32[]{:T(128)} %constant.10.clone.1), window={size=1x128 pad=0_0x127_0}, to_apply=%region_0.0 | reduce-window | flops 260096 | bytes 16388 | tf_op jit(solution)/shard_map/jit(cumsum)/reduce_window_sum | solution.py:160
  1.6 0.0 copy-start.3
  1.6 0.2 fusion.22
  1.8 1.2 %convert_add_fusion = (f32[128]{0:T(128)S(1)}, bf16[128]{0:T(256)(128)(2,1)S(1)}, f32[1,128]{1,0:T(1,128)}, f32[128,1]{0,1:T(1,128)S(1)}) fusion(s32[128]{0:T(128)} %param.19), kind=kLoop, calls=%fused_computation.65 | loop fusion | flops 384 | bytes 2304 | tf_op jit(solution)/shard_map/add | solution.py:159
  3.1 0.9 %copy.19 = bf16[128,256]{0,1:T(8,128)(2,1)S(1)} copy(bf16[128,256]{1,0:T(8,128)(2,1)} %param.17) | data formatting | bytes 131072 | tf_op args[7]
  4.0 0.1 copy.20
  4.2 1.0 %copy.21 = bf16[128,256]{0,1:T(8,128)(2,1)S(1)} copy(bf16[128,256]{1,0:T(8,128)(2,1)} %param.18) | data formatting | bytes 131072 | tf_op args[8]
  5.1 0.1 copy.22
  5.3 0.1 fusion.26
  5.4 3.2 %collective-permute-start = (bf16[528,128]{1,0:T(8,128)(2,1)S(1)}, bf16[528,128]{1,0:T(8,128)(2,1)S(1)}, u32[]{:S(2)}, u32[]{:S(2)}) collective-permute-start(bf16[528,128]{1,0:T(8,128)(2,1)S(1)} %pad_maximum_fusion.1), channel_id=1, source_target_pairs={{0,4},{2,6},{4,8},{6,10},{8,12},{10,14},{1,5},{3,7},{5,9},{7,11},{... | collective-permute-start | bytes 405512 | tf_op jit(solution)/shard_map/ppermute | solution.py:18
  8.6 3.2 %collective-permute-start.1 = (bf16[528,128]{1,0:T(8,128)(2,1)S(1)}, bf16[528,128]{1,0:T(8,128)(2,1)S(1)}, u32[]{:S(2)}, u32[]{:S(2)}) collective-permute-start(bf16[528,128]{1,0:T(8,128)(2,1)S(1)} %pad_maximum_fusion.1), channel_id=1, source_target_pairs={{0,2},{2,4},{4,6},{6,8},{8,10},{10,12},{12,14},{1,3},{3,5},{5,7},{... | collective-permute-start | bytes 405512 | tf_op jit(solution)/shard_map/ppermute | solution.py:18
  11.7 0.7 copy.23
  12.5 0.0 copy-start
  12.5 0.7 copy.24.code_col_ref.code_ref
  13.2 3.7 %shard_map.114 = bf16[16,128,128]{2,1,0:T(8,128)(2,1)} custom-call(f32[128,16]{1,0:T(8,128)} %bitcast.82, f32[128,1]{1,0:T(8,128)} %copy.24.code_col_ref.code_ref, bf16[128,2048]{1,0:T(8,128)(2,1)} %key_ref.3, bf16[128,2048]{1,0:T(8,128)(2,1)} %value_ref.3), custom_call_target="tpu_custom_call" | custom-call | flops 67108864 | bytes 786432 | tf_op jit(solution)/shard_map/pallas_call | solution.py:39
  16.9 3.1 %collective-permute-start.3 = (bf16[16,128,128]{2,1,0:T(8,128)(2,1)}, bf16[16,128,128]{2,1,0:T(8,128)(2,1)S(1)}, u32[]{:S(2)}, u32[]{:S(2)}) collective-permute-start(bf16[16,128,128]{2,1,0:T(8,128)(2,1)} %shard_map.114), channel_id=1, source_target_pairs={{0,2},{2,4},{4,6},{6,8},{8,10},{10,12},{12,14},{1,3},{3,5},{5,7},{... | collective-permute-start | bytes 1572872 | tf_op jit(solution)/shard_map/ppermute | solution.py:18
  20.0 1.9 %collective-permute-start.4 = (bf16[16,128,128]{2,1,0:T(8,128)(2,1)}, bf16[16,128,128]{2,1,0:T(8,128)(2,1)S(1)}, u32[]{:S(2)}, u32[]{:S(2)}) collective-permute-start(bf16[16,128,128]{2,1,0:T(8,128)(2,1)} %shard_map.114), channel_id=1, source_target_pairs={{0,4},{2,6},{4,8},{6,10},{8,12},{10,14},{1,5},{3,7},{5,9},{7,11},{... | collective-permute-start | bytes 1572872 | tf_op jit(solution)/shard_map/ppermute | solution.py:18
  21.9 1.1 %copy.36 = bf16[16,8,16,128]{3,2,1,0:T(8,128)(2,1)S(1)} copy(bf16[16,8,16,128]{3,1,2,0:T(8,128)(2,1)} %bitcast.87) | data formatting | bytes 1048576
  23.1 0.0 copy-done.3
  23.1 5.0 %shard_map.113.mixed_ref = f32[128,2048]{1,0:T(8,128)} custom-call(f32[16,128]{1,0:T(8,128)} %copy-done.3, f32[128,16]{1,0:T(8,128)} %bitcast.83, f32[1,128]{1,0:T(1,128)} %get-tuple-element.30.code_row_ref, f32[128,1]{1,0:T(8,128)} %copy.24.code_col_ref.code_ref, bf16[128,2048]{1,0:T(8,128)(2,1)} %query_ref.3, bf16[128,2048]{1,0:T(8,128)(2,1)} %key_ref.3, ...), custom_call_target="tpu_custom_call" | custom-call | flops 134217728 | bytes 2621440 | tf_op jit(solution)/shard_map/pallas_call | solution.py:69
  28.1 0.0 collective-permute-done
  28.2 0.0 collective-permute-done.1
  28.3 1.9 %collective-permute-start.2 = (bf16[1040,128]{1,0:T(8,128)(2,1)S(1)}, bf16[1040,128]{1,0:T(8,128)(2,1)S(1)}, u32[]{:S(2)}, u32[]{:S(2)}) collective-permute-start(bf16[1040,128]{1,0:T(8,128)(2,1)S(1)} %pad_maximum_fusion), channel_id=1, source_target_pairs={{0,4},{2,6},{4,8},{6,10},{8,12},{10,14},{1,5},{3,7},{5,9},{7,11},{... | collective-permute-start | bytes 798728 | tf_op jit(solution)/shard_map/ppermute | solution.py:18
  30.2 0.6 fusion.43
  30.8 0.6 fusion.42
  34.0 0.1 broadcast_select_fusion
  34.1 0.0 copy-done.5
  34.1 0.6 broadcast_compare_fusion
  34.7 0.1 copy.29
  34.8 0.1 copy.30
  36.2 0.0 copy-done
  36.3 0.7 exponential_select_fusion.scale_t_ref
  37.0 11.1 %collective-permute-done.2 = bf16[1040,128]{1,0:T(8,128)(2,1)S(1)} collective-permute-done((bf16[1040,128]{1,0:T(8,128)(2,1)S(1)}, bf16[1040,128]{1,0:T(8,128)(2,1)S(1)}, u32[]{:S(2)}, u32[]{:S(2)}) %collective-permute-start.2) | collective-permute-done | bytes 266272 | tf_op jit(solution)/shard_map/ppermute | solution.py:18
  48.2 0.1 copy.27
  48.4 0.1 copy.28
  48.5 0.6 slice.112
  49.1 0.2 fusion.15
  49.3 0.9 %fusion.2 = (f32[2,8,128]{2,1,0:T(8,128)S(1)}, f32[2,640,128,8]{2,1,3,0:T(8,128)S(1)}) fusion(pred[128,640]{0,1:T(8,128)(4,1)S(1)} %fusion.15, bf16[128,2,8,128]{3,2,1,0:T(8,128)(2,1)S(1)} %bitcast.81, bf16[2,640,128]{2,1,0:T(8,128)(2,1)S(1)} %bitcast_dynamic-update-slice_fusion), kind=kOutput, calls=%fused_computation.4 | convolution fusion | flops 339474432 | bytes 6184960 | tf_op jit(solution)/shard_map/tkgd,ksd->kgts/dot_general | solution.py:113
  50.3 1.1 %fusion = f32[2,8,128]{2,1,0:T(8,128)S(1)} fusion(f32[2,640,128,8]{2,1,3,0:T(8,128)S(1)} %get-tuple-element.40, f32[2,8,128]{2,1,0:T(8,128)S(1)} %get-tuple-element.39, pred[128,640]{0,1:T(8,128)(4,1)S(1)} %fusion.15), kind=kLoop, calls=%fused_computation.2 | loop fusion | flops 5240832 | bytes 5341184 | tf_op jit(solution)/shard_map/reduce_sum | solution.py:117
  51.4 0.0 collective-permute-done.3
  51.4 0.0 collective-permute-done.4
  51.4 1.3 %fusion.38 = (bf16[16,128,128]{2,1,0:T(8,128)(2,1)S(1)}, f32[16,128,128]{2,1,0:T(8,128)}) fusion(bf16[16,128,128]{2,1,0:T(8,128)(2,1)S(1)} %collective-permute-done.4, f32[16]{0:T(128)S(1)} %get-tuple-element.12, bf16[16,128,128]{2,1,0:T(8,128)(2,1)S(1)} %collective-permute-done.3), kind=kLoop, calls=%fused_computation.76 | loop fusion | flops 1310720 | bytes 2621504 | tf_op jit(solution)/shard_map/convert_element_type | solution.py:192
  52.7 3.2 %collective-permute-start.5 = (bf16[16,128,128]{2,1,0:T(8,128)(2,1)S(1)}, bf16[16,128,128]{2,1,0:T(8,128)(2,1)S(1)}, u32[]{:S(2)}, u32[]{:S(2)}) collective-permute-start(bf16[16,128,128]{2,1,0:T(8,128)(2,1)S(1)} %get-tuple-element.10), channel_id=1, source_target_pairs={{0,4},{2,6},{4,8},{6,10},{8,12},{10,14},{1,5},{3,7},{5,9},{7,11},{... | collective-permute-start | bytes 1572872 | tf_op jit(solution)/shard_map/ppermute | solution.py:18
  55.9 0.0 copy-start.1
  55.9 0.0 copy-start.4
  55.9 1.4 %divide_convert_fusion = bf16[128,2,8,128]{0,3,2,1:T(8,128)(2,1)S(1)} fusion(f32[2,640,128,8]{2,1,3,0:T(8,128)S(1)} %get-tuple-element.40, f32[2,8,128]{2,1,0:T(8,128)S(1)} %get-tuple-element.39, pred[128,640]{0,1:T(8,128)(4,1)S(1)} %fusion.15, f32[128,2,8]{0,2,1:T(8,128)S(1)} %bitcast.99, bf16[2,640,128]{1,2,0:T(8,128)(2,1)S(1)} %constant_dynamic-update-slice_fusion), kind=kOutput, calls=%fused_computation.8 | convolution fusion | flops 341311488 | bytes 6193152 | tf_op jit(solution)/shard_map/kgts,ksd->kgtd/dot_general | solution.py:118
  57.4 1.0 %copy.32 = bf16[128,2048]{1,0:T(8,128)(2,1)} copy(bf16[128,2048]{0,1:T(8,128)(2,1)S(1)} %bitcast.88) | data formatting | bytes 1048576
  59.7 0.6 broadcast_select_fusion.1.carry_ref
  60.3 5.7 %collective-permute-done.5.far_ref = bf16[16,128,128]{2,1,0:T(8,128)(2,1)S(1)} collective-permute-done((bf16[16,128,128]{2,1,0:T(8,128)(2,1)S(1)}, bf16[16,128,128]{2,1,0:T(8,128)(2,1)S(1)}, u32[]{:S(2)}, u32[]{:S(2)}) %collective-permute-start.5) | collective-permute-done | bytes 524320 | tf_op jit(solution)/shard_map/ppermute | solution.py:18
  66.0 0.0 copy-start.2
  66.0 0.8 copy-done.2
  66.8 4.2 %shard_map.115 = (f32[128,2048]{1,0:T(8,128)}, f32[128,1]{1,0:T(8,128)}) custom-call(f32[16]{0:T(128)} %broadcast_select_fusion.1.carry_ref, f32[128,16]{1,0:T(8,128)} %exponential_select_fusion.scale_t_ref, bf16[128,2048]{1,0:T(8,128)(2,1)} %query_ref.3, f32[128,2048]{1,0:T(8,128)} %shard_map.113.mixed_ref, f32[16,128,128]{2,1,0:T(8,128)} %get-tuple-element.11.pair_ref, ...), custom_call_target="tpu_custom_call" | custom-call | flops 402653184 | bytes 3145728 | tf_op jit(solution)/shard_map/pallas_call | solution.py:96
  71.0 7.0 %psum.7 = f32[128,1]{1,0:T(8,128)S(1)} all-reduce(f32[128,1]{1,0:T(8,128)} %get-tuple-element.5), channel_id=1, replica_groups=mesh['groups'=2,'ctx'=8,'tensor'=2] {'tensor'}, use_global_device_ids=true, to_apply=%region_1.2 | all-reduce | flops 128 | bytes 1024 | tf_op jit(solution)/shard_map/psum | solution.py:210
  78.0 0.1 rsqrt_reduce_fusion
  78.1 0.0 copy-done.1
  78.1 0.0 copy-done.4
  78.1 2.3 %multiply_convert_fusion = bf16[128,2048]{1,0:T(8,128)(2,1)} fusion(bf16[128,2048]{1,0:T(8,128)(2,1)S(1)} %copy-done.1, f32[128,2048]{1,0:T(8,128)} %get-tuple-element.4, f32[2048]{0:T(1024)S(1)} %copy-done.4, f32[128]{0:T(128)S(1)} %rsqrt_reduce_fusion), kind=kLoop, calls=%fused_computation.9 | loop fusion | flops 2097152 | bytes 2105856 | tf_op jit(solution)/shard_map/convert_element_type | solution.py:215
  (28 shorter events, 0.3 us)
Async XLA Ops:
  0.6 33.4 %copy-start.5 = (s32[128]{0:T(128)S(1)}, s32[128]{0:T(128)}, u32[]{:S(2)}) copy-start(s32[128]{0:T(128)} %param.19) | copy-start | bytes 1540
  1.6 21.5 %copy-start.3 = (f32[16,128]{1,0:T(8,128)}, f32[16,128]{1,0:T(8,128)S(1)}, u32[]{:S(2)}) copy-start(f32[16,128]{1,0:T(8,128)S(1)} %reduce_window_sum.13.decay_ref) | copy-start | bytes 24580
  5.4 22.8 %collective-permute-start = (bf16[528,128]{1,0:T(8,128)(2,1)S(1)}, bf16[528,128]{1,0:T(8,128)(2,1)S(1)}, u32[]{:S(2)}, u32[]{:S(2)}) collective-permute-start(bf16[528,128]{1,0:T(8,128)(2,1)S(1)} %pad_maximum_fusion.1), channel_id=1, source_target_pairs={{0,4},{2,6},{4,8},{6,10},{8,12},{10,14},{1,5},{3,7},{5,9},{7,11},{... | collective-permute-start | bytes 405512 | tf_op jit(solution)/shard_map/ppermute | solution.py:18
  8.6 19.6 %collective-permute-start.1 = (bf16[528,128]{1,0:T(8,128)(2,1)S(1)}, bf16[528,128]{1,0:T(8,128)(2,1)S(1)}, u32[]{:S(2)}, u32[]{:S(2)}) collective-permute-start(bf16[528,128]{1,0:T(8,128)(2,1)S(1)} %pad_maximum_fusion.1), channel_id=1, source_target_pairs={{0,2},{2,4},{4,6},{6,8},{8,10},{10,12},{12,14},{1,3},{3,5},{5,7},{... | collective-permute-start | bytes 405512 | tf_op jit(solution)/shard_map/ppermute | solution.py:18
  12.5 23.8 %copy-start = (f32[16,128]{0,1:T(8,128)S(1)}, f32[16,128]{0,1:T(8,128)}, u32[]{:S(2)}) copy-start(f32[16,128]{0,1:T(8,128)} %copy.23) | copy-start | bytes 24580
  16.9 34.5 %collective-permute-start.3 = (bf16[16,128,128]{2,1,0:T(8,128)(2,1)}, bf16[16,128,128]{2,1,0:T(8,128)(2,1)S(1)}, u32[]{:S(2)}, u32[]{:S(2)}) collective-permute-start(bf16[16,128,128]{2,1,0:T(8,128)(2,1)} %shard_map.114), channel_id=1, source_target_pairs={{0,2},{2,4},{4,6},{6,8},{8,10},{10,12},{12,14},{1,3},{3,5},{5,7},{... | collective-permute-start | bytes 1572872 | tf_op jit(solution)/shard_map/ppermute | solution.py:18
  20.0 31.3 %collective-permute-start.4 = (bf16[16,128,128]{2,1,0:T(8,128)(2,1)}, bf16[16,128,128]{2,1,0:T(8,128)(2,1)S(1)}, u32[]{:S(2)}, u32[]{:S(2)}) collective-permute-start(bf16[16,128,128]{2,1,0:T(8,128)(2,1)} %shard_map.114), channel_id=1, source_target_pairs={{0,4},{2,6},{4,8},{6,10},{8,12},{10,14},{1,5},{3,7},{5,9},{7,11},{... | collective-permute-start | bytes 1572872 | tf_op jit(solution)/shard_map/ppermute | solution.py:18
  28.3 19.8 %collective-permute-start.2 = (bf16[1040,128]{1,0:T(8,128)(2,1)S(1)}, bf16[1040,128]{1,0:T(8,128)(2,1)S(1)}, u32[]{:S(2)}, u32[]{:S(2)}) collective-permute-start(bf16[1040,128]{1,0:T(8,128)(2,1)S(1)} %pad_maximum_fusion), channel_id=1, source_target_pairs={{0,4},{2,6},{4,8},{6,10},{8,12},{10,14},{1,5},{3,7},{5,9},{7,11},{... | collective-permute-start | bytes 798728 | tf_op jit(solution)/shard_map/ppermute | solution.py:18
  52.7 13.3 %collective-permute-start.5 = (bf16[16,128,128]{2,1,0:T(8,128)(2,1)S(1)}, bf16[16,128,128]{2,1,0:T(8,128)(2,1)S(1)}, u32[]{:S(2)}, u32[]{:S(2)}) collective-permute-start(bf16[16,128,128]{2,1,0:T(8,128)(2,1)S(1)} %get-tuple-element.10), channel_id=1, source_target_pairs={{0,4},{2,6},{4,8},{6,10},{8,12},{10,14},{1,5},{3,7},{5,9},{7,11},{... | collective-permute-start | bytes 1572872 | tf_op jit(solution)/shard_map/ppermute | solution.py:18
  55.9 22.2 %copy-start.1 = (bf16[128,2048]{1,0:T(8,128)(2,1)S(1)}, bf16[128,2048]{1,0:T(8,128)(2,1)}, u32[]{:S(2)}) copy-start(bf16[128,2048]{1,0:T(8,128)(2,1)} %param.13) | copy-start | bytes 1572868
  55.9 22.2 %copy-start.4 = (f32[2048]{0:T(1024)S(1)}, f32[2048]{0:T(1024)}, u32[]{:S(2)}) copy-start(f32[2048]{0:T(1024)} %param.15) | copy-start | bytes 24580
  66.0 0.8 copy-start.2
